TPU v7x, 32 devices: a whole 2x2x4 slice. The times are simulated.
32 devices in a mesh: reel: 2 (over y), frame: 8 (over z, x), band: 1, chan: 2 (over core).
Axes of the slice: x: 2, y: 2, z: 4, core: 2. Of those that a mesh axis runs over, the one named last changes fastest.
Arguments:
- embed: bfloat16 [64, 256, 256], P(('reel', 'frame'), 'band', 'chan'), parts along dimension 0, may hold values from -6 to 6, as said below
- values: bfloat16 [64, 256, 256], P(('reel', 'frame'), 'band', 'chan'), parts along dimension 0, may hold values from -6 to 6
- match_frame: int32 [64, 2, 16], P(('reel', 'frame'), 'band'), parts along dimension 0, may hold values from -8 to 8, as said below
- match_block: int32 [64, 2, 16], P(('reel', 'frame'), 'band'), parts along dimension 0, may hold values from 0 to 1, as said below
- block_counts: int32 [64], P(('reel', 'frame')), parts along dimension 0, may hold values from 1 to 2, as said below
Outputs:
- denoised: bfloat16 [64, 256, 256], P(('reel', 'frame'), 'band', 'chan'), parts along dimension 0
There are 2 independent parts, one for each index of `reel`. A program takes and returns all parts, laid end to end along the dimension named above; each array names one. Nothing has to cross between parts.
Inputs may be any that keep to these rules, and one draw needn't show every extreme that they name: `embed`: floats of order one. f + match_frame[f, q, k] is a frame of the segment; entries 0 and 1 of every list are the farthest backward and the farthest forward offsets within 8 that the segment allows. `match_block`: block q belongs to band q // 2; its list names blocks of that band or the block just before or just after the band. `block_counts`: some frame has all its blocks active.
All inputs are finite; a program needn't handle non-finite values.
Results may differ from a plain program's by a relative error of at most 0.0035.
Values may be sent and summed in bfloat16 or wider, within the bound.
No kernel may reach another device: no remote copies, remote signals or barrier semaphores. Data moves between devices by JAX's collectives and lax.ppermute only.
A program may use at most 64 MiB of HBM per device.

v0:
```python
import math

import jax
import jax.numpy as jnp
from jax import lax
from jax.sharding import PartitionSpec as P

W = 256
BLOCK = 128
K = 16
HOPS = 2


def with_halo(x, sides, width):
    for axis, dim in sides:
        size, length = (lax.axis_size(axis), x.shape[dim])
        up = [(i, (i + 1) % size) for i in range(size - 1)]
        down = [(j, i) for i, j in up]
        last = lax.slice_in_dim(x, length - width, length, axis=dim)
        initial = lax.slice_in_dim(x, 0, width, axis=dim)
        before = lax.ppermute(last, axis, up)
        after = lax.ppermute(initial, axis, down)
        x = jnp.concatenate([before, x, after], axis=dim)
    return x


def passed_along(block, axis, distance):
    devices = range(lax.axis_size(axis))
    route = [(i - distance, i) for i in devices if i - distance in devices]
    return lax.ppermute(block, axis, route)


def shards(embed, values, match_frame, match_block, block_counts):
    frames = embed.shape[0]
    band_rows = embed.shape[1]
    half_width = embed.shape[2]
    blocks = band_rows // BLOCK
    band_index = lax.axis_index("band")
    full_own = lax.all_gather(embed, "chan", axis=2, tiled=True)
    features = jnp.concatenate([full_own, values], axis=2)
    rimmed = with_halo(features, (("band", 1),), BLOCK)
    lower = []
    upper = []
    for distance in range(1, HOPS + 1):
        for toward in (1, -1):
            shifted = passed_along(rimmed, "frame", toward * distance)
            if toward > 0:
                lower.append(shifted)
            else:
                upper.append(shifted)
    window = jnp.concatenate(lower[::-1] + [rimmed] + upper, axis=0)
    window_frames = window.shape[0]
    key_embed = window[:, :, :W]
    key_values = window[:, :, W:]
    key_embed = key_embed.reshape(window_frames, blocks + 2, BLOCK, W)
    key_values = key_values.reshape(window_frames, blocks + 2, BLOCK, half_width)
    score_scale = 1.0 / math.sqrt(W)
    center = HOPS * frames
    block_ids = jnp.arange(blocks, dtype=jnp.int32)

    def visit(state_pair, inputs):
        numer, masses = state_pair
        own_frame, offsets, targets, limit = inputs
        rows_idx = center + own_frame + offsets
        col_idx = targets - band_index * blocks + 1
        queries = lax.dynamic_index_in_dim(key_embed, center + own_frame, 0, keepdims=False)[
            1 : blocks + 1
        ]
        key_feat = key_embed[rows_idx, col_idx]
        key_vals = key_values[rows_idx, col_idx].reshape(blocks, K * BLOCK, half_width)
        score = (
            jnp.einsum("bid,bkjd->bikj", queries, key_feat, preferred_element_type=jnp.float32)
            * score_scale
        )
        score = score.reshape(blocks, BLOCK, K * BLOCK)
        peak = jnp.max(score, axis=-1, keepdims=True)
        exponent = jnp.exp(score - peak)
        prob = exponent / jnp.sum(exponent, axis=-1, keepdims=True)
        attention = prob.astype(jnp.bfloat16)
        estimate = jnp.einsum(
            "bin,bnc->bic", attention, key_vals, preferred_element_type=jnp.float32
        ).astype(jnp.bfloat16)
        active = band_index * blocks + block_ids < limit
        masked = attention * active.astype(jnp.bfloat16)[:, None, None]
        contrib = jnp.einsum("bin,bic->bnc", masked, estimate, preferred_element_type=jnp.float32)
        contrib = contrib.reshape(blocks, K, BLOCK, half_width)
        weights_sum = jnp.sum(prob * active.astype(jnp.float32)[:, None, None], axis=1).reshape(
            blocks, K, BLOCK
        )
        numer = numer.at[rows_idx, col_idx].add(contrib)
        masses = masses.at[rows_idx, col_idx].add(weights_sum)
        return ((numer, masses), None)

    numer_init = jnp.zeros((window_frames, blocks + 2, BLOCK, half_width), jnp.float32)
    mass_init = jnp.zeros((window_frames, blocks + 2, BLOCK), jnp.float32)
    scan_inputs = (jnp.arange(frames, dtype=jnp.int32), match_frame, match_block, block_counts)
    (numerator, masses), unused = lax.scan(visit, (numer_init, mass_init), scan_inputs)

    def slab_of(array, offset):
        return array[(offset + HOPS) * frames : (offset + HOPS + 1) * frames]

    own_numer = slab_of(numerator, 0)
    own_mass = slab_of(masses, 0)
    for distance in range(1, HOPS + 1):
        for toward in (1, -1):
            outgoing = (slab_of(numerator, toward * distance), slab_of(masses, toward * distance))
            arrived = (
                passed_along(outgoing[0].astype(jnp.bfloat16), "frame", toward * distance).astype(
                    jnp.float32
                ),
                passed_along(outgoing[1].astype(jnp.bfloat16), "frame", toward * distance).astype(
                    jnp.float32
                ),
            )
            own_numer = own_numer + arrived[0]
            own_mass = own_mass + arrived[1]
    for toward in (1, -1):
        rim_block = blocks + 1 if toward > 0 else 0
        target_block = 1 if toward > 0 else blocks
        arrived = (
            passed_along(own_numer[:, rim_block].astype(jnp.bfloat16), "band", toward).astype(
                jnp.float32
            ),
            passed_along(own_mass[:, rim_block].astype(jnp.bfloat16), "band", toward).astype(
                jnp.float32
            ),
        )
        own_numer = own_numer.at[:, target_block].add(arrived[0])
        own_mass = own_mass.at[:, target_block].add(arrived[1])
    value_blocks = values.reshape(frames, blocks, BLOCK, half_width).astype(jnp.float32)
    result = (own_numer[:, 1 : blocks + 1] + value_blocks) / (
        own_mass[:, 1 : blocks + 1][..., None] + 1.0
    )
    return result.reshape(frames, band_rows, half_width).astype(jnp.bfloat16)


def solution(mesh):
    placed = (
        P(("reel", "frame"), "band", "chan"),
        P(("reel", "frame"), "band", "chan"),
        P(("reel", "frame"), "band", None),
        P(("reel", "frame"), "band", None),
        P(("reel", "frame")),
    )
    return jax.shard_map(
        shards,
        mesh=mesh,
        in_specs=placed,
        out_specs=P(("reel", "frame"), "band", "chan"),
        check_vma=False,
    )
```

profile of v0, /device:TPU:22, one launch (start us, length us, event | category | flops | bytes accessed | tf_op | source)
XLA Modules:
  0.0 260.8 jit_solution(12146853140516965993)
XLA Ops:
  0.0 2.4 all_gather.3
  5.1 3.5 %collective-permute-start.2 = (bf16[4,512,384]{2,1,0:T(8,128)(2,1)S(1)}, bf16[4,512,384]{2,1,0:T(8,128)(2,1)}, u32[]{:S(2)}, u32[]{:S(2)}) collective-permute-start(bf16[4,512,384]{2,1,0:T(8,128)(2,1)S(1)} %pad_maximum_fusion), channel_id=1, source_target_pairs={{0,4},{2,6},{4,8},{6,10},{8,12},{10,14},{1,5},{3,7},{5,9},{7,11},{... | collective-permute-start | bytes 4718600 | tf_op jit(solution)/shard_map/ppermute | solution.py:30
  8.6 1.9 collective-permute-start.3
  10.5 3.9 %collective-permute-start.4 = (bf16[4,512,384]{2,1,0:T(8,128)(2,1)S(1)}, bf16[4,512,384]{2,1,0:T(8,128)(2,1)}, u32[]{:S(2)}, u32[]{:S(2)}) collective-permute-start(bf16[4,512,384]{2,1,0:T(8,128)(2,1)S(1)} %pad_maximum_fusion), channel_id=1, source_target_pairs={{2,0},{4,2},{6,4},{8,6},{10,8},{12,10},{14,12},{3,1},{5,3},{7,5},{... | collective-permute-start | bytes 4718600 | tf_op jit(solution)/shard_map/ppermute | solution.py:30
  14.5 2.4 collective-permute-start.5
  16.8 27.5 %collective-permute-done.2 = bf16[4,512,384]{2,1,0:T(8,128)(2,1)} collective-permute-done((bf16[4,512,384]{2,1,0:T(8,128)(2,1)S(1)}, bf16[4,512,384]{2,1,0:T(8,128)(2,1)}, u32[]{:S(2)}, u32[]{:S(2)}) %collective-permute-start.2) | collective-permute-done | bytes 1572896 | tf_op jit(solution)/shard_map/ppermute | solution.py:30
  45.9 34.5 %collective-permute-done.3 = bf16[4,512,384]{2,1,0:T(8,128)(2,1)} collective-permute-done((bf16[4,512,384]{2,1,0:T(8,128)(2,1)S(1)}, bf16[4,512,384]{2,1,0:T(8,128)(2,1)}, u32[]{:S(2)}, u32[]{:S(2)}) %collective-permute-start.3) | collective-permute-done | bytes 1572896 | tf_op jit(solution)/shard_map/ppermute | solution.py:30
  86.0 2.7 %slice.216 = bf16[20,512,256]{2,1,0:T(8,128)(2,1)} slice(bf16[20,512,384]{2,1,0:T(8,128)(2,1)S(1)} %constant_dynamic-update-slice_fusion.2), slice={[0:20], [0:512], [0:256]} | slice | bytes 10485760 | tf_op jit(solution)/shard_map/slice | solution.py:53
  88.7 2.0 slice.217
  90.7 3.0 %broadcast_in_dim.4 = f32[20,4,128,128]{3,2,1,0:T(8,128)} broadcast(f32[]{:T(128)} %constant.188.clone.1), dimensions={} | broadcast | bytes 5242884 | tf_op jit(solution)/shard_map/broadcast_in_dim | solution.py:94
  93.7 113.4 %while.20 = (s32[]{:T(128)}, f32[20,4,128,128]{3,2,1,0:T(8,128)}, f32[20,4,128]{2,1,0:T(4,128)S(1)}, s32[4]{0:T(128)S(1)}, s32[4,2,16]{2,1,0:T(2,128)}, /*index=...) while((s32[]{:T(128)}, f32[20,4,128,128]{3,2,1,0:T(8,128)}, ...), condition=%wide.region_6.7_spmd.clone, body=%wide.region_0.6_spmd.clone.sunk | while | flops 543719424 | bytes 28517636 | solution.py:97
  96.5 4.5 %gather_fusion = bf16[32,128,256]{2,1,0:T(8,128)(2,1)} fusion(bf16[20,4,128,256]{3,2,1,0:T(8,128)(2,1)} %get-tuple-element.376, s32[32]{0:T(128)S(1)} %reshape.326), kind=kCustom, calls=%fused_computation.clone.clone.1 | custom fusion | bytes 4194560 | tf_op jit(solution)/shard_map/while/body/eval_jaxpr/gather | solution.py:69
  100.9 2.4 fusion.41
  104.0 3.4 %gather_fusion.1 = bf16[32,128,128]{2,1,0:T(8,128)(2,1)} fusion(bf16[20,4,128,128]{3,2,1,0:T(8,128)(2,1)} %get-tuple-element.378, s32[32]{0:T(128)S(1)} %reshape.326), kind=kCustom, calls=%fused_computation.1.clone.clone.1 | custom fusion | bytes 2097408 | tf_op jit(solution)/shard_map/while/body/eval_jaxpr/gather | solution.py:70
  108.6 3.4 %fusion.44 = f32[2,2048,128]{2,1,0:T(8,128)} fusion(bf16[2,128,2048]{1,2,0:T(8,128)(2,1)S(1)} %fusion.43, bf16[2,2048,128]{2,1,0:T(8,128)(2,1)} %bitcast.106, bf16[2]{0:T(256)(128)(2,1)S(1)} %get-tuple-element.340), kind=kOutput, calls=%fused_computation.14.clone.1 | convolution fusion | flops 268992512 | bytes 4194308 | tf_op jit(solution)/shard_map/while/body/eval_jaxpr/bin,bic->bnc/dot_general | solution.py:85
  112.1 7.2 %scatter_fusion = f32[20,4,128,128]{3,2,1,0:T(8,128)} fusion(f32[20,4,128,128]{3,2,1,0:T(8,128)} %get-tuple-element.357, s32[32]{0:T(128)S(1)} %reshape.325, f32[32,128,128]{2,1,0:T(8,128)} %bitcast.104), kind=kCustom, calls=%fused_computation.2.clone.clone.1 | custom fusion | flops 524288 | bytes 6291712 | tf_op jit(solution)/shard_map/while/body/eval_jaxpr/scatter-add | solution.py:90
  120.0 2.1 scatter_fusion.1
  124.8 4.5 %gather_fusion = bf16[32,128,256]{2,1,0:T(8,128)(2,1)} fusion(bf16[20,4,128,256]{3,2,1,0:T(8,128)(2,1)} %get-tuple-element.376, s32[32]{0:T(128)S(1)} %reshape.326), kind=kCustom, calls=%fused_computation.clone.clone.1 | custom fusion | bytes 4194560 | tf_op jit(solution)/shard_map/while/body/eval_jaxpr/gather | solution.py:69
  129.3 2.4 fusion.41
  132.3 3.4 %gather_fusion.1 = bf16[32,128,128]{2,1,0:T(8,128)(2,1)} fusion(bf16[20,4,128,128]{3,2,1,0:T(8,128)(2,1)} %get-tuple-element.378, s32[32]{0:T(128)S(1)} %reshape.326), kind=kCustom, calls=%fused_computation.1.clone.clone.1 | custom fusion | bytes 2097408 | tf_op jit(solution)/shard_map/while/body/eval_jaxpr/gather | solution.py:70
  136.9 3.4 %fusion.44 = f32[2,2048,128]{2,1,0:T(8,128)} fusion(bf16[2,128,2048]{1,2,0:T(8,128)(2,1)S(1)} %fusion.43, bf16[2,2048,128]{2,1,0:T(8,128)(2,1)} %bitcast.106, bf16[2]{0:T(256)(128)(2,1)S(1)} %get-tuple-element.340), kind=kOutput, calls=%fused_computation.14.clone.1 | convolution fusion | flops 268992512 | bytes 4194308 | tf_op jit(solution)/shard_map/while/body/eval_jaxpr/bin,bic->bnc/dot_general | solution.py:85
  140.4 7.2 %scatter_fusion = f32[20,4,128,128]{3,2,1,0:T(8,128)} fusion(f32[20,4,128,128]{3,2,1,0:T(8,128)} %get-tuple-element.357, s32[32]{0:T(128)S(1)} %reshape.325, f32[32,128,128]{2,1,0:T(8,128)} %bitcast.104), kind=kCustom, calls=%fused_computation.2.clone.clone.1 | custom fusion | flops 524288 | bytes 6291712 | tf_op jit(solution)/shard_map/while/body/eval_jaxpr/scatter-add | solution.py:90
  148.4 2.1 scatter_fusion.1
  153.2 4.5 %gather_fusion = bf16[32,128,256]{2,1,0:T(8,128)(2,1)} fusion(bf16[20,4,128,256]{3,2,1,0:T(8,128)(2,1)} %get-tuple-element.376, s32[32]{0:T(128)S(1)} %reshape.326), kind=kCustom, calls=%fused_computation.clone.clone.1 | custom fusion | bytes 4194560 | tf_op jit(solution)/shard_map/while/body/eval_jaxpr/gather | solution.py:69
  157.6 2.4 fusion.41
  160.7 3.4 %gather_fusion.1 = bf16[32,128,128]{2,1,0:T(8,128)(2,1)} fusion(bf16[20,4,128,128]{3,2,1,0:T(8,128)(2,1)} %get-tuple-element.378, s32[32]{0:T(128)S(1)} %reshape.326), kind=kCustom, calls=%fused_computation.1.clone.clone.1 | custom fusion | bytes 2097408 | tf_op jit(solution)/shard_map/while/body/eval_jaxpr/gather | solution.py:70
  165.3 3.4 %fusion.44 = f32[2,2048,128]{2,1,0:T(8,128)} fusion(bf16[2,128,2048]{1,2,0:T(8,128)(2,1)S(1)} %fusion.43, bf16[2,2048,128]{2,1,0:T(8,128)(2,1)} %bitcast.106, bf16[2]{0:T(256)(128)(2,1)S(1)} %get-tuple-element.340), kind=kOutput, calls=%fused_computation.14.clone.1 | convolution fusion | flops 268992512 | bytes 4194308 | tf_op jit(solution)/shard_map/while/body/eval_jaxpr/bin,bic->bnc/dot_general | solution.py:85
  168.8 7.2 %scatter_fusion = f32[20,4,128,128]{3,2,1,0:T(8,128)} fusion(f32[20,4,128,128]{3,2,1,0:T(8,128)} %get-tuple-element.357, s32[32]{0:T(128)S(1)} %reshape.325, f32[32,128,128]{2,1,0:T(8,128)} %bitcast.104), kind=kCustom, calls=%fused_computation.2.clone.clone.1 | custom fusion | flops 524288 | bytes 6291712 | tf_op jit(solution)/shard_map/while/body/eval_jaxpr/scatter-add | solution.py:90
  176.7 2.1 scatter_fusion.1
  181.5 4.5 %gather_fusion = bf16[32,128,256]{2,1,0:T(8,128)(2,1)} fusion(bf16[20,4,128,256]{3,2,1,0:T(8,128)(2,1)} %get-tuple-element.376, s32[32]{0:T(128)S(1)} %reshape.326), kind=kCustom, calls=%fused_computation.clone.clone.1 | custom fusion | bytes 4194560 | tf_op jit(solution)/shard_map/while/body/eval_jaxpr/gather | solution.py:69
  186.0 2.4 fusion.41
  189.0 3.4 %gather_fusion.1 = bf16[32,128,128]{2,1,0:T(8,128)(2,1)} fusion(bf16[20,4,128,128]{3,2,1,0:T(8,128)(2,1)} %get-tuple-element.378, s32[32]{0:T(128)S(1)} %reshape.326), kind=kCustom, calls=%fused_computation.1.clone.clone.1 | custom fusion | bytes 2097408 | tf_op jit(solution)/shard_map/while/body/eval_jaxpr/gather | solution.py:70
  193.7 3.4 %fusion.44 = f32[2,2048,128]{2,1,0:T(8,128)} fusion(bf16[2,128,2048]{1,2,0:T(8,128)(2,1)S(1)} %fusion.43, bf16[2,2048,128]{2,1,0:T(8,128)(2,1)} %bitcast.106, bf16[2]{0:T(256)(128)(2,1)S(1)} %get-tuple-element.340), kind=kOutput, calls=%fused_computation.14.clone.1 | convolution fusion | flops 268992512 | bytes 4194308 | tf_op jit(solution)/shard_map/while/body/eval_jaxpr/bin,bic->bnc/dot_general | solution.py:85
  197.1 7.2 %scatter_fusion = f32[20,4,128,128]{3,2,1,0:T(8,128)} fusion(f32[20,4,128,128]{3,2,1,0:T(8,128)} %get-tuple-element.357, s32[32]{0:T(128)S(1)} %reshape.325, f32[32,128,128]{2,1,0:T(8,128)} %bitcast.104), kind=kCustom, calls=%fused_computation.2.clone.clone.1 | custom fusion | flops 524288 | bytes 6291712 | tf_op jit(solution)/shard_map/while/body/eval_jaxpr/scatter-add | solution.py:90
  205.1 2.1 scatter_fusion.1
  207.2 3.0 %convert.37 = bf16[20,4,128,128]{3,2,1,0:T(8,128)(2,1)S(1)} convert(f32[20,4,128,128]{3,2,1,0:T(8,128)} %get-tuple-element.219) | non-fusion elementwise | flops 1310720 | bytes 7864320 | tf_op jit(solution)/shard_map/convert.16
  211.4 2.6 %collective-permute-start.6 = (bf16[4,4,128,128]{3,2,1,0:T(8,128)(2,1)}, bf16[4,4,128,128]{3,2,1,0:T(8,128)(2,1)S(1)}, u32[]{:S(2)}, u32[]{:S(2)}) collective-permute-start(bf16[4,4,128,128]{3,2,1,0:T(8,128)(2,1)} %get-tuple-element.265), channel_id=1, source_target_pairs={{0,2},{2,4},{4,6},{6,8},{8,10},{10,12},{12,14},{1,3},{3,5},{5,7},{... | collective-permute-start | bytes 1572872 | tf_op jit(solution)/shard_map/ppermute | solution.py:30
  214.0 3.2 %collective-permute-start.7 = (bf16[4,4,128,128]{3,2,1,0:T(8,128)(2,1)}, bf16[4,4,128,128]{3,2,1,0:T(8,128)(2,1)S(1)}, u32[]{:S(2)}, u32[]{:S(2)}) collective-permute-start(bf16[4,4,128,128]{3,2,1,0:T(8,128)(2,1)} %get-tuple-element.268), channel_id=1, source_target_pairs={{2,0},{4,2},{6,4},{8,6},{10,8},{12,10},{14,12},{3,1},{5,3},{7,5},{... | collective-permute-start | bytes 1572872 | tf_op jit(solution)/shard_map/ppermute | solution.py:30
  217.2 1.9 collective-permute-start.8
  219.2 3.9 %collective-permute-start.9 = (bf16[4,4,128,128]{3,2,1,0:T(8,128)(2,1)S(1)}, bf16[4,4,128,128]{3,2,1,0:T(8,128)(2,1)}, u32[]{:S(2)}, u32[]{:S(2)}) collective-permute-start(bf16[4,4,128,128]{3,2,1,0:T(8,128)(2,1)S(1)} %get-tuple-element.266), channel_id=1, source_target_pairs={{4,0},{6,2},{8,4},{10,6},{12,8},{14,10},{5,1},{7,3},{9,5},{11,7},{... | collective-permute-start | bytes 1572872 | tf_op jit(solution)/shard_map/ppermute | solution.py:30
  223.1 4.7 %collective-permute-start.12 = (bf16[4,4,128]{2,1,0:T(4,128)(2,1)S(1)}, bf16[4,4,128]{2,1,0:T(4,128)(2,1)S(1)}, u32[]{:S(2)}, u32[]{:S(2)}) collective-permute-start(bf16[4,4,128]{2,1,0:T(4,128)(2,1)S(1)} %get-tuple-element.271), channel_id=1, source_target_pairs={{0,2},{2,4},{4,6},{6,8},{8,10},{10,12},{12,14},{1,3},{3,5},{5,7},{... | collective-permute-start | bytes 12296 | tf_op jit(solution)/shard_map/ppermute | solution.py:30
  227.8 9.8 %collective-permute-done.12 = bf16[4,4,128]{2,1,0:T(4,128)(2,1)S(1)} collective-permute-done((bf16[4,4,128]{2,1,0:T(4,128)(2,1)S(1)}, bf16[4,4,128]{2,1,0:T(4,128)(2,1)S(1)}, u32[]{:S(2)}, u32[]{:S(2)}) %collective-permute-start.12) | collective-permute-done | bytes 4128 | tf_op jit(solution)/shard_map/ppermute | solution.py:30
  237.6 4.1 %collective-permute-start.13 = (bf16[4,4,128]{2,1,0:T(4,128)(2,1)S(1)}, bf16[4,4,128]{2,1,0:T(4,128)(2,1)S(1)}, u32[]{:S(2)}, u32[]{:S(2)}) collective-permute-start(bf16[4,4,128]{2,1,0:T(4,128)(2,1)S(1)} %get-tuple-element.274), channel_id=1, source_target_pairs={{2,0},{4,2},{6,4},{8,6},{10,8},{12,10},{14,12},{3,1},{5,3},{7,5},{... | collective-permute-start | bytes 12296 | tf_op jit(solution)/shard_map/ppermute | solution.py:30
  241.8 2.2 collective-permute-done.13
  244.0 1.9 collective-permute-start.14
  245.9 3.6 %collective-permute-done.14 = bf16[4,4,128]{2,1,0:T(4,128)(2,1)S(1)} collective-permute-done((bf16[4,4,128]{2,1,0:T(4,128)(2,1)S(1)}, bf16[4,4,128]{2,1,0:T(4,128)(2,1)S(1)}, u32[]{:S(2)}, u32[]{:S(2)}) %collective-permute-start.14) | collective-permute-done | bytes 4128 | tf_op jit(solution)/shard_map/ppermute | solution.py:30
  249.5 2.7 %collective-permute-start.15 = (bf16[4,4,128]{2,1,0:T(4,128)(2,1)S(1)}, bf16[4,4,128]{2,1,0:T(4,128)(2,1)S(1)}, u32[]{:S(2)}, u32[]{:S(2)}) collective-permute-start(bf16[4,4,128]{2,1,0:T(4,128)(2,1)S(1)} %get-tuple-element.272), channel_id=1, source_target_pairs={{4,0},{6,2},{8,4},{10,6},{12,8},{14,10},{5,1},{7,3},{9,5},{11,7},{... | collective-permute-start | bytes 12296 | tf_op jit(solution)/shard_map/ppermute | solution.py:30
  252.2 2.8 %collective-permute-done.15 = bf16[4,4,128]{2,1,0:T(4,128)(2,1)S(1)} collective-permute-done((bf16[4,4,128]{2,1,0:T(4,128)(2,1)S(1)}, bf16[4,4,128]{2,1,0:T(4,128)(2,1)S(1)}, u32[]{:S(2)}, u32[]{:S(2)}) %collective-permute-start.15) | collective-permute-done | bytes 4128 | tf_op jit(solution)/shard_map/ppermute | solution.py:30
  (90 shorter events, 32.8 us)
Async XLA Ops:
  3.5 1.4 collective-permute-start
  4.2 0.7 collective-permute-start.1
  5.1 39.2 %collective-permute-start.2 = (bf16[4,512,384]{2,1,0:T(8,128)(2,1)S(1)}, bf16[4,512,384]{2,1,0:T(8,128)(2,1)}, u32[]{:S(2)}, u32[]{:S(2)}) collective-permute-start(bf16[4,512,384]{2,1,0:T(8,128)(2,1)S(1)} %pad_maximum_fusion), channel_id=1, source_target_pairs={{0,4},{2,6},{4,8},{6,10},{8,12},{10,14},{1,5},{3,7},{5,9},{7,11},{... | collective-permute-start | bytes 4718600 | tf_op jit(solution)/shard_map/ppermute | solution.py:30
  8.6 71.9 %collective-permute-start.3 = (bf16[4,512,384]{2,1,0:T(8,128)(2,1)S(1)}, bf16[4,512,384]{2,1,0:T(8,128)(2,1)}, u32[]{:S(2)}, u32[]{:S(2)}) collective-permute-start(bf16[4,512,384]{2,1,0:T(8,128)(2,1)S(1)} %pad_maximum_fusion), channel_id=1, source_target_pairs={{0,2},{2,4},{4,6},{6,8},{8,10},{10,12},{12,14},{1,3},{3,5},{5,7},{... | collective-permute-start | bytes 4718600 | tf_op jit(solution)/shard_map/ppermute | solution.py:30
  10.5 72.0 %collective-permute-start.4 = (bf16[4,512,384]{2,1,0:T(8,128)(2,1)S(1)}, bf16[4,512,384]{2,1,0:T(8,128)(2,1)}, u32[]{:S(2)}, u32[]{:S(2)}) collective-permute-start(bf16[4,512,384]{2,1,0:T(8,128)(2,1)S(1)} %pad_maximum_fusion), channel_id=1, source_target_pairs={{2,0},{4,2},{6,4},{8,6},{10,8},{12,10},{14,12},{3,1},{5,3},{7,5},{... | collective-permute-start | bytes 4718600 | tf_op jit(solution)/shard_map/ppermute | solution.py:30
  14.5 69.8 %collective-permute-start.5 = (bf16[4,512,384]{2,1,0:T(8,128)(2,1)S(1)}, bf16[4,512,384]{2,1,0:T(8,128)(2,1)}, u32[]{:S(2)}, u32[]{:S(2)}) collective-permute-start(bf16[4,512,384]{2,1,0:T(8,128)(2,1)S(1)} %pad_maximum_fusion), channel_id=1, source_target_pairs={{4,0},{6,2},{8,4},{10,6},{12,8},{14,10},{5,1},{7,3},{9,5},{11,7},{... | collective-permute-start | bytes 4718600 | tf_op jit(solution)/shard_map/ppermute | solution.py:30
  90.7 3.0 %copy-start.1 = (s32[4]{0:T(128)S(1)}, s32[4]{0:T(128)}, u32[]{:S(2)}) copy-start(s32[4]{0:T(128)} %param.19) | copy-start | bytes 52
  211.4 45.1 %collective-permute-start.6 = (bf16[4,4,128,128]{3,2,1,0:T(8,128)(2,1)}, bf16[4,4,128,128]{3,2,1,0:T(8,128)(2,1)S(1)}, u32[]{:S(2)}, u32[]{:S(2)}) collective-permute-start(bf16[4,4,128,128]{3,2,1,0:T(8,128)(2,1)} %get-tuple-element.265), channel_id=1, source_target_pairs={{0,2},{2,4},{4,6},{6,8},{8,10},{10,12},{12,14},{1,3},{3,5},{5,7},{... | collective-permute-start | bytes 1572872 | tf_op jit(solution)/shard_map/ppermute | solution.py:30
  214.0 42.4 %collective-permute-start.7 = (bf16[4,4,128,128]{3,2,1,0:T(8,128)(2,1)}, bf16[4,4,128,128]{3,2,1,0:T(8,128)(2,1)S(1)}, u32[]{:S(2)}, u32[]{:S(2)}) collective-permute-start(bf16[4,4,128,128]{3,2,1,0:T(8,128)(2,1)} %get-tuple-element.268), channel_id=1, source_target_pairs={{2,0},{4,2},{6,4},{8,6},{10,8},{12,10},{14,12},{3,1},{5,3},{7,5},{... | collective-permute-start | bytes 1572872 | tf_op jit(solution)/shard_map/ppermute | solution.py:30
  217.2 39.3 %collective-permute-start.8 = (bf16[4,4,128,128]{3,2,1,0:T(8,128)(2,1)S(1)}, bf16[4,4,128,128]{3,2,1,0:T(8,128)(2,1)S(1)}, u32[]{:S(2)}, u32[]{:S(2)}) collective-permute-start(bf16[4,4,128,128]{3,2,1,0:T(8,128)(2,1)S(1)} %get-tuple-element.267), channel_id=1, source_target_pairs={{0,4},{2,6},{4,8},{6,10},{8,12},{10,14},{1,5},{3,7},{5,9},{7,11},{... | collective-permute-start | bytes 1572872 | tf_op jit(solution)/shard_map/ppermute | solution.py:30
  219.2 37.3 %collective-permute-start.9 = (bf16[4,4,128,128]{3,2,1,0:T(8,128)(2,1)S(1)}, bf16[4,4,128,128]{3,2,1,0:T(8,128)(2,1)}, u32[]{:S(2)}, u32[]{:S(2)}) collective-permute-start(bf16[4,4,128,128]{3,2,1,0:T(8,128)(2,1)S(1)} %get-tuple-element.266), channel_id=1, source_target_pairs={{4,0},{6,2},{8,4},{10,6},{12,8},{14,10},{5,1},{7,3},{9,5},{11,7},{... | collective-permute-start | bytes 1572872 | tf_op jit(solution)/shard_map/ppermute | solution.py:30
  223.1 14.5 %collective-permute-start.12 = (bf16[4,4,128]{2,1,0:T(4,128)(2,1)S(1)}, bf16[4,4,128]{2,1,0:T(4,128)(2,1)S(1)}, u32[]{:S(2)}, u32[]{:S(2)}) collective-permute-start(bf16[4,4,128]{2,1,0:T(4,128)(2,1)S(1)} %get-tuple-element.271), channel_id=1, source_target_pairs={{0,2},{2,4},{4,6},{6,8},{8,10},{10,12},{12,14},{1,3},{3,5},{5,7},{... | collective-permute-start | bytes 12296 | tf_op jit(solution)/shard_map/ppermute | solution.py:30
  237.6 6.4 %collective-permute-start.13 = (bf16[4,4,128]{2,1,0:T(4,128)(2,1)S(1)}, bf16[4,4,128]{2,1,0:T(4,128)(2,1)S(1)}, u32[]{:S(2)}, u32[]{:S(2)}) collective-permute-start(bf16[4,4,128]{2,1,0:T(4,128)(2,1)S(1)} %get-tuple-element.274), channel_id=1, source_target_pairs={{2,0},{4,2},{6,4},{8,6},{10,8},{12,10},{14,12},{3,1},{5,3},{7,5},{... | collective-permute-start | bytes 12296 | tf_op jit(solution)/shard_map/ppermute | solution.py:30
  244.0 5.5 %collective-permute-start.14 = (bf16[4,4,128]{2,1,0:T(4,128)(2,1)S(1)}, bf16[4,4,128]{2,1,0:T(4,128)(2,1)S(1)}, u32[]{:S(2)}, u32[]{:S(2)}) collective-permute-start(bf16[4,4,128]{2,1,0:T(4,128)(2,1)S(1)} %get-tuple-element.273), channel_id=1, source_target_pairs={{0,4},{2,6},{4,8},{6,10},{8,12},{10,14},{1,5},{3,7},{5,9},{7,11},{... | collective-permute-start | bytes 12296 | tf_op jit(solution)/shard_map/ppermute | solution.py:30
  249.5 5.5 %collective-permute-start.15 = (bf16[4,4,128]{2,1,0:T(4,128)(2,1)S(1)}, bf16[4,4,128]{2,1,0:T(4,128)(2,1)S(1)}, u32[]{:S(2)}, u32[]{:S(2)}) collective-permute-start(bf16[4,4,128]{2,1,0:T(4,128)(2,1)S(1)} %get-tuple-element.272), channel_id=1, source_target_pairs={{4,0},{6,2},{8,4},{10,6},{12,8},{14,10},{5,1},{7,3},{9,5},{11,7},{... | collective-permute-start | bytes 12296 | tf_op jit(solution)/shard_map/ppermute | solution.py:30
  255.0 0.7 collective-permute-start.16
  255.8 0.7 collective-permute-start.17
  256.5 3.4 %copy-start = (bf16[4,256,128]{2,1,0:T(8,128)(2,1)S(1)}, bf16[4,256,128]{2,1,0:T(8,128)(2,1)}, u32[]{:S(2)}) copy-start(bf16[4,256,128]{2,1,0:T(8,128)(2,1)} %param.16) | copy-start | bytes 786436
  258.3 0.7 collective-permute-start.10
  259.1 0.7 collective-permute-start.11
where the time goes:
time: 264 us; the launch traced here: 261 us
  waiting for transfers between devices  80.5 us (30%)
  local copies, waits for them, and re-layouts  54.2 us (21%)
  other arithmetic  54.2 us (21%)
  starting transfers between devices  40.7 us (15%)
  matrix products  23.1 us (9%)
  loops' own time  5.21 us (2%)
    ppermute x16, waiting for transfers between devices, passed_along(): return lax.ppermute(block, axis, route)  80.5 us
    ppermute x16, starting transfers between devices, passed_along(): return lax.ppermute(block, axis, route)  39.4 us
    scatter-add x4, other arithmetic, visit(): numer = numer.at[rows_idx, col_idx].add(contrib)  28.8 us
    gather x4, local copies, waits for them, and re-layouts, visit(): key_feat = key_embed[rows_idx, col_idx]  17.9 us
    gather x4, local copies, waits for them, and re-layouts, visit(): key_values[rows_idx, col_idx].reshape(blocks, K * BLOCK, half_width)  13.8 us
    dot_general x4, matrix products, visit(): jnp.einsum('bin,bic->bnc', masked, estimate, preferred_element_type=jnp.f...  13.6 us
    dot_general x4, matrix products, visit(): jnp.einsum('bid,bkjd->bikj', queries, key_feat, preferred_element_type=jn...  9.54 us
    scatter-add x4, other arithmetic, visit(): masses = masses.at[rows_idx, col_idx].add(weights_sum)  8.37 us
  transfers between devices with their start and end apart: 18, of which 6 were waited for; matrix products, arithmetic and copies ran while one was open for 2% of the time, Pallas kernels for 0%

commit v1 on v0

v1 whole, which is shorter than its diff:
```python
import functools
import math

import jax
import jax.numpy as jnp
from jax import lax
from jax.experimental import pallas as pl
from jax.experimental.pallas import tpu as pltpu
from jax.sharding import PartitionSpec as P

W = 256
BLOCK = 128
K = 16
REACH = 8
MASS_ROWS = 16


def with_halo(x, sides, width):
    for axis, dim in sides:
        size, length = (lax.axis_size(axis), x.shape[dim])
        up = [(i, (i + 1) % size) for i in range(size - 1)]
        down = [(j, i) for i, j in up]
        last = lax.slice_in_dim(x, length - width, length, axis=dim)
        initial = lax.slice_in_dim(x, 0, width, axis=dim)
        before = lax.ppermute(last, axis, up)
        after = lax.ppermute(initial, axis, down)
        x = jnp.concatenate([before, x, after], axis=dim)
    return x


def passed_along(block, axis, distance):
    devices = range(lax.axis_size(axis))
    route = [(i - distance, i) for i in devices if i - distance in devices]
    return lax.ppermute(block, axis, route)


def aggregate_kernel(
    slot_ref, act_ref, *refs, slabs, per_slab, center, queries, half, blocks, rimmed, halo
):
    slab_refs = refs[:slabs]
    other_refs = refs[slabs : 2 * slabs]
    own_num_ref, own_mass_ref = refs[2 * slabs : 2 * slabs + 2]
    remote_refs = refs[2 * slabs + 2 : 3 * slabs + 1]
    key_a, key_v, key_b, acc, macc, score_ref, sems = refs[3 * slabs + 1 :]

    copies = []
    for s in range(slabs):
        dst = pl.ds(s * per_slab, per_slab)
        copies.append(
            pltpu.make_async_copy(slab_refs[s].at[:, :, pl.ds(0, half)], key_a.at[dst], sems.at[0, s])
        )
        copies.append(
            pltpu.make_async_copy(slab_refs[s].at[:, :, pl.ds(half, half)], key_v.at[dst], sems.at[1, s])
        )
        copies.append(pltpu.make_async_copy(other_refs[s], key_b.at[dst], sems.at[2, s]))
    for c in copies:
        c.start()
    acc[...] = jnp.zeros(acc.shape, acc.dtype)
    macc[...] = jnp.zeros(macc.shape, macc.dtype)
    for c in copies:
        c.wait()

    score_scale = 1.0 / math.sqrt(W)
    dims_t = (((1,), (1,)), ((), ()))

    def one_query(i, carry):
        q_slot = center + (i // blocks) * rimmed + halo + i % blocks
        qa = key_a[q_slot]
        qb = key_b[q_slot]
        slots = [slot_ref[i * K + k] for k in range(K)]
        for k in range(K):
            s = slots[k]
            part = lax.dot_general(qa, key_a[s], dims_t, preferred_element_type=jnp.float32)
            part = part + lax.dot_general(qb, key_b[s], dims_t, preferred_element_type=jnp.float32)
            score_ref[:, k * BLOCK : (k + 1) * BLOCK] = part * score_scale
        score = score_ref[...]
        peak = jnp.max(score, axis=-1, keepdims=True)
        exponent = jnp.exp(score - peak)
        prob = exponent / jnp.sum(exponent, axis=-1, keepdims=True)
        attention = prob.astype(jnp.bfloat16)
        estimate = jnp.zeros((BLOCK, half), jnp.float32)
        for k in range(K):
            estimate = estimate + jnp.dot(
                attention[:, k * BLOCK : (k + 1) * BLOCK],
                key_v[slots[k]],
                preferred_element_type=jnp.float32,
            )
        estimate = estimate.astype(jnp.bfloat16).astype(jnp.float32)
        active = act_ref[i].astype(jnp.float32)
        masked = (attention.astype(jnp.float32) * active).astype(jnp.bfloat16)
        estimate_t = estimate.T.astype(jnp.bfloat16)
        contrib_t = jnp.dot(estimate_t, masked, preferred_element_type=jnp.float32)
        weights = jnp.sum(prob * active, axis=0, keepdims=True)
        for k in range(K):
            s = slots[k]
            acc[s] = acc[s] + contrib_t[:, k * BLOCK : (k + 1) * BLOCK]
            macc[s] = macc[s] + weights[:, k * BLOCK : (k + 1) * BLOCK]
        return carry

    lax.fori_loop(0, queries, one_query, 0)

    own = pl.ds(center, per_slab)
    own_num_ref[...] = acc[own]
    own_mass_ref[...] = macc[own]
    remote = [s for s in range(slabs) if s * per_slab != center]
    for ref, s in zip(remote_refs, remote):
        rows = pl.ds(s * per_slab, per_slab)
        ref[:, :half, :] = acc[rows].astype(jnp.bfloat16)
        ref[:, half:, :] = jnp.broadcast_to(macc[rows], (per_slab, MASS_ROWS, BLOCK)).astype(
            jnp.bfloat16
        )


def shards(embed, values, match_frame, match_block, block_counts):
    frames = embed.shape[0]
    band_rows = embed.shape[1]
    half = embed.shape[2]
    blocks = band_rows // BLOCK
    hops = -(-REACH // frames)
    band_index = lax.axis_index("band")
    band_size = lax.axis_size("band")
    halo = 1 if band_size > 1 else 0
    chan_size = lax.axis_size("chan")
    chan_swap = [(i, (i + 1) % chan_size) for i in range(chan_size)]

    features = jnp.concatenate([embed, values], axis=2)
    if halo:
        features = with_halo(features, (("band", 1),), BLOCK)
    rimmed_blocks = blocks + 2 * halo
    per_slab = frames * rimmed_blocks
    window = []
    for offset in range(-hops, hops + 1):
        slab = features if offset == 0 else passed_along(features, "frame", -offset)
        window.append(slab.reshape(per_slab, BLOCK, 2 * half))
    others = [
        lax.ppermute(slab[:, :, :half], "chan", chan_swap) for slab in window
    ]
    slabs = len(window)
    center = hops * per_slab

    frame_ids = jnp.arange(frames, dtype=jnp.int32)
    key_rows = (hops * frames + frame_ids[:, None, None] + match_frame) * rimmed_blocks
    key_cols = match_block - band_index * blocks + halo
    slot = jnp.clip(key_rows + key_cols, 0, slabs * per_slab - 1).astype(jnp.int32).reshape(-1)
    block_ids = band_index * blocks + jnp.arange(blocks, dtype=jnp.int32)
    active = (block_ids[None, :] < block_counts[:, None]).astype(jnp.int32)
    queries = frames * blocks

    kernel = functools.partial(
        aggregate_kernel,
        slabs=slabs,
        per_slab=per_slab,
        center=center,
        queries=queries,
        half=half,
        blocks=blocks,
        rimmed=rimmed_blocks,
        halo=halo,
    )
    smem = pl.BlockSpec(memory_space=pltpu.SMEM)
    hbm = pl.BlockSpec(memory_space=pl.ANY)
    vmem = pl.BlockSpec(memory_space=pltpu.VMEM)
    out_shape = [
        jax.ShapeDtypeStruct((per_slab, half, BLOCK), jnp.float32),
        jax.ShapeDtypeStruct((per_slab, 1, BLOCK), jnp.float32),
    ] + [
        jax.ShapeDtypeStruct((per_slab, half + MASS_ROWS, BLOCK), jnp.bfloat16)
        for _ in range(slabs - 1)
    ]
    total = slabs * per_slab
    outs = pl.pallas_call(
        kernel,
        out_shape=out_shape,
        in_specs=[smem, smem] + [hbm] * (2 * slabs),
        out_specs=[vmem] * len(out_shape),
        scratch_shapes=[
            pltpu.VMEM((total, BLOCK, half), jnp.bfloat16),
            pltpu.VMEM((total, BLOCK, half), jnp.bfloat16),
            pltpu.VMEM((total, BLOCK, half), jnp.bfloat16),
            pltpu.VMEM((total, half, BLOCK), jnp.float32),
            pltpu.VMEM((total, 1, BLOCK), jnp.float32),
            pltpu.VMEM((BLOCK, K * BLOCK), jnp.float32),
            pltpu.SemaphoreType.DMA((3, slabs)),
        ],
    )(slot, active.reshape(-1), *window, *others)
    own_num, own_mass = outs[0], outs[1]
    remote = outs[2:]
    offsets = [o for o in range(-hops, hops + 1) if o != 0]
    for offset, outgoing in zip(offsets, remote):
        arrived = passed_along(outgoing, "frame", offset).astype(jnp.float32)
        own_num = own_num + arrived[:, :half, :]
        own_mass = own_mass + arrived[:, half : half + 1, :]
    own_num = own_num.reshape(frames, rimmed_blocks, half, BLOCK)
    own_mass = own_mass.reshape(frames, rimmed_blocks, BLOCK)
    if halo:
        for toward in (1, -1):
            rim_block = blocks + 1 if toward > 0 else 0
            target_block = 1 if toward > 0 else blocks
            arrived = (
                passed_along(own_num[:, rim_block].astype(jnp.bfloat16), "band", toward).astype(
                    jnp.float32
                ),
                passed_along(own_mass[:, rim_block].astype(jnp.bfloat16), "band", toward).astype(
                    jnp.float32
                ),
            )
            own_num = own_num.at[:, target_block].add(arrived[0])
            own_mass = own_mass.at[:, target_block].add(arrived[1])
        own_num = own_num[:, 1 : blocks + 1]
        own_mass = own_mass[:, 1 : blocks + 1]
    numer = jnp.swapaxes(own_num, -1, -2)
    value_blocks = values.reshape(frames, blocks, BLOCK, half).astype(jnp.float32)
    result = (numer + value_blocks) / (own_mass[..., None] + 1.0)
    return result.reshape(frames, band_rows, half).astype(jnp.bfloat16)


def solution(mesh):
    placed = (
        P(("reel", "frame"), "band", "chan"),
        P(("reel", "frame"), "band", "chan"),
        P(("reel", "frame"), "band", None),
        P(("reel", "frame"), "band", None),
        P(("reel", "frame")),
    )
    return jax.shard_map(
        shards,
        mesh=mesh,
        in_specs=placed,
        out_specs=P(("reel", "frame"), "band", "chan"),
        check_vma=False,
    )
```

time: 264 us -> 83.1 us (0.31); the launches traced: 261 us -> 82.7 us
  other arithmetic: 54.2 us -> 0.52 us
  waiting for transfers between devices: 80.5 us -> 29.4 us
  local copies, waits for them, and re-layouts: 54.2 us -> 8.88 us
  matrix products: 23.1 us -> 0 us
  Pallas kernels: 0 us -> 20 us
  starting transfers between devices: 40.7 us -> 23.6 us
  loops' own time: 5.21 us -> 0 us
    ppermute x16 -> x8, waiting for transfers between devices: 80.5 us -> 29.4 us  [passed_along(): return lax.ppermute(block, axis, route)]
    scatter-add x10 -> x0, other arithmetic: 37.3 us -> none  [the longest x4 28.8 us: visit(): numer = numer.at[rows_idx, col_idx].add(contrib)]
    gather x8 -> x0, local copies, waits for them, and re-layouts: 31.6 us -> none  [the longest x4 17.9 us: visit(): key_feat = key_embed[rows_idx, col_idx]]
    dot_general x8 -> x0, matrix products: 23.1 us -> none  [the longest x4 13.6 us: visit(): jnp.einsum('bin,bic->bnc', masked, estimate, preferred_element_type=jnp.f...]
    pallas_call x0 -> x1, Pallas kernels: none -> 20 us  [shards(): pl.pallas_call(kernel, out_shape=out_shape, in_specs=[smem, smem] + [hbm]...]
    ppermute x16 -> x8, starting transfers between devices: 39.4 us -> 23.2 us  [passed_along(): return lax.ppermute(block, axis, route)]
    another operation x1 -> x0, loops' own time: 5.21 us -> none  [shards(): lax.scan(visit, (numer_init, mass_init), scan_inputs)]
    dynamic_slice x8 -> x0, local copies, waits for them, and re-layouts: 4.95 us -> none  [shards(): lax.scan(visit, (numer_init, mass_init), scan_inputs)]
  transfers between devices with their start and end apart: 18 -> 13, of which waited for: 6 -> 5; matrix products, arithmetic and copies ran while one was open for 2% -> 5% of each run, Pallas kernels for 0% -> 0%
where the time goes in v1:
time: 83.1 us; the launch traced here: 82.7 us
  waiting for transfers between devices  29.4 us (35%)
  starting transfers between devices  23.6 us (28%)
  Pallas kernels  20 us (24%)
  local copies, waits for them, and re-layouts  8.88 us (11%)
    ppermute x8, waiting for transfers between devices, passed_along(): return lax.ppermute(block, axis, route)  29.4 us
    ppermute x8, starting transfers between devices, passed_along(): return lax.ppermute(block, axis, route)  23.2 us
    pallas_call x1, Pallas kernels, shards(): pl.pallas_call(kernel, out_shape=out_shape, in_specs=[smem, smem] + [hbm]...  20 us
    unnamed x31, local copies, waits for them, and re-layouts  4.06 us
    slice x5, local copies, waits for them, and re-layouts, shards(): slab[:, :, :half]  2.5 us
  transfers between devices with their start and end apart: 13, of which 5 were waited for; matrix products, arithmetic and copies ran while one was open for 5% of the time, Pallas kernels for 0%

profile of v1, /device:TPU:22, one launch (start us, length us, event | category | flops | bytes accessed | tf_op | source)
XLA Modules:
  0.0 82.7 jit_solution(3532938042956696746)
XLA Ops:
  0.0 1.0 %constant_dynamic-update-slice_fusion.1 = bf16[4,256,256]{2,1,0:T(8,128)(2,1)S(1)} fusion(bf16[4,256,128]{2,1,0:T(8,128)(2,1)} %param.5), kind=kLoop, calls=%fused_computation.6 | loop fusion | bytes 524288
  1.1 0.1 constant_dynamic-update-slice_fusion
  1.1 3.5 %collective-permute-start = (bf16[4,256,256]{2,1,0:T(8,128)(2,1)S(1)}, bf16[4,256,256]{2,1,0:T(8,128)(2,1)S(1)}, u32[]{:S(2)}, u32[]{:S(2)}) collective-permute-start(bf16[4,256,256]{2,1,0:T(8,128)(2,1)S(1)} %constant_dynamic-update-slice_fusion), channel_id=1, source_target_pairs={{0,4},{2,6},{4,8},{6,10},{8,12},{10,14},{1,5},{3,7},{5,9},{7,11},{... | collective-permute-start | bytes 1572872 | tf_op jit(solution)/shard_map/ppermute | solution.py:34
  4.6 1.9 %collective-permute-start.1 = (bf16[4,256,256]{2,1,0:T(8,128)(2,1)S(1)}, bf16[4,256,256]{2,1,0:T(8,128)(2,1)S(1)}, u32[]{:S(2)}, u32[]{:S(2)}) collective-permute-start(bf16[4,256,256]{2,1,0:T(8,128)(2,1)S(1)} %constant_dynamic-update-slice_fusion), channel_id=1, source_target_pairs={{0,2},{2,4},{4,6},{6,8},{8,10},{10,12},{12,14},{1,3},{3,5},{5,7},{... | collective-permute-start | bytes 1572872 | tf_op jit(solution)/shard_map/ppermute | solution.py:34
  6.6 3.9 %collective-permute-start.2 = (bf16[4,256,256]{2,1,0:T(8,128)(2,1)S(1)}, bf16[4,256,256]{2,1,0:T(8,128)(2,1)S(1)}, u32[]{:S(2)}, u32[]{:S(2)}) collective-permute-start(bf16[4,256,256]{2,1,0:T(8,128)(2,1)S(1)} %constant_dynamic-update-slice_fusion), channel_id=1, source_target_pairs={{2,0},{4,2},{6,4},{8,6},{10,8},{12,10},{14,12},{3,1},{5,3},{7,5},{... | collective-permute-start | bytes 1572872 | tf_op jit(solution)/shard_map/ppermute | solution.py:34
  10.5 2.4 %collective-permute-start.3 = (bf16[4,256,256]{2,1,0:T(8,128)(2,1)S(1)}, bf16[4,256,256]{2,1,0:T(8,128)(2,1)S(1)}, u32[]{:S(2)}, u32[]{:S(2)}) collective-permute-start(bf16[4,256,256]{2,1,0:T(8,128)(2,1)S(1)} %constant_dynamic-update-slice_fusion), channel_id=1, source_target_pairs={{4,0},{6,2},{8,4},{10,6},{12,8},{14,10},{5,1},{7,3},{9,5},{11,7},{... | collective-permute-start | bytes 1572872 | tf_op jit(solution)/shard_map/ppermute | solution.py:34
  12.9 0.8 slice.54
  13.6 0.0 collective-permute-start.6
  13.6 4.2 %collective-permute-done = bf16[4,256,256]{2,1,0:T(8,128)(2,1)S(1)} collective-permute-done((bf16[4,256,256]{2,1,0:T(8,128)(2,1)S(1)}, bf16[4,256,256]{2,1,0:T(8,128)(2,1)S(1)}, u32[]{:S(2)}, u32[]{:S(2)}) %collective-permute-start) | collective-permute-done | bytes 524320 | tf_op jit(solution)/shard_map/ppermute | solution.py:34
  17.8 0.8 slice.52
  18.7 0.0 collective-permute-start.4
  18.7 12.5 %collective-permute-done.1 = bf16[4,256,256]{2,1,0:T(8,128)(2,1)S(1)} collective-permute-done((bf16[4,256,256]{2,1,0:T(8,128)(2,1)S(1)}, bf16[4,256,256]{2,1,0:T(8,128)(2,1)S(1)}, u32[]{:S(2)}, u32[]{:S(2)}) %collective-permute-start.1) | collective-permute-done | bytes 524320 | tf_op jit(solution)/shard_map/ppermute | solution.py:34
  31.1 0.8 slice.53
  32.0 0.0 collective-permute-start.5
  32.0 0.4 collective-permute-done.2
  32.4 0.2 collective-permute-start.7
  32.6 0.0 collective-permute-done.3
  32.7 0.4 copy-done.3
  33.1 0.1 collective-permute-start.8
  33.3 0.0 copy-done.11
  33.3 0.1 copy-done.12
  33.4 0.1 add_clamp_fusion
  33.4 0.7 reshape.48.slot_ref
  34.1 0.1 fusion.1
  34.2 0.6 reshape.55.act_ref
  34.8 0.0 collective-permute-done.6.refs_7_
  34.8 0.0 copy-start.8
  34.8 0.0 collective-permute-done.5.refs_6_
  34.8 0.0 collective-permute-done.8.refs_9_
  34.8 0.7 copy-done.7
  35.5 0.1 copy-done.8
  35.6 0.1 copy-done.9
  35.6 0.7 copy-done.10
  36.3 20.0 %shard_map.55 = (f32[8,128,128]{2,1,0:T(8,128)}, f32[8,1,128]{2,1,0:T(1,128)}, bf16[8,144,128]{2,1,0:T(8,128)(2,1)}, bf16[8,144,128]{2,1,0:T(8,128)(2,1)}, bf16[...) custom-call(s32[128]{0:T(128)} %reshape.48.slot_ref, s32[8]{0:T(128)} %reshape.55.act_ref, ...), custom_call_target="tpu_custom_call" | custom-call | tf_op jit(solution)/shard_map/pallas_call | solution.py:171
  56.3 2.4 %collective-permute-start.9 = (bf16[8,144,128]{2,1,0:T(8,128)(2,1)}, bf16[8,144,128]{2,1,0:T(8,128)(2,1)S(1)}, u32[]{:S(2)}, u32[]{:S(2)}) collective-permute-start(bf16[8,144,128]{2,1,0:T(8,128)(2,1)} %get-tuple-element.12), channel_id=1, source_target_pairs={{4,0},{6,2},{8,4},{10,6},{12,8},{14,10},{5,1},{7,3},{9,5},{11,7},{... | collective-permute-start | bytes 884744 | tf_op jit(solution)/shard_map/ppermute | solution.py:34
  58.7 5.1 %collective-permute-start.10 = (bf16[8,144,128]{2,1,0:T(8,128)(2,1)}, bf16[8,144,128]{2,1,0:T(8,128)(2,1)S(1)}, u32[]{:S(2)}, u32[]{:S(2)}) collective-permute-start(bf16[8,144,128]{2,1,0:T(8,128)(2,1)} %get-tuple-element.13), channel_id=1, source_target_pairs={{2,0},{4,2},{6,4},{8,6},{10,8},{12,10},{14,12},{3,1},{5,3},{7,5},{... | collective-permute-start | bytes 884744 | tf_op jit(solution)/shard_map/ppermute | solution.py:34
  63.9 2.1 %collective-permute-start.11 = (bf16[8,144,128]{2,1,0:T(8,128)(2,1)}, bf16[8,144,128]{2,1,0:T(8,128)(2,1)S(1)}, u32[]{:S(2)}, u32[]{:S(2)}) collective-permute-start(bf16[8,144,128]{2,1,0:T(8,128)(2,1)} %get-tuple-element.14), channel_id=1, source_target_pairs={{0,2},{2,4},{4,6},{6,8},{8,10},{10,12},{12,14},{1,3},{3,5},{5,7},{... | collective-permute-start | bytes 884744 | tf_op jit(solution)/shard_map/ppermute | solution.py:34
  66.0 1.9 %collective-permute-start.12 = (bf16[8,144,128]{2,1,0:T(8,128)(2,1)}, bf16[8,144,128]{2,1,0:T(8,128)(2,1)S(1)}, u32[]{:S(2)}, u32[]{:S(2)}) collective-permute-start(bf16[8,144,128]{2,1,0:T(8,128)(2,1)} %get-tuple-element.15), channel_id=1, source_target_pairs={{0,4},{2,6},{4,8},{6,10},{8,12},{10,14},{1,5},{3,7},{5,9},{7,11},{... | collective-permute-start | bytes 884744 | tf_op jit(solution)/shard_map/ppermute | solution.py:34
  67.9 0.1 copy.8
  68.0 0.0 collective-permute-done.9
  68.1 8.4 %collective-permute-done.10 = bf16[8,144,128]{2,1,0:T(8,128)(2,1)S(1)} collective-permute-done((bf16[8,144,128]{2,1,0:T(8,128)(2,1)}, bf16[8,144,128]{2,1,0:T(8,128)(2,1)S(1)}, u32[]{:S(2)}, u32[]{:S(2)}) %collective-permute-start.10) | collective-permute-done | bytes 294944 | tf_op jit(solution)/shard_map/ppermute | solution.py:34
  76.6 4.0 %collective-permute-done.11 = bf16[8,144,128]{2,1,0:T(8,128)(2,1)S(1)} collective-permute-done((bf16[8,144,128]{2,1,0:T(8,128)(2,1)}, bf16[8,144,128]{2,1,0:T(8,128)(2,1)S(1)}, u32[]{:S(2)}, u32[]{:S(2)}) %collective-permute-start.11) | collective-permute-done | bytes 294944 | tf_op jit(solution)/shard_map/ppermute | solution.py:34
  80.6 0.0 collective-permute-done.12
  80.7 0.7 copy-done.13
  81.3 0.3 copy-done.6
  81.6 0.1 slice_add_fusion
  81.7 0.1 divide_convert_fusion
  81.8 0.9 %copy.9 = bf16[4,2,128,128]{3,2,1,0:T(8,128)(2,1)} copy(bf16[4,2,128,128]{2,3,1,0:T(8,128)(2,1)S(1)} %divide_convert_fusion) | data formatting | bytes 524288 | tf_op jit(solution)/shard_map/convert_element_type | solution.py:214
  (30 shorter events, 0.3 us)
Async XLA Ops:
  0.0 1.0 %copy-start.5 = (bf16[4,256,128]{2,1,0:T(8,128)(2,1)S(1)}, bf16[4,256,128]{2,1,0:T(8,128)(2,1)}, u32[]{:S(2)}) copy-start(bf16[4,256,128]{2,1,0:T(8,128)(2,1)} %param.6) | copy-start | bytes 786436
  1.1 17.5 %copy-start = (bf16[4,256,256]{2,1,0:T(8,128)(2,1)}, bf16[4,256,256]{2,1,0:T(8,128)(2,1)S(1)}, u32[]{:S(2)}) copy-start(bf16[4,256,256]{2,1,0:T(8,128)(2,1)S(1)} %constant_dynamic-update-slice_fusion) | copy-start | bytes 1572868
  1.1 16.7 %collective-permute-start = (bf16[4,256,256]{2,1,0:T(8,128)(2,1)S(1)}, bf16[4,256,256]{2,1,0:T(8,128)(2,1)S(1)}, u32[]{:S(2)}, u32[]{:S(2)}) collective-permute-start(bf16[4,256,256]{2,1,0:T(8,128)(2,1)S(1)} %constant_dynamic-update-slice_fusion), channel_id=1, source_target_pairs={{0,4},{2,6},{4,8},{6,10},{8,12},{10,14},{1,5},{3,7},{5,9},{7,11},{... | collective-permute-start | bytes 1572872 | tf_op jit(solution)/shard_map/ppermute | solution.py:34
  4.6 26.5 %collective-permute-start.1 = (bf16[4,256,256]{2,1,0:T(8,128)(2,1)S(1)}, bf16[4,256,256]{2,1,0:T(8,128)(2,1)S(1)}, u32[]{:S(2)}, u32[]{:S(2)}) collective-permute-start(bf16[4,256,256]{2,1,0:T(8,128)(2,1)S(1)} %constant_dynamic-update-slice_fusion), channel_id=1, source_target_pairs={{0,2},{2,4},{4,6},{6,8},{8,10},{10,12},{12,14},{1,3},{3,5},{5,7},{... | collective-permute-start | bytes 1572872 | tf_op jit(solution)/shard_map/ppermute | solution.py:34
  6.6 25.8 %collective-permute-start.2 = (bf16[4,256,256]{2,1,0:T(8,128)(2,1)S(1)}, bf16[4,256,256]{2,1,0:T(8,128)(2,1)S(1)}, u32[]{:S(2)}, u32[]{:S(2)}) collective-permute-start(bf16[4,256,256]{2,1,0:T(8,128)(2,1)S(1)} %constant_dynamic-update-slice_fusion), channel_id=1, source_target_pairs={{2,0},{4,2},{6,4},{8,6},{10,8},{12,10},{14,12},{3,1},{5,3},{7,5},{... | collective-permute-start | bytes 1572872 | tf_op jit(solution)/shard_map/ppermute | solution.py:34
  10.5 22.1 %collective-permute-start.3 = (bf16[4,256,256]{2,1,0:T(8,128)(2,1)S(1)}, bf16[4,256,256]{2,1,0:T(8,128)(2,1)S(1)}, u32[]{:S(2)}, u32[]{:S(2)}) collective-permute-start(bf16[4,256,256]{2,1,0:T(8,128)(2,1)S(1)} %constant_dynamic-update-slice_fusion), channel_id=1, source_target_pairs={{4,0},{6,2},{8,4},{10,6},{12,8},{14,10},{5,1},{7,3},{9,5},{11,7},{... | collective-permute-start | bytes 1572872 | tf_op jit(solution)/shard_map/ppermute | solution.py:34
  13.6 21.1 %collective-permute-start.6 = (bf16[8,128,128]{2,1,0:T(8,128)(2,1)}, bf16[8,128,128]{2,1,0:T(8,128)(2,1)S(1)}, u32[]{:S(2)}, u32[]{:S(2)}) collective-permute-start(bf16[8,128,128]{2,1,0:T(8,128)(2,1)} %slice.54), channel_id=1, source_target_pairs={{0,1},{1,0},{2,3},{3,2},{4,5},{5,4},{6,7},{7,6},{8,9},{9,8},{10,11... | collective-permute-start | bytes 786440 | tf_op jit(solution)/shard_map/ppermute | solution.py:136
  17.8 14.1 %copy-start.1 = (bf16[4,256,256]{2,1,0:T(8,128)(2,1)}, bf16[4,256,256]{2,1,0:T(8,128)(2,1)S(1)}, u32[]{:S(2)}) copy-start(bf16[4,256,256]{2,1,0:T(8,128)(2,1)S(1)} %collective-permute-done) | copy-start | bytes 1572868
  18.7 16.1 %collective-permute-start.4 = (bf16[8,128,128]{2,1,0:T(8,128)(2,1)}, bf16[8,128,128]{2,1,0:T(8,128)(2,1)S(1)}, u32[]{:S(2)}, u32[]{:S(2)}) collective-permute-start(bf16[8,128,128]{2,1,0:T(8,128)(2,1)} %slice.52), channel_id=1, source_target_pairs={{0,1},{1,0},{2,3},{3,2},{4,5},{5,4},{6,7},{7,6},{8,9},{9,8},{10,11... | collective-permute-start | bytes 786440 | tf_op jit(solution)/shard_map/ppermute | solution.py:136
  31.1 1.2 %copy-start.2 = (bf16[4,256,256]{2,1,0:T(8,128)(2,1)}, bf16[4,256,256]{2,1,0:T(8,128)(2,1)S(1)}, u32[]{:S(2)}) copy-start(bf16[4,256,256]{2,1,0:T(8,128)(2,1)S(1)} %collective-permute-done.1) | copy-start | bytes 1572868
  32.0 2.8 %collective-permute-start.5 = (bf16[8,128,128]{2,1,0:T(8,128)(2,1)}, bf16[8,128,128]{2,1,0:T(8,128)(2,1)}, u32[]{:S(2)}, u32[]{:S(2)}) collective-permute-start(bf16[8,128,128]{2,1,0:T(8,128)(2,1)} %slice.53), channel_id=1, source_target_pairs={{0,1},{1,0},{2,3},{3,2},{4,5},{5,4},{6,7},{7,6},{8,9},{9,8},{10,11... | collective-permute-start | bytes 786440 | tf_op jit(solution)/shard_map/ppermute | solution.py:136
  32.3 0.8 copy-start.3
  32.4 2.4 %collective-permute-start.7 = (bf16[8,128,128]{2,1,0:T(8,128)(2,1)S(1)}, bf16[8,128,128]{2,1,0:T(8,128)(2,1)S(1)}, u32[]{:S(2)}, u32[]{:S(2)}) collective-permute-start(bf16[8,128,128]{2,1,0:T(8,128)(2,1)S(1)} %slice.55), channel_id=1, source_target_pairs={{0,1},{1,0},{2,3},{3,2},{4,5},{5,4},{6,7},{7,6},{8,9},{9,8},{10,11... | collective-permute-start | bytes 786440 | tf_op jit(solution)/shard_map/ppermute | solution.py:136
  32.6 2.2 %copy-start.4 = (bf16[4,256,256]{2,1,0:T(8,128)(2,1)}, bf16[4,256,256]{2,1,0:T(8,128)(2,1)S(1)}, u32[]{:S(2)}) copy-start(bf16[4,256,256]{2,1,0:T(8,128)(2,1)S(1)} %collective-permute-done.3) | copy-start | bytes 1572868
  32.6 0.7 copy-start.11
  32.6 0.7 copy-start.12
  33.1 1.7 %collective-permute-start.8 = (bf16[8,128,128]{2,1,0:T(8,128)(2,1)S(1)}, bf16[8,128,128]{2,1,0:T(8,128)(2,1)S(1)}, u32[]{:S(2)}, u32[]{:S(2)}) collective-permute-start(bf16[8,128,128]{2,1,0:T(8,128)(2,1)S(1)} %slice.56), channel_id=1, source_target_pairs={{0,1},{1,0},{2,3},{3,2},{4,5},{5,4},{6,7},{7,6},{8,9},{9,8},{10,11... | collective-permute-start | bytes 786440 | tf_op jit(solution)/shard_map/ppermute | solution.py:136
  33.4 0.7 copy-start.14
  34.8 0.7 copy-start.7
  34.8 0.8 copy-start.8
  34.8 0.8 copy-start.9
  35.6 0.7 copy-start.10
  56.3 11.7 %collective-permute-start.9 = (bf16[8,144,128]{2,1,0:T(8,128)(2,1)}, bf16[8,144,128]{2,1,0:T(8,128)(2,1)S(1)}, u32[]{:S(2)}, u32[]{:S(2)}) collective-permute-start(bf16[8,144,128]{2,1,0:T(8,128)(2,1)} %get-tuple-element.12), channel_id=1, source_target_pairs={{4,0},{6,2},{8,4},{10,6},{12,8},{14,10},{5,1},{7,3},{9,5},{11,7},{... | collective-permute-start | bytes 884744 | tf_op jit(solution)/shard_map/ppermute | solution.py:34
  58.7 17.8 %collective-permute-start.10 = (bf16[8,144,128]{2,1,0:T(8,128)(2,1)}, bf16[8,144,128]{2,1,0:T(8,128)(2,1)S(1)}, u32[]{:S(2)}, u32[]{:S(2)}) collective-permute-start(bf16[8,144,128]{2,1,0:T(8,128)(2,1)} %get-tuple-element.13), channel_id=1, source_target_pairs={{2,0},{4,2},{6,4},{8,6},{10,8},{12,10},{14,12},{3,1},{5,3},{7,5},{... | collective-permute-start | bytes 884744 | tf_op jit(solution)/shard_map/ppermute | solution.py:34
  63.9 16.7 %collective-permute-start.11 = (bf16[8,144,128]{2,1,0:T(8,128)(2,1)}, bf16[8,144,128]{2,1,0:T(8,128)(2,1)S(1)}, u32[]{:S(2)}, u32[]{:S(2)}) collective-permute-start(bf16[8,144,128]{2,1,0:T(8,128)(2,1)} %get-tuple-element.14), channel_id=1, source_target_pairs={{0,2},{2,4},{4,6},{6,8},{8,10},{10,12},{12,14},{1,3},{3,5},{5,7},{... | collective-permute-start | bytes 884744 | tf_op jit(solution)/shard_map/ppermute | solution.py:34
  66.0 14.6 %collective-permute-start.12 = (bf16[8,144,128]{2,1,0:T(8,128)(2,1)}, bf16[8,144,128]{2,1,0:T(8,128)(2,1)S(1)}, u32[]{:S(2)}, u32[]{:S(2)}) collective-permute-start(bf16[8,144,128]{2,1,0:T(8,128)(2,1)} %get-tuple-element.15), channel_id=1, source_target_pairs={{0,4},{2,6},{4,8},{6,10},{8,12},{10,14},{1,5},{3,7},{5,9},{7,11},{... | collective-permute-start | bytes 884744 | tf_op jit(solution)/shard_map/ppermute | solution.py:34
  80.6 1.0 %copy-start.6 = (f32[8,128,128]{2,1,0:T(8,128)S(1)}, f32[8,128,128]{2,1,0:T(8,128)}, u32[]{:S(2)}) copy-start(f32[8,128,128]{2,1,0:T(8,128)} %get-tuple-element.11) | copy-start | bytes 1572868
  80.6 0.7 copy-start.13

commit v2 on v1

--- a/solution.py
+++ b/solution.py
@@ -41,18 +41,17 @@
     other_refs = refs[slabs : 2 * slabs]
     own_num_ref, own_mass_ref = refs[2 * slabs : 2 * slabs + 2]
     remote_refs = refs[2 * slabs + 2 : 3 * slabs + 1]
-    key_a, key_v, key_b, acc, macc, score_ref, sems = refs[3 * slabs + 1 :]
+    key_e, key_vt, acc, macc, key_stack, value_stack, sems, gather_sems = refs[3 * slabs + 1 :]
 
     copies = []
     for s in range(slabs):
         dst = pl.ds(s * per_slab, per_slab)
-        copies.append(
-            pltpu.make_async_copy(slab_refs[s].at[:, :, pl.ds(0, half)], key_a.at[dst], sems.at[0, s])
-        )
-        copies.append(
-            pltpu.make_async_copy(slab_refs[s].at[:, :, pl.ds(half, half)], key_v.at[dst], sems.at[1, s])
-        )
-        copies.append(pltpu.make_async_copy(other_refs[s], key_b.at[dst], sems.at[2, s]))
+        mine = slab_refs[s].at[:, :, pl.ds(0, half)]
+        copies.append(pltpu.make_async_copy(mine, key_e.at[dst, :, pl.ds(0, half)], sems.at[0, s]))
+        theirs = key_e.at[dst, :, pl.ds(half, half)]
+        copies.append(pltpu.make_async_copy(other_refs[s], theirs, sems.at[1, s]))
+        vals = slab_refs[s].at[:, :, pl.ds(half, half)]
+        copies.append(pltpu.make_async_copy(vals, key_vt.at[dst], sems.at[2, s]))
     for c in copies:
         c.start()
     acc[...] = jnp.zeros(acc.shape, acc.dtype)
@@ -60,41 +59,52 @@
     for c in copies:
         c.wait()
 
+    def gather(i, buf):
+        out = []
+        for k in range(K):
+            s = slot_ref[i * K + k]
+            rows = pl.ds(k * BLOCK, BLOCK)
+            out.append(pltpu.make_async_copy(key_e.at[s], key_stack.at[buf, rows], gather_sems.at[buf, 0, k]))
+            out.append(
+                pltpu.make_async_copy(key_vt.at[s], value_stack.at[buf, :, rows], gather_sems.at[buf, 1, k])
+            )
+        return out
+
+    for c in gather(0, 0):
+        c.start()
+
     score_scale = 1.0 / math.sqrt(W)
     dims_t = (((1,), (1,)), ((), ()))
 
     def one_query(i, carry):
+        buf = i % 2
+        for c in gather(i, buf):
+            c.wait()
+
+        @pl.when(i + 1 < queries)
+        def _():
+            for c in gather(i + 1, 1 - buf):
+                c.start()
+
         q_slot = center + (i // blocks) * rimmed + halo + i % blocks
-        qa = key_a[q_slot]
-        qb = key_b[q_slot]
-        slots = [slot_ref[i * K + k] for k in range(K)]
+        query = key_e[q_slot]
+        score_t = lax.dot_general(key_stack[buf], query, dims_t, preferred_element_type=jnp.float32)
+        score_t = score_t * score_scale
+        peak = jnp.max(score_t, axis=0, keepdims=True)
+        exponent = jnp.exp(score_t - peak)
+        prob_t = exponent / jnp.sum(exponent, axis=0, keepdims=True)
+        attention_t = prob_t.astype(jnp.bfloat16)
+        estimate_t = jnp.dot(value_stack[buf], attention_t, preferred_element_type=jnp.float32)
+        estimate_t = estimate_t.astype(jnp.bfloat16)
+        active = act_ref[i].astype(jnp.float32)
+        masked_t = attention_t * active.astype(jnp.bfloat16)
+        contrib = lax.dot_general(masked_t, estimate_t, dims_t, preferred_element_type=jnp.float32)
+        weights = jnp.sum(prob_t * active, axis=1, keepdims=True)
         for k in range(K):
-            s = slots[k]
-            part = lax.dot_general(qa, key_a[s], dims_t, preferred_element_type=jnp.float32)
-            part = part + lax.dot_general(qb, key_b[s], dims_t, preferred_element_type=jnp.float32)
-            score_ref[:, k * BLOCK : (k + 1) * BLOCK] = part * score_scale
-        score = score_ref[...]
-        peak = jnp.max(score, axis=-1, keepdims=True)
-        exponent = jnp.exp(score - peak)
-        prob = exponent / jnp.sum(exponent, axis=-1, keepdims=True)
-        attention = prob.astype(jnp.bfloat16)
-        estimate = jnp.zeros((BLOCK, half), jnp.float32)
-        for k in range(K):
-            estimate = estimate + jnp.dot(
-                attention[:, k * BLOCK : (k + 1) * BLOCK],
-                key_v[slots[k]],
-                preferred_element_type=jnp.float32,
-            )
-        estimate = estimate.astype(jnp.bfloat16).astype(jnp.float32)
-        active = act_ref[i].astype(jnp.float32)
-        masked = (attention.astype(jnp.float32) * active).astype(jnp.bfloat16)
-        estimate_t = estimate.T.astype(jnp.bfloat16)
-        contrib_t = jnp.dot(estimate_t, masked, preferred_element_type=jnp.float32)
-        weights = jnp.sum(prob * active, axis=0, keepdims=True)
-        for k in range(K):
-            s = slots[k]
-            acc[s] = acc[s] + contrib_t[:, k * BLOCK : (k + 1) * BLOCK]
-            macc[s] = macc[s] + weights[:, k * BLOCK : (k + 1) * BLOCK]
+            s = slot_ref[i * K + k]
+            rows = slice(k * BLOCK, (k + 1) * BLOCK)
+            acc[s] = acc[s] + contrib[rows]
+            macc[s] = macc[s] + weights[rows]
         return carry
 
     lax.fori_loop(0, queries, one_query, 0)
@@ -105,10 +115,10 @@
     remote = [s for s in range(slabs) if s * per_slab != center]
     for ref, s in zip(remote_refs, remote):
         rows = pl.ds(s * per_slab, per_slab)
-        ref[:, :half, :] = acc[rows].astype(jnp.bfloat16)
-        ref[:, half:, :] = jnp.broadcast_to(macc[rows], (per_slab, MASS_ROWS, BLOCK)).astype(
-            jnp.bfloat16
-        )
+        ref[:, :BLOCK, :] = acc[rows].astype(jnp.bfloat16)
+        for j in range(per_slab):
+            spread = jnp.broadcast_to(macc[s * per_slab + j], (BLOCK, half)).T
+            ref[j, BLOCK:, :] = spread[:MASS_ROWS].astype(jnp.bfloat16)
 
 
 def shards(embed, values, match_frame, match_block, block_counts):
@@ -123,7 +133,8 @@
     chan_size = lax.axis_size("chan")
     chan_swap = [(i, (i + 1) % chan_size) for i in range(chan_size)]
 
-    features = jnp.concatenate([embed, values], axis=2)
+    values_t = jnp.swapaxes(values.reshape(frames, blocks, BLOCK, half), -1, -2)
+    features = jnp.concatenate([embed, values_t.reshape(frames, band_rows, half)], axis=2)
     if halo:
         features = with_halo(features, (("band", 1),), BLOCK)
     rimmed_blocks = blocks + 2 * halo
@@ -161,10 +172,10 @@
     hbm = pl.BlockSpec(memory_space=pl.ANY)
     vmem = pl.BlockSpec(memory_space=pltpu.VMEM)
     out_shape = [
-        jax.ShapeDtypeStruct((per_slab, half, BLOCK), jnp.float32),
-        jax.ShapeDtypeStruct((per_slab, 1, BLOCK), jnp.float32),
+        jax.ShapeDtypeStruct((per_slab, BLOCK, half), jnp.float32),
+        jax.ShapeDtypeStruct((per_slab, BLOCK, 1), jnp.float32),
     ] + [
-        jax.ShapeDtypeStruct((per_slab, half + MASS_ROWS, BLOCK), jnp.bfloat16)
+        jax.ShapeDtypeStruct((per_slab, BLOCK + MASS_ROWS, half), jnp.bfloat16)
         for _ in range(slabs - 1)
     ]
     total = slabs * per_slab
@@ -174,13 +185,14 @@
         in_specs=[smem, smem] + [hbm] * (2 * slabs),
         out_specs=[vmem] * len(out_shape),
         scratch_shapes=[
-            pltpu.VMEM((total, BLOCK, half), jnp.bfloat16),
-            pltpu.VMEM((total, BLOCK, half), jnp.bfloat16),
-            pltpu.VMEM((total, BLOCK, half), jnp.bfloat16),
-            pltpu.VMEM((total, half, BLOCK), jnp.float32),
-            pltpu.VMEM((total, 1, BLOCK), jnp.float32),
-            pltpu.VMEM((BLOCK, K * BLOCK), jnp.float32),
+            pltpu.VMEM((total, BLOCK, 2 * half), jnp.bfloat16),
+            pltpu.VMEM((total, half, BLOCK), jnp.bfloat16),
+            pltpu.VMEM((total, BLOCK, half), jnp.float32),
+            pltpu.VMEM((total, BLOCK, 1), jnp.float32),
+            pltpu.VMEM((2, K * BLOCK, 2 * half), jnp.bfloat16),
+            pltpu.VMEM((2, half, K * BLOCK), jnp.bfloat16),
             pltpu.SemaphoreType.DMA((3, slabs)),
+            pltpu.SemaphoreType.DMA((2, 2, K)),
         ],
     )(slot, active.reshape(-1), *window, *others)
     own_num, own_mass = outs[0], outs[1]
@@ -188,9 +200,9 @@
     offsets = [o for o in range(-hops, hops + 1) if o != 0]
     for offset, outgoing in zip(offsets, remote):
         arrived = passed_along(outgoing, "frame", offset).astype(jnp.float32)
-        own_num = own_num + arrived[:, :half, :]
-        own_mass = own_mass + arrived[:, half : half + 1, :]
-    own_num = own_num.reshape(frames, rimmed_blocks, half, BLOCK)
+        own_num = own_num + arrived[:, :BLOCK, :]
+        own_mass = own_mass + arrived[:, BLOCK, :][:, :, None]
+    own_num = own_num.reshape(frames, rimmed_blocks, BLOCK, half)
     own_mass = own_mass.reshape(frames, rimmed_blocks, BLOCK)
     if halo:
         for toward in (1, -1):
@@ -208,7 +220,7 @@
             own_mass = own_mass.at[:, target_block].add(arrived[1])
         own_num = own_num[:, 1 : blocks + 1]
         own_mass = own_mass[:, 1 : blocks + 1]
-    numer = jnp.swapaxes(own_num, -1, -2)
+    numer = own_num
     value_blocks = values.reshape(frames, blocks, BLOCK, half).astype(jnp.float32)
     result = (numer + value_blocks) / (own_mass[..., None] + 1.0)
     return result.reshape(frames, band_rows, half).astype(jnp.bfloat16)

time: 83.1 us -> 96.6 us (1.16)
  the two profiles are of different devices: /device:TPU:22 before, /device:TPU:0 now
where the time goes in v2:
time: 96.6 us; the launch traced here: 96.1 us
  Pallas kernels  32.8 us (34%)
  starting transfers between devices  26.7 us (28%)
  waiting for transfers between devices  23.8 us (25%)
  local copies, waits for them, and re-layouts  9.73 us (10%)
  other arithmetic  2.74 us (3%)
    pallas_call x1, Pallas kernels, shards(): pl.pallas_call(kernel, out_shape=out_shape, in_specs=[smem, smem] + [hbm]...  32.8 us
    ppermute x8, starting transfers between devices, passed_along(): return lax.ppermute(block, axis, route)  26 us
    ppermute x8, waiting for transfers between devices, passed_along(): return lax.ppermute(block, axis, route)  23.8 us
    unnamed x34, local copies, waits for them, and re-layouts  4.05 us
  transfers between devices with their start and end apart: 13, of which 4 were waited for; matrix products, arithmetic and copies ran while one was open for 4% of the time, Pallas kernels for 0%

profile of v2, /device:TPU:0, one launch (start us, length us, event | category | flops | bytes accessed | tf_op | source)
XLA Modules:
  0.0 96.1 jit_solution(18215707176324633175)
XLA Ops:
  0.0 1.2 %copy.13 = bf16[4,2,128,128]{2,3,1,0:T(8,128)(2,1)S(1)} copy(bf16[4,2,128,128]{3,2,1,0:T(8,128)(2,1)} %bitcast.52) | data formatting | bytes 524288 | tf_op jit(solution)/shard_map/reshape | solution.py:136
  1.2 0.1 pad_maximum_fusion
  1.3 0.0 copy-start.15
  1.3 1.3 %collective-permute-start.3 = (bf16[4,256,256]{2,1,0:T(8,128)(2,1)S(1)}, bf16[4,256,256]{2,1,0:T(8,128)(2,1)S(1)}, u32[]{:S(2)}, u32[]{:S(2)}) collective-permute-start(bf16[4,256,256]{2,1,0:T(8,128)(2,1)S(1)} %pad_maximum_fusion), channel_id=1, source_target_pairs={{4,0},{6,2},{8,4},{10,6},{12,8},{14,10},{5,1},{7,3},{9,5},{11,7},{... | collective-permute-start | bytes 1572872 | tf_op jit(solution)/shard_map/ppermute | solution.py:34
  2.6 1.3 %collective-permute-start.2 = (bf16[4,256,256]{2,1,0:T(8,128)(2,1)S(1)}, bf16[4,256,256]{2,1,0:T(8,128)(2,1)S(1)}, u32[]{:S(2)}, u32[]{:S(2)}) collective-permute-start(bf16[4,256,256]{2,1,0:T(8,128)(2,1)S(1)} %pad_maximum_fusion), channel_id=1, source_target_pairs={{2,0},{4,2},{6,4},{8,6},{10,8},{12,10},{14,12},{3,1},{5,3},{7,5},{... | collective-permute-start | bytes 1572872 | tf_op jit(solution)/shard_map/ppermute | solution.py:34
  3.9 5.5 %collective-permute-start.1 = (bf16[4,256,256]{2,1,0:T(8,128)(2,1)S(1)}, bf16[4,256,256]{2,1,0:T(8,128)(2,1)S(1)}, u32[]{:S(2)}, u32[]{:S(2)}) collective-permute-start(bf16[4,256,256]{2,1,0:T(8,128)(2,1)S(1)} %pad_maximum_fusion), channel_id=1, source_target_pairs={{0,2},{2,4},{4,6},{6,8},{8,10},{10,12},{12,14},{1,3},{3,5},{5,7},{... | collective-permute-start | bytes 1572872 | tf_op jit(solution)/shard_map/ppermute | solution.py:34
  9.4 4.6 %collective-permute-start = (bf16[4,256,256]{2,1,0:T(8,128)(2,1)S(1)}, bf16[4,256,256]{2,1,0:T(8,128)(2,1)S(1)}, u32[]{:S(2)}, u32[]{:S(2)}) collective-permute-start(bf16[4,256,256]{2,1,0:T(8,128)(2,1)S(1)} %pad_maximum_fusion), channel_id=1, source_target_pairs={{0,4},{2,6},{4,8},{6,10},{8,12},{10,14},{1,5},{3,7},{5,9},{7,11},{... | collective-permute-start | bytes 1572872 | tf_op jit(solution)/shard_map/ppermute | solution.py:34
  14.0 0.1 collective-permute-start.6
  14.1 0.1 fusion.8
  14.2 0.6 reshape.63.act_ref
  14.8 4.1 %collective-permute-done.3 = bf16[4,256,256]{2,1,0:T(8,128)(2,1)S(1)} collective-permute-done((bf16[4,256,256]{2,1,0:T(8,128)(2,1)S(1)}, bf16[4,256,256]{2,1,0:T(8,128)(2,1)S(1)}, u32[]{:S(2)}, u32[]{:S(2)}) %collective-permute-start.3) | collective-permute-done | bytes 524320 | tf_op jit(solution)/shard_map/ppermute | solution.py:34
  18.9 0.8 slice.52
  19.8 0.0 collective-permute-start.8
  19.8 0.0 collective-permute-done.2
  19.8 0.8 slice.51
  20.6 0.5 collective-permute-start.7
  21.1 10.6 %collective-permute-done.1 = bf16[4,256,256]{2,1,0:T(8,128)(2,1)S(1)} collective-permute-done((bf16[4,256,256]{2,1,0:T(8,128)(2,1)S(1)}, bf16[4,256,256]{2,1,0:T(8,128)(2,1)S(1)}, u32[]{:S(2)}, u32[]{:S(2)}) %collective-permute-start.1) | collective-permute-done | bytes 524320 | tf_op jit(solution)/shard_map/ppermute | solution.py:34
  31.8 0.1 collective-permute-start.5
  31.9 0.0 copy-start.13
  31.9 0.0 copy-start.14
  32.0 0.6 copy-done.2
  32.6 0.1 copy-done.13
  32.6 0.1 copy-done.14
  32.7 0.1 add_clamp_fusion
  32.8 0.6 reshape.55.slot_ref
  33.3 0.9 pad_maximum_fusion.1.refs_2_
  34.2 0.0 collective-permute-done.6.refs_7_
  34.2 0.0 collective-permute-done.8.refs_9_
  34.3 0.7 copy-done.10
  34.9 0.1 copy-done.11
  35.0 0.7 copy-done.12
  35.7 32.8 %shard_map.55 = (f32[8,128,128]{2,1,0:T(8,128)}, f32[8,128,1]{2,1,0:T(8,128)}, bf16[8,144,128]{2,1,0:T(8,128)(2,1)}, bf16[8,144,128]{2,1,0:T(8,128)(2,1)}, bf16[...) custom-call(s32[128]{0:T(128)} %reshape.55.slot_ref, s32[8]{0:T(128)} %reshape.63.act_ref, ...), custom_call_target="tpu_custom_call" | custom-call | tf_op jit(solution)/shard_map/pallas_call | solution.py:182
  68.5 1.1 %copy.16 = bf16[8,144,128]{2,0,1:T(8,128)(2,1)S(1)} copy(bf16[8,144,128]{2,1,0:T(8,128)(2,1)} %get-tuple-element.13) | data formatting | bytes 589824 | tf_op jit(solution)/shard_map/pallas_call | solution.py:182
  69.7 0.1 copy.17
  69.7 4.5 %collective-permute-start.11 = (bf16[8,144,128]{2,0,1:T(8,128)(2,1)S(1)}, bf16[8,144,128]{2,0,1:T(8,128)(2,1)S(1)}, u32[]{:S(2)}, u32[]{:S(2)}) collective-permute-start(bf16[8,144,128]{2,0,1:T(8,128)(2,1)S(1)} %copy.17), channel_id=1, source_target_pairs={{0,2},{2,4},{4,6},{6,8},{8,10},{10,12},{12,14},{1,3},{3,5},{5,7},{... | collective-permute-start | bytes 884744 | tf_op jit(solution)/shard_map/ppermute | solution.py:34
  74.3 1.3 %collective-permute-start.10 = (bf16[8,144,128]{2,0,1:T(8,128)(2,1)S(1)}, bf16[8,144,128]{2,0,1:T(8,128)(2,1)S(1)}, u32[]{:S(2)}, u32[]{:S(2)}) collective-permute-start(bf16[8,144,128]{2,0,1:T(8,128)(2,1)S(1)} %copy.16), channel_id=1, source_target_pairs={{2,0},{4,2},{6,4},{8,6},{10,8},{12,10},{14,12},{3,1},{5,3},{7,5},{... | collective-permute-start | bytes 884744 | tf_op jit(solution)/shard_map/ppermute | solution.py:34
  75.6 0.1 copy.14
  75.7 1.3 %collective-permute-start.9 = (bf16[8,144,128]{2,0,1:T(8,128)(2,1)S(1)}, bf16[8,144,128]{2,0,1:T(8,128)(2,1)S(1)}, u32[]{:S(2)}, u32[]{:S(2)}) collective-permute-start(bf16[8,144,128]{2,0,1:T(8,128)(2,1)S(1)} %copy.14), channel_id=1, source_target_pairs={{4,0},{6,2},{8,4},{10,6},{12,8},{14,10},{5,1},{7,3},{9,5},{11,7},{... | collective-permute-start | bytes 884744 | tf_op jit(solution)/shard_map/ppermute | solution.py:34
  77.0 6.2 %collective-permute-start.12 = (bf16[8,144,128]{2,1,0:T(8,128)(2,1)S(1)}, bf16[8,144,128]{2,1,0:T(8,128)(2,1)S(1)}, u32[]{:S(2)}, u32[]{:S(2)}) collective-permute-start(bf16[8,144,128]{2,1,0:T(8,128)(2,1)S(1)} %copy-done.16), channel_id=1, source_target_pairs={{0,4},{2,6},{4,8},{6,10},{8,12},{10,14},{1,5},{3,7},{5,9},{7,11},{... | collective-permute-start | bytes 884744 | tf_op jit(solution)/shard_map/ppermute | solution.py:34
  83.2 0.2 copy.20
  83.4 4.1 %collective-permute-done.11 = bf16[8,144,128]{2,0,1:T(8,128)(2,1)S(1)} collective-permute-done((bf16[8,144,128]{2,0,1:T(8,128)(2,1)S(1)}, bf16[8,144,128]{2,0,1:T(8,128)(2,1)S(1)}, u32[]{:S(2)}, u32[]{:S(2)}) %collective-permute-start.11) | collective-permute-done | bytes 294944 | tf_op jit(solution)/shard_map/ppermute | solution.py:34
  87.6 4.9 %collective-permute-done.9 = bf16[8,144,128]{2,0,1:T(8,128)(2,1)S(1)} collective-permute-done((bf16[8,144,128]{2,0,1:T(8,128)(2,1)S(1)}, bf16[8,144,128]{2,0,1:T(8,128)(2,1)S(1)}, u32[]{:S(2)}, u32[]{:S(2)}) %collective-permute-start.9) | collective-permute-done | bytes 294944 | tf_op jit(solution)/shard_map/ppermute | solution.py:34
  92.6 1.0 %copy-done.7 = f32[8,128,128]{2,1,0:T(8,128)S(1)} copy-done((f32[8,128,128]{2,1,0:T(8,128)S(1)}, f32[8,128,128]{2,1,0:T(8,128)}, u32[]{:S(2)}) %copy-start.7) | copy-done | bytes 524312
  93.6 0.6 fusion
  94.3 0.0 copy-start.4
  94.3 0.1 copy.19
  94.4 0.8 copy-done.4
  95.2 0.9 fusion.2
  (39 shorter events, 0.3 us)
Async XLA Ops:
  0.0 1.2 %copy-start.5 = (bf16[4,256,128]{2,1,0:T(8,128)(2,1)S(1)}, bf16[4,256,128]{2,1,0:T(8,128)(2,1)}, u32[]{:S(2)}) copy-start(bf16[4,256,128]{2,1,0:T(8,128)(2,1)} %param.5) | copy-start | bytes 786436
  1.3 12.8 %copy-start.15 = (s32[4]{0:T(128)S(1)}, s32[4]{0:T(128)}, u32[]{:S(2)}) copy-start(s32[4]{0:T(128)} %param.9) | copy-start | bytes 52
  1.3 17.7 %collective-permute-start.3 = (bf16[4,256,256]{2,1,0:T(8,128)(2,1)S(1)}, bf16[4,256,256]{2,1,0:T(8,128)(2,1)S(1)}, u32[]{:S(2)}, u32[]{:S(2)}) collective-permute-start(bf16[4,256,256]{2,1,0:T(8,128)(2,1)S(1)} %pad_maximum_fusion), channel_id=1, source_target_pairs={{4,0},{6,2},{8,4},{10,6},{12,8},{14,10},{5,1},{7,3},{9,5},{11,7},{... | collective-permute-start | bytes 1572872 | tf_op jit(solution)/shard_map/ppermute | solution.py:34
  2.6 17.2 %collective-permute-start.2 = (bf16[4,256,256]{2,1,0:T(8,128)(2,1)S(1)}, bf16[4,256,256]{2,1,0:T(8,128)(2,1)S(1)}, u32[]{:S(2)}, u32[]{:S(2)}) collective-permute-start(bf16[4,256,256]{2,1,0:T(8,128)(2,1)S(1)} %pad_maximum_fusion), channel_id=1, source_target_pairs={{2,0},{4,2},{6,4},{8,6},{10,8},{12,10},{14,12},{3,1},{5,3},{7,5},{... | collective-permute-start | bytes 1572872 | tf_op jit(solution)/shard_map/ppermute | solution.py:34
  3.9 27.9 %collective-permute-start.1 = (bf16[4,256,256]{2,1,0:T(8,128)(2,1)S(1)}, bf16[4,256,256]{2,1,0:T(8,128)(2,1)S(1)}, u32[]{:S(2)}, u32[]{:S(2)}) collective-permute-start(bf16[4,256,256]{2,1,0:T(8,128)(2,1)S(1)} %pad_maximum_fusion), channel_id=1, source_target_pairs={{0,2},{2,4},{4,6},{6,8},{8,10},{10,12},{12,14},{1,3},{3,5},{5,7},{... | collective-permute-start | bytes 1572872 | tf_op jit(solution)/shard_map/ppermute | solution.py:34
  9.4 22.5 %collective-permute-start = (bf16[4,256,256]{2,1,0:T(8,128)(2,1)S(1)}, bf16[4,256,256]{2,1,0:T(8,128)(2,1)S(1)}, u32[]{:S(2)}, u32[]{:S(2)}) collective-permute-start(bf16[4,256,256]{2,1,0:T(8,128)(2,1)S(1)} %pad_maximum_fusion), channel_id=1, source_target_pairs={{0,4},{2,6},{4,8},{6,10},{8,12},{10,14},{1,5},{3,7},{5,9},{7,11},{... | collective-permute-start | bytes 1572872 | tf_op jit(solution)/shard_map/ppermute | solution.py:34
  14.0 20.2 %collective-permute-start.6 = (bf16[8,128,128]{2,1,0:T(8,128)(2,1)S(1)}, bf16[8,128,128]{2,1,0:T(8,128)(2,1)S(1)}, u32[]{:S(2)}, u32[]{:S(2)}) collective-permute-start(bf16[8,128,128]{2,1,0:T(8,128)(2,1)S(1)} %bitcast.53), channel_id=1, source_target_pairs={{0,1},{1,0},{2,3},{3,2},{4,5},{5,4},{6,7},{7,6},{8,9},{9,8},{10,11... | collective-permute-start | bytes 786440 | tf_op jit(solution)/shard_map/ppermute | solution.py:147
  18.9 1.7 %copy-start = (bf16[4,256,256]{2,1,0:T(8,128)(2,1)}, bf16[4,256,256]{2,1,0:T(8,128)(2,1)S(1)}, u32[]{:S(2)}) copy-start(bf16[4,256,256]{2,1,0:T(8,128)(2,1)S(1)} %collective-permute-done.3) | copy-start | bytes 1572868
  19.8 14.4 %collective-permute-start.8 = (bf16[8,128,128]{2,1,0:T(8,128)(2,1)}, bf16[8,128,128]{2,1,0:T(8,128)(2,1)}, u32[]{:S(2)}, u32[]{:S(2)}) collective-permute-start(bf16[8,128,128]{2,1,0:T(8,128)(2,1)} %slice.52), channel_id=1, source_target_pairs={{0,1},{1,0},{2,3},{3,2},{4,5},{5,4},{6,7},{7,6},{8,9},{9,8},{10,11... | collective-permute-start | bytes 786440 | tf_op jit(solution)/shard_map/ppermute | solution.py:147
  19.8 12.0 %copy-start.1 = (bf16[4,256,256]{2,1,0:T(8,128)(2,1)}, bf16[4,256,256]{2,1,0:T(8,128)(2,1)S(1)}, u32[]{:S(2)}) copy-start(bf16[4,256,256]{2,1,0:T(8,128)(2,1)S(1)} %collective-permute-done.2) | copy-start | bytes 1572868
  20.6 13.6 %collective-permute-start.7 = (bf16[8,128,128]{2,1,0:T(8,128)(2,1)}, bf16[8,128,128]{2,1,0:T(8,128)(2,1)}, u32[]{:S(2)}, u32[]{:S(2)}) collective-permute-start(bf16[8,128,128]{2,1,0:T(8,128)(2,1)} %slice.51), channel_id=1, source_target_pairs={{0,1},{1,0},{2,3},{3,2},{4,5},{5,4},{6,7},{7,6},{8,9},{9,8},{10,11... | collective-permute-start | bytes 786440 | tf_op jit(solution)/shard_map/ppermute | solution.py:147
  31.7 0.8 copy-start.2
  31.8 2.4 %collective-permute-start.5 = (bf16[8,128,128]{2,1,0:T(8,128)(2,1)S(1)}, bf16[8,128,128]{2,1,0:T(8,128)(2,1)S(1)}, u32[]{:S(2)}, u32[]{:S(2)}) collective-permute-start(bf16[8,128,128]{2,1,0:T(8,128)(2,1)S(1)} %slice.50), channel_id=1, source_target_pairs={{0,1},{1,0},{2,3},{3,2},{4,5},{5,4},{6,7},{7,6},{8,9},{9,8},{10,11... | collective-permute-start | bytes 786440 | tf_op jit(solution)/shard_map/ppermute | solution.py:147
  31.9 2.3 %copy-start.3 = (bf16[4,256,256]{2,1,0:T(8,128)(2,1)}, bf16[4,256,256]{2,1,0:T(8,128)(2,1)S(1)}, u32[]{:S(2)}) copy-start(bf16[4,256,256]{2,1,0:T(8,128)(2,1)S(1)} %collective-permute-done) | copy-start | bytes 1572868
  31.9 0.7 copy-start.13
  31.9 0.8 copy-start.14
  32.6 1.7 %collective-permute-start.4 = (bf16[8,128,128]{2,1,0:T(8,128)(2,1)S(1)}, bf16[8,128,128]{2,1,0:T(8,128)(2,1)S(1)}, u32[]{:S(2)}, u32[]{:S(2)}) collective-permute-start(bf16[8,128,128]{2,1,0:T(8,128)(2,1)S(1)} %slice.49), channel_id=1, source_target_pairs={{0,1},{1,0},{2,3},{3,2},{4,5},{5,4},{6,7},{7,6},{8,9},{9,8},{10,11... | collective-permute-start | bytes 786440 | tf_op jit(solution)/shard_map/ppermute | solution.py:147
  34.2 0.7 copy-start.10
  34.2 0.8 copy-start.11
  35.0 0.7 copy-start.12
  68.5 1.1 %copy-start.9 = (bf16[8,144,128]{2,1,0:T(8,128)(2,1)S(1)}, bf16[8,144,128]{2,1,0:T(8,128)(2,1)}, u32[]{:S(2)}) copy-start(bf16[8,144,128]{2,1,0:T(8,128)(2,1)} %get-tuple-element.14) | copy-start | bytes 884740
  68.5 7.1 %copy-start.8 = (bf16[8,144,128]{2,1,0:T(8,128)(2,1)S(1)}, bf16[8,144,128]{2,1,0:T(8,128)(2,1)}, u32[]{:S(2)}) copy-start(bf16[8,144,128]{2,1,0:T(8,128)(2,1)} %get-tuple-element.12) | copy-start | bytes 884740
  69.7 13.5 %copy-start.6 = (f32[8,128,1]{2,1,0:T(8,128)S(1)}, f32[8,128,1]{2,1,0:T(8,128)}, u32[]{:S(2)}) copy-start(f32[8,128,1]{2,1,0:T(8,128)} %get-tuple-element.16) | copy-start | bytes 12292
  69.7 17.7 %collective-permute-start.11 = (bf16[8,144,128]{2,0,1:T(8,128)(2,1)S(1)}, bf16[8,144,128]{2,0,1:T(8,128)(2,1)S(1)}, u32[]{:S(2)}, u32[]{:S(2)}) collective-permute-start(bf16[8,144,128]{2,0,1:T(8,128)(2,1)S(1)} %copy.17), channel_id=1, source_target_pairs={{0,2},{2,4},{4,6},{6,8},{8,10},{10,12},{12,14},{1,3},{3,5},{5,7},{... | collective-permute-start | bytes 884744 | tf_op jit(solution)/shard_map/ppermute | solution.py:34
  74.3 13.2 %collective-permute-start.10 = (bf16[8,144,128]{2,0,1:T(8,128)(2,1)S(1)}, bf16[8,144,128]{2,0,1:T(8,128)(2,1)S(1)}, u32[]{:S(2)}, u32[]{:S(2)}) collective-permute-start(bf16[8,144,128]{2,0,1:T(8,128)(2,1)S(1)} %copy.16), channel_id=1, source_target_pairs={{2,0},{4,2},{6,4},{8,6},{10,8},{12,10},{14,12},{3,1},{5,3},{7,5},{... | collective-permute-start | bytes 884744 | tf_op jit(solution)/shard_map/ppermute | solution.py:34
  75.6 1.4 %copy-start.16 = (bf16[8,144,128]{2,1,0:T(8,128)(2,1)S(1)}, bf16[8,144,128]{2,1,0:T(8,128)(2,1)}, u32[]{:S(2)}) copy-start(bf16[8,144,128]{2,1,0:T(8,128)(2,1)} %get-tuple-element.15) | copy-start | bytes 884740
  75.7 16.8 %collective-permute-start.9 = (bf16[8,144,128]{2,0,1:T(8,128)(2,1)S(1)}, bf16[8,144,128]{2,0,1:T(8,128)(2,1)S(1)}, u32[]{:S(2)}, u32[]{:S(2)}) collective-permute-start(bf16[8,144,128]{2,0,1:T(8,128)(2,1)S(1)} %copy.14), channel_id=1, source_target_pairs={{4,0},{6,2},{8,4},{10,6},{12,8},{14,10},{5,1},{7,3},{9,5},{11,7},{... | collective-permute-start | bytes 884744 | tf_op jit(solution)/shard_map/ppermute | solution.py:34
  77.0 15.5 %collective-permute-start.12 = (bf16[8,144,128]{2,1,0:T(8,128)(2,1)S(1)}, bf16[8,144,128]{2,1,0:T(8,128)(2,1)S(1)}, u32[]{:S(2)}, u32[]{:S(2)}) collective-permute-start(bf16[8,144,128]{2,1,0:T(8,128)(2,1)S(1)} %copy-done.16), channel_id=1, source_target_pairs={{0,4},{2,6},{4,8},{6,10},{8,12},{10,14},{1,5},{3,7},{5,9},{7,11},{... | collective-permute-start | bytes 884744 | tf_op jit(solution)/shard_map/ppermute | solution.py:34
  92.6 1.0 %copy-start.7 = (f32[8,128,128]{2,1,0:T(8,128)S(1)}, f32[8,128,128]{2,1,0:T(8,128)}, u32[]{:S(2)}) copy-start(f32[8,128,128]{2,1,0:T(8,128)} %get-tuple-element.11) | copy-start | bytes 1572868
  94.3 1.0 copy-start.4

commit v3 on v1

--- a/solution.py
+++ b/solution.py
@@ -37,22 +37,16 @@
 def aggregate_kernel(
     slot_ref, act_ref, *refs, slabs, per_slab, center, queries, half, blocks, rimmed, halo
 ):
-    slab_refs = refs[:slabs]
-    other_refs = refs[slabs : 2 * slabs]
-    own_num_ref, own_mass_ref = refs[2 * slabs : 2 * slabs + 2]
-    remote_refs = refs[2 * slabs + 2 : 3 * slabs + 1]
-    key_a, key_v, key_b, acc, macc, score_ref, sems = refs[3 * slabs + 1 :]
+    sources = [refs[:slabs], refs[2 * slabs : 3 * slabs], refs[slabs : 2 * slabs]]
+    own_num_ref, own_mass_ref = refs[3 * slabs : 3 * slabs + 2]
+    remote_refs = refs[3 * slabs + 2 : 4 * slabs + 1]
+    key_a, key_v, key_b, acc, macc, score_ref, sems = refs[4 * slabs + 1 :]
 
     copies = []
     for s in range(slabs):
         dst = pl.ds(s * per_slab, per_slab)
-        copies.append(
-            pltpu.make_async_copy(slab_refs[s].at[:, :, pl.ds(0, half)], key_a.at[dst], sems.at[0, s])
-        )
-        copies.append(
-            pltpu.make_async_copy(slab_refs[s].at[:, :, pl.ds(half, half)], key_v.at[dst], sems.at[1, s])
-        )
-        copies.append(pltpu.make_async_copy(other_refs[s], key_b.at[dst], sems.at[2, s]))
+        for kind, target in enumerate((key_a, key_v, key_b)):
+            copies.append(pltpu.make_async_copy(sources[kind][s], target.at[dst], sems.at[kind, s]))
     for c in copies:
         c.start()
     acc[...] = jnp.zeros(acc.shape, acc.dtype)
@@ -123,19 +117,20 @@
     chan_size = lax.axis_size("chan")
     chan_swap = [(i, (i + 1) % chan_size) for i in range(chan_size)]
 
-    features = jnp.concatenate([embed, values], axis=2)
     if halo:
-        features = with_halo(features, (("band", 1),), BLOCK)
+        embed, rim_values = (with_halo(x, (("band", 1),), BLOCK) for x in (embed, values))
+    else:
+        rim_values = values
     rimmed_blocks = blocks + 2 * halo
     per_slab = frames * rimmed_blocks
-    window = []
+    window_e = []
+    window_v = []
     for offset in range(-hops, hops + 1):
-        slab = features if offset == 0 else passed_along(features, "frame", -offset)
-        window.append(slab.reshape(per_slab, BLOCK, 2 * half))
-    others = [
-        lax.ppermute(slab[:, :, :half], "chan", chan_swap) for slab in window
-    ]
-    slabs = len(window)
+        for own, window in ((embed, window_e), (rim_values, window_v)):
+            slab = own if offset == 0 else passed_along(own, "frame", -offset)
+            window.append(slab.reshape(per_slab, BLOCK, half))
+    others = [lax.ppermute(slab, "chan", chan_swap) for slab in window_e]
+    slabs = len(window_e)
     center = hops * per_slab
 
     frame_ids = jnp.arange(frames, dtype=jnp.int32)
@@ -171,7 +166,7 @@
     outs = pl.pallas_call(
         kernel,
         out_shape=out_shape,
-        in_specs=[smem, smem] + [hbm] * (2 * slabs),
+        in_specs=[smem, smem] + [hbm] * (3 * slabs),
         out_specs=[vmem] * len(out_shape),
         scratch_shapes=[
             pltpu.VMEM((total, BLOCK, half), jnp.bfloat16),
@@ -182,7 +177,7 @@
             pltpu.VMEM((BLOCK, K * BLOCK), jnp.float32),
             pltpu.SemaphoreType.DMA((3, slabs)),
         ],
-    )(slot, active.reshape(-1), *window, *others)
+    )(slot, active.reshape(-1), *window_e, *others, *window_v)
     own_num, own_mass = outs[0], outs[1]
     remote = outs[2:]
     offsets = [o for o in range(-hops, hops + 1) if o != 0]

time: 83.1 us -> 81.7 us (0.983)
  starting transfers between devices: 23.6 us -> 35.9 us
  waiting for transfers between devices: 29.4 us -> 20.3 us
  local copies, waits for them, and re-layouts: 8.88 us -> 3.9 us
    ppermute x8 -> x12, starting transfers between devices: 23.2 us -> 35.3 us  [passed_along(): return lax.ppermute(block, axis, route)]
    ppermute x8 -> x12, waiting for transfers between devices: 29.4 us -> 20.2 us  [passed_along(): return lax.ppermute(block, axis, route)]
    slice x5 -> x0, local copies, waits for them, and re-layouts: 2.5 us -> none  [shards(): slab[:, :, :half]]
    unnamed x31 -> x38, local copies, waits for them, and re-layouts: 4.06 us -> 1.67 us
  transfers between devices with their start and end apart: 13 -> 17, of which waited for: 5 -> 5; matrix products, arithmetic and copies ran while one was open for 5% -> 2% of each run, Pallas kernels for 0% -> 0%
where the time goes in v3:
time: 81.7 us; the launch traced here: 81.1 us
  starting transfers between devices  35.9 us (44%)
  waiting for transfers between devices  20.3 us (25%)
  Pallas kernels  20.1 us (25%)
  local copies, waits for them, and re-layouts  3.9 us (5%)
    ppermute x12, starting transfers between devices, passed_along(): return lax.ppermute(block, axis, route)  35.3 us
    ppermute x12, waiting for transfers between devices, passed_along(): return lax.ppermute(block, axis, route)  20.2 us
    pallas_call x1, Pallas kernels, shards(): pl.pallas_call(kernel, out_shape=out_shape, in_specs=[smem, smem] + [hbm]...  20.1 us
    unnamed x38, local copies, waits for them, and re-layouts  1.67 us
  transfers between devices with their start and end apart: 17, of which 5 were waited for; matrix products, arithmetic and copies ran while one was open for 2% of the time, Pallas kernels for 0%

profile of v3, /device:TPU:22, one launch (start us, length us, event | category | flops | bytes accessed | tf_op | source)
XLA Modules:
  0.0 81.1 jit_solution(4110984853943462924)
XLA Ops:
  0.0 0.0 collective-permute-start.6
  0.0 3.6 %collective-permute-start.1 = (bf16[4,256,128]{2,1,0:T(8,128)(2,1)}, bf16[4,256,128]{2,1,0:T(8,128)(2,1)S(1)}, u32[]{:S(2)}, u32[]{:S(2)}) collective-permute-start(bf16[4,256,128]{2,1,0:T(8,128)(2,1)} %param.5), channel_id=1, source_target_pairs={{0,2},{2,4},{4,6},{6,8},{8,10},{10,12},{12,14},{1,3},{3,5},{5,7},{... | collective-permute-start | bytes 786440 | tf_op jit(solution)/shard_map/ppermute | solution.py:34
  3.6 1.9 %collective-permute-start = (bf16[4,256,128]{2,1,0:T(8,128)(2,1)}, bf16[4,256,128]{2,1,0:T(8,128)(2,1)S(1)}, u32[]{:S(2)}, u32[]{:S(2)}) collective-permute-start(bf16[4,256,128]{2,1,0:T(8,128)(2,1)} %param.5), channel_id=1, source_target_pairs={{0,4},{2,6},{4,8},{6,10},{8,12},{10,14},{1,5},{3,7},{5,9},{7,11},{... | collective-permute-start | bytes 786440 | tf_op jit(solution)/shard_map/ppermute | solution.py:34
  5.5 3.9 %collective-permute-start.3 = (bf16[4,256,128]{2,1,0:T(8,128)(2,1)}, bf16[4,256,128]{2,1,0:T(8,128)(2,1)S(1)}, u32[]{:S(2)}, u32[]{:S(2)}) collective-permute-start(bf16[4,256,128]{2,1,0:T(8,128)(2,1)} %param.5), channel_id=1, source_target_pairs={{4,0},{6,2},{8,4},{10,6},{12,8},{14,10},{5,1},{7,3},{9,5},{11,7},{... | collective-permute-start | bytes 786440 | tf_op jit(solution)/shard_map/ppermute | solution.py:34
  9.5 2.4 %collective-permute-start.2 = (bf16[4,256,128]{2,1,0:T(8,128)(2,1)}, bf16[4,256,128]{2,1,0:T(8,128)(2,1)S(1)}, u32[]{:S(2)}, u32[]{:S(2)}) collective-permute-start(bf16[4,256,128]{2,1,0:T(8,128)(2,1)} %param.5), channel_id=1, source_target_pairs={{2,0},{4,2},{6,4},{8,6},{10,8},{12,10},{14,12},{3,1},{5,3},{7,5},{... | collective-permute-start | bytes 786440 | tf_op jit(solution)/shard_map/ppermute | solution.py:34
  11.9 0.0 collective-permute-done.6.refs_7_
  11.9 3.4 %collective-permute-start.11 = (bf16[4,256,128]{2,1,0:T(8,128)(2,1)}, bf16[4,256,128]{2,1,0:T(8,128)(2,1)S(1)}, u32[]{:S(2)}, u32[]{:S(2)}) collective-permute-start(bf16[4,256,128]{2,1,0:T(8,128)(2,1)} %param.6), channel_id=1, source_target_pairs={{2,0},{4,2},{6,4},{8,6},{10,8},{12,10},{14,12},{3,1},{5,3},{7,5},{... | collective-permute-start | bytes 786440 | tf_op jit(solution)/shard_map/ppermute | solution.py:34
  15.3 0.0 collective-permute-done.1
  15.3 3.4 %collective-permute-start.10 = (bf16[4,256,128]{2,1,0:T(8,128)(2,1)}, bf16[4,256,128]{2,1,0:T(8,128)(2,1)S(1)}, u32[]{:S(2)}, u32[]{:S(2)}) collective-permute-start(bf16[4,256,128]{2,1,0:T(8,128)(2,1)} %param.6), channel_id=1, source_target_pairs={{0,2},{2,4},{4,6},{6,8},{8,10},{10,12},{12,14},{1,3},{3,5},{5,7},{... | collective-permute-start | bytes 786440 | tf_op jit(solution)/shard_map/ppermute | solution.py:34
  18.7 0.0 collective-permute-done
  18.7 0.0 copy-start.4
  18.7 1.9 %collective-permute-start.9 = (bf16[4,256,128]{2,1,0:T(8,128)(2,1)}, bf16[4,256,128]{2,1,0:T(8,128)(2,1)S(1)}, u32[]{:S(2)}, u32[]{:S(2)}) collective-permute-start(bf16[4,256,128]{2,1,0:T(8,128)(2,1)} %param.6), channel_id=1, source_target_pairs={{0,4},{2,6},{4,8},{6,10},{8,12},{10,14},{1,5},{3,7},{5,9},{7,11},{... | collective-permute-start | bytes 786440 | tf_op jit(solution)/shard_map/ppermute | solution.py:34
  20.6 0.1 fusion.1
  20.7 0.0 collective-permute-done.3
  20.7 3.9 %collective-permute-start.12 = (bf16[4,256,128]{2,1,0:T(8,128)(2,1)}, bf16[4,256,128]{2,1,0:T(8,128)(2,1)S(1)}, u32[]{:S(2)}, u32[]{:S(2)}) collective-permute-start(bf16[4,256,128]{2,1,0:T(8,128)(2,1)} %param.6), channel_id=1, source_target_pairs={{4,0},{6,2},{8,4},{10,6},{12,8},{14,10},{5,1},{7,3},{9,5},{11,7},{... | collective-permute-start | bytes 786440 | tf_op jit(solution)/shard_map/ppermute | solution.py:34
  24.6 0.0 collective-permute-done.2
  24.7 0.1 collective-permute-start.5
  24.7 4.9 %collective-permute-done.11 = bf16[4,256,128]{2,1,0:T(8,128)(2,1)S(1)} collective-permute-done((bf16[4,256,128]{2,1,0:T(8,128)(2,1)}, bf16[4,256,128]{2,1,0:T(8,128)(2,1)S(1)}, u32[]{:S(2)}, u32[]{:S(2)}) %collective-permute-start.11) | collective-permute-done | bytes 262176 | tf_op jit(solution)/shard_map/ppermute | solution.py:34
  29.6 0.0 collective-permute-start.4
  29.6 4.4 %collective-permute-done.10 = bf16[4,256,128]{2,1,0:T(8,128)(2,1)S(1)} collective-permute-done((bf16[4,256,128]{2,1,0:T(8,128)(2,1)}, bf16[4,256,128]{2,1,0:T(8,128)(2,1)S(1)}, u32[]{:S(2)}, u32[]{:S(2)}) %collective-permute-start.10) | collective-permute-done | bytes 262176 | tf_op jit(solution)/shard_map/ppermute | solution.py:34
  34.0 0.0 collective-permute-start.8
  34.0 0.0 collective-permute-done.9
  34.0 0.5 collective-permute-start.7
  34.5 0.6 reshape.75.act_ref
  35.1 0.1 add_clamp_fusion
  35.2 0.6 reshape.63.slot_ref
  35.8 0.0 collective-permute-done.12
  35.8 0.0 collective-permute-done.5.refs_6_
  35.9 0.0 collective-permute-done.4.refs_5_
  35.9 0.0 collective-permute-done.8.refs_9_
  35.9 0.0 collective-permute-done.7.refs_8_
  35.9 0.8 %copy-done.14 = bf16[8,128,128]{2,1,0:T(8,128)(2,1)} copy-done((bf16[8,128,128]{2,1,0:T(8,128)(2,1)}, bf16[8,128,128]{2,1,0:T(8,128)(2,1)S(1)}, u32[]{:S(2)}) %copy-start.14) | copy-done | bytes 262168
  36.8 0.0 copy-done.12
  36.8 0.1 copy-done.13
  37.0 20.1 %shard_map.55 = (f32[8,128,128]{2,1,0:T(8,128)}, f32[8,1,128]{2,1,0:T(1,128)}, bf16[8,144,128]{2,1,0:T(8,128)(2,1)}, bf16[8,144,128]{2,1,0:T(8,128)(2,1)}, bf16[...) custom-call(s32[128]{0:T(128)} %reshape.63.slot_ref, s32[8]{0:T(128)} %reshape.75.act_ref, ...), custom_call_target="tpu_custom_call" | custom-call | tf_op jit(solution)/shard_map/pallas_call | solution.py:166
  57.1 2.3 %collective-permute-start.13 = (bf16[8,144,128]{2,1,0:T(8,128)(2,1)}, bf16[8,144,128]{2,1,0:T(8,128)(2,1)S(1)}, u32[]{:S(2)}, u32[]{:S(2)}) collective-permute-start(bf16[8,144,128]{2,1,0:T(8,128)(2,1)} %get-tuple-element.12), channel_id=1, source_target_pairs={{4,0},{6,2},{8,4},{10,6},{12,8},{14,10},{5,1},{7,3},{9,5},{11,7},{... | collective-permute-start | bytes 884744 | tf_op jit(solution)/shard_map/ppermute | solution.py:34
  59.4 1.9 %collective-permute-start.14 = (bf16[8,144,128]{2,1,0:T(8,128)(2,1)}, bf16[8,144,128]{2,1,0:T(8,128)(2,1)S(1)}, u32[]{:S(2)}, u32[]{:S(2)}) collective-permute-start(bf16[8,144,128]{2,1,0:T(8,128)(2,1)} %get-tuple-element.13), channel_id=1, source_target_pairs={{2,0},{4,2},{6,4},{8,6},{10,8},{12,10},{14,12},{3,1},{5,3},{7,5},{... | collective-permute-start | bytes 884744 | tf_op jit(solution)/shard_map/ppermute | solution.py:34
  61.3 4.8 %collective-permute-start.15 = (bf16[8,144,128]{2,1,0:T(8,128)(2,1)}, bf16[8,144,128]{2,1,0:T(8,128)(2,1)S(1)}, u32[]{:S(2)}, u32[]{:S(2)}) collective-permute-start(bf16[8,144,128]{2,1,0:T(8,128)(2,1)} %get-tuple-element.14), channel_id=1, source_target_pairs={{0,2},{2,4},{4,6},{6,8},{8,10},{10,12},{12,14},{1,3},{3,5},{5,7},{... | collective-permute-start | bytes 884744 | tf_op jit(solution)/shard_map/ppermute | solution.py:34
  66.1 1.9 %collective-permute-start.16 = (bf16[8,144,128]{2,1,0:T(8,128)(2,1)}, bf16[8,144,128]{2,1,0:T(8,128)(2,1)S(1)}, u32[]{:S(2)}, u32[]{:S(2)}) collective-permute-start(bf16[8,144,128]{2,1,0:T(8,128)(2,1)} %get-tuple-element.15), channel_id=1, source_target_pairs={{0,4},{2,6},{4,8},{6,10},{8,12},{10,14},{1,5},{3,7},{5,9},{7,11},{... | collective-permute-start | bytes 884744 | tf_op jit(solution)/shard_map/ppermute | solution.py:34
  68.0 0.1 copy.8
  68.2 0.0 collective-permute-done.13
  68.3 6.1 %collective-permute-done.14 = bf16[8,144,128]{2,1,0:T(8,128)(2,1)S(1)} collective-permute-done((bf16[8,144,128]{2,1,0:T(8,128)(2,1)}, bf16[8,144,128]{2,1,0:T(8,128)(2,1)S(1)}, u32[]{:S(2)}, u32[]{:S(2)}) %collective-permute-start.14) | collective-permute-done | bytes 294944 | tf_op jit(solution)/shard_map/ppermute | solution.py:34
  74.4 4.0 %collective-permute-done.15 = bf16[8,144,128]{2,1,0:T(8,128)(2,1)S(1)} collective-permute-done((bf16[8,144,128]{2,1,0:T(8,128)(2,1)}, bf16[8,144,128]{2,1,0:T(8,128)(2,1)S(1)}, u32[]{:S(2)}, u32[]{:S(2)}) %collective-permute-start.15) | collective-permute-done | bytes 294944 | tf_op jit(solution)/shard_map/ppermute | solution.py:34
  78.5 0.9 %collective-permute-done.16 = bf16[8,144,128]{2,1,0:T(8,128)(2,1)S(1)} collective-permute-done((bf16[8,144,128]{2,1,0:T(8,128)(2,1)}, bf16[8,144,128]{2,1,0:T(8,128)(2,1)S(1)}, u32[]{:S(2)}, u32[]{:S(2)}) %collective-permute-start.16) | collective-permute-done | bytes 294944 | tf_op jit(solution)/shard_map/ppermute | solution.py:34
  79.4 0.6 copy-done.17
  80.1 0.1 slice_add_fusion
  80.2 0.1 divide_convert_fusion
  80.3 0.8 %copy.9 = bf16[4,2,128,128]{3,2,1,0:T(8,128)(2,1)} copy(bf16[4,2,128,128]{2,3,1,0:T(8,128)(2,1)S(1)} %divide_convert_fusion) | data formatting | bytes 524288 | tf_op jit(solution)/shard_map/convert_element_type | solution.py:209
  (39 shorter events, 0.2 us)
Async XLA Ops:
  0.0 20.6 %copy-start.18 = (s32[4]{0:T(128)S(1)}, s32[4]{0:T(128)}, u32[]{:S(2)}) copy-start(s32[4]{0:T(128)} %param.9) | copy-start | bytes 52
  0.0 11.9 %collective-permute-start.6 = (bf16[8,128,128]{2,1,0:T(8,128)(2,1)}, bf16[8,128,128]{2,1,0:T(8,128)(2,1)S(1)}, u32[]{:S(2)}, u32[]{:S(2)}) collective-permute-start(bf16[8,128,128]{2,1,0:T(8,128)(2,1)} %bitcast.20), channel_id=1, source_target_pairs={{0,1},{1,0},{2,3},{3,2},{4,5},{5,4},{6,7},{7,6},{8,9},{9,8},{10,11... | collective-permute-start | bytes 786440 | tf_op jit(solution)/shard_map/ppermute | solution.py:132
  0.0 15.3 %collective-permute-start.1 = (bf16[4,256,128]{2,1,0:T(8,128)(2,1)}, bf16[4,256,128]{2,1,0:T(8,128)(2,1)S(1)}, u32[]{:S(2)}, u32[]{:S(2)}) collective-permute-start(bf16[4,256,128]{2,1,0:T(8,128)(2,1)} %param.5), channel_id=1, source_target_pairs={{0,2},{2,4},{4,6},{6,8},{8,10},{10,12},{12,14},{1,3},{3,5},{5,7},{... | collective-permute-start | bytes 786440 | tf_op jit(solution)/shard_map/ppermute | solution.py:34
  3.6 15.1 %collective-permute-start = (bf16[4,256,128]{2,1,0:T(8,128)(2,1)}, bf16[4,256,128]{2,1,0:T(8,128)(2,1)S(1)}, u32[]{:S(2)}, u32[]{:S(2)}) collective-permute-start(bf16[4,256,128]{2,1,0:T(8,128)(2,1)} %param.5), channel_id=1, source_target_pairs={{0,4},{2,6},{4,8},{6,10},{8,12},{10,14},{1,5},{3,7},{5,9},{7,11},{... | collective-permute-start | bytes 786440 | tf_op jit(solution)/shard_map/ppermute | solution.py:34
  5.5 15.2 %collective-permute-start.3 = (bf16[4,256,128]{2,1,0:T(8,128)(2,1)}, bf16[4,256,128]{2,1,0:T(8,128)(2,1)S(1)}, u32[]{:S(2)}, u32[]{:S(2)}) collective-permute-start(bf16[4,256,128]{2,1,0:T(8,128)(2,1)} %param.5), channel_id=1, source_target_pairs={{4,0},{6,2},{8,4},{10,6},{12,8},{14,10},{5,1},{7,3},{9,5},{11,7},{... | collective-permute-start | bytes 786440 | tf_op jit(solution)/shard_map/ppermute | solution.py:34
  9.5 15.2 %collective-permute-start.2 = (bf16[4,256,128]{2,1,0:T(8,128)(2,1)}, bf16[4,256,128]{2,1,0:T(8,128)(2,1)S(1)}, u32[]{:S(2)}, u32[]{:S(2)}) collective-permute-start(bf16[4,256,128]{2,1,0:T(8,128)(2,1)} %param.5), channel_id=1, source_target_pairs={{2,0},{4,2},{6,4},{8,6},{10,8},{12,10},{14,12},{3,1},{5,3},{7,5},{... | collective-permute-start | bytes 786440 | tf_op jit(solution)/shard_map/ppermute | solution.py:34
  11.9 24.9 %copy-start.2 = (bf16[8,128,128]{2,1,0:T(8,128)(2,1)}, bf16[8,128,128]{2,1,0:T(8,128)(2,1)S(1)}, u32[]{:S(2)}) copy-start(bf16[8,128,128]{2,1,0:T(8,128)(2,1)S(1)} %collective-permute-done.6.refs_7_) | copy-start | bytes 786436
  11.9 17.7 %collective-permute-start.11 = (bf16[4,256,128]{2,1,0:T(8,128)(2,1)}, bf16[4,256,128]{2,1,0:T(8,128)(2,1)S(1)}, u32[]{:S(2)}, u32[]{:S(2)}) collective-permute-start(bf16[4,256,128]{2,1,0:T(8,128)(2,1)} %param.6), channel_id=1, source_target_pairs={{2,0},{4,2},{6,4},{8,6},{10,8},{12,10},{14,12},{3,1},{5,3},{7,5},{... | collective-permute-start | bytes 786440 | tf_op jit(solution)/shard_map/ppermute | solution.py:34
  15.3 21.5 %copy-start.3 = (bf16[4,256,128]{2,1,0:T(8,128)(2,1)}, bf16[4,256,128]{2,1,0:T(8,128)(2,1)S(1)}, u32[]{:S(2)}) copy-start(bf16[4,256,128]{2,1,0:T(8,128)(2,1)S(1)} %collective-permute-done.1) | copy-start | bytes 786436
  15.3 18.7 %collective-permute-start.10 = (bf16[4,256,128]{2,1,0:T(8,128)(2,1)}, bf16[4,256,128]{2,1,0:T(8,128)(2,1)S(1)}, u32[]{:S(2)}, u32[]{:S(2)}) collective-permute-start(bf16[4,256,128]{2,1,0:T(8,128)(2,1)} %param.6), channel_id=1, source_target_pairs={{0,2},{2,4},{4,6},{6,8},{8,10},{10,12},{12,14},{1,3},{3,5},{5,7},{... | collective-permute-start | bytes 786440 | tf_op jit(solution)/shard_map/ppermute | solution.py:34
  18.7 18.1 %copy-start.4 = (bf16[4,256,128]{2,1,0:T(8,128)(2,1)}, bf16[4,256,128]{2,1,0:T(8,128)(2,1)S(1)}, u32[]{:S(2)}) copy-start(bf16[4,256,128]{2,1,0:T(8,128)(2,1)S(1)} %collective-permute-done) | copy-start | bytes 786436
  18.7 15.3 %collective-permute-start.9 = (bf16[4,256,128]{2,1,0:T(8,128)(2,1)}, bf16[4,256,128]{2,1,0:T(8,128)(2,1)S(1)}, u32[]{:S(2)}, u32[]{:S(2)}) collective-permute-start(bf16[4,256,128]{2,1,0:T(8,128)(2,1)} %param.6), channel_id=1, source_target_pairs={{0,4},{2,6},{4,8},{6,10},{8,12},{10,14},{1,5},{3,7},{5,9},{7,11},{... | collective-permute-start | bytes 786440 | tf_op jit(solution)/shard_map/ppermute | solution.py:34
  20.7 16.0 %copy-start.5 = (bf16[4,256,128]{2,1,0:T(8,128)(2,1)}, bf16[4,256,128]{2,1,0:T(8,128)(2,1)S(1)}, u32[]{:S(2)}) copy-start(bf16[4,256,128]{2,1,0:T(8,128)(2,1)S(1)} %collective-permute-done.3) | copy-start | bytes 786436
  20.7 15.1 %collective-permute-start.12 = (bf16[4,256,128]{2,1,0:T(8,128)(2,1)}, bf16[4,256,128]{2,1,0:T(8,128)(2,1)S(1)}, u32[]{:S(2)}, u32[]{:S(2)}) collective-permute-start(bf16[4,256,128]{2,1,0:T(8,128)(2,1)} %param.6), channel_id=1, source_target_pairs={{4,0},{6,2},{8,4},{10,6},{12,8},{14,10},{5,1},{7,3},{9,5},{11,7},{... | collective-permute-start | bytes 786440 | tf_op jit(solution)/shard_map/ppermute | solution.py:34
  24.6 12.1 %copy-start.6 = (bf16[4,256,128]{2,1,0:T(8,128)(2,1)}, bf16[4,256,128]{2,1,0:T(8,128)(2,1)S(1)}, u32[]{:S(2)}) copy-start(bf16[4,256,128]{2,1,0:T(8,128)(2,1)S(1)} %collective-permute-done.2) | copy-start | bytes 786436
  24.7 11.2 %collective-permute-start.5 = (bf16[8,128,128]{2,1,0:T(8,128)(2,1)S(1)}, bf16[8,128,128]{2,1,0:T(8,128)(2,1)S(1)}, u32[]{:S(2)}, u32[]{:S(2)}) collective-permute-start(bf16[8,128,128]{2,1,0:T(8,128)(2,1)S(1)} %bitcast.22), channel_id=1, source_target_pairs={{0,1},{1,0},{2,3},{3,2},{4,5},{5,4},{6,7},{7,6},{8,9},{9,8},{10,11... | collective-permute-start | bytes 786440 | tf_op jit(solution)/shard_map/ppermute | solution.py:132
  29.6 7.1 %copy-start.7 = (bf16[4,256,128]{2,1,0:T(8,128)(2,1)}, bf16[4,256,128]{2,1,0:T(8,128)(2,1)S(1)}, u32[]{:S(2)}) copy-start(bf16[4,256,128]{2,1,0:T(8,128)(2,1)S(1)} %collective-permute-done.11) | copy-start | bytes 786436
  29.6 5.5 %copy-start.15 = (s32[4,2,16]{2,1,0:T(2,128)S(1)}, s32[4,2,16]{2,1,0:T(2,128)}, u32[]{:S(2)}) copy-start(s32[4,2,16]{2,1,0:T(2,128)} %param.8) | copy-start | bytes 1540
  29.6 5.5 %copy-start.16 = (s32[4,2,16]{2,1,0:T(2,128)S(1)}, s32[4,2,16]{2,1,0:T(2,128)}, u32[]{:S(2)}) copy-start(s32[4,2,16]{2,1,0:T(2,128)} %param.7) | copy-start | bytes 1540
  29.6 6.2 %collective-permute-start.4 = (bf16[8,128,128]{2,1,0:T(8,128)(2,1)S(1)}, bf16[8,128,128]{2,1,0:T(8,128)(2,1)S(1)}, u32[]{:S(2)}, u32[]{:S(2)}) collective-permute-start(bf16[8,128,128]{2,1,0:T(8,128)(2,1)S(1)} %bitcast.24), channel_id=1, source_target_pairs={{0,1},{1,0},{2,3},{3,2},{4,5},{5,4},{6,7},{7,6},{8,9},{9,8},{10,11... | collective-permute-start | bytes 786440 | tf_op jit(solution)/shard_map/ppermute | solution.py:132
  34.0 2.8 %copy-start.8 = (bf16[4,256,128]{2,1,0:T(8,128)(2,1)}, bf16[4,256,128]{2,1,0:T(8,128)(2,1)S(1)}, u32[]{:S(2)}) copy-start(bf16[4,256,128]{2,1,0:T(8,128)(2,1)S(1)} %collective-permute-done.10) | copy-start | bytes 786436
  34.0 1.9 %collective-permute-start.8 = (bf16[8,128,128]{2,1,0:T(8,128)(2,1)S(1)}, bf16[8,128,128]{2,1,0:T(8,128)(2,1)S(1)}, u32[]{:S(2)}, u32[]{:S(2)}) collective-permute-start(bf16[8,128,128]{2,1,0:T(8,128)(2,1)S(1)} %bitcast.26), channel_id=1, source_target_pairs={{0,1},{1,0},{2,3},{3,2},{4,5},{5,4},{6,7},{7,6},{8,9},{9,8},{10,11... | collective-permute-start | bytes 786440 | tf_op jit(solution)/shard_map/ppermute | solution.py:132
  34.0 2.8 %copy-start.9 = (bf16[4,256,128]{2,1,0:T(8,128)(2,1)}, bf16[4,256,128]{2,1,0:T(8,128)(2,1)S(1)}, u32[]{:S(2)}) copy-start(bf16[4,256,128]{2,1,0:T(8,128)(2,1)S(1)} %collective-permute-done.9) | copy-start | bytes 786436
  34.0 1.9 %collective-permute-start.7 = (bf16[8,128,128]{2,1,0:T(8,128)(2,1)S(1)}, bf16[8,128,128]{2,1,0:T(8,128)(2,1)S(1)}, u32[]{:S(2)}, u32[]{:S(2)}) collective-permute-start(bf16[8,128,128]{2,1,0:T(8,128)(2,1)S(1)} %bitcast.28), channel_id=1, source_target_pairs={{0,1},{1,0},{2,3},{3,2},{4,5},{5,4},{6,7},{7,6},{8,9},{9,8},{10,11... | collective-permute-start | bytes 786440 | tf_op jit(solution)/shard_map/ppermute | solution.py:132
  35.8 1.0 %copy-start.10 = (bf16[4,256,128]{2,1,0:T(8,128)(2,1)}, bf16[4,256,128]{2,1,0:T(8,128)(2,1)S(1)}, u32[]{:S(2)}) copy-start(bf16[4,256,128]{2,1,0:T(8,128)(2,1)S(1)} %collective-permute-done.12) | copy-start | bytes 786436
  35.8 1.0 %copy-start.11 = (bf16[8,128,128]{2,1,0:T(8,128)(2,1)}, bf16[8,128,128]{2,1,0:T(8,128)(2,1)S(1)}, u32[]{:S(2)}) copy-start(bf16[8,128,128]{2,1,0:T(8,128)(2,1)S(1)} %collective-permute-done.5.refs_6_) | copy-start | bytes 786436
  35.9 1.0 %copy-start.12 = (bf16[8,128,128]{2,1,0:T(8,128)(2,1)}, bf16[8,128,128]{2,1,0:T(8,128)(2,1)S(1)}, u32[]{:S(2)}) copy-start(bf16[8,128,128]{2,1,0:T(8,128)(2,1)S(1)} %collective-permute-done.4.refs_5_) | copy-start | bytes 786436
  35.9 1.1 %copy-start.13 = (bf16[8,128,128]{2,1,0:T(8,128)(2,1)}, bf16[8,128,128]{2,1,0:T(8,128)(2,1)S(1)}, u32[]{:S(2)}) copy-start(bf16[8,128,128]{2,1,0:T(8,128)(2,1)S(1)} %collective-permute-done.8.refs_9_) | copy-start | bytes 786436
  35.9 0.8 %copy-start.14 = (bf16[8,128,128]{2,1,0:T(8,128)(2,1)}, bf16[8,128,128]{2,1,0:T(8,128)(2,1)S(1)}, u32[]{:S(2)}) copy-start(bf16[8,128,128]{2,1,0:T(8,128)(2,1)S(1)} %collective-permute-done.7.refs_8_) | copy-start | bytes 786436
  37.0 31.1 %copy-start = (bf16[4,256,128]{2,1,0:T(8,128)(2,1)S(1)}, bf16[4,256,128]{2,1,0:T(8,128)(2,1)}, u32[]{:S(2)}) copy-start(bf16[4,256,128]{2,1,0:T(8,128)(2,1)} %param.6) | copy-start | bytes 786436
  57.1 11.1 %collective-permute-start.13 = (bf16[8,144,128]{2,1,0:T(8,128)(2,1)}, bf16[8,144,128]{2,1,0:T(8,128)(2,1)S(1)}, u32[]{:S(2)}, u32[]{:S(2)}) collective-permute-start(bf16[8,144,128]{2,1,0:T(8,128)(2,1)} %get-tuple-element.12), channel_id=1, source_target_pairs={{4,0},{6,2},{8,4},{10,6},{12,8},{14,10},{5,1},{7,3},{9,5},{11,7},{... | collective-permute-start | bytes 884744 | tf_op jit(solution)/shard_map/ppermute | solution.py:34
  59.4 15.0 %collective-permute-start.14 = (bf16[8,144,128]{2,1,0:T(8,128)(2,1)}, bf16[8,144,128]{2,1,0:T(8,128)(2,1)S(1)}, u32[]{:S(2)}, u32[]{:S(2)}) collective-permute-start(bf16[8,144,128]{2,1,0:T(8,128)(2,1)} %get-tuple-element.13), channel_id=1, source_target_pairs={{2,0},{4,2},{6,4},{8,6},{10,8},{12,10},{14,12},{3,1},{5,3},{7,5},{... | collective-permute-start | bytes 884744 | tf_op jit(solution)/shard_map/ppermute | solution.py:34
  61.3 17.1 %collective-permute-start.15 = (bf16[8,144,128]{2,1,0:T(8,128)(2,1)}, bf16[8,144,128]{2,1,0:T(8,128)(2,1)S(1)}, u32[]{:S(2)}, u32[]{:S(2)}) collective-permute-start(bf16[8,144,128]{2,1,0:T(8,128)(2,1)} %get-tuple-element.14), channel_id=1, source_target_pairs={{0,2},{2,4},{4,6},{6,8},{8,10},{10,12},{12,14},{1,3},{3,5},{5,7},{... | collective-permute-start | bytes 884744 | tf_op jit(solution)/shard_map/ppermute | solution.py:34
  66.1 13.2 %collective-permute-start.16 = (bf16[8,144,128]{2,1,0:T(8,128)(2,1)}, bf16[8,144,128]{2,1,0:T(8,128)(2,1)S(1)}, u32[]{:S(2)}, u32[]{:S(2)}) collective-permute-start(bf16[8,144,128]{2,1,0:T(8,128)(2,1)} %get-tuple-element.15), channel_id=1, source_target_pairs={{0,4},{2,6},{4,8},{6,10},{8,12},{10,14},{1,5},{3,7},{5,9},{7,11},{... | collective-permute-start | bytes 884744 | tf_op jit(solution)/shard_map/ppermute | solution.py:34
  78.5 1.6 %copy-start.1 = (f32[8,128,128]{2,1,0:T(8,128)S(1)}, f32[8,128,128]{2,1,0:T(8,128)}, u32[]{:S(2)}) copy-start(f32[8,128,128]{2,1,0:T(8,128)} %get-tuple-element.11) | copy-start | bytes 1572868
  79.4 0.7 copy-start.17

commit v4 on v3

--- a/solution.py
+++ b/solution.py
@@ -34,23 +34,19 @@
     return lax.ppermute(block, axis, route)
 
 
-def aggregate_kernel(
-    slot_ref, act_ref, *refs, slabs, per_slab, center, queries, half, blocks, rimmed, halo
-):
-    sources = [refs[:slabs], refs[2 * slabs : 3 * slabs], refs[slabs : 2 * slabs]]
-    own_num_ref, own_mass_ref = refs[3 * slabs : 3 * slabs + 2]
-    remote_refs = refs[3 * slabs + 2 : 4 * slabs + 1]
-    key_a, key_v, key_b, acc, macc, score_ref, sems = refs[4 * slabs + 1 :]
+def score_kernel(slot_ref, act_ref, *refs, slabs, per_slab, center, queries, blocks, rimmed, halo):
+    sources = [refs[:slabs], refs[slabs : 2 * slabs]]
+    att_ref, mass_ref = refs[2 * slabs : 2 * slabs + 2]
+    key_a, key_b, score_ref, sems = refs[2 * slabs + 2 :]
 
     copies = []
     for s in range(slabs):
         dst = pl.ds(s * per_slab, per_slab)
-        for kind, target in enumerate((key_a, key_v, key_b)):
+        for kind, target in enumerate((key_a, key_b)):
             copies.append(pltpu.make_async_copy(sources[kind][s], target.at[dst], sems.at[kind, s]))
     for c in copies:
         c.start()
-    acc[...] = jnp.zeros(acc.shape, acc.dtype)
-    macc[...] = jnp.zeros(macc.shape, macc.dtype)
+    mass_ref[...] = jnp.zeros(mass_ref.shape, mass_ref.dtype)
     for c in copies:
         c.wait()
 
@@ -71,7 +67,37 @@
         peak = jnp.max(score, axis=-1, keepdims=True)
         exponent = jnp.exp(score - peak)
         prob = exponent / jnp.sum(exponent, axis=-1, keepdims=True)
-        attention = prob.astype(jnp.bfloat16)
+        att_ref[i] = prob.astype(jnp.bfloat16)
+        active = act_ref[i].astype(jnp.float32)
+        weights = jnp.sum(prob * active, axis=0, keepdims=True)
+        for k in range(K):
+            s = slots[k]
+            mass_ref[s] = mass_ref[s] + weights[:, k * BLOCK : (k + 1) * BLOCK]
+        return carry
+
+    lax.fori_loop(0, queries, one_query, 0)
+
+
+def value_kernel(slot_ref, act_ref, *refs, slabs, per_slab, center, queries, half):
+    sources = refs[:slabs]
+    att_ref, mass_ref = refs[slabs : slabs + 2]
+    own_num_ref, own_mass_ref = refs[slabs + 2 : slabs + 4]
+    remote_refs = refs[slabs + 4 : 2 * slabs + 3]
+    key_v, acc, sems = refs[2 * slabs + 3 :]
+
+    copies = []
+    for s in range(slabs):
+        dst = pl.ds(s * per_slab, per_slab)
+        copies.append(pltpu.make_async_copy(sources[s], key_v.at[dst], sems.at[s]))
+    for c in copies:
+        c.start()
+    acc[...] = jnp.zeros(acc.shape, acc.dtype)
+    for c in copies:
+        c.wait()
+
+    def one_query(i, carry):
+        slots = [slot_ref[i * K + k] for k in range(K)]
+        attention = att_ref[i]
         estimate = jnp.zeros((BLOCK, half), jnp.float32)
         for k in range(K):
             estimate = estimate + jnp.dot(
@@ -84,23 +110,21 @@
         masked = (attention.astype(jnp.float32) * active).astype(jnp.bfloat16)
         estimate_t = estimate.T.astype(jnp.bfloat16)
         contrib_t = jnp.dot(estimate_t, masked, preferred_element_type=jnp.float32)
-        weights = jnp.sum(prob * active, axis=0, keepdims=True)
         for k in range(K):
             s = slots[k]
             acc[s] = acc[s] + contrib_t[:, k * BLOCK : (k + 1) * BLOCK]
-            macc[s] = macc[s] + weights[:, k * BLOCK : (k + 1) * BLOCK]
         return carry
 
     lax.fori_loop(0, queries, one_query, 0)
 
     own = pl.ds(center, per_slab)
     own_num_ref[...] = acc[own]
-    own_mass_ref[...] = macc[own]
+    own_mass_ref[...] = mass_ref[own]
     remote = [s for s in range(slabs) if s * per_slab != center]
     for ref, s in zip(remote_refs, remote):
         rows = pl.ds(s * per_slab, per_slab)
         ref[:, :half, :] = acc[rows].astype(jnp.bfloat16)
-        ref[:, half:, :] = jnp.broadcast_to(macc[rows], (per_slab, MASS_ROWS, BLOCK)).astype(
+        ref[:, half:, :] = jnp.broadcast_to(mass_ref[rows], (per_slab, MASS_ROWS, BLOCK)).astype(
             jnp.bfloat16
         )
 
@@ -125,8 +149,8 @@
     per_slab = frames * rimmed_blocks
     window_e = []
     window_v = []
-    for offset in range(-hops, hops + 1):
-        for own, window in ((embed, window_e), (rim_values, window_v)):
+    for own, window in ((embed, window_e), (rim_values, window_v)):
+        for offset in range(-hops, hops + 1):
             slab = own if offset == 0 else passed_along(own, "frame", -offset)
             window.append(slab.reshape(per_slab, BLOCK, half))
     others = [lax.ppermute(slab, "chan", chan_swap) for slab in window_e]
@@ -141,20 +165,35 @@
     active = (block_ids[None, :] < block_counts[:, None]).astype(jnp.int32)
     queries = frames * blocks
 
-    kernel = functools.partial(
-        aggregate_kernel,
-        slabs=slabs,
-        per_slab=per_slab,
-        center=center,
-        queries=queries,
-        half=half,
-        blocks=blocks,
-        rimmed=rimmed_blocks,
-        halo=halo,
-    )
     smem = pl.BlockSpec(memory_space=pltpu.SMEM)
     hbm = pl.BlockSpec(memory_space=pl.ANY)
     vmem = pl.BlockSpec(memory_space=pltpu.VMEM)
+    total = slabs * per_slab
+    gates = active.reshape(-1)
+    attention, mass = pl.pallas_call(
+        functools.partial(
+            score_kernel,
+            slabs=slabs,
+            per_slab=per_slab,
+            center=center,
+            queries=queries,
+            blocks=blocks,
+            rimmed=rimmed_blocks,
+            halo=halo,
+        ),
+        out_shape=[
+            jax.ShapeDtypeStruct((queries, BLOCK, K * BLOCK), jnp.bfloat16),
+            jax.ShapeDtypeStruct((total, 1, BLOCK), jnp.float32),
+        ],
+        in_specs=[smem, smem] + [hbm] * (2 * slabs),
+        out_specs=[vmem, vmem],
+        scratch_shapes=[
+            pltpu.VMEM((total, BLOCK, half), jnp.bfloat16),
+            pltpu.VMEM((total, BLOCK, half), jnp.bfloat16),
+            pltpu.VMEM((BLOCK, K * BLOCK), jnp.float32),
+            pltpu.SemaphoreType.DMA((2, slabs)),
+        ],
+    )(slot, gates, *window_e, *others)
     out_shape = [
         jax.ShapeDtypeStruct((per_slab, half, BLOCK), jnp.float32),
         jax.ShapeDtypeStruct((per_slab, 1, BLOCK), jnp.float32),
@@ -162,22 +201,24 @@
         jax.ShapeDtypeStruct((per_slab, half + MASS_ROWS, BLOCK), jnp.bfloat16)
         for _ in range(slabs - 1)
     ]
-    total = slabs * per_slab
     outs = pl.pallas_call(
-        kernel,
+        functools.partial(
+            value_kernel,
+            slabs=slabs,
+            per_slab=per_slab,
+            center=center,
+            queries=queries,
+            half=half,
+        ),
         out_shape=out_shape,
-        in_specs=[smem, smem] + [hbm] * (3 * slabs),
+        in_specs=[smem, smem] + [hbm] * slabs + [vmem, vmem],
         out_specs=[vmem] * len(out_shape),
         scratch_shapes=[
             pltpu.VMEM((total, BLOCK, half), jnp.bfloat16),
-            pltpu.VMEM((total, BLOCK, half), jnp.bfloat16),
-            pltpu.VMEM((total, BLOCK, half), jnp.bfloat16),
             pltpu.VMEM((total, half, BLOCK), jnp.float32),
-            pltpu.VMEM((total, 1, BLOCK), jnp.float32),
-            pltpu.VMEM((BLOCK, K * BLOCK), jnp.float32),
-            pltpu.SemaphoreType.DMA((3, slabs)),
+            pltpu.SemaphoreType.DMA((slabs,)),
         ],
-    )(slot, active.reshape(-1), *window_e, *others, *window_v)
+    )(slot, gates, *window_v, attention, mass)
     own_num, own_mass = outs[0], outs[1]
     remote = outs[2:]
     offsets = [o for o in range(-hops, hops + 1) if o != 0]

time: 81.7 us -> 88 us (1.077)
  Pallas kernels: 20.1 us -> 25.8 us
  other arithmetic: 0.52 us -> 1.9 us
    pallas_call x1 -> x2, Pallas kernels: 20.1 us -> 25.8 us  [the longest x1 14.3 us: shards(): pl.pallas_call(functools.partial(score_kernel, slabs=slabs, per_slab=per_...]
  transfers between devices with their start and end apart: 17 -> 17, of which waited for: 5 -> 7; matrix products, arithmetic and copies ran while one was open for 2% -> 4% of each run, Pallas kernels for 0% -> 16%
where the time goes in v4:
time: 88 us; the launch traced here: 87.5 us
  starting transfers between devices  35.2 us (40%)
  Pallas kernels  25.8 us (29%)
  waiting for transfers between devices  20.3 us (23%)
  local copies, waits for them, and re-layouts  3.83 us (4%)
  other arithmetic  1.9 us (2%)
    ppermute x12, starting transfers between devices, passed_along(): return lax.ppermute(block, axis, route)  34.6 us
    ppermute x12, waiting for transfers between devices, passed_along(): return lax.ppermute(block, axis, route)  20.3 us
    pallas_call x1, Pallas kernels, shards(): pl.pallas_call(functools.partial(score_kernel, slabs=slabs, per_slab=per_...  14.3 us
    pallas_call x1, Pallas kernels, shards(): pl.pallas_call(functools.partial(value_kernel, slabs=slabs, per_slab=per_...  11.6 us
  transfers between devices with their start and end apart: 17, of which 7 were waited for; matrix products, arithmetic and copies ran while one was open for 4% of the time, Pallas kernels for 16%

profile of v4, /device:TPU:22, one launch (start us, length us, event | category | flops | bytes accessed | tf_op | source)
XLA Modules:
  0.0 87.5 jit_solution(17073672780185505608)
XLA Ops:
  0.0 2.6 %collective-permute-start.6 = (bf16[4,256,128]{2,1,0:T(8,128)(2,1)}, bf16[4,256,128]{2,1,0:T(8,128)(2,1)S(1)}, u32[]{:S(2)}, u32[]{:S(2)}) collective-permute-start(bf16[4,256,128]{2,1,0:T(8,128)(2,1)} %param.5), channel_id=1, source_target_pairs={{2,0},{4,2},{6,4},{8,6},{10,8},{12,10},{14,12},{3,1},{5,3},{7,5},{... | collective-permute-start | bytes 786440 | tf_op jit(solution)/shard_map/ppermute | solution.py:34
  2.6 2.4 %collective-permute-start.7 = (bf16[4,256,128]{2,1,0:T(8,128)(2,1)}, bf16[4,256,128]{2,1,0:T(8,128)(2,1)S(1)}, u32[]{:S(2)}, u32[]{:S(2)}) collective-permute-start(bf16[4,256,128]{2,1,0:T(8,128)(2,1)} %param.5), channel_id=1, source_target_pairs={{4,0},{6,2},{8,4},{10,6},{12,8},{14,10},{5,1},{7,3},{9,5},{11,7},{... | collective-permute-start | bytes 786440 | tf_op jit(solution)/shard_map/ppermute | solution.py:34
  4.9 3.5 %collective-permute-start.4 = (bf16[4,256,128]{2,1,0:T(8,128)(2,1)}, bf16[4,256,128]{2,1,0:T(8,128)(2,1)S(1)}, u32[]{:S(2)}, u32[]{:S(2)}) collective-permute-start(bf16[4,256,128]{2,1,0:T(8,128)(2,1)} %param.5), channel_id=1, source_target_pairs={{0,4},{2,6},{4,8},{6,10},{8,12},{10,14},{1,5},{3,7},{5,9},{7,11},{... | collective-permute-start | bytes 786440 | tf_op jit(solution)/shard_map/ppermute | solution.py:34
  8.4 2.1 %collective-permute-start.5 = (bf16[4,256,128]{2,1,0:T(8,128)(2,1)}, bf16[4,256,128]{2,1,0:T(8,128)(2,1)S(1)}, u32[]{:S(2)}, u32[]{:S(2)}) collective-permute-start(bf16[4,256,128]{2,1,0:T(8,128)(2,1)} %param.5), channel_id=1, source_target_pairs={{0,2},{2,4},{4,6},{6,8},{8,10},{10,12},{12,14},{1,3},{3,5},{5,7},{... | collective-permute-start | bytes 786440 | tf_op jit(solution)/shard_map/ppermute | solution.py:34
  10.6 0.1 collective-permute-start.10
  10.6 1.7 %collective-permute-done.6 = bf16[4,256,128]{2,1,0:T(8,128)(2,1)S(1)} collective-permute-done((bf16[4,256,128]{2,1,0:T(8,128)(2,1)}, bf16[4,256,128]{2,1,0:T(8,128)(2,1)S(1)}, u32[]{:S(2)}, u32[]{:S(2)}) %collective-permute-start.6) | collective-permute-done | bytes 262176 | tf_op jit(solution)/shard_map/ppermute | solution.py:34
  12.3 0.0 collective-permute-start.11
  12.3 0.1 collective-permute-done.7
  12.4 0.4 collective-permute-start.12
  12.8 3.2 %collective-permute-done.4 = bf16[4,256,128]{2,1,0:T(8,128)(2,1)S(1)} collective-permute-done((bf16[4,256,128]{2,1,0:T(8,128)(2,1)}, bf16[4,256,128]{2,1,0:T(8,128)(2,1)S(1)}, u32[]{:S(2)}, u32[]{:S(2)}) %collective-permute-start.4) | collective-permute-done | bytes 262176 | tf_op jit(solution)/shard_map/ppermute | solution.py:34
  16.0 0.0 collective-permute-start.8
  16.1 3.3 %collective-permute-done.5 = bf16[4,256,128]{2,1,0:T(8,128)(2,1)S(1)} collective-permute-done((bf16[4,256,128]{2,1,0:T(8,128)(2,1)}, bf16[4,256,128]{2,1,0:T(8,128)(2,1)S(1)}, u32[]{:S(2)}, u32[]{:S(2)}) %collective-permute-start.5) | collective-permute-done | bytes 262176 | tf_op jit(solution)/shard_map/ppermute | solution.py:34
  19.4 1.9 %collective-permute-start = (bf16[4,256,128]{2,1,0:T(8,128)(2,1)}, bf16[4,256,128]{2,1,0:T(8,128)(2,1)S(1)}, u32[]{:S(2)}, u32[]{:S(2)}) collective-permute-start(bf16[4,256,128]{2,1,0:T(8,128)(2,1)} %param.6), channel_id=1, source_target_pairs={{0,4},{2,6},{4,8},{6,10},{8,12},{10,14},{1,5},{3,7},{5,9},{7,11},{... | collective-permute-start | bytes 786440 | tf_op jit(solution)/shard_map/ppermute | solution.py:34
  21.3 0.0 collective-permute-done.10.refs_7_
  21.3 4.6 %collective-permute-start.1 = (bf16[4,256,128]{2,1,0:T(8,128)(2,1)}, bf16[4,256,128]{2,1,0:T(8,128)(2,1)S(1)}, u32[]{:S(2)}, u32[]{:S(2)}) collective-permute-start(bf16[4,256,128]{2,1,0:T(8,128)(2,1)} %param.6), channel_id=1, source_target_pairs={{0,2},{2,4},{4,6},{6,8},{8,10},{10,12},{12,14},{1,3},{3,5},{5,7},{... | collective-permute-start | bytes 786440 | tf_op jit(solution)/shard_map/ppermute | solution.py:34
  25.9 0.0 collective-permute-done.11.refs_8_
  25.9 3.1 %collective-permute-start.2 = (bf16[4,256,128]{2,1,0:T(8,128)(2,1)}, bf16[4,256,128]{2,1,0:T(8,128)(2,1)S(1)}, u32[]{:S(2)}, u32[]{:S(2)}) collective-permute-start(bf16[4,256,128]{2,1,0:T(8,128)(2,1)} %param.6), channel_id=1, source_target_pairs={{2,0},{4,2},{6,4},{8,6},{10,8},{12,10},{14,12},{3,1},{5,3},{7,5},{... | collective-permute-start | bytes 786440 | tf_op jit(solution)/shard_map/ppermute | solution.py:34
  29.0 0.0 collective-permute-done.12.refs_9_
  29.0 3.4 %collective-permute-start.3 = (bf16[4,256,128]{2,1,0:T(8,128)(2,1)}, bf16[4,256,128]{2,1,0:T(8,128)(2,1)}, u32[]{:S(2)}, u32[]{:S(2)}) collective-permute-start(bf16[4,256,128]{2,1,0:T(8,128)(2,1)} %param.6), channel_id=1, source_target_pairs={{4,0},{6,2},{8,4},{10,6},{12,8},{14,10},{5,1},{7,3},{9,5},{11,7},{... | collective-permute-start | bytes 786440 | tf_op jit(solution)/shard_map/ppermute | solution.py:34
  32.4 0.0 collective-permute-done.8.refs_5_
  32.4 0.1 collective-permute-start.9
  32.5 0.8 add_clamp_fusion
  33.3 0.7 reshape.63.slot_ref
  34.0 0.7 fusion.1
  34.7 0.6 reshape.75.act_ref
  35.3 0.0 collective-permute-done.9.refs_6_
  35.4 0.7 copy-done.10
  36.1 14.3 %shard_map.55 = (bf16[8,128,2048]{2,1,0:T(8,128)(2,1)}, f32[40,1,128]{2,1,0:T(1,128)}) custom-call(s32[128]{0:T(128)} %reshape.63.slot_ref, s32[8]{0:T(128)} %reshape.75.act_ref, bf16[8,128,128]{2,1,0:T(8,128)(2,1)} %bitcast.27, bf16[8,128,128]{2,1,0:T(8,128)(2,1)} %bitcast.29, bf16[8,128,128]{2,1,0:T(8,128)(2,1)} %bitcast.21, ...), custom_call_target="tpu_custom_call" | custom-call | tf_op jit(solution)/shard_map/pallas_call | solution.py:173
  50.3 0.0 collective-permute-done
  50.4 0.0 copy-start.11
  50.4 0.0 collective-permute-done.1
  50.4 0.0 collective-permute-done.2
  50.4 0.0 collective-permute-done.3
  50.4 0.6 copy-done.11
  51.1 0.1 copy-done.12
  51.2 0.1 copy-done.13
  51.2 11.6 %shard_map.56 = (f32[8,128,128]{2,1,0:T(8,128)}, f32[8,1,128]{2,1,0:T(1,128)}, bf16[8,144,128]{2,1,0:T(8,128)(2,1)}, bf16[8,144,128]{2,1,0:T(8,128)(2,1)}, bf16[...) custom-call(s32[128]{0:T(128)} %reshape.63.slot_ref, s32[8]{0:T(128)} %reshape.75.act_ref, ...), custom_call_target="tpu_custom_call" | custom-call | tf_op jit(solution)/shard_map/pallas_call | solution.py:204
  62.9 2.5 %collective-permute-start.13 = (bf16[8,144,128]{2,1,0:T(8,128)(2,1)}, bf16[8,144,128]{2,1,0:T(8,128)(2,1)S(1)}, u32[]{:S(2)}, u32[]{:S(2)}) collective-permute-start(bf16[8,144,128]{2,1,0:T(8,128)(2,1)} %get-tuple-element.16), channel_id=1, source_target_pairs={{4,0},{6,2},{8,4},{10,6},{12,8},{14,10},{5,1},{7,3},{9,5},{11,7},{... | collective-permute-start | bytes 884744 | tf_op jit(solution)/shard_map/ppermute | solution.py:34
  65.3 3.4 %collective-permute-start.14 = (bf16[8,144,128]{2,1,0:T(8,128)(2,1)}, bf16[8,144,128]{2,1,0:T(8,128)(2,1)S(1)}, u32[]{:S(2)}, u32[]{:S(2)}) collective-permute-start(bf16[8,144,128]{2,1,0:T(8,128)(2,1)} %get-tuple-element.17), channel_id=1, source_target_pairs={{2,0},{4,2},{6,4},{8,6},{10,8},{12,10},{14,12},{3,1},{5,3},{7,5},{... | collective-permute-start | bytes 884744 | tf_op jit(solution)/shard_map/ppermute | solution.py:34
  68.7 3.4 %collective-permute-start.15 = (bf16[8,144,128]{2,1,0:T(8,128)(2,1)}, bf16[8,144,128]{2,1,0:T(8,128)(2,1)S(1)}, u32[]{:S(2)}, u32[]{:S(2)}) collective-permute-start(bf16[8,144,128]{2,1,0:T(8,128)(2,1)} %get-tuple-element.18), channel_id=1, source_target_pairs={{0,2},{2,4},{4,6},{6,8},{8,10},{10,12},{12,14},{1,3},{3,5},{5,7},{... | collective-permute-start | bytes 884744 | tf_op jit(solution)/shard_map/ppermute | solution.py:34
  72.1 1.9 %collective-permute-start.16 = (bf16[8,144,128]{2,1,0:T(8,128)(2,1)}, bf16[8,144,128]{2,1,0:T(8,128)(2,1)S(1)}, u32[]{:S(2)}, u32[]{:S(2)}) collective-permute-start(bf16[8,144,128]{2,1,0:T(8,128)(2,1)} %get-tuple-element.19), channel_id=1, source_target_pairs={{0,4},{2,6},{4,8},{6,10},{8,12},{10,14},{1,5},{3,7},{5,9},{7,11},{... | collective-permute-start | bytes 884744 | tf_op jit(solution)/shard_map/ppermute | solution.py:34
  74.1 0.1 copy.8
  74.2 0.3 collective-permute-done.13
  74.5 7.7 %collective-permute-done.14 = bf16[8,144,128]{2,1,0:T(8,128)(2,1)S(1)} collective-permute-done((bf16[8,144,128]{2,1,0:T(8,128)(2,1)}, bf16[8,144,128]{2,1,0:T(8,128)(2,1)S(1)}, u32[]{:S(2)}, u32[]{:S(2)}) %collective-permute-start.14) | collective-permute-done | bytes 294944 | tf_op jit(solution)/shard_map/ppermute | solution.py:34
  82.3 4.0 %collective-permute-done.15 = bf16[8,144,128]{2,1,0:T(8,128)(2,1)S(1)} collective-permute-done((bf16[8,144,128]{2,1,0:T(8,128)(2,1)}, bf16[8,144,128]{2,1,0:T(8,128)(2,1)S(1)}, u32[]{:S(2)}, u32[]{:S(2)}) %collective-permute-start.15) | collective-permute-done | bytes 294944 | tf_op jit(solution)/shard_map/ppermute | solution.py:34
  86.4 0.1 slice_add_fusion
  86.5 0.1 divide_convert_fusion
  86.6 0.9 copy.9
  (32 shorter events, 0.2 us)
Async XLA Ops:
  0.0 74.0 %copy-start = (bf16[4,256,128]{2,1,0:T(8,128)(2,1)S(1)}, bf16[4,256,128]{2,1,0:T(8,128)(2,1)}, u32[]{:S(2)}) copy-start(bf16[4,256,128]{2,1,0:T(8,128)(2,1)} %param.6) | copy-start | bytes 786436
  0.0 12.3 %collective-permute-start.6 = (bf16[4,256,128]{2,1,0:T(8,128)(2,1)}, bf16[4,256,128]{2,1,0:T(8,128)(2,1)S(1)}, u32[]{:S(2)}, u32[]{:S(2)}) collective-permute-start(bf16[4,256,128]{2,1,0:T(8,128)(2,1)} %param.5), channel_id=1, source_target_pairs={{2,0},{4,2},{6,4},{8,6},{10,8},{12,10},{14,12},{3,1},{5,3},{7,5},{... | collective-permute-start | bytes 786440 | tf_op jit(solution)/shard_map/ppermute | solution.py:34
  2.6 9.9 %collective-permute-start.7 = (bf16[4,256,128]{2,1,0:T(8,128)(2,1)}, bf16[4,256,128]{2,1,0:T(8,128)(2,1)S(1)}, u32[]{:S(2)}, u32[]{:S(2)}) collective-permute-start(bf16[4,256,128]{2,1,0:T(8,128)(2,1)} %param.5), channel_id=1, source_target_pairs={{4,0},{6,2},{8,4},{10,6},{12,8},{14,10},{5,1},{7,3},{9,5},{11,7},{... | collective-permute-start | bytes 786440 | tf_op jit(solution)/shard_map/ppermute | solution.py:34
  4.9 11.1 %collective-permute-start.4 = (bf16[4,256,128]{2,1,0:T(8,128)(2,1)}, bf16[4,256,128]{2,1,0:T(8,128)(2,1)S(1)}, u32[]{:S(2)}, u32[]{:S(2)}) collective-permute-start(bf16[4,256,128]{2,1,0:T(8,128)(2,1)} %param.5), channel_id=1, source_target_pairs={{0,4},{2,6},{4,8},{6,10},{8,12},{10,14},{1,5},{3,7},{5,9},{7,11},{... | collective-permute-start | bytes 786440 | tf_op jit(solution)/shard_map/ppermute | solution.py:34
  8.4 10.9 %collective-permute-start.5 = (bf16[4,256,128]{2,1,0:T(8,128)(2,1)}, bf16[4,256,128]{2,1,0:T(8,128)(2,1)S(1)}, u32[]{:S(2)}, u32[]{:S(2)}) collective-permute-start(bf16[4,256,128]{2,1,0:T(8,128)(2,1)} %param.5), channel_id=1, source_target_pairs={{0,2},{2,4},{4,6},{6,8},{8,10},{10,12},{12,14},{1,3},{3,5},{5,7},{... | collective-permute-start | bytes 786440 | tf_op jit(solution)/shard_map/ppermute | solution.py:34
  10.6 10.7 %collective-permute-start.10 = (bf16[8,128,128]{2,1,0:T(8,128)(2,1)}, bf16[8,128,128]{2,1,0:T(8,128)(2,1)S(1)}, u32[]{:S(2)}, u32[]{:S(2)}) collective-permute-start(bf16[8,128,128]{2,1,0:T(8,128)(2,1)} %bitcast.20), channel_id=1, source_target_pairs={{0,1},{1,0},{2,3},{3,2},{4,5},{5,4},{6,7},{7,6},{8,9},{9,8},{10,11... | collective-permute-start | bytes 786440 | tf_op jit(solution)/shard_map/ppermute | solution.py:156
  12.3 23.0 %copy-start.2 = (bf16[4,256,128]{2,1,0:T(8,128)(2,1)}, bf16[4,256,128]{2,1,0:T(8,128)(2,1)S(1)}, u32[]{:S(2)}) copy-start(bf16[4,256,128]{2,1,0:T(8,128)(2,1)S(1)} %collective-permute-done.6) | copy-start | bytes 786436
  12.3 13.6 %collective-permute-start.11 = (bf16[8,128,128]{2,1,0:T(8,128)(2,1)S(1)}, bf16[8,128,128]{2,1,0:T(8,128)(2,1)S(1)}, u32[]{:S(2)}, u32[]{:S(2)}) collective-permute-start(bf16[8,128,128]{2,1,0:T(8,128)(2,1)S(1)} %bitcast.22), channel_id=1, source_target_pairs={{0,1},{1,0},{2,3},{3,2},{4,5},{5,4},{6,7},{7,6},{8,9},{9,8},{10,11... | collective-permute-start | bytes 786440 | tf_op jit(solution)/shard_map/ppermute | solution.py:156
  12.4 22.9 %copy-start.3 = (bf16[4,256,128]{2,1,0:T(8,128)(2,1)}, bf16[4,256,128]{2,1,0:T(8,128)(2,1)S(1)}, u32[]{:S(2)}) copy-start(bf16[4,256,128]{2,1,0:T(8,128)(2,1)S(1)} %collective-permute-done.7) | copy-start | bytes 786436
  12.4 16.6 %collective-permute-start.12 = (bf16[8,128,128]{2,1,0:T(8,128)(2,1)S(1)}, bf16[8,128,128]{2,1,0:T(8,128)(2,1)S(1)}, u32[]{:S(2)}, u32[]{:S(2)}) collective-permute-start(bf16[8,128,128]{2,1,0:T(8,128)(2,1)S(1)} %bitcast.24), channel_id=1, source_target_pairs={{0,1},{1,0},{2,3},{3,2},{4,5},{5,4},{6,7},{7,6},{8,9},{9,8},{10,11... | collective-permute-start | bytes 786440 | tf_op jit(solution)/shard_map/ppermute | solution.py:156
  16.0 19.3 %copy-start.4 = (bf16[4,256,128]{2,1,0:T(8,128)(2,1)}, bf16[4,256,128]{2,1,0:T(8,128)(2,1)S(1)}, u32[]{:S(2)}) copy-start(bf16[4,256,128]{2,1,0:T(8,128)(2,1)S(1)} %collective-permute-done.4) | copy-start | bytes 786436
  16.0 16.4 %collective-permute-start.8 = (bf16[8,128,128]{2,1,0:T(8,128)(2,1)S(1)}, bf16[8,128,128]{2,1,0:T(8,128)(2,1)S(1)}, u32[]{:S(2)}, u32[]{:S(2)}) collective-permute-start(bf16[8,128,128]{2,1,0:T(8,128)(2,1)S(1)} %bitcast.26), channel_id=1, source_target_pairs={{0,1},{1,0},{2,3},{3,2},{4,5},{5,4},{6,7},{7,6},{8,9},{9,8},{10,11... | collective-permute-start | bytes 786440 | tf_op jit(solution)/shard_map/ppermute | solution.py:156
  19.4 16.0 %copy-start.5 = (bf16[4,256,128]{2,1,0:T(8,128)(2,1)}, bf16[4,256,128]{2,1,0:T(8,128)(2,1)S(1)}, u32[]{:S(2)}) copy-start(bf16[4,256,128]{2,1,0:T(8,128)(2,1)S(1)} %collective-permute-done.5) | copy-start | bytes 786436
  19.4 31.0 %collective-permute-start = (bf16[4,256,128]{2,1,0:T(8,128)(2,1)}, bf16[4,256,128]{2,1,0:T(8,128)(2,1)S(1)}, u32[]{:S(2)}, u32[]{:S(2)}) collective-permute-start(bf16[4,256,128]{2,1,0:T(8,128)(2,1)} %param.6), channel_id=1, source_target_pairs={{0,4},{2,6},{4,8},{6,10},{8,12},{10,14},{1,5},{3,7},{5,9},{7,11},{... | collective-permute-start | bytes 786440 | tf_op jit(solution)/shard_map/ppermute | solution.py:34
  21.3 14.0 %copy-start.6 = (bf16[8,128,128]{2,1,0:T(8,128)(2,1)}, bf16[8,128,128]{2,1,0:T(8,128)(2,1)S(1)}, u32[]{:S(2)}) copy-start(bf16[8,128,128]{2,1,0:T(8,128)(2,1)S(1)} %collective-permute-done.10.refs_7_) | copy-start | bytes 786436
  21.3 29.1 %collective-permute-start.1 = (bf16[4,256,128]{2,1,0:T(8,128)(2,1)}, bf16[4,256,128]{2,1,0:T(8,128)(2,1)S(1)}, u32[]{:S(2)}, u32[]{:S(2)}) collective-permute-start(bf16[4,256,128]{2,1,0:T(8,128)(2,1)} %param.6), channel_id=1, source_target_pairs={{0,2},{2,4},{4,6},{6,8},{8,10},{10,12},{12,14},{1,3},{3,5},{5,7},{... | collective-permute-start | bytes 786440 | tf_op jit(solution)/shard_map/ppermute | solution.py:34
  25.9 9.5 %copy-start.7 = (bf16[8,128,128]{2,1,0:T(8,128)(2,1)}, bf16[8,128,128]{2,1,0:T(8,128)(2,1)S(1)}, u32[]{:S(2)}) copy-start(bf16[8,128,128]{2,1,0:T(8,128)(2,1)S(1)} %collective-permute-done.11.refs_8_) | copy-start | bytes 786436
  25.9 24.5 %collective-permute-start.2 = (bf16[4,256,128]{2,1,0:T(8,128)(2,1)}, bf16[4,256,128]{2,1,0:T(8,128)(2,1)S(1)}, u32[]{:S(2)}, u32[]{:S(2)}) collective-permute-start(bf16[4,256,128]{2,1,0:T(8,128)(2,1)} %param.6), channel_id=1, source_target_pairs={{2,0},{4,2},{6,4},{8,6},{10,8},{12,10},{14,12},{3,1},{5,3},{7,5},{... | collective-permute-start | bytes 786440 | tf_op jit(solution)/shard_map/ppermute | solution.py:34
  29.0 6.3 %copy-start.8 = (bf16[8,128,128]{2,1,0:T(8,128)(2,1)}, bf16[8,128,128]{2,1,0:T(8,128)(2,1)S(1)}, u32[]{:S(2)}) copy-start(bf16[8,128,128]{2,1,0:T(8,128)(2,1)S(1)} %collective-permute-done.12.refs_9_) | copy-start | bytes 786436
  29.0 21.4 %collective-permute-start.3 = (bf16[4,256,128]{2,1,0:T(8,128)(2,1)}, bf16[4,256,128]{2,1,0:T(8,128)(2,1)}, u32[]{:S(2)}, u32[]{:S(2)}) collective-permute-start(bf16[4,256,128]{2,1,0:T(8,128)(2,1)} %param.6), channel_id=1, source_target_pairs={{4,0},{6,2},{8,4},{10,6},{12,8},{14,10},{5,1},{7,3},{9,5},{11,7},{... | collective-permute-start | bytes 786440 | tf_op jit(solution)/shard_map/ppermute | solution.py:34
  32.4 3.0 %copy-start.9 = (bf16[8,128,128]{2,1,0:T(8,128)(2,1)}, bf16[8,128,128]{2,1,0:T(8,128)(2,1)S(1)}, u32[]{:S(2)}) copy-start(bf16[8,128,128]{2,1,0:T(8,128)(2,1)S(1)} %collective-permute-done.8.refs_5_) | copy-start | bytes 786436
  32.4 2.9 %collective-permute-start.9 = (bf16[8,128,128]{2,1,0:T(8,128)(2,1)S(1)}, bf16[8,128,128]{2,1,0:T(8,128)(2,1)S(1)}, u32[]{:S(2)}, u32[]{:S(2)}) collective-permute-start(bf16[8,128,128]{2,1,0:T(8,128)(2,1)S(1)} %bitcast.28), channel_id=1, source_target_pairs={{0,1},{1,0},{2,3},{3,2},{4,5},{5,4},{6,7},{7,6},{8,9},{9,8},{10,11... | collective-permute-start | bytes 786440 | tf_op jit(solution)/shard_map/ppermute | solution.py:156
  35.4 0.7 copy-start.10
  50.4 0.7 copy-start.11
  50.4 0.8 copy-start.12
  50.4 0.8 copy-start.13
  62.8 23.5 %copy-start.14 = (f32[8,1,128]{2,1,0:T(1,128)S(1)}, f32[8,1,128]{2,1,0:T(1,128)}, u32[]{:S(2)}) copy-start(f32[8,1,128]{2,1,0:T(1,128)} %get-tuple-element.20) | copy-start | bytes 12292
  62.8 23.6 %copy-start.1 = (f32[8,128,128]{2,1,0:T(8,128)S(1)}, f32[8,128,128]{2,1,0:T(8,128)}, u32[]{:S(2)}) copy-start(f32[8,128,128]{2,1,0:T(8,128)} %get-tuple-element.15) | copy-start | bytes 1572868
  62.9 11.6 %collective-permute-start.13 = (bf16[8,144,128]{2,1,0:T(8,128)(2,1)}, bf16[8,144,128]{2,1,0:T(8,128)(2,1)S(1)}, u32[]{:S(2)}, u32[]{:S(2)}) collective-permute-start(bf16[8,144,128]{2,1,0:T(8,128)(2,1)} %get-tuple-element.16), channel_id=1, source_target_pairs={{4,0},{6,2},{8,4},{10,6},{12,8},{14,10},{5,1},{7,3},{9,5},{11,7},{... | collective-permute-start | bytes 884744 | tf_op jit(solution)/shard_map/ppermute | solution.py:34
  65.3 16.9 %collective-permute-start.14 = (bf16[8,144,128]{2,1,0:T(8,128)(2,1)}, bf16[8,144,128]{2,1,0:T(8,128)(2,1)S(1)}, u32[]{:S(2)}, u32[]{:S(2)}) collective-permute-start(bf16[8,144,128]{2,1,0:T(8,128)(2,1)} %get-tuple-element.17), channel_id=1, source_target_pairs={{2,0},{4,2},{6,4},{8,6},{10,8},{12,10},{14,12},{3,1},{5,3},{7,5},{... | collective-permute-start | bytes 884744 | tf_op jit(solution)/shard_map/ppermute | solution.py:34
  68.7 17.5 %collective-permute-start.15 = (bf16[8,144,128]{2,1,0:T(8,128)(2,1)}, bf16[8,144,128]{2,1,0:T(8,128)(2,1)S(1)}, u32[]{:S(2)}, u32[]{:S(2)}) collective-permute-start(bf16[8,144,128]{2,1,0:T(8,128)(2,1)} %get-tuple-element.18), channel_id=1, source_target_pairs={{0,2},{2,4},{4,6},{6,8},{8,10},{10,12},{12,14},{1,3},{3,5},{5,7},{... | collective-permute-start | bytes 884744 | tf_op jit(solution)/shard_map/ppermute | solution.py:34
  72.1 14.2 %collective-permute-start.16 = (bf16[8,144,128]{2,1,0:T(8,128)(2,1)}, bf16[8,144,128]{2,1,0:T(8,128)(2,1)S(1)}, u32[]{:S(2)}, u32[]{:S(2)}) collective-permute-start(bf16[8,144,128]{2,1,0:T(8,128)(2,1)} %get-tuple-element.19), channel_id=1, source_target_pairs={{0,4},{2,6},{4,8},{6,10},{8,12},{10,14},{1,5},{3,7},{5,9},{7,11},{... | collective-permute-start | bytes 884744 | tf_op jit(solution)/shard_map/ppermute | solution.py:34

commit v5 on v3

--- a/solution.py
+++ b/solution.py
@@ -40,13 +40,18 @@
     sources = [refs[:slabs], refs[2 * slabs : 3 * slabs], refs[slabs : 2 * slabs]]
     own_num_ref, own_mass_ref = refs[3 * slabs : 3 * slabs + 2]
     remote_refs = refs[3 * slabs + 2 : 4 * slabs + 1]
-    key_a, key_v, key_b, acc, macc, score_ref, sems = refs[4 * slabs + 1 :]
+    key_e, key_v, acc, macc, score_ref, value_ref, sems = refs[4 * slabs + 1 :]
 
     copies = []
     for s in range(slabs):
         dst = pl.ds(s * per_slab, per_slab)
-        for kind, target in enumerate((key_a, key_v, key_b)):
-            copies.append(pltpu.make_async_copy(sources[kind][s], target.at[dst], sems.at[kind, s]))
+        targets = (
+            key_e.at[dst, :, pl.ds(0, half)],
+            key_v.at[dst],
+            key_e.at[dst, :, pl.ds(half, half)],
+        )
+        for kind, target in enumerate(targets):
+            copies.append(pltpu.make_async_copy(sources[kind][s], target, sems.at[kind, s]))
     for c in copies:
         c.start()
     acc[...] = jnp.zeros(acc.shape, acc.dtype)
@@ -59,26 +64,19 @@
 
     def one_query(i, carry):
         q_slot = center + (i // blocks) * rimmed + halo + i % blocks
-        qa = key_a[q_slot]
-        qb = key_b[q_slot]
+        query = key_e[q_slot]
         slots = [slot_ref[i * K + k] for k in range(K)]
         for k in range(K):
             s = slots[k]
-            part = lax.dot_general(qa, key_a[s], dims_t, preferred_element_type=jnp.float32)
-            part = part + lax.dot_general(qb, key_b[s], dims_t, preferred_element_type=jnp.float32)
+            part = lax.dot_general(query, key_e[s], dims_t, preferred_element_type=jnp.float32)
             score_ref[:, k * BLOCK : (k + 1) * BLOCK] = part * score_scale
+            value_ref[k * BLOCK : (k + 1) * BLOCK, :] = key_v[s]
         score = score_ref[...]
         peak = jnp.max(score, axis=-1, keepdims=True)
         exponent = jnp.exp(score - peak)
         prob = exponent / jnp.sum(exponent, axis=-1, keepdims=True)
         attention = prob.astype(jnp.bfloat16)
-        estimate = jnp.zeros((BLOCK, half), jnp.float32)
-        for k in range(K):
-            estimate = estimate + jnp.dot(
-                attention[:, k * BLOCK : (k + 1) * BLOCK],
-                key_v[slots[k]],
-                preferred_element_type=jnp.float32,
-            )
+        estimate = jnp.dot(attention, value_ref[...], preferred_element_type=jnp.float32)
         estimate = estimate.astype(jnp.bfloat16).astype(jnp.float32)
         active = act_ref[i].astype(jnp.float32)
         masked = (attention.astype(jnp.float32) * active).astype(jnp.bfloat16)
@@ -169,12 +167,12 @@
         in_specs=[smem, smem] + [hbm] * (3 * slabs),
         out_specs=[vmem] * len(out_shape),
         scratch_shapes=[
-            pltpu.VMEM((total, BLOCK, half), jnp.bfloat16),
-            pltpu.VMEM((total, BLOCK, half), jnp.bfloat16),
+            pltpu.VMEM((total, BLOCK, 2 * half), jnp.bfloat16),
             pltpu.VMEM((total, BLOCK, half), jnp.bfloat16),
             pltpu.VMEM((total, half, BLOCK), jnp.float32),
             pltpu.VMEM((total, 1, BLOCK), jnp.float32),
             pltpu.VMEM((BLOCK, K * BLOCK), jnp.float32),
+            pltpu.VMEM((K * BLOCK, half), jnp.bfloat16),
             pltpu.SemaphoreType.DMA((3, slabs)),
         ],
     )(slot, active.reshape(-1), *window_e, *others, *window_v)

time: 81.7 us -> 76.8 us (0.940)
  Pallas kernels: 20.1 us -> 15.1 us
    pallas_call x1, Pallas kernels: 20.1 us -> 15.1 us  [shards(): pl.pallas_call(kernel, out_shape=out_shape, in_specs=[smem, smem] + [hbm]...]
where the time goes in v5:
time: 76.8 us; the launch traced here: 76.1 us
  starting transfers between devices  35.9 us (47%)
  waiting for transfers between devices  20.3 us (26%)
  Pallas kernels  15.1 us (20%)
  local copies, waits for them, and re-layouts  3.9 us (5%)
    ppermute x12, starting transfers between devices, passed_along(): return lax.ppermute(block, axis, route)  35.3 us
    ppermute x12, waiting for transfers between devices, passed_along(): return lax.ppermute(block, axis, route)  20.2 us
    pallas_call x1, Pallas kernels, shards(): pl.pallas_call(kernel, out_shape=out_shape, in_specs=[smem, smem] + [hbm]...  15.1 us
    unnamed x38, local copies, waits for them, and re-layouts  1.67 us
  transfers between devices with their start and end apart: 17, of which 5 were waited for; matrix products, arithmetic and copies ran while one was open for 2% of the time, Pallas kernels for 0%

profile of v5, /device:TPU:22, one launch (start us, length us, event | category | flops | bytes accessed | tf_op | source)
XLA Modules:
  0.0 76.1 jit_solution(13015538280573072534)
XLA Ops:
  0.0 0.0 collective-permute-start.6
  0.0 3.6 %collective-permute-start.1 = (bf16[4,256,128]{2,1,0:T(8,128)(2,1)}, bf16[4,256,128]{2,1,0:T(8,128)(2,1)S(1)}, u32[]{:S(2)}, u32[]{:S(2)}) collective-permute-start(bf16[4,256,128]{2,1,0:T(8,128)(2,1)} %param.5), channel_id=1, source_target_pairs={{0,2},{2,4},{4,6},{6,8},{8,10},{10,12},{12,14},{1,3},{3,5},{5,7},{... | collective-permute-start | bytes 786440 | tf_op jit(solution)/shard_map/ppermute | solution.py:34
  3.6 1.9 %collective-permute-start = (bf16[4,256,128]{2,1,0:T(8,128)(2,1)}, bf16[4,256,128]{2,1,0:T(8,128)(2,1)S(1)}, u32[]{:S(2)}, u32[]{:S(2)}) collective-permute-start(bf16[4,256,128]{2,1,0:T(8,128)(2,1)} %param.5), channel_id=1, source_target_pairs={{0,4},{2,6},{4,8},{6,10},{8,12},{10,14},{1,5},{3,7},{5,9},{7,11},{... | collective-permute-start | bytes 786440 | tf_op jit(solution)/shard_map/ppermute | solution.py:34
  5.5 3.9 %collective-permute-start.3 = (bf16[4,256,128]{2,1,0:T(8,128)(2,1)}, bf16[4,256,128]{2,1,0:T(8,128)(2,1)S(1)}, u32[]{:S(2)}, u32[]{:S(2)}) collective-permute-start(bf16[4,256,128]{2,1,0:T(8,128)(2,1)} %param.5), channel_id=1, source_target_pairs={{4,0},{6,2},{8,4},{10,6},{12,8},{14,10},{5,1},{7,3},{9,5},{11,7},{... | collective-permute-start | bytes 786440 | tf_op jit(solution)/shard_map/ppermute | solution.py:34
  9.5 2.4 %collective-permute-start.2 = (bf16[4,256,128]{2,1,0:T(8,128)(2,1)}, bf16[4,256,128]{2,1,0:T(8,128)(2,1)S(1)}, u32[]{:S(2)}, u32[]{:S(2)}) collective-permute-start(bf16[4,256,128]{2,1,0:T(8,128)(2,1)} %param.5), channel_id=1, source_target_pairs={{2,0},{4,2},{6,4},{8,6},{10,8},{12,10},{14,12},{3,1},{5,3},{7,5},{... | collective-permute-start | bytes 786440 | tf_op jit(solution)/shard_map/ppermute | solution.py:34
  11.9 0.0 collective-permute-done.6.refs_7_
  11.9 3.4 %collective-permute-start.11 = (bf16[4,256,128]{2,1,0:T(8,128)(2,1)}, bf16[4,256,128]{2,1,0:T(8,128)(2,1)S(1)}, u32[]{:S(2)}, u32[]{:S(2)}) collective-permute-start(bf16[4,256,128]{2,1,0:T(8,128)(2,1)} %param.6), channel_id=1, source_target_pairs={{2,0},{4,2},{6,4},{8,6},{10,8},{12,10},{14,12},{3,1},{5,3},{7,5},{... | collective-permute-start | bytes 786440 | tf_op jit(solution)/shard_map/ppermute | solution.py:34
  15.3 0.0 collective-permute-done.1
  15.3 3.4 %collective-permute-start.10 = (bf16[4,256,128]{2,1,0:T(8,128)(2,1)}, bf16[4,256,128]{2,1,0:T(8,128)(2,1)S(1)}, u32[]{:S(2)}, u32[]{:S(2)}) collective-permute-start(bf16[4,256,128]{2,1,0:T(8,128)(2,1)} %param.6), channel_id=1, source_target_pairs={{0,2},{2,4},{4,6},{6,8},{8,10},{10,12},{12,14},{1,3},{3,5},{5,7},{... | collective-permute-start | bytes 786440 | tf_op jit(solution)/shard_map/ppermute | solution.py:34
  18.7 0.0 collective-permute-done
  18.7 0.0 copy-start.4
  18.7 1.9 %collective-permute-start.9 = (bf16[4,256,128]{2,1,0:T(8,128)(2,1)}, bf16[4,256,128]{2,1,0:T(8,128)(2,1)S(1)}, u32[]{:S(2)}, u32[]{:S(2)}) collective-permute-start(bf16[4,256,128]{2,1,0:T(8,128)(2,1)} %param.6), channel_id=1, source_target_pairs={{0,4},{2,6},{4,8},{6,10},{8,12},{10,14},{1,5},{3,7},{5,9},{7,11},{... | collective-permute-start | bytes 786440 | tf_op jit(solution)/shard_map/ppermute | solution.py:34
  20.6 0.1 fusion.1
  20.7 0.0 collective-permute-done.3
  20.7 3.9 %collective-permute-start.12 = (bf16[4,256,128]{2,1,0:T(8,128)(2,1)}, bf16[4,256,128]{2,1,0:T(8,128)(2,1)S(1)}, u32[]{:S(2)}, u32[]{:S(2)}) collective-permute-start(bf16[4,256,128]{2,1,0:T(8,128)(2,1)} %param.6), channel_id=1, source_target_pairs={{4,0},{6,2},{8,4},{10,6},{12,8},{14,10},{5,1},{7,3},{9,5},{11,7},{... | collective-permute-start | bytes 786440 | tf_op jit(solution)/shard_map/ppermute | solution.py:34
  24.6 0.0 collective-permute-done.2
  24.7 0.1 collective-permute-start.5
  24.7 4.9 %collective-permute-done.11 = bf16[4,256,128]{2,1,0:T(8,128)(2,1)S(1)} collective-permute-done((bf16[4,256,128]{2,1,0:T(8,128)(2,1)}, bf16[4,256,128]{2,1,0:T(8,128)(2,1)S(1)}, u32[]{:S(2)}, u32[]{:S(2)}) %collective-permute-start.11) | collective-permute-done | bytes 262176 | tf_op jit(solution)/shard_map/ppermute | solution.py:34
  29.6 0.0 collective-permute-start.4
  29.6 4.4 %collective-permute-done.10 = bf16[4,256,128]{2,1,0:T(8,128)(2,1)S(1)} collective-permute-done((bf16[4,256,128]{2,1,0:T(8,128)(2,1)}, bf16[4,256,128]{2,1,0:T(8,128)(2,1)S(1)}, u32[]{:S(2)}, u32[]{:S(2)}) %collective-permute-start.10) | collective-permute-done | bytes 262176 | tf_op jit(solution)/shard_map/ppermute | solution.py:34
  34.0 0.0 collective-permute-start.8
  34.0 0.0 collective-permute-done.9
  34.0 0.5 collective-permute-start.7
  34.5 0.6 reshape.75.act_ref
  35.1 0.1 add_clamp_fusion
  35.2 0.6 reshape.63.slot_ref
  35.8 0.0 collective-permute-done.12
  35.8 0.0 collective-permute-done.5.refs_6_
  35.9 0.0 collective-permute-done.4.refs_5_
  35.9 0.0 collective-permute-done.8.refs_9_
  35.9 0.0 collective-permute-done.7.refs_8_
  35.9 0.8 %copy-done.14 = bf16[8,128,128]{2,1,0:T(8,128)(2,1)} copy-done((bf16[8,128,128]{2,1,0:T(8,128)(2,1)}, bf16[8,128,128]{2,1,0:T(8,128)(2,1)S(1)}, u32[]{:S(2)}) %copy-start.14) | copy-done | bytes 262168
  36.8 0.0 copy-done.12
  36.8 0.1 copy-done.13
  37.0 15.1 %shard_map.55 = (f32[8,128,128]{2,1,0:T(8,128)}, f32[8,1,128]{2,1,0:T(1,128)}, bf16[8,144,128]{2,1,0:T(8,128)(2,1)}, bf16[8,144,128]{2,1,0:T(8,128)(2,1)}, bf16[...) custom-call(s32[128]{0:T(128)} %reshape.63.slot_ref, s32[8]{0:T(128)} %reshape.75.act_ref, ...), custom_call_target="tpu_custom_call" | custom-call | tf_op jit(solution)/shard_map/pallas_call | solution.py:164
  52.1 2.3 %collective-permute-start.13 = (bf16[8,144,128]{2,1,0:T(8,128)(2,1)}, bf16[8,144,128]{2,1,0:T(8,128)(2,1)S(1)}, u32[]{:S(2)}, u32[]{:S(2)}) collective-permute-start(bf16[8,144,128]{2,1,0:T(8,128)(2,1)} %get-tuple-element.12), channel_id=1, source_target_pairs={{4,0},{6,2},{8,4},{10,6},{12,8},{14,10},{5,1},{7,3},{9,5},{11,7},{... | collective-permute-start | bytes 884744 | tf_op jit(solution)/shard_map/ppermute | solution.py:34
  54.4 1.9 %collective-permute-start.14 = (bf16[8,144,128]{2,1,0:T(8,128)(2,1)}, bf16[8,144,128]{2,1,0:T(8,128)(2,1)S(1)}, u32[]{:S(2)}, u32[]{:S(2)}) collective-permute-start(bf16[8,144,128]{2,1,0:T(8,128)(2,1)} %get-tuple-element.13), channel_id=1, source_target_pairs={{2,0},{4,2},{6,4},{8,6},{10,8},{12,10},{14,12},{3,1},{5,3},{7,5},{... | collective-permute-start | bytes 884744 | tf_op jit(solution)/shard_map/ppermute | solution.py:34
  56.3 4.8 %collective-permute-start.15 = (bf16[8,144,128]{2,1,0:T(8,128)(2,1)}, bf16[8,144,128]{2,1,0:T(8,128)(2,1)S(1)}, u32[]{:S(2)}, u32[]{:S(2)}) collective-permute-start(bf16[8,144,128]{2,1,0:T(8,128)(2,1)} %get-tuple-element.14), channel_id=1, source_target_pairs={{0,2},{2,4},{4,6},{6,8},{8,10},{10,12},{12,14},{1,3},{3,5},{5,7},{... | collective-permute-start | bytes 884744 | tf_op jit(solution)/shard_map/ppermute | solution.py:34
  61.1 1.9 %collective-permute-start.16 = (bf16[8,144,128]{2,1,0:T(8,128)(2,1)}, bf16[8,144,128]{2,1,0:T(8,128)(2,1)S(1)}, u32[]{:S(2)}, u32[]{:S(2)}) collective-permute-start(bf16[8,144,128]{2,1,0:T(8,128)(2,1)} %get-tuple-element.15), channel_id=1, source_target_pairs={{0,4},{2,6},{4,8},{6,10},{8,12},{10,14},{1,5},{3,7},{5,9},{7,11},{... | collective-permute-start | bytes 884744 | tf_op jit(solution)/shard_map/ppermute | solution.py:34
  63.1 0.1 copy.8
  63.2 0.0 collective-permute-done.13
  63.3 6.1 %collective-permute-done.14 = bf16[8,144,128]{2,1,0:T(8,128)(2,1)S(1)} collective-permute-done((bf16[8,144,128]{2,1,0:T(8,128)(2,1)}, bf16[8,144,128]{2,1,0:T(8,128)(2,1)S(1)}, u32[]{:S(2)}, u32[]{:S(2)}) %collective-permute-start.14) | collective-permute-done | bytes 294944 | tf_op jit(solution)/shard_map/ppermute | solution.py:34
  69.5 4.0 %collective-permute-done.15 = bf16[8,144,128]{2,1,0:T(8,128)(2,1)S(1)} collective-permute-done((bf16[8,144,128]{2,1,0:T(8,128)(2,1)}, bf16[8,144,128]{2,1,0:T(8,128)(2,1)S(1)}, u32[]{:S(2)}, u32[]{:S(2)}) %collective-permute-start.15) | collective-permute-done | bytes 294944 | tf_op jit(solution)/shard_map/ppermute | solution.py:34
  73.5 0.9 %collective-permute-done.16 = bf16[8,144,128]{2,1,0:T(8,128)(2,1)S(1)} collective-permute-done((bf16[8,144,128]{2,1,0:T(8,128)(2,1)}, bf16[8,144,128]{2,1,0:T(8,128)(2,1)S(1)}, u32[]{:S(2)}, u32[]{:S(2)}) %collective-permute-start.16) | collective-permute-done | bytes 294944 | tf_op jit(solution)/shard_map/ppermute | solution.py:34
  74.4 0.6 copy-done.17
  75.1 0.1 slice_add_fusion
  75.2 0.1 divide_convert_fusion
  75.3 0.8 %copy.9 = bf16[4,2,128,128]{3,2,1,0:T(8,128)(2,1)} copy(bf16[4,2,128,128]{2,3,1,0:T(8,128)(2,1)S(1)} %divide_convert_fusion) | data formatting | bytes 524288 | tf_op jit(solution)/shard_map/convert_element_type | solution.py:207
  (39 shorter events, 0.2 us)
Async XLA Ops:
  0.0 20.6 %copy-start.18 = (s32[4]{0:T(128)S(1)}, s32[4]{0:T(128)}, u32[]{:S(2)}) copy-start(s32[4]{0:T(128)} %param.9) | copy-start | bytes 52
  0.0 11.9 %collective-permute-start.6 = (bf16[8,128,128]{2,1,0:T(8,128)(2,1)}, bf16[8,128,128]{2,1,0:T(8,128)(2,1)S(1)}, u32[]{:S(2)}, u32[]{:S(2)}) collective-permute-start(bf16[8,128,128]{2,1,0:T(8,128)(2,1)} %bitcast.20), channel_id=1, source_target_pairs={{0,1},{1,0},{2,3},{3,2},{4,5},{5,4},{6,7},{7,6},{8,9},{9,8},{10,11... | collective-permute-start | bytes 786440 | tf_op jit(solution)/shard_map/ppermute | solution.py:130
  0.0 15.3 %collective-permute-start.1 = (bf16[4,256,128]{2,1,0:T(8,128)(2,1)}, bf16[4,256,128]{2,1,0:T(8,128)(2,1)S(1)}, u32[]{:S(2)}, u32[]{:S(2)}) collective-permute-start(bf16[4,256,128]{2,1,0:T(8,128)(2,1)} %param.5), channel_id=1, source_target_pairs={{0,2},{2,4},{4,6},{6,8},{8,10},{10,12},{12,14},{1,3},{3,5},{5,7},{... | collective-permute-start | bytes 786440 | tf_op jit(solution)/shard_map/ppermute | solution.py:34
  3.6 15.1 %collective-permute-start = (bf16[4,256,128]{2,1,0:T(8,128)(2,1)}, bf16[4,256,128]{2,1,0:T(8,128)(2,1)S(1)}, u32[]{:S(2)}, u32[]{:S(2)}) collective-permute-start(bf16[4,256,128]{2,1,0:T(8,128)(2,1)} %param.5), channel_id=1, source_target_pairs={{0,4},{2,6},{4,8},{6,10},{8,12},{10,14},{1,5},{3,7},{5,9},{7,11},{... | collective-permute-start | bytes 786440 | tf_op jit(solution)/shard_map/ppermute | solution.py:34
  5.5 15.2 %collective-permute-start.3 = (bf16[4,256,128]{2,1,0:T(8,128)(2,1)}, bf16[4,256,128]{2,1,0:T(8,128)(2,1)S(1)}, u32[]{:S(2)}, u32[]{:S(2)}) collective-permute-start(bf16[4,256,128]{2,1,0:T(8,128)(2,1)} %param.5), channel_id=1, source_target_pairs={{4,0},{6,2},{8,4},{10,6},{12,8},{14,10},{5,1},{7,3},{9,5},{11,7},{... | collective-permute-start | bytes 786440 | tf_op jit(solution)/shard_map/ppermute | solution.py:34
  9.5 15.2 %collective-permute-start.2 = (bf16[4,256,128]{2,1,0:T(8,128)(2,1)}, bf16[4,256,128]{2,1,0:T(8,128)(2,1)S(1)}, u32[]{:S(2)}, u32[]{:S(2)}) collective-permute-start(bf16[4,256,128]{2,1,0:T(8,128)(2,1)} %param.5), channel_id=1, source_target_pairs={{2,0},{4,2},{6,4},{8,6},{10,8},{12,10},{14,12},{3,1},{5,3},{7,5},{... | collective-permute-start | bytes 786440 | tf_op jit(solution)/shard_map/ppermute | solution.py:34
  11.9 24.9 %copy-start.2 = (bf16[8,128,128]{2,1,0:T(8,128)(2,1)}, bf16[8,128,128]{2,1,0:T(8,128)(2,1)S(1)}, u32[]{:S(2)}) copy-start(bf16[8,128,128]{2,1,0:T(8,128)(2,1)S(1)} %collective-permute-done.6.refs_7_) | copy-start | bytes 786436
  11.9 17.7 %collective-permute-start.11 = (bf16[4,256,128]{2,1,0:T(8,128)(2,1)}, bf16[4,256,128]{2,1,0:T(8,128)(2,1)S(1)}, u32[]{:S(2)}, u32[]{:S(2)}) collective-permute-start(bf16[4,256,128]{2,1,0:T(8,128)(2,1)} %param.6), channel_id=1, source_target_pairs={{2,0},{4,2},{6,4},{8,6},{10,8},{12,10},{14,12},{3,1},{5,3},{7,5},{... | collective-permute-start | bytes 786440 | tf_op jit(solution)/shard_map/ppermute | solution.py:34
  15.3 21.5 %copy-start.3 = (bf16[4,256,128]{2,1,0:T(8,128)(2,1)}, bf16[4,256,128]{2,1,0:T(8,128)(2,1)S(1)}, u32[]{:S(2)}) copy-start(bf16[4,256,128]{2,1,0:T(8,128)(2,1)S(1)} %collective-permute-done.1) | copy-start | bytes 786436
  15.3 18.7 %collective-permute-start.10 = (bf16[4,256,128]{2,1,0:T(8,128)(2,1)}, bf16[4,256,128]{2,1,0:T(8,128)(2,1)S(1)}, u32[]{:S(2)}, u32[]{:S(2)}) collective-permute-start(bf16[4,256,128]{2,1,0:T(8,128)(2,1)} %param.6), channel_id=1, source_target_pairs={{0,2},{2,4},{4,6},{6,8},{8,10},{10,12},{12,14},{1,3},{3,5},{5,7},{... | collective-permute-start | bytes 786440 | tf_op jit(solution)/shard_map/ppermute | solution.py:34
  18.7 18.1 %copy-start.4 = (bf16[4,256,128]{2,1,0:T(8,128)(2,1)}, bf16[4,256,128]{2,1,0:T(8,128)(2,1)S(1)}, u32[]{:S(2)}) copy-start(bf16[4,256,128]{2,1,0:T(8,128)(2,1)S(1)} %collective-permute-done) | copy-start | bytes 786436
  18.7 15.3 %collective-permute-start.9 = (bf16[4,256,128]{2,1,0:T(8,128)(2,1)}, bf16[4,256,128]{2,1,0:T(8,128)(2,1)S(1)}, u32[]{:S(2)}, u32[]{:S(2)}) collective-permute-start(bf16[4,256,128]{2,1,0:T(8,128)(2,1)} %param.6), channel_id=1, source_target_pairs={{0,4},{2,6},{4,8},{6,10},{8,12},{10,14},{1,5},{3,7},{5,9},{7,11},{... | collective-permute-start | bytes 786440 | tf_op jit(solution)/shard_map/ppermute | solution.py:34
  20.7 16.0 %copy-start.5 = (bf16[4,256,128]{2,1,0:T(8,128)(2,1)}, bf16[4,256,128]{2,1,0:T(8,128)(2,1)S(1)}, u32[]{:S(2)}) copy-start(bf16[4,256,128]{2,1,0:T(8,128)(2,1)S(1)} %collective-permute-done.3) | copy-start | bytes 786436
  20.7 15.1 %collective-permute-start.12 = (bf16[4,256,128]{2,1,0:T(8,128)(2,1)}, bf16[4,256,128]{2,1,0:T(8,128)(2,1)S(1)}, u32[]{:S(2)}, u32[]{:S(2)}) collective-permute-start(bf16[4,256,128]{2,1,0:T(8,128)(2,1)} %param.6), channel_id=1, source_target_pairs={{4,0},{6,2},{8,4},{10,6},{12,8},{14,10},{5,1},{7,3},{9,5},{11,7},{... | collective-permute-start | bytes 786440 | tf_op jit(solution)/shard_map/ppermute | solution.py:34
  24.6 12.1 %copy-start.6 = (bf16[4,256,128]{2,1,0:T(8,128)(2,1)}, bf16[4,256,128]{2,1,0:T(8,128)(2,1)S(1)}, u32[]{:S(2)}) copy-start(bf16[4,256,128]{2,1,0:T(8,128)(2,1)S(1)} %collective-permute-done.2) | copy-start | bytes 786436
  24.7 11.2 %collective-permute-start.5 = (bf16[8,128,128]{2,1,0:T(8,128)(2,1)S(1)}, bf16[8,128,128]{2,1,0:T(8,128)(2,1)S(1)}, u32[]{:S(2)}, u32[]{:S(2)}) collective-permute-start(bf16[8,128,128]{2,1,0:T(8,128)(2,1)S(1)} %bitcast.22), channel_id=1, source_target_pairs={{0,1},{1,0},{2,3},{3,2},{4,5},{5,4},{6,7},{7,6},{8,9},{9,8},{10,11... | collective-permute-start | bytes 786440 | tf_op jit(solution)/shard_map/ppermute | solution.py:130
  29.6 7.1 %copy-start.7 = (bf16[4,256,128]{2,1,0:T(8,128)(2,1)}, bf16[4,256,128]{2,1,0:T(8,128)(2,1)S(1)}, u32[]{:S(2)}) copy-start(bf16[4,256,128]{2,1,0:T(8,128)(2,1)S(1)} %collective-permute-done.11) | copy-start | bytes 786436
  29.6 5.5 %copy-start.15 = (s32[4,2,16]{2,1,0:T(2,128)S(1)}, s32[4,2,16]{2,1,0:T(2,128)}, u32[]{:S(2)}) copy-start(s32[4,2,16]{2,1,0:T(2,128)} %param.8) | copy-start | bytes 1540
  29.6 5.5 %copy-start.16 = (s32[4,2,16]{2,1,0:T(2,128)S(1)}, s32[4,2,16]{2,1,0:T(2,128)}, u32[]{:S(2)}) copy-start(s32[4,2,16]{2,1,0:T(2,128)} %param.7) | copy-start | bytes 1540
  29.6 6.2 %collective-permute-start.4 = (bf16[8,128,128]{2,1,0:T(8,128)(2,1)S(1)}, bf16[8,128,128]{2,1,0:T(8,128)(2,1)S(1)}, u32[]{:S(2)}, u32[]{:S(2)}) collective-permute-start(bf16[8,128,128]{2,1,0:T(8,128)(2,1)S(1)} %bitcast.24), channel_id=1, source_target_pairs={{0,1},{1,0},{2,3},{3,2},{4,5},{5,4},{6,7},{7,6},{8,9},{9,8},{10,11... | collective-permute-start | bytes 786440 | tf_op jit(solution)/shard_map/ppermute | solution.py:130
  34.0 2.8 %copy-start.8 = (bf16[4,256,128]{2,1,0:T(8,128)(2,1)}, bf16[4,256,128]{2,1,0:T(8,128)(2,1)S(1)}, u32[]{:S(2)}) copy-start(bf16[4,256,128]{2,1,0:T(8,128)(2,1)S(1)} %collective-permute-done.10) | copy-start | bytes 786436
  34.0 1.9 %collective-permute-start.8 = (bf16[8,128,128]{2,1,0:T(8,128)(2,1)S(1)}, bf16[8,128,128]{2,1,0:T(8,128)(2,1)S(1)}, u32[]{:S(2)}, u32[]{:S(2)}) collective-permute-start(bf16[8,128,128]{2,1,0:T(8,128)(2,1)S(1)} %bitcast.26), channel_id=1, source_target_pairs={{0,1},{1,0},{2,3},{3,2},{4,5},{5,4},{6,7},{7,6},{8,9},{9,8},{10,11... | collective-permute-start | bytes 786440 | tf_op jit(solution)/shard_map/ppermute | solution.py:130
  34.0 2.8 %copy-start.9 = (bf16[4,256,128]{2,1,0:T(8,128)(2,1)}, bf16[4,256,128]{2,1,0:T(8,128)(2,1)S(1)}, u32[]{:S(2)}) copy-start(bf16[4,256,128]{2,1,0:T(8,128)(2,1)S(1)} %collective-permute-done.9) | copy-start | bytes 786436
  34.0 1.9 %collective-permute-start.7 = (bf16[8,128,128]{2,1,0:T(8,128)(2,1)S(1)}, bf16[8,128,128]{2,1,0:T(8,128)(2,1)S(1)}, u32[]{:S(2)}, u32[]{:S(2)}) collective-permute-start(bf16[8,128,128]{2,1,0:T(8,128)(2,1)S(1)} %bitcast.28), channel_id=1, source_target_pairs={{0,1},{1,0},{2,3},{3,2},{4,5},{5,4},{6,7},{7,6},{8,9},{9,8},{10,11... | collective-permute-start | bytes 786440 | tf_op jit(solution)/shard_map/ppermute | solution.py:130
  35.8 1.0 %copy-start.10 = (bf16[4,256,128]{2,1,0:T(8,128)(2,1)}, bf16[4,256,128]{2,1,0:T(8,128)(2,1)S(1)}, u32[]{:S(2)}) copy-start(bf16[4,256,128]{2,1,0:T(8,128)(2,1)S(1)} %collective-permute-done.12) | copy-start | bytes 786436
  35.8 1.0 %copy-start.11 = (bf16[8,128,128]{2,1,0:T(8,128)(2,1)}, bf16[8,128,128]{2,1,0:T(8,128)(2,1)S(1)}, u32[]{:S(2)}) copy-start(bf16[8,128,128]{2,1,0:T(8,128)(2,1)S(1)} %collective-permute-done.5.refs_6_) | copy-start | bytes 786436
  35.9 1.0 %copy-start.12 = (bf16[8,128,128]{2,1,0:T(8,128)(2,1)}, bf16[8,128,128]{2,1,0:T(8,128)(2,1)S(1)}, u32[]{:S(2)}) copy-start(bf16[8,128,128]{2,1,0:T(8,128)(2,1)S(1)} %collective-permute-done.4.refs_5_) | copy-start | bytes 786436
  35.9 1.1 %copy-start.13 = (bf16[8,128,128]{2,1,0:T(8,128)(2,1)}, bf16[8,128,128]{2,1,0:T(8,128)(2,1)S(1)}, u32[]{:S(2)}) copy-start(bf16[8,128,128]{2,1,0:T(8,128)(2,1)S(1)} %collective-permute-done.8.refs_9_) | copy-start | bytes 786436
  35.9 0.8 %copy-start.14 = (bf16[8,128,128]{2,1,0:T(8,128)(2,1)}, bf16[8,128,128]{2,1,0:T(8,128)(2,1)S(1)}, u32[]{:S(2)}) copy-start(bf16[8,128,128]{2,1,0:T(8,128)(2,1)S(1)} %collective-permute-done.7.refs_8_) | copy-start | bytes 786436
  37.0 26.1 %copy-start = (bf16[4,256,128]{2,1,0:T(8,128)(2,1)S(1)}, bf16[4,256,128]{2,1,0:T(8,128)(2,1)}, u32[]{:S(2)}) copy-start(bf16[4,256,128]{2,1,0:T(8,128)(2,1)} %param.6) | copy-start | bytes 786436
  52.1 11.1 %collective-permute-start.13 = (bf16[8,144,128]{2,1,0:T(8,128)(2,1)}, bf16[8,144,128]{2,1,0:T(8,128)(2,1)S(1)}, u32[]{:S(2)}, u32[]{:S(2)}) collective-permute-start(bf16[8,144,128]{2,1,0:T(8,128)(2,1)} %get-tuple-element.12), channel_id=1, source_target_pairs={{4,0},{6,2},{8,4},{10,6},{12,8},{14,10},{5,1},{7,3},{9,5},{11,7},{... | collective-permute-start | bytes 884744 | tf_op jit(solution)/shard_map/ppermute | solution.py:34
  54.4 15.0 %collective-permute-start.14 = (bf16[8,144,128]{2,1,0:T(8,128)(2,1)}, bf16[8,144,128]{2,1,0:T(8,128)(2,1)S(1)}, u32[]{:S(2)}, u32[]{:S(2)}) collective-permute-start(bf16[8,144,128]{2,1,0:T(8,128)(2,1)} %get-tuple-element.13), channel_id=1, source_target_pairs={{2,0},{4,2},{6,4},{8,6},{10,8},{12,10},{14,12},{3,1},{5,3},{7,5},{... | collective-permute-start | bytes 884744 | tf_op jit(solution)/shard_map/ppermute | solution.py:34
  56.3 17.1 %collective-permute-start.15 = (bf16[8,144,128]{2,1,0:T(8,128)(2,1)}, bf16[8,144,128]{2,1,0:T(8,128)(2,1)S(1)}, u32[]{:S(2)}, u32[]{:S(2)}) collective-permute-start(bf16[8,144,128]{2,1,0:T(8,128)(2,1)} %get-tuple-element.14), channel_id=1, source_target_pairs={{0,2},{2,4},{4,6},{6,8},{8,10},{10,12},{12,14},{1,3},{3,5},{5,7},{... | collective-permute-start | bytes 884744 | tf_op jit(solution)/shard_map/ppermute | solution.py:34
  61.1 13.2 %collective-permute-start.16 = (bf16[8,144,128]{2,1,0:T(8,128)(2,1)}, bf16[8,144,128]{2,1,0:T(8,128)(2,1)S(1)}, u32[]{:S(2)}, u32[]{:S(2)}) collective-permute-start(bf16[8,144,128]{2,1,0:T(8,128)(2,1)} %get-tuple-element.15), channel_id=1, source_target_pairs={{0,4},{2,6},{4,8},{6,10},{8,12},{10,14},{1,5},{3,7},{5,9},{7,11},{... | collective-permute-start | bytes 884744 | tf_op jit(solution)/shard_map/ppermute | solution.py:34
  73.5 1.6 %copy-start.1 = (f32[8,128,128]{2,1,0:T(8,128)S(1)}, f32[8,128,128]{2,1,0:T(8,128)}, u32[]{:S(2)}) copy-start(f32[8,128,128]{2,1,0:T(8,128)} %get-tuple-element.11) | copy-start | bytes 1572868
  74.4 0.7 copy-start.17

commit v6 on v5

--- a/solution.py
+++ b/solution.py
@@ -64,12 +64,12 @@
 
     def one_query(i, carry):
         q_slot = center + (i // blocks) * rimmed + halo + i % blocks
-        query = key_e[q_slot]
+        query = key_e[q_slot] * jnp.asarray(score_scale, jnp.bfloat16)
         slots = [slot_ref[i * K + k] for k in range(K)]
         for k in range(K):
             s = slots[k]
             part = lax.dot_general(query, key_e[s], dims_t, preferred_element_type=jnp.float32)
-            score_ref[:, k * BLOCK : (k + 1) * BLOCK] = part * score_scale
+            score_ref[:, k * BLOCK : (k + 1) * BLOCK] = part
             value_ref[k * BLOCK : (k + 1) * BLOCK, :] = key_v[s]
         score = score_ref[...]
         peak = jnp.max(score, axis=-1, keepdims=True)
@@ -77,12 +77,11 @@
         prob = exponent / jnp.sum(exponent, axis=-1, keepdims=True)
         attention = prob.astype(jnp.bfloat16)
         estimate = jnp.dot(attention, value_ref[...], preferred_element_type=jnp.float32)
-        estimate = estimate.astype(jnp.bfloat16).astype(jnp.float32)
         active = act_ref[i].astype(jnp.float32)
-        masked = (attention.astype(jnp.float32) * active).astype(jnp.bfloat16)
+        estimate = estimate.astype(jnp.bfloat16).astype(jnp.float32) * active
         estimate_t = estimate.T.astype(jnp.bfloat16)
-        contrib_t = jnp.dot(estimate_t, masked, preferred_element_type=jnp.float32)
-        weights = jnp.sum(prob * active, axis=0, keepdims=True)
+        contrib_t = jnp.dot(estimate_t, attention, preferred_element_type=jnp.float32)
+        weights = jnp.sum(prob, axis=0, keepdims=True) * active
         for k in range(K):
             s = slots[k]
             acc[s] = acc[s] + contrib_t[:, k * BLOCK : (k + 1) * BLOCK]

time: 76.8 us -> 76.4 us (level)
  no operation moved by 1% of the time
where the time goes in v6:
time: 76.4 us; the launch traced here: 75.8 us
  starting transfers between devices  35.9 us (47%)
  waiting for transfers between devices  20.3 us (27%)
  Pallas kernels  14.8 us (19%)
  local copies, waits for them, and re-layouts  3.9 us (5%)
    ppermute x12, starting transfers between devices, passed_along(): return lax.ppermute(block, axis, route)  35.3 us
    ppermute x12, waiting for transfers between devices, passed_along(): return lax.ppermute(block, axis, route)  20.3 us
    pallas_call x1, Pallas kernels, shards(): pl.pallas_call(kernel, out_shape=out_shape, in_specs=[smem, smem] + [hbm]...  14.8 us
    unnamed x38, local copies, waits for them, and re-layouts  1.67 us
  transfers between devices with their start and end apart: 17, of which 5 were waited for; matrix products, arithmetic and copies ran while one was open for 2% of the time, Pallas kernels for 0%

profile of v6, /device:TPU:22, one launch (start us, length us, event | category | flops | bytes accessed | tf_op | source)
XLA Modules:
  0.0 75.8 jit_solution(18269104225675368791)
XLA Ops:
  0.0 0.0 collective-permute-start.6
  0.0 3.6 %collective-permute-start.1 = (bf16[4,256,128]{2,1,0:T(8,128)(2,1)}, bf16[4,256,128]{2,1,0:T(8,128)(2,1)S(1)}, u32[]{:S(2)}, u32[]{:S(2)}) collective-permute-start(bf16[4,256,128]{2,1,0:T(8,128)(2,1)} %param.5), channel_id=1, source_target_pairs={{0,2},{2,4},{4,6},{6,8},{8,10},{10,12},{12,14},{1,3},{3,5},{5,7},{... | collective-permute-start | bytes 786440 | tf_op jit(solution)/shard_map/ppermute | solution.py:34
  3.6 1.9 %collective-permute-start = (bf16[4,256,128]{2,1,0:T(8,128)(2,1)}, bf16[4,256,128]{2,1,0:T(8,128)(2,1)S(1)}, u32[]{:S(2)}, u32[]{:S(2)}) collective-permute-start(bf16[4,256,128]{2,1,0:T(8,128)(2,1)} %param.5), channel_id=1, source_target_pairs={{0,4},{2,6},{4,8},{6,10},{8,12},{10,14},{1,5},{3,7},{5,9},{7,11},{... | collective-permute-start | bytes 786440 | tf_op jit(solution)/shard_map/ppermute | solution.py:34
  5.5 3.9 %collective-permute-start.3 = (bf16[4,256,128]{2,1,0:T(8,128)(2,1)}, bf16[4,256,128]{2,1,0:T(8,128)(2,1)S(1)}, u32[]{:S(2)}, u32[]{:S(2)}) collective-permute-start(bf16[4,256,128]{2,1,0:T(8,128)(2,1)} %param.5), channel_id=1, source_target_pairs={{4,0},{6,2},{8,4},{10,6},{12,8},{14,10},{5,1},{7,3},{9,5},{11,7},{... | collective-permute-start | bytes 786440 | tf_op jit(solution)/shard_map/ppermute | solution.py:34
  9.5 2.4 %collective-permute-start.2 = (bf16[4,256,128]{2,1,0:T(8,128)(2,1)}, bf16[4,256,128]{2,1,0:T(8,128)(2,1)S(1)}, u32[]{:S(2)}, u32[]{:S(2)}) collective-permute-start(bf16[4,256,128]{2,1,0:T(8,128)(2,1)} %param.5), channel_id=1, source_target_pairs={{2,0},{4,2},{6,4},{8,6},{10,8},{12,10},{14,12},{3,1},{5,3},{7,5},{... | collective-permute-start | bytes 786440 | tf_op jit(solution)/shard_map/ppermute | solution.py:34
  11.9 0.0 collective-permute-done.6.refs_7_
  11.9 3.4 %collective-permute-start.11 = (bf16[4,256,128]{2,1,0:T(8,128)(2,1)}, bf16[4,256,128]{2,1,0:T(8,128)(2,1)S(1)}, u32[]{:S(2)}, u32[]{:S(2)}) collective-permute-start(bf16[4,256,128]{2,1,0:T(8,128)(2,1)} %param.6), channel_id=1, source_target_pairs={{2,0},{4,2},{6,4},{8,6},{10,8},{12,10},{14,12},{3,1},{5,3},{7,5},{... | collective-permute-start | bytes 786440 | tf_op jit(solution)/shard_map/ppermute | solution.py:34
  15.3 0.0 collective-permute-done.1
  15.3 3.4 %collective-permute-start.10 = (bf16[4,256,128]{2,1,0:T(8,128)(2,1)}, bf16[4,256,128]{2,1,0:T(8,128)(2,1)S(1)}, u32[]{:S(2)}, u32[]{:S(2)}) collective-permute-start(bf16[4,256,128]{2,1,0:T(8,128)(2,1)} %param.6), channel_id=1, source_target_pairs={{0,2},{2,4},{4,6},{6,8},{8,10},{10,12},{12,14},{1,3},{3,5},{5,7},{... | collective-permute-start | bytes 786440 | tf_op jit(solution)/shard_map/ppermute | solution.py:34
  18.7 0.0 collective-permute-done
  18.7 0.0 copy-start.4
  18.7 1.9 %collective-permute-start.9 = (bf16[4,256,128]{2,1,0:T(8,128)(2,1)}, bf16[4,256,128]{2,1,0:T(8,128)(2,1)S(1)}, u32[]{:S(2)}, u32[]{:S(2)}) collective-permute-start(bf16[4,256,128]{2,1,0:T(8,128)(2,1)} %param.6), channel_id=1, source_target_pairs={{0,4},{2,6},{4,8},{6,10},{8,12},{10,14},{1,5},{3,7},{5,9},{7,11},{... | collective-permute-start | bytes 786440 | tf_op jit(solution)/shard_map/ppermute | solution.py:34
  20.6 0.1 fusion.1
  20.7 0.0 collective-permute-done.3
  20.7 3.9 %collective-permute-start.12 = (bf16[4,256,128]{2,1,0:T(8,128)(2,1)}, bf16[4,256,128]{2,1,0:T(8,128)(2,1)S(1)}, u32[]{:S(2)}, u32[]{:S(2)}) collective-permute-start(bf16[4,256,128]{2,1,0:T(8,128)(2,1)} %param.6), channel_id=1, source_target_pairs={{4,0},{6,2},{8,4},{10,6},{12,8},{14,10},{5,1},{7,3},{9,5},{11,7},{... | collective-permute-start | bytes 786440 | tf_op jit(solution)/shard_map/ppermute | solution.py:34
  24.6 0.0 collective-permute-done.2
  24.7 0.1 collective-permute-start.5
  24.7 4.9 %collective-permute-done.11 = bf16[4,256,128]{2,1,0:T(8,128)(2,1)S(1)} collective-permute-done((bf16[4,256,128]{2,1,0:T(8,128)(2,1)}, bf16[4,256,128]{2,1,0:T(8,128)(2,1)S(1)}, u32[]{:S(2)}, u32[]{:S(2)}) %collective-permute-start.11) | collective-permute-done | bytes 262176 | tf_op jit(solution)/shard_map/ppermute | solution.py:34
  29.6 0.0 collective-permute-start.4
  29.6 4.4 %collective-permute-done.10 = bf16[4,256,128]{2,1,0:T(8,128)(2,1)S(1)} collective-permute-done((bf16[4,256,128]{2,1,0:T(8,128)(2,1)}, bf16[4,256,128]{2,1,0:T(8,128)(2,1)S(1)}, u32[]{:S(2)}, u32[]{:S(2)}) %collective-permute-start.10) | collective-permute-done | bytes 262176 | tf_op jit(solution)/shard_map/ppermute | solution.py:34
  34.0 0.0 collective-permute-start.8
  34.0 0.0 collective-permute-done.9
  34.0 0.5 collective-permute-start.7
  34.5 0.6 reshape.75.act_ref
  35.1 0.1 add_clamp_fusion
  35.2 0.6 reshape.63.slot_ref
  35.8 0.0 collective-permute-done.12
  35.8 0.0 collective-permute-done.5.refs_6_
  35.9 0.0 collective-permute-done.4.refs_5_
  35.9 0.0 collective-permute-done.8.refs_9_
  35.9 0.0 collective-permute-done.7.refs_8_
  35.9 0.8 %copy-done.14 = bf16[8,128,128]{2,1,0:T(8,128)(2,1)} copy-done((bf16[8,128,128]{2,1,0:T(8,128)(2,1)}, bf16[8,128,128]{2,1,0:T(8,128)(2,1)S(1)}, u32[]{:S(2)}) %copy-start.14) | copy-done | bytes 262168
  36.8 0.0 copy-done.12
  36.8 0.1 copy-done.13
  37.0 14.8 %shard_map.55 = (f32[8,128,128]{2,1,0:T(8,128)}, f32[8,1,128]{2,1,0:T(1,128)}, bf16[8,144,128]{2,1,0:T(8,128)(2,1)}, bf16[8,144,128]{2,1,0:T(8,128)(2,1)}, bf16[...) custom-call(s32[128]{0:T(128)} %reshape.63.slot_ref, s32[8]{0:T(128)} %reshape.75.act_ref, ...), custom_call_target="tpu_custom_call" | custom-call | tf_op jit(solution)/shard_map/pallas_call | solution.py:163
  51.8 2.3 %collective-permute-start.13 = (bf16[8,144,128]{2,1,0:T(8,128)(2,1)}, bf16[8,144,128]{2,1,0:T(8,128)(2,1)S(1)}, u32[]{:S(2)}, u32[]{:S(2)}) collective-permute-start(bf16[8,144,128]{2,1,0:T(8,128)(2,1)} %get-tuple-element.12), channel_id=1, source_target_pairs={{4,0},{6,2},{8,4},{10,6},{12,8},{14,10},{5,1},{7,3},{9,5},{11,7},{... | collective-permute-start | bytes 884744 | tf_op jit(solution)/shard_map/ppermute | solution.py:34
  54.0 1.9 %collective-permute-start.14 = (bf16[8,144,128]{2,1,0:T(8,128)(2,1)}, bf16[8,144,128]{2,1,0:T(8,128)(2,1)S(1)}, u32[]{:S(2)}, u32[]{:S(2)}) collective-permute-start(bf16[8,144,128]{2,1,0:T(8,128)(2,1)} %get-tuple-element.13), channel_id=1, source_target_pairs={{2,0},{4,2},{6,4},{8,6},{10,8},{12,10},{14,12},{3,1},{5,3},{7,5},{... | collective-permute-start | bytes 884744 | tf_op jit(solution)/shard_map/ppermute | solution.py:34
  56.0 4.8 %collective-permute-start.15 = (bf16[8,144,128]{2,1,0:T(8,128)(2,1)}, bf16[8,144,128]{2,1,0:T(8,128)(2,1)S(1)}, u32[]{:S(2)}, u32[]{:S(2)}) collective-permute-start(bf16[8,144,128]{2,1,0:T(8,128)(2,1)} %get-tuple-element.14), channel_id=1, source_target_pairs={{0,2},{2,4},{4,6},{6,8},{8,10},{10,12},{12,14},{1,3},{3,5},{5,7},{... | collective-permute-start | bytes 884744 | tf_op jit(solution)/shard_map/ppermute | solution.py:34
  60.8 1.9 %collective-permute-start.16 = (bf16[8,144,128]{2,1,0:T(8,128)(2,1)}, bf16[8,144,128]{2,1,0:T(8,128)(2,1)S(1)}, u32[]{:S(2)}, u32[]{:S(2)}) collective-permute-start(bf16[8,144,128]{2,1,0:T(8,128)(2,1)} %get-tuple-element.15), channel_id=1, source_target_pairs={{0,4},{2,6},{4,8},{6,10},{8,12},{10,14},{1,5},{3,7},{5,9},{7,11},{... | collective-permute-start | bytes 884744 | tf_op jit(solution)/shard_map/ppermute | solution.py:34
  62.7 0.1 copy.8
  62.9 0.0 collective-permute-done.13
  63.0 6.1 %collective-permute-done.14 = bf16[8,144,128]{2,1,0:T(8,128)(2,1)S(1)} collective-permute-done((bf16[8,144,128]{2,1,0:T(8,128)(2,1)}, bf16[8,144,128]{2,1,0:T(8,128)(2,1)S(1)}, u32[]{:S(2)}, u32[]{:S(2)}) %collective-permute-start.14) | collective-permute-done | bytes 294944 | tf_op jit(solution)/shard_map/ppermute | solution.py:34
  69.1 4.0 %collective-permute-done.15 = bf16[8,144,128]{2,1,0:T(8,128)(2,1)S(1)} collective-permute-done((bf16[8,144,128]{2,1,0:T(8,128)(2,1)}, bf16[8,144,128]{2,1,0:T(8,128)(2,1)S(1)}, u32[]{:S(2)}, u32[]{:S(2)}) %collective-permute-start.15) | collective-permute-done | bytes 294944 | tf_op jit(solution)/shard_map/ppermute | solution.py:34
  73.2 0.9 %collective-permute-done.16 = bf16[8,144,128]{2,1,0:T(8,128)(2,1)S(1)} collective-permute-done((bf16[8,144,128]{2,1,0:T(8,128)(2,1)}, bf16[8,144,128]{2,1,0:T(8,128)(2,1)S(1)}, u32[]{:S(2)}, u32[]{:S(2)}) %collective-permute-start.16) | collective-permute-done | bytes 294944 | tf_op jit(solution)/shard_map/ppermute | solution.py:34
  74.1 0.6 copy-done.17
  74.8 0.1 slice_add_fusion
  74.9 0.1 divide_convert_fusion
  75.0 0.8 %copy.9 = bf16[4,2,128,128]{3,2,1,0:T(8,128)(2,1)} copy(bf16[4,2,128,128]{2,3,1,0:T(8,128)(2,1)S(1)} %divide_convert_fusion) | data formatting | bytes 524288 | tf_op jit(solution)/shard_map/convert_element_type | solution.py:206
  (39 shorter events, 0.2 us)
Async XLA Ops:
  0.0 20.6 %copy-start.18 = (s32[4]{0:T(128)S(1)}, s32[4]{0:T(128)}, u32[]{:S(2)}) copy-start(s32[4]{0:T(128)} %param.9) | copy-start | bytes 52
  0.0 11.9 %collective-permute-start.6 = (bf16[8,128,128]{2,1,0:T(8,128)(2,1)}, bf16[8,128,128]{2,1,0:T(8,128)(2,1)S(1)}, u32[]{:S(2)}, u32[]{:S(2)}) collective-permute-start(bf16[8,128,128]{2,1,0:T(8,128)(2,1)} %bitcast.20), channel_id=1, source_target_pairs={{0,1},{1,0},{2,3},{3,2},{4,5},{5,4},{6,7},{7,6},{8,9},{9,8},{10,11... | collective-permute-start | bytes 786440 | tf_op jit(solution)/shard_map/ppermute | solution.py:129
  0.0 15.3 %collective-permute-start.1 = (bf16[4,256,128]{2,1,0:T(8,128)(2,1)}, bf16[4,256,128]{2,1,0:T(8,128)(2,1)S(1)}, u32[]{:S(2)}, u32[]{:S(2)}) collective-permute-start(bf16[4,256,128]{2,1,0:T(8,128)(2,1)} %param.5), channel_id=1, source_target_pairs={{0,2},{2,4},{4,6},{6,8},{8,10},{10,12},{12,14},{1,3},{3,5},{5,7},{... | collective-permute-start | bytes 786440 | tf_op jit(solution)/shard_map/ppermute | solution.py:34
  3.6 15.1 %collective-permute-start = (bf16[4,256,128]{2,1,0:T(8,128)(2,1)}, bf16[4,256,128]{2,1,0:T(8,128)(2,1)S(1)}, u32[]{:S(2)}, u32[]{:S(2)}) collective-permute-start(bf16[4,256,128]{2,1,0:T(8,128)(2,1)} %param.5), channel_id=1, source_target_pairs={{0,4},{2,6},{4,8},{6,10},{8,12},{10,14},{1,5},{3,7},{5,9},{7,11},{... | collective-permute-start | bytes 786440 | tf_op jit(solution)/shard_map/ppermute | solution.py:34
  5.5 15.2 %collective-permute-start.3 = (bf16[4,256,128]{2,1,0:T(8,128)(2,1)}, bf16[4,256,128]{2,1,0:T(8,128)(2,1)S(1)}, u32[]{:S(2)}, u32[]{:S(2)}) collective-permute-start(bf16[4,256,128]{2,1,0:T(8,128)(2,1)} %param.5), channel_id=1, source_target_pairs={{4,0},{6,2},{8,4},{10,6},{12,8},{14,10},{5,1},{7,3},{9,5},{11,7},{... | collective-permute-start | bytes 786440 | tf_op jit(solution)/shard_map/ppermute | solution.py:34
  9.5 15.2 %collective-permute-start.2 = (bf16[4,256,128]{2,1,0:T(8,128)(2,1)}, bf16[4,256,128]{2,1,0:T(8,128)(2,1)S(1)}, u32[]{:S(2)}, u32[]{:S(2)}) collective-permute-start(bf16[4,256,128]{2,1,0:T(8,128)(2,1)} %param.5), channel_id=1, source_target_pairs={{2,0},{4,2},{6,4},{8,6},{10,8},{12,10},{14,12},{3,1},{5,3},{7,5},{... | collective-permute-start | bytes 786440 | tf_op jit(solution)/shard_map/ppermute | solution.py:34
  11.9 24.9 %copy-start.2 = (bf16[8,128,128]{2,1,0:T(8,128)(2,1)}, bf16[8,128,128]{2,1,0:T(8,128)(2,1)S(1)}, u32[]{:S(2)}) copy-start(bf16[8,128,128]{2,1,0:T(8,128)(2,1)S(1)} %collective-permute-done.6.refs_7_) | copy-start | bytes 786436
  11.9 17.7 %collective-permute-start.11 = (bf16[4,256,128]{2,1,0:T(8,128)(2,1)}, bf16[4,256,128]{2,1,0:T(8,128)(2,1)S(1)}, u32[]{:S(2)}, u32[]{:S(2)}) collective-permute-start(bf16[4,256,128]{2,1,0:T(8,128)(2,1)} %param.6), channel_id=1, source_target_pairs={{2,0},{4,2},{6,4},{8,6},{10,8},{12,10},{14,12},{3,1},{5,3},{7,5},{... | collective-permute-start | bytes 786440 | tf_op jit(solution)/shard_map/ppermute | solution.py:34
  15.3 21.5 %copy-start.3 = (bf16[4,256,128]{2,1,0:T(8,128)(2,1)}, bf16[4,256,128]{2,1,0:T(8,128)(2,1)S(1)}, u32[]{:S(2)}) copy-start(bf16[4,256,128]{2,1,0:T(8,128)(2,1)S(1)} %collective-permute-done.1) | copy-start | bytes 786436
  15.3 18.7 %collective-permute-start.10 = (bf16[4,256,128]{2,1,0:T(8,128)(2,1)}, bf16[4,256,128]{2,1,0:T(8,128)(2,1)S(1)}, u32[]{:S(2)}, u32[]{:S(2)}) collective-permute-start(bf16[4,256,128]{2,1,0:T(8,128)(2,1)} %param.6), channel_id=1, source_target_pairs={{0,2},{2,4},{4,6},{6,8},{8,10},{10,12},{12,14},{1,3},{3,5},{5,7},{... | collective-permute-start | bytes 786440 | tf_op jit(solution)/shard_map/ppermute | solution.py:34
  18.7 18.1 %copy-start.4 = (bf16[4,256,128]{2,1,0:T(8,128)(2,1)}, bf16[4,256,128]{2,1,0:T(8,128)(2,1)S(1)}, u32[]{:S(2)}) copy-start(bf16[4,256,128]{2,1,0:T(8,128)(2,1)S(1)} %collective-permute-done) | copy-start | bytes 786436
  18.7 15.3 %collective-permute-start.9 = (bf16[4,256,128]{2,1,0:T(8,128)(2,1)}, bf16[4,256,128]{2,1,0:T(8,128)(2,1)S(1)}, u32[]{:S(2)}, u32[]{:S(2)}) collective-permute-start(bf16[4,256,128]{2,1,0:T(8,128)(2,1)} %param.6), channel_id=1, source_target_pairs={{0,4},{2,6},{4,8},{6,10},{8,12},{10,14},{1,5},{3,7},{5,9},{7,11},{... | collective-permute-start | bytes 786440 | tf_op jit(solution)/shard_map/ppermute | solution.py:34
  20.7 16.0 %copy-start.5 = (bf16[4,256,128]{2,1,0:T(8,128)(2,1)}, bf16[4,256,128]{2,1,0:T(8,128)(2,1)S(1)}, u32[]{:S(2)}) copy-start(bf16[4,256,128]{2,1,0:T(8,128)(2,1)S(1)} %collective-permute-done.3) | copy-start | bytes 786436
  20.7 15.1 %collective-permute-start.12 = (bf16[4,256,128]{2,1,0:T(8,128)(2,1)}, bf16[4,256,128]{2,1,0:T(8,128)(2,1)S(1)}, u32[]{:S(2)}, u32[]{:S(2)}) collective-permute-start(bf16[4,256,128]{2,1,0:T(8,128)(2,1)} %param.6), channel_id=1, source_target_pairs={{4,0},{6,2},{8,4},{10,6},{12,8},{14,10},{5,1},{7,3},{9,5},{11,7},{... | collective-permute-start | bytes 786440 | tf_op jit(solution)/shard_map/ppermute | solution.py:34
  24.6 12.1 %copy-start.6 = (bf16[4,256,128]{2,1,0:T(8,128)(2,1)}, bf16[4,256,128]{2,1,0:T(8,128)(2,1)S(1)}, u32[]{:S(2)}) copy-start(bf16[4,256,128]{2,1,0:T(8,128)(2,1)S(1)} %collective-permute-done.2) | copy-start | bytes 786436
  24.7 11.2 %collective-permute-start.5 = (bf16[8,128,128]{2,1,0:T(8,128)(2,1)S(1)}, bf16[8,128,128]{2,1,0:T(8,128)(2,1)S(1)}, u32[]{:S(2)}, u32[]{:S(2)}) collective-permute-start(bf16[8,128,128]{2,1,0:T(8,128)(2,1)S(1)} %bitcast.22), channel_id=1, source_target_pairs={{0,1},{1,0},{2,3},{3,2},{4,5},{5,4},{6,7},{7,6},{8,9},{9,8},{10,11... | collective-permute-start | bytes 786440 | tf_op jit(solution)/shard_map/ppermute | solution.py:129
  29.6 7.1 %copy-start.7 = (bf16[4,256,128]{2,1,0:T(8,128)(2,1)}, bf16[4,256,128]{2,1,0:T(8,128)(2,1)S(1)}, u32[]{:S(2)}) copy-start(bf16[4,256,128]{2,1,0:T(8,128)(2,1)S(1)} %collective-permute-done.11) | copy-start | bytes 786436
  29.6 5.5 %copy-start.15 = (s32[4,2,16]{2,1,0:T(2,128)S(1)}, s32[4,2,16]{2,1,0:T(2,128)}, u32[]{:S(2)}) copy-start(s32[4,2,16]{2,1,0:T(2,128)} %param.8) | copy-start | bytes 1540
  29.6 5.5 %copy-start.16 = (s32[4,2,16]{2,1,0:T(2,128)S(1)}, s32[4,2,16]{2,1,0:T(2,128)}, u32[]{:S(2)}) copy-start(s32[4,2,16]{2,1,0:T(2,128)} %param.7) | copy-start | bytes 1540
  29.6 6.2 %collective-permute-start.4 = (bf16[8,128,128]{2,1,0:T(8,128)(2,1)S(1)}, bf16[8,128,128]{2,1,0:T(8,128)(2,1)S(1)}, u32[]{:S(2)}, u32[]{:S(2)}) collective-permute-start(bf16[8,128,128]{2,1,0:T(8,128)(2,1)S(1)} %bitcast.24), channel_id=1, source_target_pairs={{0,1},{1,0},{2,3},{3,2},{4,5},{5,4},{6,7},{7,6},{8,9},{9,8},{10,11... | collective-permute-start | bytes 786440 | tf_op jit(solution)/shard_map/ppermute | solution.py:129
  34.0 2.8 %copy-start.8 = (bf16[4,256,128]{2,1,0:T(8,128)(2,1)}, bf16[4,256,128]{2,1,0:T(8,128)(2,1)S(1)}, u32[]{:S(2)}) copy-start(bf16[4,256,128]{2,1,0:T(8,128)(2,1)S(1)} %collective-permute-done.10) | copy-start | bytes 786436
  34.0 1.9 %collective-permute-start.8 = (bf16[8,128,128]{2,1,0:T(8,128)(2,1)S(1)}, bf16[8,128,128]{2,1,0:T(8,128)(2,1)S(1)}, u32[]{:S(2)}, u32[]{:S(2)}) collective-permute-start(bf16[8,128,128]{2,1,0:T(8,128)(2,1)S(1)} %bitcast.26), channel_id=1, source_target_pairs={{0,1},{1,0},{2,3},{3,2},{4,5},{5,4},{6,7},{7,6},{8,9},{9,8},{10,11... | collective-permute-start | bytes 786440 | tf_op jit(solution)/shard_map/ppermute | solution.py:129
  34.0 2.8 %copy-start.9 = (bf16[4,256,128]{2,1,0:T(8,128)(2,1)}, bf16[4,256,128]{2,1,0:T(8,128)(2,1)S(1)}, u32[]{:S(2)}) copy-start(bf16[4,256,128]{2,1,0:T(8,128)(2,1)S(1)} %collective-permute-done.9) | copy-start | bytes 786436
  34.0 1.9 %collective-permute-start.7 = (bf16[8,128,128]{2,1,0:T(8,128)(2,1)S(1)}, bf16[8,128,128]{2,1,0:T(8,128)(2,1)S(1)}, u32[]{:S(2)}, u32[]{:S(2)}) collective-permute-start(bf16[8,128,128]{2,1,0:T(8,128)(2,1)S(1)} %bitcast.28), channel_id=1, source_target_pairs={{0,1},{1,0},{2,3},{3,2},{4,5},{5,4},{6,7},{7,6},{8,9},{9,8},{10,11... | collective-permute-start | bytes 786440 | tf_op jit(solution)/shard_map/ppermute | solution.py:129
  35.8 1.0 %copy-start.10 = (bf16[4,256,128]{2,1,0:T(8,128)(2,1)}, bf16[4,256,128]{2,1,0:T(8,128)(2,1)S(1)}, u32[]{:S(2)}) copy-start(bf16[4,256,128]{2,1,0:T(8,128)(2,1)S(1)} %collective-permute-done.12) | copy-start | bytes 786436
  35.8 1.0 %copy-start.11 = (bf16[8,128,128]{2,1,0:T(8,128)(2,1)}, bf16[8,128,128]{2,1,0:T(8,128)(2,1)S(1)}, u32[]{:S(2)}) copy-start(bf16[8,128,128]{2,1,0:T(8,128)(2,1)S(1)} %collective-permute-done.5.refs_6_) | copy-start | bytes 786436
  35.9 1.0 %copy-start.12 = (bf16[8,128,128]{2,1,0:T(8,128)(2,1)}, bf16[8,128,128]{2,1,0:T(8,128)(2,1)S(1)}, u32[]{:S(2)}) copy-start(bf16[8,128,128]{2,1,0:T(8,128)(2,1)S(1)} %collective-permute-done.4.refs_5_) | copy-start | bytes 786436
  35.9 1.1 %copy-start.13 = (bf16[8,128,128]{2,1,0:T(8,128)(2,1)}, bf16[8,128,128]{2,1,0:T(8,128)(2,1)S(1)}, u32[]{:S(2)}) copy-start(bf16[8,128,128]{2,1,0:T(8,128)(2,1)S(1)} %collective-permute-done.8.refs_9_) | copy-start | bytes 786436
  35.9 0.8 %copy-start.14 = (bf16[8,128,128]{2,1,0:T(8,128)(2,1)}, bf16[8,128,128]{2,1,0:T(8,128)(2,1)S(1)}, u32[]{:S(2)}) copy-start(bf16[8,128,128]{2,1,0:T(8,128)(2,1)S(1)} %collective-permute-done.7.refs_8_) | copy-start | bytes 786436
  37.0 25.8 %copy-start = (bf16[4,256,128]{2,1,0:T(8,128)(2,1)S(1)}, bf16[4,256,128]{2,1,0:T(8,128)(2,1)}, u32[]{:S(2)}) copy-start(bf16[4,256,128]{2,1,0:T(8,128)(2,1)} %param.6) | copy-start | bytes 786436
  51.8 11.1 %collective-permute-start.13 = (bf16[8,144,128]{2,1,0:T(8,128)(2,1)}, bf16[8,144,128]{2,1,0:T(8,128)(2,1)S(1)}, u32[]{:S(2)}, u32[]{:S(2)}) collective-permute-start(bf16[8,144,128]{2,1,0:T(8,128)(2,1)} %get-tuple-element.12), channel_id=1, source_target_pairs={{4,0},{6,2},{8,4},{10,6},{12,8},{14,10},{5,1},{7,3},{9,5},{11,7},{... | collective-permute-start | bytes 884744 | tf_op jit(solution)/shard_map/ppermute | solution.py:34
  54.0 15.0 %collective-permute-start.14 = (bf16[8,144,128]{2,1,0:T(8,128)(2,1)}, bf16[8,144,128]{2,1,0:T(8,128)(2,1)S(1)}, u32[]{:S(2)}, u32[]{:S(2)}) collective-permute-start(bf16[8,144,128]{2,1,0:T(8,128)(2,1)} %get-tuple-element.13), channel_id=1, source_target_pairs={{2,0},{4,2},{6,4},{8,6},{10,8},{12,10},{14,12},{3,1},{5,3},{7,5},{... | collective-permute-start | bytes 884744 | tf_op jit(solution)/shard_map/ppermute | solution.py:34
  56.0 17.1 %collective-permute-start.15 = (bf16[8,144,128]{2,1,0:T(8,128)(2,1)}, bf16[8,144,128]{2,1,0:T(8,128)(2,1)S(1)}, u32[]{:S(2)}, u32[]{:S(2)}) collective-permute-start(bf16[8,144,128]{2,1,0:T(8,128)(2,1)} %get-tuple-element.14), channel_id=1, source_target_pairs={{0,2},{2,4},{4,6},{6,8},{8,10},{10,12},{12,14},{1,3},{3,5},{5,7},{... | collective-permute-start | bytes 884744 | tf_op jit(solution)/shard_map/ppermute | solution.py:34
  60.8 13.2 %collective-permute-start.16 = (bf16[8,144,128]{2,1,0:T(8,128)(2,1)}, bf16[8,144,128]{2,1,0:T(8,128)(2,1)S(1)}, u32[]{:S(2)}, u32[]{:S(2)}) collective-permute-start(bf16[8,144,128]{2,1,0:T(8,128)(2,1)} %get-tuple-element.15), channel_id=1, source_target_pairs={{0,4},{2,6},{4,8},{6,10},{8,12},{10,14},{1,5},{3,7},{5,9},{7,11},{... | collective-permute-start | bytes 884744 | tf_op jit(solution)/shard_map/ppermute | solution.py:34
  73.1 1.6 %copy-start.1 = (f32[8,128,128]{2,1,0:T(8,128)S(1)}, f32[8,128,128]{2,1,0:T(8,128)}, u32[]{:S(2)}) copy-start(f32[8,128,128]{2,1,0:T(8,128)} %get-tuple-element.11) | copy-start | bytes 1572868
  74.0 0.7 copy-start.17

commit v7 on v6

--- a/solution.py
+++ b/solution.py
@@ -163,7 +163,7 @@
     outs = pl.pallas_call(
         kernel,
         out_shape=out_shape,
-        in_specs=[smem, smem] + [hbm] * (3 * slabs),
+        in_specs=[smem, smem] + [vmem] * (3 * slabs),
         out_specs=[vmem] * len(out_shape),
         scratch_shapes=[
             pltpu.VMEM((total, BLOCK, 2 * half), jnp.bfloat16),

time: 76.4 us -> 76.4 us (level)
  no operation moved by 1% of the time
where the time goes in v7:
time: 76.4 us; the launch traced here: 75.8 us
  starting transfers between devices  35.9 us (47%)
  waiting for transfers between devices  20.3 us (27%)
  Pallas kernels  14.8 us (19%)
  local copies, waits for them, and re-layouts  3.9 us (5%)
    ppermute x12, starting transfers between devices, passed_along(): return lax.ppermute(block, axis, route)  35.3 us
    ppermute x12, waiting for transfers between devices, passed_along(): return lax.ppermute(block, axis, route)  20.2 us
    pallas_call x1, Pallas kernels, shards(): pl.pallas_call(kernel, out_shape=out_shape, in_specs=[smem, smem] + [vmem...  14.8 us
    unnamed x38, local copies, waits for them, and re-layouts  1.67 us
  transfers between devices with their start and end apart: 17, of which 5 were waited for; matrix products, arithmetic and copies ran while one was open for 2% of the time, Pallas kernels for 0%

profile of v7, /device:TPU:22, one launch (start us, length us, event | category | flops | bytes accessed | tf_op | source)
XLA Modules:
  0.0 75.8 jit_solution(2737423682435332333)
XLA Ops:
  0.0 0.0 collective-permute-start.6
  0.0 3.6 %collective-permute-start.1 = (bf16[4,256,128]{2,1,0:T(8,128)(2,1)}, bf16[4,256,128]{2,1,0:T(8,128)(2,1)S(1)}, u32[]{:S(2)}, u32[]{:S(2)}) collective-permute-start(bf16[4,256,128]{2,1,0:T(8,128)(2,1)} %param.5), channel_id=1, source_target_pairs={{0,2},{2,4},{4,6},{6,8},{8,10},{10,12},{12,14},{1,3},{3,5},{5,7},{... | collective-permute-start | bytes 786440 | tf_op jit(solution)/shard_map/ppermute | solution.py:34
  3.6 1.9 %collective-permute-start = (bf16[4,256,128]{2,1,0:T(8,128)(2,1)}, bf16[4,256,128]{2,1,0:T(8,128)(2,1)S(1)}, u32[]{:S(2)}, u32[]{:S(2)}) collective-permute-start(bf16[4,256,128]{2,1,0:T(8,128)(2,1)} %param.5), channel_id=1, source_target_pairs={{0,4},{2,6},{4,8},{6,10},{8,12},{10,14},{1,5},{3,7},{5,9},{7,11},{... | collective-permute-start | bytes 786440 | tf_op jit(solution)/shard_map/ppermute | solution.py:34
  5.5 3.9 %collective-permute-start.3 = (bf16[4,256,128]{2,1,0:T(8,128)(2,1)}, bf16[4,256,128]{2,1,0:T(8,128)(2,1)S(1)}, u32[]{:S(2)}, u32[]{:S(2)}) collective-permute-start(bf16[4,256,128]{2,1,0:T(8,128)(2,1)} %param.5), channel_id=1, source_target_pairs={{4,0},{6,2},{8,4},{10,6},{12,8},{14,10},{5,1},{7,3},{9,5},{11,7},{... | collective-permute-start | bytes 786440 | tf_op jit(solution)/shard_map/ppermute | solution.py:34
  9.5 2.4 %collective-permute-start.2 = (bf16[4,256,128]{2,1,0:T(8,128)(2,1)}, bf16[4,256,128]{2,1,0:T(8,128)(2,1)S(1)}, u32[]{:S(2)}, u32[]{:S(2)}) collective-permute-start(bf16[4,256,128]{2,1,0:T(8,128)(2,1)} %param.5), channel_id=1, source_target_pairs={{2,0},{4,2},{6,4},{8,6},{10,8},{12,10},{14,12},{3,1},{5,3},{7,5},{... | collective-permute-start | bytes 786440 | tf_op jit(solution)/shard_map/ppermute | solution.py:34
  11.9 0.0 collective-permute-done.6.refs_7_
  11.9 3.4 %collective-permute-start.11 = (bf16[4,256,128]{2,1,0:T(8,128)(2,1)}, bf16[4,256,128]{2,1,0:T(8,128)(2,1)S(1)}, u32[]{:S(2)}, u32[]{:S(2)}) collective-permute-start(bf16[4,256,128]{2,1,0:T(8,128)(2,1)} %param.6), channel_id=1, source_target_pairs={{2,0},{4,2},{6,4},{8,6},{10,8},{12,10},{14,12},{3,1},{5,3},{7,5},{... | collective-permute-start | bytes 786440 | tf_op jit(solution)/shard_map/ppermute | solution.py:34
  15.3 0.0 collective-permute-done.1
  15.3 3.4 %collective-permute-start.10 = (bf16[4,256,128]{2,1,0:T(8,128)(2,1)}, bf16[4,256,128]{2,1,0:T(8,128)(2,1)S(1)}, u32[]{:S(2)}, u32[]{:S(2)}) collective-permute-start(bf16[4,256,128]{2,1,0:T(8,128)(2,1)} %param.6), channel_id=1, source_target_pairs={{0,2},{2,4},{4,6},{6,8},{8,10},{10,12},{12,14},{1,3},{3,5},{5,7},{... | collective-permute-start | bytes 786440 | tf_op jit(solution)/shard_map/ppermute | solution.py:34
  18.7 0.0 collective-permute-done
  18.7 0.0 copy-start.4
  18.7 1.9 %collective-permute-start.9 = (bf16[4,256,128]{2,1,0:T(8,128)(2,1)}, bf16[4,256,128]{2,1,0:T(8,128)(2,1)S(1)}, u32[]{:S(2)}, u32[]{:S(2)}) collective-permute-start(bf16[4,256,128]{2,1,0:T(8,128)(2,1)} %param.6), channel_id=1, source_target_pairs={{0,4},{2,6},{4,8},{6,10},{8,12},{10,14},{1,5},{3,7},{5,9},{7,11},{... | collective-permute-start | bytes 786440 | tf_op jit(solution)/shard_map/ppermute | solution.py:34
  20.6 0.1 fusion.1
  20.7 0.0 collective-permute-done.3
  20.7 3.9 %collective-permute-start.12 = (bf16[4,256,128]{2,1,0:T(8,128)(2,1)}, bf16[4,256,128]{2,1,0:T(8,128)(2,1)S(1)}, u32[]{:S(2)}, u32[]{:S(2)}) collective-permute-start(bf16[4,256,128]{2,1,0:T(8,128)(2,1)} %param.6), channel_id=1, source_target_pairs={{4,0},{6,2},{8,4},{10,6},{12,8},{14,10},{5,1},{7,3},{9,5},{11,7},{... | collective-permute-start | bytes 786440 | tf_op jit(solution)/shard_map/ppermute | solution.py:34
  24.6 0.0 collective-permute-done.2
  24.7 0.1 collective-permute-start.5
  24.7 4.9 %collective-permute-done.11 = bf16[4,256,128]{2,1,0:T(8,128)(2,1)S(1)} collective-permute-done((bf16[4,256,128]{2,1,0:T(8,128)(2,1)}, bf16[4,256,128]{2,1,0:T(8,128)(2,1)S(1)}, u32[]{:S(2)}, u32[]{:S(2)}) %collective-permute-start.11) | collective-permute-done | bytes 262176 | tf_op jit(solution)/shard_map/ppermute | solution.py:34
  29.6 0.0 collective-permute-start.4
  29.6 4.4 %collective-permute-done.10 = bf16[4,256,128]{2,1,0:T(8,128)(2,1)S(1)} collective-permute-done((bf16[4,256,128]{2,1,0:T(8,128)(2,1)}, bf16[4,256,128]{2,1,0:T(8,128)(2,1)S(1)}, u32[]{:S(2)}, u32[]{:S(2)}) %collective-permute-start.10) | collective-permute-done | bytes 262176 | tf_op jit(solution)/shard_map/ppermute | solution.py:34
  34.0 0.0 collective-permute-start.8
  34.0 0.0 collective-permute-done.9
  34.0 0.5 collective-permute-start.7
  34.5 0.6 reshape.75.act_ref
  35.1 0.1 add_clamp_fusion
  35.2 0.6 reshape.63.slot_ref
  35.8 0.0 collective-permute-done.12
  35.8 0.0 collective-permute-done.5.refs_6_
  35.9 0.0 collective-permute-done.4.refs_5_
  35.9 0.0 collective-permute-done.8.refs_9_
  35.9 0.0 collective-permute-done.7.refs_8_
  35.9 0.8 %copy-done.14 = bf16[8,128,128]{2,1,0:T(8,128)(2,1)} copy-done((bf16[8,128,128]{2,1,0:T(8,128)(2,1)}, bf16[8,128,128]{2,1,0:T(8,128)(2,1)S(1)}, u32[]{:S(2)}) %copy-start.14) | copy-done | bytes 262168
  36.8 0.0 copy-done.12
  36.8 0.1 copy-done.13
  37.0 14.8 %shard_map.55 = (f32[8,128,128]{2,1,0:T(8,128)}, f32[8,1,128]{2,1,0:T(1,128)}, bf16[8,144,128]{2,1,0:T(8,128)(2,1)}, bf16[8,144,128]{2,1,0:T(8,128)(2,1)}, bf16[...) custom-call(s32[128]{0:T(128)} %reshape.63.slot_ref, s32[8]{0:T(128)} %reshape.75.act_ref, ...), custom_call_target="tpu_custom_call" | custom-call | tf_op jit(solution)/shard_map/pallas_call | solution.py:163
  51.8 2.3 %collective-permute-start.13 = (bf16[8,144,128]{2,1,0:T(8,128)(2,1)}, bf16[8,144,128]{2,1,0:T(8,128)(2,1)S(1)}, u32[]{:S(2)}, u32[]{:S(2)}) collective-permute-start(bf16[8,144,128]{2,1,0:T(8,128)(2,1)} %get-tuple-element.12), channel_id=1, source_target_pairs={{4,0},{6,2},{8,4},{10,6},{12,8},{14,10},{5,1},{7,3},{9,5},{11,7},{... | collective-permute-start | bytes 884744 | tf_op jit(solution)/shard_map/ppermute | solution.py:34
  54.0 1.9 %collective-permute-start.14 = (bf16[8,144,128]{2,1,0:T(8,128)(2,1)}, bf16[8,144,128]{2,1,0:T(8,128)(2,1)S(1)}, u32[]{:S(2)}, u32[]{:S(2)}) collective-permute-start(bf16[8,144,128]{2,1,0:T(8,128)(2,1)} %get-tuple-element.13), channel_id=1, source_target_pairs={{2,0},{4,2},{6,4},{8,6},{10,8},{12,10},{14,12},{3,1},{5,3},{7,5},{... | collective-permute-start | bytes 884744 | tf_op jit(solution)/shard_map/ppermute | solution.py:34
  56.0 4.8 %collective-permute-start.15 = (bf16[8,144,128]{2,1,0:T(8,128)(2,1)}, bf16[8,144,128]{2,1,0:T(8,128)(2,1)S(1)}, u32[]{:S(2)}, u32[]{:S(2)}) collective-permute-start(bf16[8,144,128]{2,1,0:T(8,128)(2,1)} %get-tuple-element.14), channel_id=1, source_target_pairs={{0,2},{2,4},{4,6},{6,8},{8,10},{10,12},{12,14},{1,3},{3,5},{5,7},{... | collective-permute-start | bytes 884744 | tf_op jit(solution)/shard_map/ppermute | solution.py:34
  60.8 1.9 %collective-permute-start.16 = (bf16[8,144,128]{2,1,0:T(8,128)(2,1)}, bf16[8,144,128]{2,1,0:T(8,128)(2,1)S(1)}, u32[]{:S(2)}, u32[]{:S(2)}) collective-permute-start(bf16[8,144,128]{2,1,0:T(8,128)(2,1)} %get-tuple-element.15), channel_id=1, source_target_pairs={{0,4},{2,6},{4,8},{6,10},{8,12},{10,14},{1,5},{3,7},{5,9},{7,11},{... | collective-permute-start | bytes 884744 | tf_op jit(solution)/shard_map/ppermute | solution.py:34
  62.7 0.1 copy.8
  62.9 0.0 collective-permute-done.13
  63.0 6.1 %collective-permute-done.14 = bf16[8,144,128]{2,1,0:T(8,128)(2,1)S(1)} collective-permute-done((bf16[8,144,128]{2,1,0:T(8,128)(2,1)}, bf16[8,144,128]{2,1,0:T(8,128)(2,1)S(1)}, u32[]{:S(2)}, u32[]{:S(2)}) %collective-permute-start.14) | collective-permute-done | bytes 294944 | tf_op jit(solution)/shard_map/ppermute | solution.py:34
  69.1 4.0 %collective-permute-done.15 = bf16[8,144,128]{2,1,0:T(8,128)(2,1)S(1)} collective-permute-done((bf16[8,144,128]{2,1,0:T(8,128)(2,1)}, bf16[8,144,128]{2,1,0:T(8,128)(2,1)S(1)}, u32[]{:S(2)}, u32[]{:S(2)}) %collective-permute-start.15) | collective-permute-done | bytes 294944 | tf_op jit(solution)/shard_map/ppermute | solution.py:34
  73.2 0.9 %collective-permute-done.16 = bf16[8,144,128]{2,1,0:T(8,128)(2,1)S(1)} collective-permute-done((bf16[8,144,128]{2,1,0:T(8,128)(2,1)}, bf16[8,144,128]{2,1,0:T(8,128)(2,1)S(1)}, u32[]{:S(2)}, u32[]{:S(2)}) %collective-permute-start.16) | collective-permute-done | bytes 294944 | tf_op jit(solution)/shard_map/ppermute | solution.py:34
  74.1 0.6 copy-done.17
  74.8 0.1 slice_add_fusion
  74.9 0.1 divide_convert_fusion
  75.0 0.8 %copy.9 = bf16[4,2,128,128]{3,2,1,0:T(8,128)(2,1)} copy(bf16[4,2,128,128]{2,3,1,0:T(8,128)(2,1)S(1)} %divide_convert_fusion) | data formatting | bytes 524288 | tf_op jit(solution)/shard_map/convert_element_type | solution.py:206
  (39 shorter events, 0.2 us)
Async XLA Ops:
  0.0 20.6 %copy-start.18 = (s32[4]{0:T(128)S(1)}, s32[4]{0:T(128)}, u32[]{:S(2)}) copy-start(s32[4]{0:T(128)} %param.9) | copy-start | bytes 52
  0.0 11.9 %collective-permute-start.6 = (bf16[8,128,128]{2,1,0:T(8,128)(2,1)}, bf16[8,128,128]{2,1,0:T(8,128)(2,1)S(1)}, u32[]{:S(2)}, u32[]{:S(2)}) collective-permute-start(bf16[8,128,128]{2,1,0:T(8,128)(2,1)} %bitcast.20), channel_id=1, source_target_pairs={{0,1},{1,0},{2,3},{3,2},{4,5},{5,4},{6,7},{7,6},{8,9},{9,8},{10,11... | collective-permute-start | bytes 786440 | tf_op jit(solution)/shard_map/ppermute | solution.py:129
  0.0 15.3 %collective-permute-start.1 = (bf16[4,256,128]{2,1,0:T(8,128)(2,1)}, bf16[4,256,128]{2,1,0:T(8,128)(2,1)S(1)}, u32[]{:S(2)}, u32[]{:S(2)}) collective-permute-start(bf16[4,256,128]{2,1,0:T(8,128)(2,1)} %param.5), channel_id=1, source_target_pairs={{0,2},{2,4},{4,6},{6,8},{8,10},{10,12},{12,14},{1,3},{3,5},{5,7},{... | collective-permute-start | bytes 786440 | tf_op jit(solution)/shard_map/ppermute | solution.py:34
  3.6 15.1 %collective-permute-start = (bf16[4,256,128]{2,1,0:T(8,128)(2,1)}, bf16[4,256,128]{2,1,0:T(8,128)(2,1)S(1)}, u32[]{:S(2)}, u32[]{:S(2)}) collective-permute-start(bf16[4,256,128]{2,1,0:T(8,128)(2,1)} %param.5), channel_id=1, source_target_pairs={{0,4},{2,6},{4,8},{6,10},{8,12},{10,14},{1,5},{3,7},{5,9},{7,11},{... | collective-permute-start | bytes 786440 | tf_op jit(solution)/shard_map/ppermute | solution.py:34
  5.5 15.2 %collective-permute-start.3 = (bf16[4,256,128]{2,1,0:T(8,128)(2,1)}, bf16[4,256,128]{2,1,0:T(8,128)(2,1)S(1)}, u32[]{:S(2)}, u32[]{:S(2)}) collective-permute-start(bf16[4,256,128]{2,1,0:T(8,128)(2,1)} %param.5), channel_id=1, source_target_pairs={{4,0},{6,2},{8,4},{10,6},{12,8},{14,10},{5,1},{7,3},{9,5},{11,7},{... | collective-permute-start | bytes 786440 | tf_op jit(solution)/shard_map/ppermute | solution.py:34
  9.5 15.2 %collective-permute-start.2 = (bf16[4,256,128]{2,1,0:T(8,128)(2,1)}, bf16[4,256,128]{2,1,0:T(8,128)(2,1)S(1)}, u32[]{:S(2)}, u32[]{:S(2)}) collective-permute-start(bf16[4,256,128]{2,1,0:T(8,128)(2,1)} %param.5), channel_id=1, source_target_pairs={{2,0},{4,2},{6,4},{8,6},{10,8},{12,10},{14,12},{3,1},{5,3},{7,5},{... | collective-permute-start | bytes 786440 | tf_op jit(solution)/shard_map/ppermute | solution.py:34
  11.9 24.9 %copy-start.2 = (bf16[8,128,128]{2,1,0:T(8,128)(2,1)}, bf16[8,128,128]{2,1,0:T(8,128)(2,1)S(1)}, u32[]{:S(2)}) copy-start(bf16[8,128,128]{2,1,0:T(8,128)(2,1)S(1)} %collective-permute-done.6.refs_7_) | copy-start | bytes 786436
  11.9 17.7 %collective-permute-start.11 = (bf16[4,256,128]{2,1,0:T(8,128)(2,1)}, bf16[4,256,128]{2,1,0:T(8,128)(2,1)S(1)}, u32[]{:S(2)}, u32[]{:S(2)}) collective-permute-start(bf16[4,256,128]{2,1,0:T(8,128)(2,1)} %param.6), channel_id=1, source_target_pairs={{2,0},{4,2},{6,4},{8,6},{10,8},{12,10},{14,12},{3,1},{5,3},{7,5},{... | collective-permute-start | bytes 786440 | tf_op jit(solution)/shard_map/ppermute | solution.py:34
  15.3 21.5 %copy-start.3 = (bf16[4,256,128]{2,1,0:T(8,128)(2,1)}, bf16[4,256,128]{2,1,0:T(8,128)(2,1)S(1)}, u32[]{:S(2)}) copy-start(bf16[4,256,128]{2,1,0:T(8,128)(2,1)S(1)} %collective-permute-done.1) | copy-start | bytes 786436
  15.3 18.7 %collective-permute-start.10 = (bf16[4,256,128]{2,1,0:T(8,128)(2,1)}, bf16[4,256,128]{2,1,0:T(8,128)(2,1)S(1)}, u32[]{:S(2)}, u32[]{:S(2)}) collective-permute-start(bf16[4,256,128]{2,1,0:T(8,128)(2,1)} %param.6), channel_id=1, source_target_pairs={{0,2},{2,4},{4,6},{6,8},{8,10},{10,12},{12,14},{1,3},{3,5},{5,7},{... | collective-permute-start | bytes 786440 | tf_op jit(solution)/shard_map/ppermute | solution.py:34
  18.7 18.1 %copy-start.4 = (bf16[4,256,128]{2,1,0:T(8,128)(2,1)}, bf16[4,256,128]{2,1,0:T(8,128)(2,1)S(1)}, u32[]{:S(2)}) copy-start(bf16[4,256,128]{2,1,0:T(8,128)(2,1)S(1)} %collective-permute-done) | copy-start | bytes 786436
  18.7 15.3 %collective-permute-start.9 = (bf16[4,256,128]{2,1,0:T(8,128)(2,1)}, bf16[4,256,128]{2,1,0:T(8,128)(2,1)S(1)}, u32[]{:S(2)}, u32[]{:S(2)}) collective-permute-start(bf16[4,256,128]{2,1,0:T(8,128)(2,1)} %param.6), channel_id=1, source_target_pairs={{0,4},{2,6},{4,8},{6,10},{8,12},{10,14},{1,5},{3,7},{5,9},{7,11},{... | collective-permute-start | bytes 786440 | tf_op jit(solution)/shard_map/ppermute | solution.py:34
  20.7 16.0 %copy-start.5 = (bf16[4,256,128]{2,1,0:T(8,128)(2,1)}, bf16[4,256,128]{2,1,0:T(8,128)(2,1)S(1)}, u32[]{:S(2)}) copy-start(bf16[4,256,128]{2,1,0:T(8,128)(2,1)S(1)} %collective-permute-done.3) | copy-start | bytes 786436
  20.7 15.1 %collective-permute-start.12 = (bf16[4,256,128]{2,1,0:T(8,128)(2,1)}, bf16[4,256,128]{2,1,0:T(8,128)(2,1)S(1)}, u32[]{:S(2)}, u32[]{:S(2)}) collective-permute-start(bf16[4,256,128]{2,1,0:T(8,128)(2,1)} %param.6), channel_id=1, source_target_pairs={{4,0},{6,2},{8,4},{10,6},{12,8},{14,10},{5,1},{7,3},{9,5},{11,7},{... | collective-permute-start | bytes 786440 | tf_op jit(solution)/shard_map/ppermute | solution.py:34
  24.6 12.1 %copy-start.6 = (bf16[4,256,128]{2,1,0:T(8,128)(2,1)}, bf16[4,256,128]{2,1,0:T(8,128)(2,1)S(1)}, u32[]{:S(2)}) copy-start(bf16[4,256,128]{2,1,0:T(8,128)(2,1)S(1)} %collective-permute-done.2) | copy-start | bytes 786436
  24.7 11.2 %collective-permute-start.5 = (bf16[8,128,128]{2,1,0:T(8,128)(2,1)S(1)}, bf16[8,128,128]{2,1,0:T(8,128)(2,1)S(1)}, u32[]{:S(2)}, u32[]{:S(2)}) collective-permute-start(bf16[8,128,128]{2,1,0:T(8,128)(2,1)S(1)} %bitcast.22), channel_id=1, source_target_pairs={{0,1},{1,0},{2,3},{3,2},{4,5},{5,4},{6,7},{7,6},{8,9},{9,8},{10,11... | collective-permute-start | bytes 786440 | tf_op jit(solution)/shard_map/ppermute | solution.py:129
  29.6 7.1 %copy-start.7 = (bf16[4,256,128]{2,1,0:T(8,128)(2,1)}, bf16[4,256,128]{2,1,0:T(8,128)(2,1)S(1)}, u32[]{:S(2)}) copy-start(bf16[4,256,128]{2,1,0:T(8,128)(2,1)S(1)} %collective-permute-done.11) | copy-start | bytes 786436
  29.6 5.5 %copy-start.15 = (s32[4,2,16]{2,1,0:T(2,128)S(1)}, s32[4,2,16]{2,1,0:T(2,128)}, u32[]{:S(2)}) copy-start(s32[4,2,16]{2,1,0:T(2,128)} %param.8) | copy-start | bytes 1540
  29.6 5.5 %copy-start.16 = (s32[4,2,16]{2,1,0:T(2,128)S(1)}, s32[4,2,16]{2,1,0:T(2,128)}, u32[]{:S(2)}) copy-start(s32[4,2,16]{2,1,0:T(2,128)} %param.7) | copy-start | bytes 1540
  29.6 6.2 %collective-permute-start.4 = (bf16[8,128,128]{2,1,0:T(8,128)(2,1)S(1)}, bf16[8,128,128]{2,1,0:T(8,128)(2,1)S(1)}, u32[]{:S(2)}, u32[]{:S(2)}) collective-permute-start(bf16[8,128,128]{2,1,0:T(8,128)(2,1)S(1)} %bitcast.24), channel_id=1, source_target_pairs={{0,1},{1,0},{2,3},{3,2},{4,5},{5,4},{6,7},{7,6},{8,9},{9,8},{10,11... | collective-permute-start | bytes 786440 | tf_op jit(solution)/shard_map/ppermute | solution.py:129
  34.0 2.8 %copy-start.8 = (bf16[4,256,128]{2,1,0:T(8,128)(2,1)}, bf16[4,256,128]{2,1,0:T(8,128)(2,1)S(1)}, u32[]{:S(2)}) copy-start(bf16[4,256,128]{2,1,0:T(8,128)(2,1)S(1)} %collective-permute-done.10) | copy-start | bytes 786436
  34.0 1.9 %collective-permute-start.8 = (bf16[8,128,128]{2,1,0:T(8,128)(2,1)S(1)}, bf16[8,128,128]{2,1,0:T(8,128)(2,1)S(1)}, u32[]{:S(2)}, u32[]{:S(2)}) collective-permute-start(bf16[8,128,128]{2,1,0:T(8,128)(2,1)S(1)} %bitcast.26), channel_id=1, source_target_pairs={{0,1},{1,0},{2,3},{3,2},{4,5},{5,4},{6,7},{7,6},{8,9},{9,8},{10,11... | collective-permute-start | bytes 786440 | tf_op jit(solution)/shard_map/ppermute | solution.py:129
  34.0 2.8 %copy-start.9 = (bf16[4,256,128]{2,1,0:T(8,128)(2,1)}, bf16[4,256,128]{2,1,0:T(8,128)(2,1)S(1)}, u32[]{:S(2)}) copy-start(bf16[4,256,128]{2,1,0:T(8,128)(2,1)S(1)} %collective-permute-done.9) | copy-start | bytes 786436
  34.0 1.9 %collective-permute-start.7 = (bf16[8,128,128]{2,1,0:T(8,128)(2,1)S(1)}, bf16[8,128,128]{2,1,0:T(8,128)(2,1)S(1)}, u32[]{:S(2)}, u32[]{:S(2)}) collective-permute-start(bf16[8,128,128]{2,1,0:T(8,128)(2,1)S(1)} %bitcast.28), channel_id=1, source_target_pairs={{0,1},{1,0},{2,3},{3,2},{4,5},{5,4},{6,7},{7,6},{8,9},{9,8},{10,11... | collective-permute-start | bytes 786440 | tf_op jit(solution)/shard_map/ppermute | solution.py:129
  35.8 1.0 %copy-start.10 = (bf16[4,256,128]{2,1,0:T(8,128)(2,1)}, bf16[4,256,128]{2,1,0:T(8,128)(2,1)S(1)}, u32[]{:S(2)}) copy-start(bf16[4,256,128]{2,1,0:T(8,128)(2,1)S(1)} %collective-permute-done.12) | copy-start | bytes 786436
  35.8 1.0 %copy-start.11 = (bf16[8,128,128]{2,1,0:T(8,128)(2,1)}, bf16[8,128,128]{2,1,0:T(8,128)(2,1)S(1)}, u32[]{:S(2)}) copy-start(bf16[8,128,128]{2,1,0:T(8,128)(2,1)S(1)} %collective-permute-done.5.refs_6_) | copy-start | bytes 786436
  35.9 1.0 %copy-start.12 = (bf16[8,128,128]{2,1,0:T(8,128)(2,1)}, bf16[8,128,128]{2,1,0:T(8,128)(2,1)S(1)}, u32[]{:S(2)}) copy-start(bf16[8,128,128]{2,1,0:T(8,128)(2,1)S(1)} %collective-permute-done.4.refs_5_) | copy-start | bytes 786436
  35.9 1.1 %copy-start.13 = (bf16[8,128,128]{2,1,0:T(8,128)(2,1)}, bf16[8,128,128]{2,1,0:T(8,128)(2,1)S(1)}, u32[]{:S(2)}) copy-start(bf16[8,128,128]{2,1,0:T(8,128)(2,1)S(1)} %collective-permute-done.8.refs_9_) | copy-start | bytes 786436
  35.9 0.8 %copy-start.14 = (bf16[8,128,128]{2,1,0:T(8,128)(2,1)}, bf16[8,128,128]{2,1,0:T(8,128)(2,1)S(1)}, u32[]{:S(2)}) copy-start(bf16[8,128,128]{2,1,0:T(8,128)(2,1)S(1)} %collective-permute-done.7.refs_8_) | copy-start | bytes 786436
  37.0 25.8 %copy-start = (bf16[4,256,128]{2,1,0:T(8,128)(2,1)S(1)}, bf16[4,256,128]{2,1,0:T(8,128)(2,1)}, u32[]{:S(2)}) copy-start(bf16[4,256,128]{2,1,0:T(8,128)(2,1)} %param.6) | copy-start | bytes 786436
  51.8 11.1 %collective-permute-start.13 = (bf16[8,144,128]{2,1,0:T(8,128)(2,1)}, bf16[8,144,128]{2,1,0:T(8,128)(2,1)S(1)}, u32[]{:S(2)}, u32[]{:S(2)}) collective-permute-start(bf16[8,144,128]{2,1,0:T(8,128)(2,1)} %get-tuple-element.12), channel_id=1, source_target_pairs={{4,0},{6,2},{8,4},{10,6},{12,8},{14,10},{5,1},{7,3},{9,5},{11,7},{... | collective-permute-start | bytes 884744 | tf_op jit(solution)/shard_map/ppermute | solution.py:34
  54.0 15.0 %collective-permute-start.14 = (bf16[8,144,128]{2,1,0:T(8,128)(2,1)}, bf16[8,144,128]{2,1,0:T(8,128)(2,1)S(1)}, u32[]{:S(2)}, u32[]{:S(2)}) collective-permute-start(bf16[8,144,128]{2,1,0:T(8,128)(2,1)} %get-tuple-element.13), channel_id=1, source_target_pairs={{2,0},{4,2},{6,4},{8,6},{10,8},{12,10},{14,12},{3,1},{5,3},{7,5},{... | collective-permute-start | bytes 884744 | tf_op jit(solution)/shard_map/ppermute | solution.py:34
  56.0 17.1 %collective-permute-start.15 = (bf16[8,144,128]{2,1,0:T(8,128)(2,1)}, bf16[8,144,128]{2,1,0:T(8,128)(2,1)S(1)}, u32[]{:S(2)}, u32[]{:S(2)}) collective-permute-start(bf16[8,144,128]{2,1,0:T(8,128)(2,1)} %get-tuple-element.14), channel_id=1, source_target_pairs={{0,2},{2,4},{4,6},{6,8},{8,10},{10,12},{12,14},{1,3},{3,5},{5,7},{... | collective-permute-start | bytes 884744 | tf_op jit(solution)/shard_map/ppermute | solution.py:34
  60.8 13.2 %collective-permute-start.16 = (bf16[8,144,128]{2,1,0:T(8,128)(2,1)}, bf16[8,144,128]{2,1,0:T(8,128)(2,1)S(1)}, u32[]{:S(2)}, u32[]{:S(2)}) collective-permute-start(bf16[8,144,128]{2,1,0:T(8,128)(2,1)} %get-tuple-element.15), channel_id=1, source_target_pairs={{0,4},{2,6},{4,8},{6,10},{8,12},{10,14},{1,5},{3,7},{5,9},{7,11},{... | collective-permute-start | bytes 884744 | tf_op jit(solution)/shard_map/ppermute | solution.py:34
  73.1 1.6 %copy-start.1 = (f32[8,128,128]{2,1,0:T(8,128)S(1)}, f32[8,128,128]{2,1,0:T(8,128)}, u32[]{:S(2)}) copy-start(f32[8,128,128]{2,1,0:T(8,128)} %get-tuple-element.11) | copy-start | bytes 1572868
  74.0 0.7 copy-start.17

commit v8 on v7

--- a/solution.py
+++ b/solution.py
@@ -94,12 +94,14 @@
     own_num_ref[...] = acc[own]
     own_mass_ref[...] = macc[own]
     remote = [s for s in range(slabs) if s * per_slab != center]
+    mass_rows = -(-per_slab // MASS_ROWS) * MASS_ROWS
     for ref, s in zip(remote_refs, remote):
         rows = pl.ds(s * per_slab, per_slab)
-        ref[:, :half, :] = acc[rows].astype(jnp.bfloat16)
-        ref[:, half:, :] = jnp.broadcast_to(macc[rows], (per_slab, MASS_ROWS, BLOCK)).astype(
-            jnp.bfloat16
-        )
+        ref[: per_slab * half, :] = acc[rows].reshape(per_slab * half, BLOCK).astype(jnp.bfloat16)
+        spread = [macc[s * per_slab + j] for j in range(per_slab)]
+        if mass_rows > per_slab:
+            spread.append(jnp.zeros((mass_rows - per_slab, BLOCK), jnp.float32))
+        ref[per_slab * half :, :] = jnp.concatenate(spread, axis=0).astype(jnp.bfloat16)
 
 
 def shards(embed, values, match_frame, match_block, block_counts):
@@ -152,11 +154,12 @@
     smem = pl.BlockSpec(memory_space=pltpu.SMEM)
     hbm = pl.BlockSpec(memory_space=pl.ANY)
     vmem = pl.BlockSpec(memory_space=pltpu.VMEM)
+    mass_rows = -(-per_slab // MASS_ROWS) * MASS_ROWS
     out_shape = [
         jax.ShapeDtypeStruct((per_slab, half, BLOCK), jnp.float32),
         jax.ShapeDtypeStruct((per_slab, 1, BLOCK), jnp.float32),
     ] + [
-        jax.ShapeDtypeStruct((per_slab, half + MASS_ROWS, BLOCK), jnp.bfloat16)
+        jax.ShapeDtypeStruct((per_slab * half + mass_rows, BLOCK), jnp.bfloat16)
         for _ in range(slabs - 1)
     ]
     total = slabs * per_slab
@@ -180,8 +183,8 @@
     offsets = [o for o in range(-hops, hops + 1) if o != 0]
     for offset, outgoing in zip(offsets, remote):
         arrived = passed_along(outgoing, "frame", offset).astype(jnp.float32)
-        own_num = own_num + arrived[:, :half, :]
-        own_mass = own_mass + arrived[:, half : half + 1, :]
+        own_num = own_num + arrived[: per_slab * half].reshape(per_slab, half, BLOCK)
+        own_mass = own_mass + arrived[per_slab * half : per_slab * half + per_slab][:, None, :]
     own_num = own_num.reshape(frames, rimmed_blocks, half, BLOCK)
     own_mass = own_mass.reshape(frames, rimmed_blocks, BLOCK)
     if halo:

time: 76.4 us -> 76.5 us (level)
  local copies, waits for them, and re-layouts: 3.9 us -> 5.02 us
    ppermute x12, starting transfers between devices: 35.3 us -> 34.1 us  [passed_along(): return lax.ppermute(block, axis, route)]
    unnamed x38, local copies, waits for them, and re-layouts: 1.67 us -> 2.62 us
  transfers between devices with their start and end apart: 17 -> 17, of which waited for: 5 -> 4; matrix products, arithmetic and copies ran while one was open for 2% -> 2% of each run, Pallas kernels for 0% -> 0%
where the time goes in v8:
time: 76.5 us; the launch traced here: 76 us
  starting transfers between devices  35.2 us (46%)
  waiting for transfers between devices  19.9 us (26%)
  Pallas kernels  14.8 us (19%)
  local copies, waits for them, and re-layouts  5.02 us (7%)
    ppermute x12, starting transfers between devices, passed_along(): return lax.ppermute(block, axis, route)  34.1 us
    ppermute x12, waiting for transfers between devices, passed_along(): return lax.ppermute(block, axis, route)  19.9 us
    pallas_call x1, Pallas kernels, shards(): pl.pallas_call(kernel, out_shape=out_shape, in_specs=[smem, smem] + [vmem...  14.8 us
    unnamed x38, local copies, waits for them, and re-layouts  2.62 us
  transfers between devices with their start and end apart: 17, of which 4 were waited for; matrix products, arithmetic and copies ran while one was open for 2% of the time, Pallas kernels for 0%

profile of v8, /device:TPU:22, one launch (start us, length us, event | category | flops | bytes accessed | tf_op | source)
XLA Modules:
  0.0 76.0 jit_solution(2702650011945330194)
XLA Ops:
  0.0 3.5 %collective-permute-start = (bf16[4,256,128]{2,1,0:T(8,128)(2,1)}, bf16[4,256,128]{2,1,0:T(8,128)(2,1)S(1)}, u32[]{:S(2)}, u32[]{:S(2)}) collective-permute-start(bf16[4,256,128]{2,1,0:T(8,128)(2,1)} %param.5), channel_id=1, source_target_pairs={{0,4},{2,6},{4,8},{6,10},{8,12},{10,14},{1,5},{3,7},{5,9},{7,11},{... | collective-permute-start | bytes 786440 | tf_op jit(solution)/shard_map/ppermute | solution.py:34
  3.5 1.9 %collective-permute-start.1 = (bf16[4,256,128]{2,1,0:T(8,128)(2,1)}, bf16[4,256,128]{2,1,0:T(8,128)(2,1)S(1)}, u32[]{:S(2)}, u32[]{:S(2)}) collective-permute-start(bf16[4,256,128]{2,1,0:T(8,128)(2,1)} %param.5), channel_id=1, source_target_pairs={{0,2},{2,4},{4,6},{6,8},{8,10},{10,12},{12,14},{1,3},{3,5},{5,7},{... | collective-permute-start | bytes 786440 | tf_op jit(solution)/shard_map/ppermute | solution.py:34
  5.4 3.9 %collective-permute-start.2 = (bf16[4,256,128]{2,1,0:T(8,128)(2,1)}, bf16[4,256,128]{2,1,0:T(8,128)(2,1)S(1)}, u32[]{:S(2)}, u32[]{:S(2)}) collective-permute-start(bf16[4,256,128]{2,1,0:T(8,128)(2,1)} %param.5), channel_id=1, source_target_pairs={{2,0},{4,2},{6,4},{8,6},{10,8},{12,10},{14,12},{3,1},{5,3},{7,5},{... | collective-permute-start | bytes 786440 | tf_op jit(solution)/shard_map/ppermute | solution.py:34
  9.3 2.4 %collective-permute-start.3 = (bf16[4,256,128]{2,1,0:T(8,128)(2,1)}, bf16[4,256,128]{2,1,0:T(8,128)(2,1)S(1)}, u32[]{:S(2)}, u32[]{:S(2)}) collective-permute-start(bf16[4,256,128]{2,1,0:T(8,128)(2,1)} %param.5), channel_id=1, source_target_pairs={{4,0},{6,2},{8,4},{10,6},{12,8},{14,10},{5,1},{7,3},{9,5},{11,7},{... | collective-permute-start | bytes 786440 | tf_op jit(solution)/shard_map/ppermute | solution.py:34
  11.7 0.1 collective-permute-start.6
  11.8 0.0 collective-permute-done
  11.8 0.0 copy-start.2
  11.8 3.5 %collective-permute-start.9 = (bf16[4,256,128]{2,1,0:T(8,128)(2,1)}, bf16[4,256,128]{2,1,0:T(8,128)(2,1)S(1)}, u32[]{:S(2)}, u32[]{:S(2)}) collective-permute-start(bf16[4,256,128]{2,1,0:T(8,128)(2,1)} %param.6), channel_id=1, source_target_pairs={{0,4},{2,6},{4,8},{6,10},{8,12},{10,14},{1,5},{3,7},{5,9},{7,11},{... | collective-permute-start | bytes 786440 | tf_op jit(solution)/shard_map/ppermute | solution.py:34
  15.3 3.6 %collective-permute-done.1 = bf16[4,256,128]{2,1,0:T(8,128)(2,1)S(1)} collective-permute-done((bf16[4,256,128]{2,1,0:T(8,128)(2,1)}, bf16[4,256,128]{2,1,0:T(8,128)(2,1)S(1)}, u32[]{:S(2)}, u32[]{:S(2)}) %collective-permute-start.1) | collective-permute-done | bytes 262176 | tf_op jit(solution)/shard_map/ppermute | solution.py:34
  19.0 1.9 %collective-permute-start.10 = (bf16[4,256,128]{2,1,0:T(8,128)(2,1)}, bf16[4,256,128]{2,1,0:T(8,128)(2,1)S(1)}, u32[]{:S(2)}, u32[]{:S(2)}) collective-permute-start(bf16[4,256,128]{2,1,0:T(8,128)(2,1)} %param.6), channel_id=1, source_target_pairs={{0,2},{2,4},{4,6},{6,8},{8,10},{10,12},{12,14},{1,3},{3,5},{5,7},{... | collective-permute-start | bytes 786440 | tf_op jit(solution)/shard_map/ppermute | solution.py:34
  20.9 0.0 collective-permute-done.2
  20.9 3.9 %collective-permute-start.11 = (bf16[4,256,128]{2,1,0:T(8,128)(2,1)}, bf16[4,256,128]{2,1,0:T(8,128)(2,1)S(1)}, u32[]{:S(2)}, u32[]{:S(2)}) collective-permute-start(bf16[4,256,128]{2,1,0:T(8,128)(2,1)} %param.6), channel_id=1, source_target_pairs={{2,0},{4,2},{6,4},{8,6},{10,8},{12,10},{14,12},{3,1},{5,3},{7,5},{... | collective-permute-start | bytes 786440 | tf_op jit(solution)/shard_map/ppermute | solution.py:34
  24.9 0.0 copy-start.15
  24.9 0.0 collective-permute-done.3
  24.9 2.1 %collective-permute-start.12 = (bf16[4,256,128]{2,1,0:T(8,128)(2,1)}, bf16[4,256,128]{2,1,0:T(8,128)(2,1)S(1)}, u32[]{:S(2)}, u32[]{:S(2)}) collective-permute-start(bf16[4,256,128]{2,1,0:T(8,128)(2,1)} %param.6), channel_id=1, source_target_pairs={{4,0},{6,2},{8,4},{10,6},{12,8},{14,10},{5,1},{7,3},{9,5},{11,7},{... | collective-permute-start | bytes 786440 | tf_op jit(solution)/shard_map/ppermute | solution.py:34
  27.0 0.0 collective-permute-done.6.refs_7_
  27.1 0.1 collective-permute-start.4
  27.1 0.0 collective-permute-done.9
  27.2 0.5 collective-permute-start.5
  27.6 5.8 %collective-permute-done.10 = bf16[4,256,128]{2,1,0:T(8,128)(2,1)S(1)} collective-permute-done((bf16[4,256,128]{2,1,0:T(8,128)(2,1)}, bf16[4,256,128]{2,1,0:T(8,128)(2,1)S(1)}, u32[]{:S(2)}, u32[]{:S(2)}) %collective-permute-start.10) | collective-permute-done | bytes 262176 | tf_op jit(solution)/shard_map/ppermute | solution.py:34
  33.4 0.0 collective-permute-start.7
  33.4 0.0 collective-permute-done.11
  33.4 0.5 collective-permute-start.8
  33.9 0.1 add_clamp_fusion
  34.0 0.6 reshape.75.slot_ref
  34.6 0.1 copy-done.18
  34.6 0.1 fusion.5
  34.7 0.7 reshape.91.act_ref
  35.4 0.0 collective-permute-done.12
  35.4 0.0 collective-permute-done.4.refs_5_
  35.4 0.0 collective-permute-done.5.refs_6_
  35.4 0.0 collective-permute-done.8.refs_9_
  35.5 0.8 %copy-done.14 = bf16[8,128,128]{2,1,0:T(8,128)(2,1)} copy-done((bf16[8,128,128]{2,1,0:T(8,128)(2,1)}, bf16[8,128,128]{2,1,0:T(8,128)(2,1)S(1)}, u32[]{:S(2)}) %copy-start.14) | copy-done | bytes 262168
  36.3 0.0 copy-done.12
  36.3 0.1 copy-done.13
  36.4 14.8 %shard_map.55 = (f32[8,128,128]{2,1,0:T(8,128)}, f32[8,1,128]{2,1,0:T(1,128)}, bf16[1040,128]{1,0:T(8,128)(2,1)}, bf16[1040,128]{1,0:T(8,128)(2,1)}, bf16[1040,1...) custom-call(s32[128]{0:T(128)} %reshape.75.slot_ref, s32[8]{0:T(128)} %reshape.91.act_ref, bf16[8,128,128]{2,1,0:T(8,128)(2,1)} %bitcast.56, ...), custom_call_target="tpu_custom_call" | custom-call | tf_op jit(solution)/shard_map/pallas_call | solution.py:166
  51.2 2.3 %collective-permute-start.13 = (bf16[1040,128]{1,0:T(8,128)(2,1)}, bf16[1040,128]{1,0:T(8,128)(2,1)S(1)}, u32[]{:S(2)}, u32[]{:S(2)}) collective-permute-start(bf16[1040,128]{1,0:T(8,128)(2,1)} %get-tuple-element.12), channel_id=1, source_target_pairs={{4,0},{6,2},{8,4},{10,6},{12,8},{14,10},{5,1},{7,3},{9,5},{11,7},{... | collective-permute-start | bytes 798728 | tf_op jit(solution)/shard_map/ppermute | solution.py:34
  53.5 3.8 %collective-permute-start.14 = (bf16[1040,128]{1,0:T(8,128)(2,1)}, bf16[1040,128]{1,0:T(8,128)(2,1)S(1)}, u32[]{:S(2)}, u32[]{:S(2)}) collective-permute-start(bf16[1040,128]{1,0:T(8,128)(2,1)} %get-tuple-element.13), channel_id=1, source_target_pairs={{2,0},{4,2},{6,4},{8,6},{10,8},{12,10},{14,12},{3,1},{5,3},{7,5},{... | collective-permute-start | bytes 798728 | tf_op jit(solution)/shard_map/ppermute | solution.py:34
  57.4 2.9 %collective-permute-start.15 = (bf16[1040,128]{1,0:T(8,128)(2,1)}, bf16[1040,128]{1,0:T(8,128)(2,1)S(1)}, u32[]{:S(2)}, u32[]{:S(2)}) collective-permute-start(bf16[1040,128]{1,0:T(8,128)(2,1)} %get-tuple-element.14), channel_id=1, source_target_pairs={{0,2},{2,4},{4,6},{6,8},{8,10},{10,12},{12,14},{1,3},{3,5},{5,7},{... | collective-permute-start | bytes 798728 | tf_op jit(solution)/shard_map/ppermute | solution.py:34
  60.3 1.9 %collective-permute-start.16 = (bf16[1040,128]{1,0:T(8,128)(2,1)}, bf16[1040,128]{1,0:T(8,128)(2,1)S(1)}, u32[]{:S(2)}, u32[]{:S(2)}) collective-permute-start(bf16[1040,128]{1,0:T(8,128)(2,1)} %get-tuple-element.15), channel_id=1, source_target_pairs={{0,4},{2,6},{4,8},{6,10},{8,12},{10,14},{1,5},{3,7},{5,9},{7,11},{... | collective-permute-start | bytes 798728 | tf_op jit(solution)/shard_map/ppermute | solution.py:34
  62.2 0.1 copy.9
  62.4 6.5 %collective-permute-done.14 = bf16[1040,128]{1,0:T(8,128)(2,1)S(1)} collective-permute-done((bf16[1040,128]{1,0:T(8,128)(2,1)}, bf16[1040,128]{1,0:T(8,128)(2,1)S(1)}, u32[]{:S(2)}, u32[]{:S(2)}) %collective-permute-start.14) | collective-permute-done | bytes 266272 | tf_op jit(solution)/shard_map/ppermute | solution.py:34
  69.0 4.0 %collective-permute-done.15 = bf16[1040,128]{1,0:T(8,128)(2,1)S(1)} collective-permute-done((bf16[1040,128]{1,0:T(8,128)(2,1)}, bf16[1040,128]{1,0:T(8,128)(2,1)S(1)}, u32[]{:S(2)}, u32[]{:S(2)}) %collective-permute-start.15) | collective-permute-done | bytes 266272 | tf_op jit(solution)/shard_map/ppermute | solution.py:34
  73.1 0.6 copy-done.17
  73.9 1.0 %copy-done.1 = f32[8,128,128]{2,1,0:T(8,128)S(1)} copy-done((f32[8,128,128]{2,1,0:T(8,128)S(1)}, f32[8,128,128]{2,1,0:T(8,128)}, u32[]{:S(2)}) %copy-start.1) | copy-done | bytes 524312
  74.9 0.2 add_add_fusion
  75.0 0.1 divide_convert_fusion
  75.1 0.9 %copy.11 = bf16[4,2,128,128]{3,2,1,0:T(8,128)(2,1)} copy(bf16[4,2,128,128]{2,3,1,0:T(8,128)(2,1)S(1)} %divide_convert_fusion) | data formatting | bytes 524288 | tf_op jit(solution)/shard_map/convert_element_type | solution.py:209
  (43 shorter events, 0.4 us)
Async XLA Ops:
  0.0 11.8 %collective-permute-start = (bf16[4,256,128]{2,1,0:T(8,128)(2,1)}, bf16[4,256,128]{2,1,0:T(8,128)(2,1)S(1)}, u32[]{:S(2)}, u32[]{:S(2)}) collective-permute-start(bf16[4,256,128]{2,1,0:T(8,128)(2,1)} %param.5), channel_id=1, source_target_pairs={{0,4},{2,6},{4,8},{6,10},{8,12},{10,14},{1,5},{3,7},{5,9},{7,11},{... | collective-permute-start | bytes 786440 | tf_op jit(solution)/shard_map/ppermute | solution.py:34
  3.5 15.5 %collective-permute-start.1 = (bf16[4,256,128]{2,1,0:T(8,128)(2,1)}, bf16[4,256,128]{2,1,0:T(8,128)(2,1)S(1)}, u32[]{:S(2)}, u32[]{:S(2)}) collective-permute-start(bf16[4,256,128]{2,1,0:T(8,128)(2,1)} %param.5), channel_id=1, source_target_pairs={{0,2},{2,4},{4,6},{6,8},{8,10},{10,12},{12,14},{1,3},{3,5},{5,7},{... | collective-permute-start | bytes 786440 | tf_op jit(solution)/shard_map/ppermute | solution.py:34
  5.4 15.5 %collective-permute-start.2 = (bf16[4,256,128]{2,1,0:T(8,128)(2,1)}, bf16[4,256,128]{2,1,0:T(8,128)(2,1)S(1)}, u32[]{:S(2)}, u32[]{:S(2)}) collective-permute-start(bf16[4,256,128]{2,1,0:T(8,128)(2,1)} %param.5), channel_id=1, source_target_pairs={{2,0},{4,2},{6,4},{8,6},{10,8},{12,10},{14,12},{3,1},{5,3},{7,5},{... | collective-permute-start | bytes 786440 | tf_op jit(solution)/shard_map/ppermute | solution.py:34
  9.3 15.5 %collective-permute-start.3 = (bf16[4,256,128]{2,1,0:T(8,128)(2,1)}, bf16[4,256,128]{2,1,0:T(8,128)(2,1)S(1)}, u32[]{:S(2)}, u32[]{:S(2)}) collective-permute-start(bf16[4,256,128]{2,1,0:T(8,128)(2,1)} %param.5), channel_id=1, source_target_pairs={{4,0},{6,2},{8,4},{10,6},{12,8},{14,10},{5,1},{7,3},{9,5},{11,7},{... | collective-permute-start | bytes 786440 | tf_op jit(solution)/shard_map/ppermute | solution.py:34
  11.7 15.3 %collective-permute-start.6 = (bf16[8,128,128]{2,1,0:T(8,128)(2,1)}, bf16[8,128,128]{2,1,0:T(8,128)(2,1)S(1)}, u32[]{:S(2)}, u32[]{:S(2)}) collective-permute-start(bf16[8,128,128]{2,1,0:T(8,128)(2,1)} %bitcast.53), channel_id=1, source_target_pairs={{0,1},{1,0},{2,3},{3,2},{4,5},{5,4},{6,7},{7,6},{8,9},{9,8},{10,11... | collective-permute-start | bytes 786440 | tf_op jit(solution)/shard_map/ppermute | solution.py:131
  11.8 24.4 %copy-start.2 = (bf16[4,256,128]{2,1,0:T(8,128)(2,1)}, bf16[4,256,128]{2,1,0:T(8,128)(2,1)S(1)}, u32[]{:S(2)}) copy-start(bf16[4,256,128]{2,1,0:T(8,128)(2,1)S(1)} %collective-permute-done) | copy-start | bytes 786436
  11.8 15.3 %collective-permute-start.9 = (bf16[4,256,128]{2,1,0:T(8,128)(2,1)}, bf16[4,256,128]{2,1,0:T(8,128)(2,1)S(1)}, u32[]{:S(2)}, u32[]{:S(2)}) collective-permute-start(bf16[4,256,128]{2,1,0:T(8,128)(2,1)} %param.6), channel_id=1, source_target_pairs={{0,4},{2,6},{4,8},{6,10},{8,12},{10,14},{1,5},{3,7},{5,9},{7,11},{... | collective-permute-start | bytes 786440 | tf_op jit(solution)/shard_map/ppermute | solution.py:34
  19.0 17.3 %copy-start.3 = (bf16[4,256,128]{2,1,0:T(8,128)(2,1)}, bf16[4,256,128]{2,1,0:T(8,128)(2,1)S(1)}, u32[]{:S(2)}) copy-start(bf16[4,256,128]{2,1,0:T(8,128)(2,1)S(1)} %collective-permute-done.1) | copy-start | bytes 786436
  19.0 14.4 %collective-permute-start.10 = (bf16[4,256,128]{2,1,0:T(8,128)(2,1)}, bf16[4,256,128]{2,1,0:T(8,128)(2,1)S(1)}, u32[]{:S(2)}, u32[]{:S(2)}) collective-permute-start(bf16[4,256,128]{2,1,0:T(8,128)(2,1)} %param.6), channel_id=1, source_target_pairs={{0,2},{2,4},{4,6},{6,8},{8,10},{10,12},{12,14},{1,3},{3,5},{5,7},{... | collective-permute-start | bytes 786440 | tf_op jit(solution)/shard_map/ppermute | solution.py:34
  20.9 15.3 %copy-start.4 = (bf16[4,256,128]{2,1,0:T(8,128)(2,1)}, bf16[4,256,128]{2,1,0:T(8,128)(2,1)S(1)}, u32[]{:S(2)}) copy-start(bf16[4,256,128]{2,1,0:T(8,128)(2,1)S(1)} %collective-permute-done.2) | copy-start | bytes 786436
  20.9 12.5 %collective-permute-start.11 = (bf16[4,256,128]{2,1,0:T(8,128)(2,1)}, bf16[4,256,128]{2,1,0:T(8,128)(2,1)S(1)}, u32[]{:S(2)}, u32[]{:S(2)}) collective-permute-start(bf16[4,256,128]{2,1,0:T(8,128)(2,1)} %param.6), channel_id=1, source_target_pairs={{2,0},{4,2},{6,4},{8,6},{10,8},{12,10},{14,12},{3,1},{5,3},{7,5},{... | collective-permute-start | bytes 786440 | tf_op jit(solution)/shard_map/ppermute | solution.py:34
  24.8 9.1 %copy-start.16 = (s32[4,2,16]{2,1,0:T(2,128)S(1)}, s32[4,2,16]{2,1,0:T(2,128)}, u32[]{:S(2)}) copy-start(s32[4,2,16]{2,1,0:T(2,128)} %param.7) | copy-start | bytes 1540
  24.9 9.0 %copy-start.15 = (s32[4,2,16]{2,1,0:T(2,128)S(1)}, s32[4,2,16]{2,1,0:T(2,128)}, u32[]{:S(2)}) copy-start(s32[4,2,16]{2,1,0:T(2,128)} %param.8) | copy-start | bytes 1540
  24.9 11.3 %copy-start.5 = (bf16[4,256,128]{2,1,0:T(8,128)(2,1)}, bf16[4,256,128]{2,1,0:T(8,128)(2,1)S(1)}, u32[]{:S(2)}) copy-start(bf16[4,256,128]{2,1,0:T(8,128)(2,1)S(1)} %collective-permute-done.3) | copy-start | bytes 786436
  24.9 10.5 %collective-permute-start.12 = (bf16[4,256,128]{2,1,0:T(8,128)(2,1)}, bf16[4,256,128]{2,1,0:T(8,128)(2,1)S(1)}, u32[]{:S(2)}, u32[]{:S(2)}) collective-permute-start(bf16[4,256,128]{2,1,0:T(8,128)(2,1)} %param.6), channel_id=1, source_target_pairs={{4,0},{6,2},{8,4},{10,6},{12,8},{14,10},{5,1},{7,3},{9,5},{11,7},{... | collective-permute-start | bytes 786440 | tf_op jit(solution)/shard_map/ppermute | solution.py:34
  27.0 9.2 %copy-start.6 = (bf16[8,128,128]{2,1,0:T(8,128)(2,1)}, bf16[8,128,128]{2,1,0:T(8,128)(2,1)S(1)}, u32[]{:S(2)}) copy-start(bf16[8,128,128]{2,1,0:T(8,128)(2,1)S(1)} %collective-permute-done.6.refs_7_) | copy-start | bytes 786436
  27.1 8.3 %collective-permute-start.4 = (bf16[8,128,128]{2,1,0:T(8,128)(2,1)S(1)}, bf16[8,128,128]{2,1,0:T(8,128)(2,1)S(1)}, u32[]{:S(2)}, u32[]{:S(2)}) collective-permute-start(bf16[8,128,128]{2,1,0:T(8,128)(2,1)S(1)} %bitcast.55), channel_id=1, source_target_pairs={{0,1},{1,0},{2,3},{3,2},{4,5},{5,4},{6,7},{7,6},{8,9},{9,8},{10,11... | collective-permute-start | bytes 786440 | tf_op jit(solution)/shard_map/ppermute | solution.py:131
  27.1 9.1 %copy-start.7 = (bf16[4,256,128]{2,1,0:T(8,128)(2,1)}, bf16[4,256,128]{2,1,0:T(8,128)(2,1)S(1)}, u32[]{:S(2)}) copy-start(bf16[4,256,128]{2,1,0:T(8,128)(2,1)S(1)} %collective-permute-done.9) | copy-start | bytes 786436
  27.2 8.2 %collective-permute-start.5 = (bf16[8,128,128]{2,1,0:T(8,128)(2,1)S(1)}, bf16[8,128,128]{2,1,0:T(8,128)(2,1)S(1)}, u32[]{:S(2)}, u32[]{:S(2)}) collective-permute-start(bf16[8,128,128]{2,1,0:T(8,128)(2,1)S(1)} %bitcast.57), channel_id=1, source_target_pairs={{0,1},{1,0},{2,3},{3,2},{4,5},{5,4},{6,7},{7,6},{8,9},{9,8},{10,11... | collective-permute-start | bytes 786440 | tf_op jit(solution)/shard_map/ppermute | solution.py:131
  33.4 2.9 %copy-start.8 = (bf16[4,256,128]{2,1,0:T(8,128)(2,1)}, bf16[4,256,128]{2,1,0:T(8,128)(2,1)S(1)}, u32[]{:S(2)}) copy-start(bf16[4,256,128]{2,1,0:T(8,128)(2,1)S(1)} %collective-permute-done.10) | copy-start | bytes 786436
  33.4 2.0 %collective-permute-start.7 = (bf16[8,128,128]{2,1,0:T(8,128)(2,1)S(1)}, bf16[8,128,128]{2,1,0:T(8,128)(2,1)S(1)}, u32[]{:S(2)}, u32[]{:S(2)}) collective-permute-start(bf16[8,128,128]{2,1,0:T(8,128)(2,1)S(1)} %bitcast.59), channel_id=1, source_target_pairs={{0,1},{1,0},{2,3},{3,2},{4,5},{5,4},{6,7},{7,6},{8,9},{9,8},{10,11... | collective-permute-start | bytes 786440 | tf_op jit(solution)/shard_map/ppermute | solution.py:131
  33.4 2.9 %copy-start.9 = (bf16[4,256,128]{2,1,0:T(8,128)(2,1)}, bf16[4,256,128]{2,1,0:T(8,128)(2,1)S(1)}, u32[]{:S(2)}) copy-start(bf16[4,256,128]{2,1,0:T(8,128)(2,1)S(1)} %collective-permute-done.11) | copy-start | bytes 786436
  33.4 2.0 %collective-permute-start.8 = (bf16[8,128,128]{2,1,0:T(8,128)(2,1)S(1)}, bf16[8,128,128]{2,1,0:T(8,128)(2,1)S(1)}, u32[]{:S(2)}, u32[]{:S(2)}) collective-permute-start(bf16[8,128,128]{2,1,0:T(8,128)(2,1)S(1)} %bitcast.61), channel_id=1, source_target_pairs={{0,1},{1,0},{2,3},{3,2},{4,5},{5,4},{6,7},{7,6},{8,9},{9,8},{10,11... | collective-permute-start | bytes 786440 | tf_op jit(solution)/shard_map/ppermute | solution.py:131
  34.0 0.7 copy-start.18
  35.4 0.9 %copy-start.10 = (bf16[4,256,128]{2,1,0:T(8,128)(2,1)}, bf16[4,256,128]{2,1,0:T(8,128)(2,1)S(1)}, u32[]{:S(2)}) copy-start(bf16[4,256,128]{2,1,0:T(8,128)(2,1)S(1)} %collective-permute-done.12) | copy-start | bytes 786436
  35.4 0.9 %copy-start.11 = (bf16[8,128,128]{2,1,0:T(8,128)(2,1)}, bf16[8,128,128]{2,1,0:T(8,128)(2,1)S(1)}, u32[]{:S(2)}) copy-start(bf16[8,128,128]{2,1,0:T(8,128)(2,1)S(1)} %collective-permute-done.4.refs_5_) | copy-start | bytes 786436
  35.4 0.9 %copy-start.12 = (bf16[8,128,128]{2,1,0:T(8,128)(2,1)}, bf16[8,128,128]{2,1,0:T(8,128)(2,1)S(1)}, u32[]{:S(2)}) copy-start(bf16[8,128,128]{2,1,0:T(8,128)(2,1)S(1)} %collective-permute-done.5.refs_6_) | copy-start | bytes 786436
  35.4 1.0 %copy-start.13 = (bf16[8,128,128]{2,1,0:T(8,128)(2,1)}, bf16[8,128,128]{2,1,0:T(8,128)(2,1)S(1)}, u32[]{:S(2)}) copy-start(bf16[8,128,128]{2,1,0:T(8,128)(2,1)S(1)} %collective-permute-done.7.refs_8_) | copy-start | bytes 786436
  35.5 0.8 %copy-start.14 = (bf16[8,128,128]{2,1,0:T(8,128)(2,1)}, bf16[8,128,128]{2,1,0:T(8,128)(2,1)S(1)}, u32[]{:S(2)}) copy-start(bf16[8,128,128]{2,1,0:T(8,128)(2,1)S(1)} %collective-permute-done.8.refs_9_) | copy-start | bytes 786436
  36.4 25.8 %copy-start = (bf16[4,256,128]{2,1,0:T(8,128)(2,1)S(1)}, bf16[4,256,128]{2,1,0:T(8,128)(2,1)}, u32[]{:S(2)}) copy-start(bf16[4,256,128]{2,1,0:T(8,128)(2,1)} %param.6) | copy-start | bytes 786436
  51.2 11.2 %collective-permute-start.13 = (bf16[1040,128]{1,0:T(8,128)(2,1)}, bf16[1040,128]{1,0:T(8,128)(2,1)S(1)}, u32[]{:S(2)}, u32[]{:S(2)}) collective-permute-start(bf16[1040,128]{1,0:T(8,128)(2,1)} %get-tuple-element.12), channel_id=1, source_target_pairs={{4,0},{6,2},{8,4},{10,6},{12,8},{14,10},{5,1},{7,3},{9,5},{11,7},{... | collective-permute-start | bytes 798728 | tf_op jit(solution)/shard_map/ppermute | solution.py:34
  53.5 15.4 %collective-permute-start.14 = (bf16[1040,128]{1,0:T(8,128)(2,1)}, bf16[1040,128]{1,0:T(8,128)(2,1)S(1)}, u32[]{:S(2)}, u32[]{:S(2)}) collective-permute-start(bf16[1040,128]{1,0:T(8,128)(2,1)} %get-tuple-element.13), channel_id=1, source_target_pairs={{2,0},{4,2},{6,4},{8,6},{10,8},{12,10},{14,12},{3,1},{5,3},{7,5},{... | collective-permute-start | bytes 798728 | tf_op jit(solution)/shard_map/ppermute | solution.py:34
  57.4 15.6 %collective-permute-start.15 = (bf16[1040,128]{1,0:T(8,128)(2,1)}, bf16[1040,128]{1,0:T(8,128)(2,1)S(1)}, u32[]{:S(2)}, u32[]{:S(2)}) collective-permute-start(bf16[1040,128]{1,0:T(8,128)(2,1)} %get-tuple-element.14), channel_id=1, source_target_pairs={{0,2},{2,4},{4,6},{6,8},{8,10},{10,12},{12,14},{1,3},{3,5},{5,7},{... | collective-permute-start | bytes 798728 | tf_op jit(solution)/shard_map/ppermute | solution.py:34
  60.3 12.7 %collective-permute-start.16 = (bf16[1040,128]{1,0:T(8,128)(2,1)}, bf16[1040,128]{1,0:T(8,128)(2,1)S(1)}, u32[]{:S(2)}, u32[]{:S(2)}) collective-permute-start(bf16[1040,128]{1,0:T(8,128)(2,1)} %get-tuple-element.15), channel_id=1, source_target_pairs={{0,4},{2,6},{4,8},{6,10},{8,12},{10,14},{1,5},{3,7},{5,9},{7,11},{... | collective-permute-start | bytes 798728 | tf_op jit(solution)/shard_map/ppermute | solution.py:34
  73.0 0.7 copy-start.17
  73.8 1.0 %copy-start.1 = (f32[8,128,128]{2,1,0:T(8,128)S(1)}, f32[8,128,128]{2,1,0:T(8,128)}, u32[]{:S(2)}) copy-start(f32[8,128,128]{2,1,0:T(8,128)} %get-tuple-element.11) | copy-start | bytes 1572868

commit v9 on v8

--- a/solution.py
+++ b/solution.py
@@ -40,7 +40,7 @@
     sources = [refs[:slabs], refs[2 * slabs : 3 * slabs], refs[slabs : 2 * slabs]]
     own_num_ref, own_mass_ref = refs[3 * slabs : 3 * slabs + 2]
     remote_refs = refs[3 * slabs + 2 : 4 * slabs + 1]
-    key_e, key_v, acc, macc, score_ref, value_ref, sems = refs[4 * slabs + 1 :]
+    key_e, key_v, acc, macc, key_ref, value_ref, sems = refs[4 * slabs + 1 :]
 
     copies = []
     for s in range(slabs):
@@ -68,10 +68,9 @@
         slots = [slot_ref[i * K + k] for k in range(K)]
         for k in range(K):
             s = slots[k]
-            part = lax.dot_general(query, key_e[s], dims_t, preferred_element_type=jnp.float32)
-            score_ref[:, k * BLOCK : (k + 1) * BLOCK] = part
+            key_ref[k * BLOCK : (k + 1) * BLOCK, :] = key_e[s]
             value_ref[k * BLOCK : (k + 1) * BLOCK, :] = key_v[s]
-        score = score_ref[...]
+        score = lax.dot_general(query, key_ref[...], dims_t, preferred_element_type=jnp.float32)
         peak = jnp.max(score, axis=-1, keepdims=True)
         exponent = jnp.exp(score - peak)
         prob = exponent / jnp.sum(exponent, axis=-1, keepdims=True)
@@ -173,7 +172,7 @@
             pltpu.VMEM((total, BLOCK, half), jnp.bfloat16),
             pltpu.VMEM((total, half, BLOCK), jnp.float32),
             pltpu.VMEM((total, 1, BLOCK), jnp.float32),
-            pltpu.VMEM((BLOCK, K * BLOCK), jnp.float32),
+            pltpu.VMEM((K * BLOCK, 2 * half), jnp.bfloat16),
             pltpu.VMEM((K * BLOCK, half), jnp.bfloat16),
             pltpu.SemaphoreType.DMA((3, slabs)),
         ],

time: 76.5 us -> 76.7 us (level)
  no operation moved by 1% of the time
where the time goes in v9:
time: 76.7 us; the launch traced here: 76.2 us
  starting transfers between devices  35.2 us (46%)
  waiting for transfers between devices  20 us (26%)
  Pallas kernels  15 us (20%)
  local copies, waits for them, and re-layouts  5.02 us (7%)
    ppermute x12, starting transfers between devices, passed_along(): return lax.ppermute(block, axis, route)  34.1 us
    ppermute x12, waiting for transfers between devices, passed_along(): return lax.ppermute(block, axis, route)  19.9 us
    pallas_call x1, Pallas kernels, shards(): pl.pallas_call(kernel, out_shape=out_shape, in_specs=[smem, smem] + [vmem...  15 us
    unnamed x38, local copies, waits for them, and re-layouts  2.62 us
  transfers between devices with their start and end apart: 17, of which 4 were waited for; matrix products, arithmetic and copies ran while one was open for 2% of the time, Pallas kernels for 0%

profile of v9, /device:TPU:22, one launch (start us, length us, event | category | flops | bytes accessed | tf_op | source)
XLA Modules:
  0.0 76.2 jit_solution(15211590162553686665)
XLA Ops:
  0.0 3.5 %collective-permute-start = (bf16[4,256,128]{2,1,0:T(8,128)(2,1)}, bf16[4,256,128]{2,1,0:T(8,128)(2,1)S(1)}, u32[]{:S(2)}, u32[]{:S(2)}) collective-permute-start(bf16[4,256,128]{2,1,0:T(8,128)(2,1)} %param.5), channel_id=1, source_target_pairs={{0,4},{2,6},{4,8},{6,10},{8,12},{10,14},{1,5},{3,7},{5,9},{7,11},{... | collective-permute-start | bytes 786440 | tf_op jit(solution)/shard_map/ppermute | solution.py:34
  3.5 1.9 %collective-permute-start.1 = (bf16[4,256,128]{2,1,0:T(8,128)(2,1)}, bf16[4,256,128]{2,1,0:T(8,128)(2,1)S(1)}, u32[]{:S(2)}, u32[]{:S(2)}) collective-permute-start(bf16[4,256,128]{2,1,0:T(8,128)(2,1)} %param.5), channel_id=1, source_target_pairs={{0,2},{2,4},{4,6},{6,8},{8,10},{10,12},{12,14},{1,3},{3,5},{5,7},{... | collective-permute-start | bytes 786440 | tf_op jit(solution)/shard_map/ppermute | solution.py:34
  5.4 3.9 %collective-permute-start.2 = (bf16[4,256,128]{2,1,0:T(8,128)(2,1)}, bf16[4,256,128]{2,1,0:T(8,128)(2,1)S(1)}, u32[]{:S(2)}, u32[]{:S(2)}) collective-permute-start(bf16[4,256,128]{2,1,0:T(8,128)(2,1)} %param.5), channel_id=1, source_target_pairs={{2,0},{4,2},{6,4},{8,6},{10,8},{12,10},{14,12},{3,1},{5,3},{7,5},{... | collective-permute-start | bytes 786440 | tf_op jit(solution)/shard_map/ppermute | solution.py:34
  9.3 2.4 %collective-permute-start.3 = (bf16[4,256,128]{2,1,0:T(8,128)(2,1)}, bf16[4,256,128]{2,1,0:T(8,128)(2,1)S(1)}, u32[]{:S(2)}, u32[]{:S(2)}) collective-permute-start(bf16[4,256,128]{2,1,0:T(8,128)(2,1)} %param.5), channel_id=1, source_target_pairs={{4,0},{6,2},{8,4},{10,6},{12,8},{14,10},{5,1},{7,3},{9,5},{11,7},{... | collective-permute-start | bytes 786440 | tf_op jit(solution)/shard_map/ppermute | solution.py:34
  11.7 0.1 collective-permute-start.6
  11.8 0.0 collective-permute-done
  11.8 0.0 copy-start.2
  11.8 3.5 %collective-permute-start.9 = (bf16[4,256,128]{2,1,0:T(8,128)(2,1)}, bf16[4,256,128]{2,1,0:T(8,128)(2,1)S(1)}, u32[]{:S(2)}, u32[]{:S(2)}) collective-permute-start(bf16[4,256,128]{2,1,0:T(8,128)(2,1)} %param.6), channel_id=1, source_target_pairs={{0,4},{2,6},{4,8},{6,10},{8,12},{10,14},{1,5},{3,7},{5,9},{7,11},{... | collective-permute-start | bytes 786440 | tf_op jit(solution)/shard_map/ppermute | solution.py:34
  15.3 3.6 %collective-permute-done.1 = bf16[4,256,128]{2,1,0:T(8,128)(2,1)S(1)} collective-permute-done((bf16[4,256,128]{2,1,0:T(8,128)(2,1)}, bf16[4,256,128]{2,1,0:T(8,128)(2,1)S(1)}, u32[]{:S(2)}, u32[]{:S(2)}) %collective-permute-start.1) | collective-permute-done | bytes 262176 | tf_op jit(solution)/shard_map/ppermute | solution.py:34
  19.0 1.9 %collective-permute-start.10 = (bf16[4,256,128]{2,1,0:T(8,128)(2,1)}, bf16[4,256,128]{2,1,0:T(8,128)(2,1)S(1)}, u32[]{:S(2)}, u32[]{:S(2)}) collective-permute-start(bf16[4,256,128]{2,1,0:T(8,128)(2,1)} %param.6), channel_id=1, source_target_pairs={{0,2},{2,4},{4,6},{6,8},{8,10},{10,12},{12,14},{1,3},{3,5},{5,7},{... | collective-permute-start | bytes 786440 | tf_op jit(solution)/shard_map/ppermute | solution.py:34
  20.9 0.0 collective-permute-done.2
  20.9 3.9 %collective-permute-start.11 = (bf16[4,256,128]{2,1,0:T(8,128)(2,1)}, bf16[4,256,128]{2,1,0:T(8,128)(2,1)S(1)}, u32[]{:S(2)}, u32[]{:S(2)}) collective-permute-start(bf16[4,256,128]{2,1,0:T(8,128)(2,1)} %param.6), channel_id=1, source_target_pairs={{2,0},{4,2},{6,4},{8,6},{10,8},{12,10},{14,12},{3,1},{5,3},{7,5},{... | collective-permute-start | bytes 786440 | tf_op jit(solution)/shard_map/ppermute | solution.py:34
  24.9 0.0 copy-start.15
  24.9 0.0 collective-permute-done.3
  24.9 2.1 %collective-permute-start.12 = (bf16[4,256,128]{2,1,0:T(8,128)(2,1)}, bf16[4,256,128]{2,1,0:T(8,128)(2,1)S(1)}, u32[]{:S(2)}, u32[]{:S(2)}) collective-permute-start(bf16[4,256,128]{2,1,0:T(8,128)(2,1)} %param.6), channel_id=1, source_target_pairs={{4,0},{6,2},{8,4},{10,6},{12,8},{14,10},{5,1},{7,3},{9,5},{11,7},{... | collective-permute-start | bytes 786440 | tf_op jit(solution)/shard_map/ppermute | solution.py:34
  27.0 0.0 collective-permute-done.6.refs_7_
  27.1 0.1 collective-permute-start.4
  27.1 0.0 collective-permute-done.9
  27.2 0.5 collective-permute-start.5
  27.6 5.8 %collective-permute-done.10 = bf16[4,256,128]{2,1,0:T(8,128)(2,1)S(1)} collective-permute-done((bf16[4,256,128]{2,1,0:T(8,128)(2,1)}, bf16[4,256,128]{2,1,0:T(8,128)(2,1)S(1)}, u32[]{:S(2)}, u32[]{:S(2)}) %collective-permute-start.10) | collective-permute-done | bytes 262176 | tf_op jit(solution)/shard_map/ppermute | solution.py:34
  33.4 0.0 collective-permute-start.7
  33.4 0.0 collective-permute-done.11
  33.4 0.5 collective-permute-start.8
  33.9 0.1 add_clamp_fusion
  34.0 0.6 reshape.75.slot_ref
  34.6 0.1 copy-done.18
  34.6 0.1 fusion.5
  34.7 0.7 reshape.91.act_ref
  35.4 0.0 collective-permute-done.12
  35.4 0.0 collective-permute-done.4.refs_5_
  35.4 0.0 collective-permute-done.5.refs_6_
  35.4 0.0 collective-permute-done.7.refs_8_
  35.5 0.8 copy-done.14
  36.3 0.0 copy-done.12
  36.3 0.1 copy-done.13
  36.4 15.0 %shard_map.55 = (f32[8,128,128]{2,1,0:T(8,128)}, f32[8,1,128]{2,1,0:T(1,128)}, bf16[1040,128]{1,0:T(8,128)(2,1)}, bf16[1040,128]{1,0:T(8,128)(2,1)}, bf16[1040,1...) custom-call(s32[128]{0:T(128)} %reshape.75.slot_ref, s32[8]{0:T(128)} %reshape.91.act_ref, bf16[8,128,128]{2,1,0:T(8,128)(2,1)} %bitcast.56, ...), custom_call_target="tpu_custom_call" | custom-call | tf_op jit(solution)/shard_map/pallas_call | solution.py:165
  51.4 2.3 %collective-permute-start.13 = (bf16[1040,128]{1,0:T(8,128)(2,1)}, bf16[1040,128]{1,0:T(8,128)(2,1)S(1)}, u32[]{:S(2)}, u32[]{:S(2)}) collective-permute-start(bf16[1040,128]{1,0:T(8,128)(2,1)} %get-tuple-element.12), channel_id=1, source_target_pairs={{4,0},{6,2},{8,4},{10,6},{12,8},{14,10},{5,1},{7,3},{9,5},{11,7},{... | collective-permute-start | bytes 798728 | tf_op jit(solution)/shard_map/ppermute | solution.py:34
  53.7 3.9 %collective-permute-start.14 = (bf16[1040,128]{1,0:T(8,128)(2,1)}, bf16[1040,128]{1,0:T(8,128)(2,1)S(1)}, u32[]{:S(2)}, u32[]{:S(2)}) collective-permute-start(bf16[1040,128]{1,0:T(8,128)(2,1)} %get-tuple-element.13), channel_id=1, source_target_pairs={{2,0},{4,2},{6,4},{8,6},{10,8},{12,10},{14,12},{3,1},{5,3},{7,5},{... | collective-permute-start | bytes 798728 | tf_op jit(solution)/shard_map/ppermute | solution.py:34
  57.6 2.9 %collective-permute-start.15 = (bf16[1040,128]{1,0:T(8,128)(2,1)}, bf16[1040,128]{1,0:T(8,128)(2,1)S(1)}, u32[]{:S(2)}, u32[]{:S(2)}) collective-permute-start(bf16[1040,128]{1,0:T(8,128)(2,1)} %get-tuple-element.14), channel_id=1, source_target_pairs={{0,2},{2,4},{4,6},{6,8},{8,10},{10,12},{12,14},{1,3},{3,5},{5,7},{... | collective-permute-start | bytes 798728 | tf_op jit(solution)/shard_map/ppermute | solution.py:34
  60.5 1.9 %collective-permute-start.16 = (bf16[1040,128]{1,0:T(8,128)(2,1)}, bf16[1040,128]{1,0:T(8,128)(2,1)S(1)}, u32[]{:S(2)}, u32[]{:S(2)}) collective-permute-start(bf16[1040,128]{1,0:T(8,128)(2,1)} %get-tuple-element.15), channel_id=1, source_target_pairs={{0,4},{2,6},{4,8},{6,10},{8,12},{10,14},{1,5},{3,7},{5,9},{7,11},{... | collective-permute-start | bytes 798728 | tf_op jit(solution)/shard_map/ppermute | solution.py:34
  62.4 0.1 copy.9
  62.6 6.6 %collective-permute-done.14 = bf16[1040,128]{1,0:T(8,128)(2,1)S(1)} collective-permute-done((bf16[1040,128]{1,0:T(8,128)(2,1)}, bf16[1040,128]{1,0:T(8,128)(2,1)S(1)}, u32[]{:S(2)}, u32[]{:S(2)}) %collective-permute-start.14) | collective-permute-done | bytes 266272 | tf_op jit(solution)/shard_map/ppermute | solution.py:34
  69.2 4.0 %collective-permute-done.15 = bf16[1040,128]{1,0:T(8,128)(2,1)S(1)} collective-permute-done((bf16[1040,128]{1,0:T(8,128)(2,1)}, bf16[1040,128]{1,0:T(8,128)(2,1)S(1)}, u32[]{:S(2)}, u32[]{:S(2)}) %collective-permute-start.15) | collective-permute-done | bytes 266272 | tf_op jit(solution)/shard_map/ppermute | solution.py:34
  73.3 0.6 copy-done.17
  74.1 1.0 %copy-done.1 = f32[8,128,128]{2,1,0:T(8,128)S(1)} copy-done((f32[8,128,128]{2,1,0:T(8,128)S(1)}, f32[8,128,128]{2,1,0:T(8,128)}, u32[]{:S(2)}) %copy-start.1) | copy-done | bytes 524312
  75.1 0.2 add_add_fusion
  75.3 0.1 divide_convert_fusion
  75.4 0.9 %copy.11 = bf16[4,2,128,128]{3,2,1,0:T(8,128)(2,1)} copy(bf16[4,2,128,128]{2,3,1,0:T(8,128)(2,1)S(1)} %divide_convert_fusion) | data formatting | bytes 524288 | tf_op jit(solution)/shard_map/convert_element_type | solution.py:208
  (43 shorter events, 0.4 us)
Async XLA Ops:
  0.0 11.8 %collective-permute-start = (bf16[4,256,128]{2,1,0:T(8,128)(2,1)}, bf16[4,256,128]{2,1,0:T(8,128)(2,1)S(1)}, u32[]{:S(2)}, u32[]{:S(2)}) collective-permute-start(bf16[4,256,128]{2,1,0:T(8,128)(2,1)} %param.5), channel_id=1, source_target_pairs={{0,4},{2,6},{4,8},{6,10},{8,12},{10,14},{1,5},{3,7},{5,9},{7,11},{... | collective-permute-start | bytes 786440 | tf_op jit(solution)/shard_map/ppermute | solution.py:34
  3.5 15.5 %collective-permute-start.1 = (bf16[4,256,128]{2,1,0:T(8,128)(2,1)}, bf16[4,256,128]{2,1,0:T(8,128)(2,1)S(1)}, u32[]{:S(2)}, u32[]{:S(2)}) collective-permute-start(bf16[4,256,128]{2,1,0:T(8,128)(2,1)} %param.5), channel_id=1, source_target_pairs={{0,2},{2,4},{4,6},{6,8},{8,10},{10,12},{12,14},{1,3},{3,5},{5,7},{... | collective-permute-start | bytes 786440 | tf_op jit(solution)/shard_map/ppermute | solution.py:34
  5.4 15.5 %collective-permute-start.2 = (bf16[4,256,128]{2,1,0:T(8,128)(2,1)}, bf16[4,256,128]{2,1,0:T(8,128)(2,1)S(1)}, u32[]{:S(2)}, u32[]{:S(2)}) collective-permute-start(bf16[4,256,128]{2,1,0:T(8,128)(2,1)} %param.5), channel_id=1, source_target_pairs={{2,0},{4,2},{6,4},{8,6},{10,8},{12,10},{14,12},{3,1},{5,3},{7,5},{... | collective-permute-start | bytes 786440 | tf_op jit(solution)/shard_map/ppermute | solution.py:34
  9.3 15.5 %collective-permute-start.3 = (bf16[4,256,128]{2,1,0:T(8,128)(2,1)}, bf16[4,256,128]{2,1,0:T(8,128)(2,1)S(1)}, u32[]{:S(2)}, u32[]{:S(2)}) collective-permute-start(bf16[4,256,128]{2,1,0:T(8,128)(2,1)} %param.5), channel_id=1, source_target_pairs={{4,0},{6,2},{8,4},{10,6},{12,8},{14,10},{5,1},{7,3},{9,5},{11,7},{... | collective-permute-start | bytes 786440 | tf_op jit(solution)/shard_map/ppermute | solution.py:34
  11.7 15.3 %collective-permute-start.6 = (bf16[8,128,128]{2,1,0:T(8,128)(2,1)}, bf16[8,128,128]{2,1,0:T(8,128)(2,1)S(1)}, u32[]{:S(2)}, u32[]{:S(2)}) collective-permute-start(bf16[8,128,128]{2,1,0:T(8,128)(2,1)} %bitcast.53), channel_id=1, source_target_pairs={{0,1},{1,0},{2,3},{3,2},{4,5},{5,4},{6,7},{7,6},{8,9},{9,8},{10,11... | collective-permute-start | bytes 786440 | tf_op jit(solution)/shard_map/ppermute | solution.py:130
  11.8 24.4 %copy-start.2 = (bf16[4,256,128]{2,1,0:T(8,128)(2,1)}, bf16[4,256,128]{2,1,0:T(8,128)(2,1)S(1)}, u32[]{:S(2)}) copy-start(bf16[4,256,128]{2,1,0:T(8,128)(2,1)S(1)} %collective-permute-done) | copy-start | bytes 786436
  11.8 15.3 %collective-permute-start.9 = (bf16[4,256,128]{2,1,0:T(8,128)(2,1)}, bf16[4,256,128]{2,1,0:T(8,128)(2,1)S(1)}, u32[]{:S(2)}, u32[]{:S(2)}) collective-permute-start(bf16[4,256,128]{2,1,0:T(8,128)(2,1)} %param.6), channel_id=1, source_target_pairs={{0,4},{2,6},{4,8},{6,10},{8,12},{10,14},{1,5},{3,7},{5,9},{7,11},{... | collective-permute-start | bytes 786440 | tf_op jit(solution)/shard_map/ppermute | solution.py:34
  19.0 17.3 %copy-start.3 = (bf16[4,256,128]{2,1,0:T(8,128)(2,1)}, bf16[4,256,128]{2,1,0:T(8,128)(2,1)S(1)}, u32[]{:S(2)}) copy-start(bf16[4,256,128]{2,1,0:T(8,128)(2,1)S(1)} %collective-permute-done.1) | copy-start | bytes 786436
  19.0 14.4 %collective-permute-start.10 = (bf16[4,256,128]{2,1,0:T(8,128)(2,1)}, bf16[4,256,128]{2,1,0:T(8,128)(2,1)S(1)}, u32[]{:S(2)}, u32[]{:S(2)}) collective-permute-start(bf16[4,256,128]{2,1,0:T(8,128)(2,1)} %param.6), channel_id=1, source_target_pairs={{0,2},{2,4},{4,6},{6,8},{8,10},{10,12},{12,14},{1,3},{3,5},{5,7},{... | collective-permute-start | bytes 786440 | tf_op jit(solution)/shard_map/ppermute | solution.py:34
  20.9 15.3 %copy-start.4 = (bf16[4,256,128]{2,1,0:T(8,128)(2,1)}, bf16[4,256,128]{2,1,0:T(8,128)(2,1)S(1)}, u32[]{:S(2)}) copy-start(bf16[4,256,128]{2,1,0:T(8,128)(2,1)S(1)} %collective-permute-done.2) | copy-start | bytes 786436
  20.9 12.5 %collective-permute-start.11 = (bf16[4,256,128]{2,1,0:T(8,128)(2,1)}, bf16[4,256,128]{2,1,0:T(8,128)(2,1)S(1)}, u32[]{:S(2)}, u32[]{:S(2)}) collective-permute-start(bf16[4,256,128]{2,1,0:T(8,128)(2,1)} %param.6), channel_id=1, source_target_pairs={{2,0},{4,2},{6,4},{8,6},{10,8},{12,10},{14,12},{3,1},{5,3},{7,5},{... | collective-permute-start | bytes 786440 | tf_op jit(solution)/shard_map/ppermute | solution.py:34
  24.8 9.1 %copy-start.16 = (s32[4,2,16]{2,1,0:T(2,128)S(1)}, s32[4,2,16]{2,1,0:T(2,128)}, u32[]{:S(2)}) copy-start(s32[4,2,16]{2,1,0:T(2,128)} %param.7) | copy-start | bytes 1540
  24.9 9.0 %copy-start.15 = (s32[4,2,16]{2,1,0:T(2,128)S(1)}, s32[4,2,16]{2,1,0:T(2,128)}, u32[]{:S(2)}) copy-start(s32[4,2,16]{2,1,0:T(2,128)} %param.8) | copy-start | bytes 1540
  24.9 11.3 %copy-start.5 = (bf16[4,256,128]{2,1,0:T(8,128)(2,1)}, bf16[4,256,128]{2,1,0:T(8,128)(2,1)S(1)}, u32[]{:S(2)}) copy-start(bf16[4,256,128]{2,1,0:T(8,128)(2,1)S(1)} %collective-permute-done.3) | copy-start | bytes 786436
  24.9 10.5 %collective-permute-start.12 = (bf16[4,256,128]{2,1,0:T(8,128)(2,1)}, bf16[4,256,128]{2,1,0:T(8,128)(2,1)S(1)}, u32[]{:S(2)}, u32[]{:S(2)}) collective-permute-start(bf16[4,256,128]{2,1,0:T(8,128)(2,1)} %param.6), channel_id=1, source_target_pairs={{4,0},{6,2},{8,4},{10,6},{12,8},{14,10},{5,1},{7,3},{9,5},{11,7},{... | collective-permute-start | bytes 786440 | tf_op jit(solution)/shard_map/ppermute | solution.py:34
  27.0 9.2 %copy-start.6 = (bf16[8,128,128]{2,1,0:T(8,128)(2,1)}, bf16[8,128,128]{2,1,0:T(8,128)(2,1)S(1)}, u32[]{:S(2)}) copy-start(bf16[8,128,128]{2,1,0:T(8,128)(2,1)S(1)} %collective-permute-done.6.refs_7_) | copy-start | bytes 786436
  27.1 8.3 %collective-permute-start.4 = (bf16[8,128,128]{2,1,0:T(8,128)(2,1)S(1)}, bf16[8,128,128]{2,1,0:T(8,128)(2,1)S(1)}, u32[]{:S(2)}, u32[]{:S(2)}) collective-permute-start(bf16[8,128,128]{2,1,0:T(8,128)(2,1)S(1)} %bitcast.55), channel_id=1, source_target_pairs={{0,1},{1,0},{2,3},{3,2},{4,5},{5,4},{6,7},{7,6},{8,9},{9,8},{10,11... | collective-permute-start | bytes 786440 | tf_op jit(solution)/shard_map/ppermute | solution.py:130
  27.1 9.1 %copy-start.7 = (bf16[4,256,128]{2,1,0:T(8,128)(2,1)}, bf16[4,256,128]{2,1,0:T(8,128)(2,1)S(1)}, u32[]{:S(2)}) copy-start(bf16[4,256,128]{2,1,0:T(8,128)(2,1)S(1)} %collective-permute-done.9) | copy-start | bytes 786436
  27.2 8.2 %collective-permute-start.5 = (bf16[8,128,128]{2,1,0:T(8,128)(2,1)S(1)}, bf16[8,128,128]{2,1,0:T(8,128)(2,1)S(1)}, u32[]{:S(2)}, u32[]{:S(2)}) collective-permute-start(bf16[8,128,128]{2,1,0:T(8,128)(2,1)S(1)} %bitcast.57), channel_id=1, source_target_pairs={{0,1},{1,0},{2,3},{3,2},{4,5},{5,4},{6,7},{7,6},{8,9},{9,8},{10,11... | collective-permute-start | bytes 786440 | tf_op jit(solution)/shard_map/ppermute | solution.py:130
  33.4 2.9 %copy-start.8 = (bf16[4,256,128]{2,1,0:T(8,128)(2,1)}, bf16[4,256,128]{2,1,0:T(8,128)(2,1)S(1)}, u32[]{:S(2)}) copy-start(bf16[4,256,128]{2,1,0:T(8,128)(2,1)S(1)} %collective-permute-done.10) | copy-start | bytes 786436
  33.4 2.0 %collective-permute-start.7 = (bf16[8,128,128]{2,1,0:T(8,128)(2,1)S(1)}, bf16[8,128,128]{2,1,0:T(8,128)(2,1)S(1)}, u32[]{:S(2)}, u32[]{:S(2)}) collective-permute-start(bf16[8,128,128]{2,1,0:T(8,128)(2,1)S(1)} %bitcast.59), channel_id=1, source_target_pairs={{0,1},{1,0},{2,3},{3,2},{4,5},{5,4},{6,7},{7,6},{8,9},{9,8},{10,11... | collective-permute-start | bytes 786440 | tf_op jit(solution)/shard_map/ppermute | solution.py:130
  33.4 2.9 %copy-start.9 = (bf16[4,256,128]{2,1,0:T(8,128)(2,1)}, bf16[4,256,128]{2,1,0:T(8,128)(2,1)S(1)}, u32[]{:S(2)}) copy-start(bf16[4,256,128]{2,1,0:T(8,128)(2,1)S(1)} %collective-permute-done.11) | copy-start | bytes 786436
  33.4 2.0 %collective-permute-start.8 = (bf16[8,128,128]{2,1,0:T(8,128)(2,1)S(1)}, bf16[8,128,128]{2,1,0:T(8,128)(2,1)S(1)}, u32[]{:S(2)}, u32[]{:S(2)}) collective-permute-start(bf16[8,128,128]{2,1,0:T(8,128)(2,1)S(1)} %bitcast.61), channel_id=1, source_target_pairs={{0,1},{1,0},{2,3},{3,2},{4,5},{5,4},{6,7},{7,6},{8,9},{9,8},{10,11... | collective-permute-start | bytes 786440 | tf_op jit(solution)/shard_map/ppermute | solution.py:130
  34.0 0.7 copy-start.18
  35.4 0.9 %copy-start.10 = (bf16[4,256,128]{2,1,0:T(8,128)(2,1)}, bf16[4,256,128]{2,1,0:T(8,128)(2,1)S(1)}, u32[]{:S(2)}) copy-start(bf16[4,256,128]{2,1,0:T(8,128)(2,1)S(1)} %collective-permute-done.12) | copy-start | bytes 786436
  35.4 0.9 %copy-start.11 = (bf16[8,128,128]{2,1,0:T(8,128)(2,1)}, bf16[8,128,128]{2,1,0:T(8,128)(2,1)S(1)}, u32[]{:S(2)}) copy-start(bf16[8,128,128]{2,1,0:T(8,128)(2,1)S(1)} %collective-permute-done.4.refs_5_) | copy-start | bytes 786436
  35.4 0.9 %copy-start.12 = (bf16[8,128,128]{2,1,0:T(8,128)(2,1)}, bf16[8,128,128]{2,1,0:T(8,128)(2,1)S(1)}, u32[]{:S(2)}) copy-start(bf16[8,128,128]{2,1,0:T(8,128)(2,1)S(1)} %collective-permute-done.5.refs_6_) | copy-start | bytes 786436
  35.4 1.0 %copy-start.13 = (bf16[8,128,128]{2,1,0:T(8,128)(2,1)}, bf16[8,128,128]{2,1,0:T(8,128)(2,1)S(1)}, u32[]{:S(2)}) copy-start(bf16[8,128,128]{2,1,0:T(8,128)(2,1)S(1)} %collective-permute-done.7.refs_8_) | copy-start | bytes 786436
  35.5 0.8 %copy-start.14 = (bf16[8,128,128]{2,1,0:T(8,128)(2,1)}, bf16[8,128,128]{2,1,0:T(8,128)(2,1)S(1)}, u32[]{:S(2)}) copy-start(bf16[8,128,128]{2,1,0:T(8,128)(2,1)S(1)} %collective-permute-done.8.refs_9_) | copy-start | bytes 786436
  36.4 26.0 %copy-start = (bf16[4,256,128]{2,1,0:T(8,128)(2,1)S(1)}, bf16[4,256,128]{2,1,0:T(8,128)(2,1)}, u32[]{:S(2)}) copy-start(bf16[4,256,128]{2,1,0:T(8,128)(2,1)} %param.6) | copy-start | bytes 786436
  51.4 11.2 %collective-permute-start.13 = (bf16[1040,128]{1,0:T(8,128)(2,1)}, bf16[1040,128]{1,0:T(8,128)(2,1)S(1)}, u32[]{:S(2)}, u32[]{:S(2)}) collective-permute-start(bf16[1040,128]{1,0:T(8,128)(2,1)} %get-tuple-element.12), channel_id=1, source_target_pairs={{4,0},{6,2},{8,4},{10,6},{12,8},{14,10},{5,1},{7,3},{9,5},{11,7},{... | collective-permute-start | bytes 798728 | tf_op jit(solution)/shard_map/ppermute | solution.py:34
  53.7 15.5 %collective-permute-start.14 = (bf16[1040,128]{1,0:T(8,128)(2,1)}, bf16[1040,128]{1,0:T(8,128)(2,1)S(1)}, u32[]{:S(2)}, u32[]{:S(2)}) collective-permute-start(bf16[1040,128]{1,0:T(8,128)(2,1)} %get-tuple-element.13), channel_id=1, source_target_pairs={{2,0},{4,2},{6,4},{8,6},{10,8},{12,10},{14,12},{3,1},{5,3},{7,5},{... | collective-permute-start | bytes 798728 | tf_op jit(solution)/shard_map/ppermute | solution.py:34
  57.6 15.6 %collective-permute-start.15 = (bf16[1040,128]{1,0:T(8,128)(2,1)}, bf16[1040,128]{1,0:T(8,128)(2,1)S(1)}, u32[]{:S(2)}, u32[]{:S(2)}) collective-permute-start(bf16[1040,128]{1,0:T(8,128)(2,1)} %get-tuple-element.14), channel_id=1, source_target_pairs={{0,2},{2,4},{4,6},{6,8},{8,10},{10,12},{12,14},{1,3},{3,5},{5,7},{... | collective-permute-start | bytes 798728 | tf_op jit(solution)/shard_map/ppermute | solution.py:34
  60.5 12.8 %collective-permute-start.16 = (bf16[1040,128]{1,0:T(8,128)(2,1)}, bf16[1040,128]{1,0:T(8,128)(2,1)S(1)}, u32[]{:S(2)}, u32[]{:S(2)}) collective-permute-start(bf16[1040,128]{1,0:T(8,128)(2,1)} %get-tuple-element.15), channel_id=1, source_target_pairs={{0,4},{2,6},{4,8},{6,10},{8,12},{10,14},{1,5},{3,7},{5,9},{7,11},{... | collective-permute-start | bytes 798728 | tf_op jit(solution)/shard_map/ppermute | solution.py:34
  73.3 0.7 copy-start.17
  74.1 1.0 %copy-start.1 = (f32[8,128,128]{2,1,0:T(8,128)S(1)}, f32[8,128,128]{2,1,0:T(8,128)}, u32[]{:S(2)}) copy-start(f32[8,128,128]{2,1,0:T(8,128)} %get-tuple-element.11) | copy-start | bytes 1572868

commit v10 on v9

--- a/solution.py
+++ b/solution.py
@@ -37,39 +37,36 @@
 def aggregate_kernel(
     slot_ref, act_ref, *refs, slabs, per_slab, center, queries, half, blocks, rimmed, halo
 ):
-    sources = [refs[:slabs], refs[2 * slabs : 3 * slabs], refs[slabs : 2 * slabs]]
+    mine_refs, other_refs, value_refs = refs[:slabs], refs[slabs : 2 * slabs], refs[2 * slabs : 3 * slabs]
     own_num_ref, own_mass_ref = refs[3 * slabs : 3 * slabs + 2]
     remote_refs = refs[3 * slabs + 2 : 4 * slabs + 1]
-    key_e, key_v, acc, macc, key_ref, value_ref, sems = refs[4 * slabs + 1 :]
-
-    copies = []
-    for s in range(slabs):
-        dst = pl.ds(s * per_slab, per_slab)
-        targets = (
-            key_e.at[dst, :, pl.ds(0, half)],
-            key_v.at[dst],
-            key_e.at[dst, :, pl.ds(half, half)],
-        )
-        for kind, target in enumerate(targets):
-            copies.append(pltpu.make_async_copy(sources[kind][s], target, sems.at[kind, s]))
-    for c in copies:
-        c.start()
+    acc, macc, query_ref, key_ref, value_ref = refs[4 * slabs + 1 :]
+
     acc[...] = jnp.zeros(acc.shape, acc.dtype)
     macc[...] = jnp.zeros(macc.shape, macc.dtype)
-    for c in copies:
-        c.wait()
 
     score_scale = 1.0 / math.sqrt(W)
     dims_t = (((1,), (1,)), ((), ()))
+    middle = center // per_slab
 
     def one_query(i, carry):
-        q_slot = center + (i // blocks) * rimmed + halo + i % blocks
-        query = key_e[q_slot] * jnp.asarray(score_scale, jnp.bfloat16)
+        q_local = (i // blocks) * rimmed + halo + i % blocks
+        query_ref[:, :half] = mine_refs[middle][q_local]
+        query_ref[:, half:] = other_refs[middle][q_local]
+        query = query_ref[...] * jnp.asarray(score_scale, jnp.bfloat16)
         slots = [slot_ref[i * K + k] for k in range(K)]
         for k in range(K):
-            s = slots[k]
-            key_ref[k * BLOCK : (k + 1) * BLOCK, :] = key_e[s]
-            value_ref[k * BLOCK : (k + 1) * BLOCK, :] = key_v[s]
+            slab = slots[k] // per_slab
+            local = slots[k] % per_slab
+            rows = pl.ds(k * BLOCK, BLOCK)
+            for j in range(slabs):
+
+                @pl.when(slab == j)
+                def _():
+                    key_ref[rows, :half] = mine_refs[j][local]
+                    key_ref[rows, half:] = other_refs[j][local]
+                    value_ref[rows, :] = value_refs[j][local]
+
         score = lax.dot_general(query, key_ref[...], dims_t, preferred_element_type=jnp.float32)
         peak = jnp.max(score, axis=-1, keepdims=True)
         exponent = jnp.exp(score - peak)
@@ -168,13 +165,11 @@
         in_specs=[smem, smem] + [vmem] * (3 * slabs),
         out_specs=[vmem] * len(out_shape),
         scratch_shapes=[
-            pltpu.VMEM((total, BLOCK, 2 * half), jnp.bfloat16),
-            pltpu.VMEM((total, BLOCK, half), jnp.bfloat16),
             pltpu.VMEM((total, half, BLOCK), jnp.float32),
             pltpu.VMEM((total, 1, BLOCK), jnp.float32),
+            pltpu.VMEM((BLOCK, 2 * half), jnp.bfloat16),
             pltpu.VMEM((K * BLOCK, 2 * half), jnp.bfloat16),
             pltpu.VMEM((K * BLOCK, half), jnp.bfloat16),
-            pltpu.SemaphoreType.DMA((3, slabs)),
         ],
     )(slot, active.reshape(-1), *window_e, *others, *window_v)
     own_num, own_mass = outs[0], outs[1]

time: 76.7 us -> 81.6 us (1.064)
  Pallas kernels: 15 us -> 19.8 us
    pallas_call x1, Pallas kernels: 15 us -> 19.8 us  [shards(): pl.pallas_call(kernel, out_shape=out_shape, in_specs=[smem, smem] + [vmem...]
where the time goes in v10:
time: 81.6 us; the launch traced here: 81 us
  starting transfers between devices  35.2 us (43%)
  waiting for transfers between devices  20 us (25%)
  Pallas kernels  19.8 us (24%)
  local copies, waits for them, and re-layouts  5.02 us (6%)
    ppermute x12, starting transfers between devices, passed_along(): return lax.ppermute(block, axis, route)  34.1 us
    ppermute x12, waiting for transfers between devices, passed_along(): return lax.ppermute(block, axis, route)  19.9 us
    pallas_call x1, Pallas kernels, shards(): pl.pallas_call(kernel, out_shape=out_shape, in_specs=[smem, smem] + [vmem...  19.8 us
    unnamed x38, local copies, waits for them, and re-layouts  2.62 us
  transfers between devices with their start and end apart: 17, of which 4 were waited for; matrix products, arithmetic and copies ran while one was open for 2% of the time, Pallas kernels for 0%

profile of v10, /device:TPU:22, one launch (start us, length us, event | category | flops | bytes accessed | tf_op | source)
XLA Modules:
  0.0 81.0 jit_solution(2458285457034767337)
XLA Ops:
  0.0 3.5 %collective-permute-start = (bf16[4,256,128]{2,1,0:T(8,128)(2,1)}, bf16[4,256,128]{2,1,0:T(8,128)(2,1)S(1)}, u32[]{:S(2)}, u32[]{:S(2)}) collective-permute-start(bf16[4,256,128]{2,1,0:T(8,128)(2,1)} %param.5), channel_id=1, source_target_pairs={{0,4},{2,6},{4,8},{6,10},{8,12},{10,14},{1,5},{3,7},{5,9},{7,11},{... | collective-permute-start | bytes 786440 | tf_op jit(solution)/shard_map/ppermute | solution.py:34
  3.5 1.9 %collective-permute-start.1 = (bf16[4,256,128]{2,1,0:T(8,128)(2,1)}, bf16[4,256,128]{2,1,0:T(8,128)(2,1)S(1)}, u32[]{:S(2)}, u32[]{:S(2)}) collective-permute-start(bf16[4,256,128]{2,1,0:T(8,128)(2,1)} %param.5), channel_id=1, source_target_pairs={{0,2},{2,4},{4,6},{6,8},{8,10},{10,12},{12,14},{1,3},{3,5},{5,7},{... | collective-permute-start | bytes 786440 | tf_op jit(solution)/shard_map/ppermute | solution.py:34
  5.4 3.9 %collective-permute-start.2 = (bf16[4,256,128]{2,1,0:T(8,128)(2,1)}, bf16[4,256,128]{2,1,0:T(8,128)(2,1)S(1)}, u32[]{:S(2)}, u32[]{:S(2)}) collective-permute-start(bf16[4,256,128]{2,1,0:T(8,128)(2,1)} %param.5), channel_id=1, source_target_pairs={{2,0},{4,2},{6,4},{8,6},{10,8},{12,10},{14,12},{3,1},{5,3},{7,5},{... | collective-permute-start | bytes 786440 | tf_op jit(solution)/shard_map/ppermute | solution.py:34
  9.3 2.4 %collective-permute-start.3 = (bf16[4,256,128]{2,1,0:T(8,128)(2,1)}, bf16[4,256,128]{2,1,0:T(8,128)(2,1)S(1)}, u32[]{:S(2)}, u32[]{:S(2)}) collective-permute-start(bf16[4,256,128]{2,1,0:T(8,128)(2,1)} %param.5), channel_id=1, source_target_pairs={{4,0},{6,2},{8,4},{10,6},{12,8},{14,10},{5,1},{7,3},{9,5},{11,7},{... | collective-permute-start | bytes 786440 | tf_op jit(solution)/shard_map/ppermute | solution.py:34
  11.7 0.1 collective-permute-start.6
  11.8 0.0 collective-permute-done
  11.8 0.0 copy-start.2
  11.8 3.5 %collective-permute-start.9 = (bf16[4,256,128]{2,1,0:T(8,128)(2,1)}, bf16[4,256,128]{2,1,0:T(8,128)(2,1)S(1)}, u32[]{:S(2)}, u32[]{:S(2)}) collective-permute-start(bf16[4,256,128]{2,1,0:T(8,128)(2,1)} %param.6), channel_id=1, source_target_pairs={{0,4},{2,6},{4,8},{6,10},{8,12},{10,14},{1,5},{3,7},{5,9},{7,11},{... | collective-permute-start | bytes 786440 | tf_op jit(solution)/shard_map/ppermute | solution.py:34
  15.3 3.6 %collective-permute-done.1 = bf16[4,256,128]{2,1,0:T(8,128)(2,1)S(1)} collective-permute-done((bf16[4,256,128]{2,1,0:T(8,128)(2,1)}, bf16[4,256,128]{2,1,0:T(8,128)(2,1)S(1)}, u32[]{:S(2)}, u32[]{:S(2)}) %collective-permute-start.1) | collective-permute-done | bytes 262176 | tf_op jit(solution)/shard_map/ppermute | solution.py:34
  19.0 1.9 %collective-permute-start.10 = (bf16[4,256,128]{2,1,0:T(8,128)(2,1)}, bf16[4,256,128]{2,1,0:T(8,128)(2,1)S(1)}, u32[]{:S(2)}, u32[]{:S(2)}) collective-permute-start(bf16[4,256,128]{2,1,0:T(8,128)(2,1)} %param.6), channel_id=1, source_target_pairs={{0,2},{2,4},{4,6},{6,8},{8,10},{10,12},{12,14},{1,3},{3,5},{5,7},{... | collective-permute-start | bytes 786440 | tf_op jit(solution)/shard_map/ppermute | solution.py:34
  20.9 0.0 collective-permute-done.2
  20.9 3.9 %collective-permute-start.11 = (bf16[4,256,128]{2,1,0:T(8,128)(2,1)}, bf16[4,256,128]{2,1,0:T(8,128)(2,1)S(1)}, u32[]{:S(2)}, u32[]{:S(2)}) collective-permute-start(bf16[4,256,128]{2,1,0:T(8,128)(2,1)} %param.6), channel_id=1, source_target_pairs={{2,0},{4,2},{6,4},{8,6},{10,8},{12,10},{14,12},{3,1},{5,3},{7,5},{... | collective-permute-start | bytes 786440 | tf_op jit(solution)/shard_map/ppermute | solution.py:34
  24.9 0.0 copy-start.15
  24.9 2.1 %collective-permute-start.12 = (bf16[4,256,128]{2,1,0:T(8,128)(2,1)}, bf16[4,256,128]{2,1,0:T(8,128)(2,1)S(1)}, u32[]{:S(2)}, u32[]{:S(2)}) collective-permute-start(bf16[4,256,128]{2,1,0:T(8,128)(2,1)} %param.6), channel_id=1, source_target_pairs={{4,0},{6,2},{8,4},{10,6},{12,8},{14,10},{5,1},{7,3},{9,5},{11,7},{... | collective-permute-start | bytes 786440 | tf_op jit(solution)/shard_map/ppermute | solution.py:34
  27.0 0.0 collective-permute-done.6.refs_7_
  27.1 0.1 collective-permute-start.4
  27.1 0.0 collective-permute-done.9
  27.2 0.5 collective-permute-start.5
  27.6 5.8 %collective-permute-done.10 = bf16[4,256,128]{2,1,0:T(8,128)(2,1)S(1)} collective-permute-done((bf16[4,256,128]{2,1,0:T(8,128)(2,1)}, bf16[4,256,128]{2,1,0:T(8,128)(2,1)S(1)}, u32[]{:S(2)}, u32[]{:S(2)}) %collective-permute-start.10) | collective-permute-done | bytes 262176 | tf_op jit(solution)/shard_map/ppermute | solution.py:34
  33.4 0.0 collective-permute-start.7
  33.4 0.0 collective-permute-done.11
  33.4 0.5 collective-permute-start.8
  33.9 0.1 add_clamp_fusion
  34.0 0.6 reshape.75.slot_ref
  34.6 0.1 copy-done.18
  34.6 0.1 fusion.5
  34.7 0.7 reshape.91.act_ref
  35.4 0.0 collective-permute-done.4.refs_5_
  35.4 0.0 collective-permute-done.5.refs_6_
  35.4 0.0 collective-permute-done.8.refs_9_
  35.5 0.8 copy-done.14
  36.3 0.0 copy-done.12
  36.3 0.1 copy-done.13
  36.4 19.8 %shard_map.55 = (f32[8,128,128]{2,1,0:T(8,128)}, f32[8,1,128]{2,1,0:T(1,128)}, bf16[1040,128]{1,0:T(8,128)(2,1)}, bf16[1040,128]{1,0:T(8,128)(2,1)}, bf16[1040,1...) custom-call(s32[128]{0:T(128)} %reshape.75.slot_ref, s32[8]{0:T(128)} %reshape.91.act_ref, bf16[8,128,128]{2,1,0:T(8,128)(2,1)} %bitcast.56, ...), custom_call_target="tpu_custom_call" | custom-call | tf_op jit(solution)/shard_map/pallas_call | solution.py:162
  56.3 2.3 %collective-permute-start.13 = (bf16[1040,128]{1,0:T(8,128)(2,1)}, bf16[1040,128]{1,0:T(8,128)(2,1)S(1)}, u32[]{:S(2)}, u32[]{:S(2)}) collective-permute-start(bf16[1040,128]{1,0:T(8,128)(2,1)} %get-tuple-element.12), channel_id=1, source_target_pairs={{4,0},{6,2},{8,4},{10,6},{12,8},{14,10},{5,1},{7,3},{9,5},{11,7},{... | collective-permute-start | bytes 798728 | tf_op jit(solution)/shard_map/ppermute | solution.py:34
  58.6 3.9 %collective-permute-start.14 = (bf16[1040,128]{1,0:T(8,128)(2,1)}, bf16[1040,128]{1,0:T(8,128)(2,1)S(1)}, u32[]{:S(2)}, u32[]{:S(2)}) collective-permute-start(bf16[1040,128]{1,0:T(8,128)(2,1)} %get-tuple-element.13), channel_id=1, source_target_pairs={{2,0},{4,2},{6,4},{8,6},{10,8},{12,10},{14,12},{3,1},{5,3},{7,5},{... | collective-permute-start | bytes 798728 | tf_op jit(solution)/shard_map/ppermute | solution.py:34
  62.4 2.9 %collective-permute-start.15 = (bf16[1040,128]{1,0:T(8,128)(2,1)}, bf16[1040,128]{1,0:T(8,128)(2,1)S(1)}, u32[]{:S(2)}, u32[]{:S(2)}) collective-permute-start(bf16[1040,128]{1,0:T(8,128)(2,1)} %get-tuple-element.14), channel_id=1, source_target_pairs={{0,2},{2,4},{4,6},{6,8},{8,10},{10,12},{12,14},{1,3},{3,5},{5,7},{... | collective-permute-start | bytes 798728 | tf_op jit(solution)/shard_map/ppermute | solution.py:34
  65.3 1.9 %collective-permute-start.16 = (bf16[1040,128]{1,0:T(8,128)(2,1)}, bf16[1040,128]{1,0:T(8,128)(2,1)S(1)}, u32[]{:S(2)}, u32[]{:S(2)}) collective-permute-start(bf16[1040,128]{1,0:T(8,128)(2,1)} %get-tuple-element.15), channel_id=1, source_target_pairs={{0,4},{2,6},{4,8},{6,10},{8,12},{10,14},{1,5},{3,7},{5,9},{7,11},{... | collective-permute-start | bytes 798728 | tf_op jit(solution)/shard_map/ppermute | solution.py:34
  67.3 0.1 copy.9
  67.4 0.0 collective-permute-done.13
  67.5 6.5 %collective-permute-done.14 = bf16[1040,128]{1,0:T(8,128)(2,1)S(1)} collective-permute-done((bf16[1040,128]{1,0:T(8,128)(2,1)}, bf16[1040,128]{1,0:T(8,128)(2,1)S(1)}, u32[]{:S(2)}, u32[]{:S(2)}) %collective-permute-start.14) | collective-permute-done | bytes 266272 | tf_op jit(solution)/shard_map/ppermute | solution.py:34
  74.0 4.0 %collective-permute-done.15 = bf16[1040,128]{1,0:T(8,128)(2,1)S(1)} collective-permute-done((bf16[1040,128]{1,0:T(8,128)(2,1)}, bf16[1040,128]{1,0:T(8,128)(2,1)S(1)}, u32[]{:S(2)}, u32[]{:S(2)}) %collective-permute-start.15) | collective-permute-done | bytes 266272 | tf_op jit(solution)/shard_map/ppermute | solution.py:34
  78.1 0.0 collective-permute-done.16
  78.1 0.6 copy-done.17
  78.9 1.0 %copy-done.1 = f32[8,128,128]{2,1,0:T(8,128)S(1)} copy-done((f32[8,128,128]{2,1,0:T(8,128)S(1)}, f32[8,128,128]{2,1,0:T(8,128)}, u32[]{:S(2)}) %copy-start.1) | copy-done | bytes 524312
  79.9 0.2 add_add_fusion
  80.1 0.1 divide_convert_fusion
  80.2 0.9 %copy.11 = bf16[4,2,128,128]{3,2,1,0:T(8,128)(2,1)} copy(bf16[4,2,128,128]{2,3,1,0:T(8,128)(2,1)S(1)} %divide_convert_fusion) | data formatting | bytes 524288 | tf_op jit(solution)/shard_map/convert_element_type | solution.py:203
  (43 shorter events, 0.4 us)
Async XLA Ops:
  0.0 11.8 %collective-permute-start = (bf16[4,256,128]{2,1,0:T(8,128)(2,1)}, bf16[4,256,128]{2,1,0:T(8,128)(2,1)S(1)}, u32[]{:S(2)}, u32[]{:S(2)}) collective-permute-start(bf16[4,256,128]{2,1,0:T(8,128)(2,1)} %param.5), channel_id=1, source_target_pairs={{0,4},{2,6},{4,8},{6,10},{8,12},{10,14},{1,5},{3,7},{5,9},{7,11},{... | collective-permute-start | bytes 786440 | tf_op jit(solution)/shard_map/ppermute | solution.py:34
  3.5 15.5 %collective-permute-start.1 = (bf16[4,256,128]{2,1,0:T(8,128)(2,1)}, bf16[4,256,128]{2,1,0:T(8,128)(2,1)S(1)}, u32[]{:S(2)}, u32[]{:S(2)}) collective-permute-start(bf16[4,256,128]{2,1,0:T(8,128)(2,1)} %param.5), channel_id=1, source_target_pairs={{0,2},{2,4},{4,6},{6,8},{8,10},{10,12},{12,14},{1,3},{3,5},{5,7},{... | collective-permute-start | bytes 786440 | tf_op jit(solution)/shard_map/ppermute | solution.py:34
  5.4 15.5 %collective-permute-start.2 = (bf16[4,256,128]{2,1,0:T(8,128)(2,1)}, bf16[4,256,128]{2,1,0:T(8,128)(2,1)S(1)}, u32[]{:S(2)}, u32[]{:S(2)}) collective-permute-start(bf16[4,256,128]{2,1,0:T(8,128)(2,1)} %param.5), channel_id=1, source_target_pairs={{2,0},{4,2},{6,4},{8,6},{10,8},{12,10},{14,12},{3,1},{5,3},{7,5},{... | collective-permute-start | bytes 786440 | tf_op jit(solution)/shard_map/ppermute | solution.py:34
  9.3 15.5 %collective-permute-start.3 = (bf16[4,256,128]{2,1,0:T(8,128)(2,1)}, bf16[4,256,128]{2,1,0:T(8,128)(2,1)S(1)}, u32[]{:S(2)}, u32[]{:S(2)}) collective-permute-start(bf16[4,256,128]{2,1,0:T(8,128)(2,1)} %param.5), channel_id=1, source_target_pairs={{4,0},{6,2},{8,4},{10,6},{12,8},{14,10},{5,1},{7,3},{9,5},{11,7},{... | collective-permute-start | bytes 786440 | tf_op jit(solution)/shard_map/ppermute | solution.py:34
  11.7 15.3 %collective-permute-start.6 = (bf16[8,128,128]{2,1,0:T(8,128)(2,1)}, bf16[8,128,128]{2,1,0:T(8,128)(2,1)S(1)}, u32[]{:S(2)}, u32[]{:S(2)}) collective-permute-start(bf16[8,128,128]{2,1,0:T(8,128)(2,1)} %bitcast.53), channel_id=1, source_target_pairs={{0,1},{1,0},{2,3},{3,2},{4,5},{5,4},{6,7},{7,6},{8,9},{9,8},{10,11... | collective-permute-start | bytes 786440 | tf_op jit(solution)/shard_map/ppermute | solution.py:127
  11.8 24.4 %copy-start.2 = (bf16[4,256,128]{2,1,0:T(8,128)(2,1)}, bf16[4,256,128]{2,1,0:T(8,128)(2,1)S(1)}, u32[]{:S(2)}) copy-start(bf16[4,256,128]{2,1,0:T(8,128)(2,1)S(1)} %collective-permute-done) | copy-start | bytes 786436
  11.8 15.3 %collective-permute-start.9 = (bf16[4,256,128]{2,1,0:T(8,128)(2,1)}, bf16[4,256,128]{2,1,0:T(8,128)(2,1)S(1)}, u32[]{:S(2)}, u32[]{:S(2)}) collective-permute-start(bf16[4,256,128]{2,1,0:T(8,128)(2,1)} %param.6), channel_id=1, source_target_pairs={{0,4},{2,6},{4,8},{6,10},{8,12},{10,14},{1,5},{3,7},{5,9},{7,11},{... | collective-permute-start | bytes 786440 | tf_op jit(solution)/shard_map/ppermute | solution.py:34
  19.0 17.3 %copy-start.3 = (bf16[4,256,128]{2,1,0:T(8,128)(2,1)}, bf16[4,256,128]{2,1,0:T(8,128)(2,1)S(1)}, u32[]{:S(2)}) copy-start(bf16[4,256,128]{2,1,0:T(8,128)(2,1)S(1)} %collective-permute-done.1) | copy-start | bytes 786436
  19.0 14.4 %collective-permute-start.10 = (bf16[4,256,128]{2,1,0:T(8,128)(2,1)}, bf16[4,256,128]{2,1,0:T(8,128)(2,1)S(1)}, u32[]{:S(2)}, u32[]{:S(2)}) collective-permute-start(bf16[4,256,128]{2,1,0:T(8,128)(2,1)} %param.6), channel_id=1, source_target_pairs={{0,2},{2,4},{4,6},{6,8},{8,10},{10,12},{12,14},{1,3},{3,5},{5,7},{... | collective-permute-start | bytes 786440 | tf_op jit(solution)/shard_map/ppermute | solution.py:34
  20.9 15.3 %copy-start.4 = (bf16[4,256,128]{2,1,0:T(8,128)(2,1)}, bf16[4,256,128]{2,1,0:T(8,128)(2,1)S(1)}, u32[]{:S(2)}) copy-start(bf16[4,256,128]{2,1,0:T(8,128)(2,1)S(1)} %collective-permute-done.2) | copy-start | bytes 786436
  20.9 12.5 %collective-permute-start.11 = (bf16[4,256,128]{2,1,0:T(8,128)(2,1)}, bf16[4,256,128]{2,1,0:T(8,128)(2,1)S(1)}, u32[]{:S(2)}, u32[]{:S(2)}) collective-permute-start(bf16[4,256,128]{2,1,0:T(8,128)(2,1)} %param.6), channel_id=1, source_target_pairs={{2,0},{4,2},{6,4},{8,6},{10,8},{12,10},{14,12},{3,1},{5,3},{7,5},{... | collective-permute-start | bytes 786440 | tf_op jit(solution)/shard_map/ppermute | solution.py:34
  24.8 9.1 %copy-start.16 = (s32[4,2,16]{2,1,0:T(2,128)S(1)}, s32[4,2,16]{2,1,0:T(2,128)}, u32[]{:S(2)}) copy-start(s32[4,2,16]{2,1,0:T(2,128)} %param.7) | copy-start | bytes 1540
  24.9 9.0 %copy-start.15 = (s32[4,2,16]{2,1,0:T(2,128)S(1)}, s32[4,2,16]{2,1,0:T(2,128)}, u32[]{:S(2)}) copy-start(s32[4,2,16]{2,1,0:T(2,128)} %param.8) | copy-start | bytes 1540
  24.9 11.3 %copy-start.5 = (bf16[4,256,128]{2,1,0:T(8,128)(2,1)}, bf16[4,256,128]{2,1,0:T(8,128)(2,1)S(1)}, u32[]{:S(2)}) copy-start(bf16[4,256,128]{2,1,0:T(8,128)(2,1)S(1)} %collective-permute-done.3) | copy-start | bytes 786436
  24.9 10.5 %collective-permute-start.12 = (bf16[4,256,128]{2,1,0:T(8,128)(2,1)}, bf16[4,256,128]{2,1,0:T(8,128)(2,1)S(1)}, u32[]{:S(2)}, u32[]{:S(2)}) collective-permute-start(bf16[4,256,128]{2,1,0:T(8,128)(2,1)} %param.6), channel_id=1, source_target_pairs={{4,0},{6,2},{8,4},{10,6},{12,8},{14,10},{5,1},{7,3},{9,5},{11,7},{... | collective-permute-start | bytes 786440 | tf_op jit(solution)/shard_map/ppermute | solution.py:34
  27.0 9.2 %copy-start.6 = (bf16[8,128,128]{2,1,0:T(8,128)(2,1)}, bf16[8,128,128]{2,1,0:T(8,128)(2,1)S(1)}, u32[]{:S(2)}) copy-start(bf16[8,128,128]{2,1,0:T(8,128)(2,1)S(1)} %collective-permute-done.6.refs_7_) | copy-start | bytes 786436
  27.1 8.3 %collective-permute-start.4 = (bf16[8,128,128]{2,1,0:T(8,128)(2,1)S(1)}, bf16[8,128,128]{2,1,0:T(8,128)(2,1)S(1)}, u32[]{:S(2)}, u32[]{:S(2)}) collective-permute-start(bf16[8,128,128]{2,1,0:T(8,128)(2,1)S(1)} %bitcast.55), channel_id=1, source_target_pairs={{0,1},{1,0},{2,3},{3,2},{4,5},{5,4},{6,7},{7,6},{8,9},{9,8},{10,11... | collective-permute-start | bytes 786440 | tf_op jit(solution)/shard_map/ppermute | solution.py:127
  27.1 9.1 %copy-start.7 = (bf16[4,256,128]{2,1,0:T(8,128)(2,1)}, bf16[4,256,128]{2,1,0:T(8,128)(2,1)S(1)}, u32[]{:S(2)}) copy-start(bf16[4,256,128]{2,1,0:T(8,128)(2,1)S(1)} %collective-permute-done.9) | copy-start | bytes 786436
  27.2 8.2 %collective-permute-start.5 = (bf16[8,128,128]{2,1,0:T(8,128)(2,1)S(1)}, bf16[8,128,128]{2,1,0:T(8,128)(2,1)S(1)}, u32[]{:S(2)}, u32[]{:S(2)}) collective-permute-start(bf16[8,128,128]{2,1,0:T(8,128)(2,1)S(1)} %bitcast.57), channel_id=1, source_target_pairs={{0,1},{1,0},{2,3},{3,2},{4,5},{5,4},{6,7},{7,6},{8,9},{9,8},{10,11... | collective-permute-start | bytes 786440 | tf_op jit(solution)/shard_map/ppermute | solution.py:127
  33.4 2.9 %copy-start.8 = (bf16[4,256,128]{2,1,0:T(8,128)(2,1)}, bf16[4,256,128]{2,1,0:T(8,128)(2,1)S(1)}, u32[]{:S(2)}) copy-start(bf16[4,256,128]{2,1,0:T(8,128)(2,1)S(1)} %collective-permute-done.10) | copy-start | bytes 786436
  33.4 2.0 %collective-permute-start.7 = (bf16[8,128,128]{2,1,0:T(8,128)(2,1)S(1)}, bf16[8,128,128]{2,1,0:T(8,128)(2,1)S(1)}, u32[]{:S(2)}, u32[]{:S(2)}) collective-permute-start(bf16[8,128,128]{2,1,0:T(8,128)(2,1)S(1)} %bitcast.59), channel_id=1, source_target_pairs={{0,1},{1,0},{2,3},{3,2},{4,5},{5,4},{6,7},{7,6},{8,9},{9,8},{10,11... | collective-permute-start | bytes 786440 | tf_op jit(solution)/shard_map/ppermute | solution.py:127
  33.4 2.9 %copy-start.9 = (bf16[4,256,128]{2,1,0:T(8,128)(2,1)}, bf16[4,256,128]{2,1,0:T(8,128)(2,1)S(1)}, u32[]{:S(2)}) copy-start(bf16[4,256,128]{2,1,0:T(8,128)(2,1)S(1)} %collective-permute-done.11) | copy-start | bytes 786436
  33.4 2.0 %collective-permute-start.8 = (bf16[8,128,128]{2,1,0:T(8,128)(2,1)S(1)}, bf16[8,128,128]{2,1,0:T(8,128)(2,1)S(1)}, u32[]{:S(2)}, u32[]{:S(2)}) collective-permute-start(bf16[8,128,128]{2,1,0:T(8,128)(2,1)S(1)} %bitcast.61), channel_id=1, source_target_pairs={{0,1},{1,0},{2,3},{3,2},{4,5},{5,4},{6,7},{7,6},{8,9},{9,8},{10,11... | collective-permute-start | bytes 786440 | tf_op jit(solution)/shard_map/ppermute | solution.py:127
  34.0 0.7 copy-start.18
  35.4 0.9 %copy-start.10 = (bf16[4,256,128]{2,1,0:T(8,128)(2,1)}, bf16[4,256,128]{2,1,0:T(8,128)(2,1)S(1)}, u32[]{:S(2)}) copy-start(bf16[4,256,128]{2,1,0:T(8,128)(2,1)S(1)} %collective-permute-done.12) | copy-start | bytes 786436
  35.4 0.9 %copy-start.11 = (bf16[8,128,128]{2,1,0:T(8,128)(2,1)}, bf16[8,128,128]{2,1,0:T(8,128)(2,1)S(1)}, u32[]{:S(2)}) copy-start(bf16[8,128,128]{2,1,0:T(8,128)(2,1)S(1)} %collective-permute-done.4.refs_5_) | copy-start | bytes 786436
  35.4 0.9 %copy-start.12 = (bf16[8,128,128]{2,1,0:T(8,128)(2,1)}, bf16[8,128,128]{2,1,0:T(8,128)(2,1)S(1)}, u32[]{:S(2)}) copy-start(bf16[8,128,128]{2,1,0:T(8,128)(2,1)S(1)} %collective-permute-done.5.refs_6_) | copy-start | bytes 786436
  35.4 1.0 %copy-start.13 = (bf16[8,128,128]{2,1,0:T(8,128)(2,1)}, bf16[8,128,128]{2,1,0:T(8,128)(2,1)S(1)}, u32[]{:S(2)}) copy-start(bf16[8,128,128]{2,1,0:T(8,128)(2,1)S(1)} %collective-permute-done.7.refs_8_) | copy-start | bytes 786436
  35.5 0.8 copy-start.14
  36.4 30.8 %copy-start = (bf16[4,256,128]{2,1,0:T(8,128)(2,1)S(1)}, bf16[4,256,128]{2,1,0:T(8,128)(2,1)}, u32[]{:S(2)}) copy-start(bf16[4,256,128]{2,1,0:T(8,128)(2,1)} %param.6) | copy-start | bytes 786436
  56.3 11.1 %collective-permute-start.13 = (bf16[1040,128]{1,0:T(8,128)(2,1)}, bf16[1040,128]{1,0:T(8,128)(2,1)S(1)}, u32[]{:S(2)}, u32[]{:S(2)}) collective-permute-start(bf16[1040,128]{1,0:T(8,128)(2,1)} %get-tuple-element.12), channel_id=1, source_target_pairs={{4,0},{6,2},{8,4},{10,6},{12,8},{14,10},{5,1},{7,3},{9,5},{11,7},{... | collective-permute-start | bytes 798728 | tf_op jit(solution)/shard_map/ppermute | solution.py:34
  58.6 15.4 %collective-permute-start.14 = (bf16[1040,128]{1,0:T(8,128)(2,1)}, bf16[1040,128]{1,0:T(8,128)(2,1)S(1)}, u32[]{:S(2)}, u32[]{:S(2)}) collective-permute-start(bf16[1040,128]{1,0:T(8,128)(2,1)} %get-tuple-element.13), channel_id=1, source_target_pairs={{2,0},{4,2},{6,4},{8,6},{10,8},{12,10},{14,12},{3,1},{5,3},{7,5},{... | collective-permute-start | bytes 798728 | tf_op jit(solution)/shard_map/ppermute | solution.py:34
  62.4 15.6 %collective-permute-start.15 = (bf16[1040,128]{1,0:T(8,128)(2,1)}, bf16[1040,128]{1,0:T(8,128)(2,1)S(1)}, u32[]{:S(2)}, u32[]{:S(2)}) collective-permute-start(bf16[1040,128]{1,0:T(8,128)(2,1)} %get-tuple-element.14), channel_id=1, source_target_pairs={{0,2},{2,4},{4,6},{6,8},{8,10},{10,12},{12,14},{1,3},{3,5},{5,7},{... | collective-permute-start | bytes 798728 | tf_op jit(solution)/shard_map/ppermute | solution.py:34
  65.3 12.7 %collective-permute-start.16 = (bf16[1040,128]{1,0:T(8,128)(2,1)}, bf16[1040,128]{1,0:T(8,128)(2,1)S(1)}, u32[]{:S(2)}, u32[]{:S(2)}) collective-permute-start(bf16[1040,128]{1,0:T(8,128)(2,1)} %get-tuple-element.15), channel_id=1, source_target_pairs={{0,4},{2,6},{4,8},{6,10},{8,12},{10,14},{1,5},{3,7},{5,9},{7,11},{... | collective-permute-start | bytes 798728 | tf_op jit(solution)/shard_map/ppermute | solution.py:34
  78.1 0.7 copy-start.17
  78.9 1.0 %copy-start.1 = (f32[8,128,128]{2,1,0:T(8,128)S(1)}, f32[8,128,128]{2,1,0:T(8,128)}, u32[]{:S(2)}) copy-start(f32[8,128,128]{2,1,0:T(8,128)} %get-tuple-element.11) | copy-start | bytes 1572868

commit v11 on v8

--- a/solution.py
+++ b/solution.py
@@ -102,6 +102,22 @@
         if mass_rows > per_slab:
             spread.append(jnp.zeros((mass_rows - per_slab, BLOCK), jnp.float32))
         ref[per_slab * half :, :] = jnp.concatenate(spread, axis=0).astype(jnp.bfloat16)
+
+
+def combine_kernel(num_ref, mass_ref, values_ref, *refs, per_slab, half):
+    arrived_refs = refs[:-1]
+    out_ref = refs[-1]
+    tail = per_slab * half
+    masses = [ref[tail:, :].astype(jnp.float32) for ref in arrived_refs]
+    for j in range(per_slab):
+        numer = num_ref[j]
+        mass = mass_ref[j]
+        for ref, rows in zip(arrived_refs, masses):
+            numer = numer + ref[j * half : (j + 1) * half, :].astype(jnp.float32)
+            mass = mass + rows[j : j + 1]
+        own = values_ref[j].astype(jnp.float32).T
+        result = (numer + own) / (mass + 1.0)
+        out_ref[j] = result.T.astype(jnp.bfloat16)
 
 
 def shards(embed, values, match_frame, match_block, block_counts):
@@ -181,6 +197,15 @@
     own_num, own_mass = outs[0], outs[1]
     remote = outs[2:]
     offsets = [o for o in range(-hops, hops + 1) if o != 0]
+    if not halo:
+        arrivals = [passed_along(outgoing, "frame", offset) for offset, outgoing in zip(offsets, remote)]
+        result = pl.pallas_call(
+            functools.partial(combine_kernel, per_slab=per_slab, half=half),
+            out_shape=jax.ShapeDtypeStruct((per_slab, BLOCK, half), jnp.bfloat16),
+            in_specs=[vmem] * (3 + len(arrivals)),
+            out_specs=vmem,
+        )(own_num, own_mass, values.reshape(per_slab, BLOCK, half), *arrivals)
+        return result.reshape(frames, band_rows, half)
     for offset, outgoing in zip(offsets, remote):
         arrived = passed_along(outgoing, "frame", offset).astype(jnp.float32)
         own_num = own_num + arrived[: per_slab * half].reshape(per_slab, half, BLOCK)

time: 76.5 us -> 73.3 us (0.958)
  waiting for transfers between devices: 19.9 us -> 16.7 us
  Pallas kernels: 14.8 us -> 17.2 us
  local copies, waits for them, and re-layouts: 5.02 us -> 3.01 us
    ppermute x12, waiting for transfers between devices: 19.9 us -> 16.7 us  [passed_along(): return lax.ppermute(block, axis, route)]
    pallas_call x0 -> x1, Pallas kernels: none -> 2.45 us  [shards(): pl.pallas_call(functools.partial(combine_kernel, per_slab=per_slab, half=...]
    convert_element_type x2 -> x0, local copies, waits for them, and re-layouts: 0.99 us -> none  [the longest x1 0.85 us: shards(): return result.reshape(frames, band_rows, half).astype(jnp.bfloat16)]
    unnamed x38 -> x40, local copies, waits for them, and re-layouts: 2.62 us -> 1.69 us
    ppermute x12, starting transfers between devices: 34.1 us -> 34.9 us  [passed_along(): return lax.ppermute(block, axis, route)]
  transfers between devices with their start and end apart: 17 -> 17, of which waited for: 4 -> 6; matrix products, arithmetic and copies ran while one was open for 2% -> 2% of each run, Pallas kernels for 0% -> 0%
where the time goes in v11:
time: 73.3 us; the launch traced here: 72.9 us
  starting transfers between devices  35.5 us (48%)
  Pallas kernels  17.2 us (23%)
  waiting for transfers between devices  16.7 us (23%)
  local copies, waits for them, and re-layouts  3.01 us (4%)
    ppermute x12, starting transfers between devices, passed_along(): return lax.ppermute(block, axis, route)  34.9 us
    ppermute x12, waiting for transfers between devices, passed_along(): return lax.ppermute(block, axis, route)  16.7 us
    pallas_call x1, Pallas kernels, shards(): pl.pallas_call(kernel, out_shape=out_shape, in_specs=[smem, smem] + [vmem...  14.7 us
    pallas_call x1, Pallas kernels, shards(): pl.pallas_call(functools.partial(combine_kernel, per_slab=per_slab, half=...  2.45 us
    unnamed x40, local copies, waits for them, and re-layouts  1.69 us
  transfers between devices with their start and end apart: 17, of which 6 were waited for; matrix products, arithmetic and copies ran while one was open for 2% of the time, Pallas kernels for 0%

profile of v11, /device:TPU:22, one launch (start us, length us, event | category | flops | bytes accessed | tf_op | source)
XLA Modules:
  0.0 72.9 jit_solution(4818345759687061276)
XLA Ops:
  0.0 0.0 collective-permute-start.6
  0.0 3.6 %collective-permute-start.1 = (bf16[4,256,128]{2,1,0:T(8,128)(2,1)}, bf16[4,256,128]{2,1,0:T(8,128)(2,1)S(1)}, u32[]{:S(2)}, u32[]{:S(2)}) collective-permute-start(bf16[4,256,128]{2,1,0:T(8,128)(2,1)} %param.5), channel_id=1, source_target_pairs={{0,2},{2,4},{4,6},{6,8},{8,10},{10,12},{12,14},{1,3},{3,5},{5,7},{... | collective-permute-start | bytes 786440 | tf_op jit(solution)/shard_map/ppermute | solution.py:34
  3.6 1.9 %collective-permute-start = (bf16[4,256,128]{2,1,0:T(8,128)(2,1)}, bf16[4,256,128]{2,1,0:T(8,128)(2,1)S(1)}, u32[]{:S(2)}, u32[]{:S(2)}) collective-permute-start(bf16[4,256,128]{2,1,0:T(8,128)(2,1)} %param.5), channel_id=1, source_target_pairs={{0,4},{2,6},{4,8},{6,10},{8,12},{10,14},{1,5},{3,7},{5,9},{7,11},{... | collective-permute-start | bytes 786440 | tf_op jit(solution)/shard_map/ppermute | solution.py:34
  5.5 3.9 %collective-permute-start.3 = (bf16[4,256,128]{2,1,0:T(8,128)(2,1)}, bf16[4,256,128]{2,1,0:T(8,128)(2,1)S(1)}, u32[]{:S(2)}, u32[]{:S(2)}) collective-permute-start(bf16[4,256,128]{2,1,0:T(8,128)(2,1)} %param.5), channel_id=1, source_target_pairs={{4,0},{6,2},{8,4},{10,6},{12,8},{14,10},{5,1},{7,3},{9,5},{11,7},{... | collective-permute-start | bytes 786440 | tf_op jit(solution)/shard_map/ppermute | solution.py:34
  9.5 2.4 %collective-permute-start.2 = (bf16[4,256,128]{2,1,0:T(8,128)(2,1)}, bf16[4,256,128]{2,1,0:T(8,128)(2,1)S(1)}, u32[]{:S(2)}, u32[]{:S(2)}) collective-permute-start(bf16[4,256,128]{2,1,0:T(8,128)(2,1)} %param.5), channel_id=1, source_target_pairs={{2,0},{4,2},{6,4},{8,6},{10,8},{12,10},{14,12},{3,1},{5,3},{7,5},{... | collective-permute-start | bytes 786440 | tf_op jit(solution)/shard_map/ppermute | solution.py:34
  11.9 0.0 collective-permute-done.6.refs_7_
  11.9 4.4 %collective-permute-start.10 = (bf16[4,256,128]{2,1,0:T(8,128)(2,1)}, bf16[4,256,128]{2,1,0:T(8,128)(2,1)S(1)}, u32[]{:S(2)}, u32[]{:S(2)}) collective-permute-start(bf16[4,256,128]{2,1,0:T(8,128)(2,1)} %param.6), channel_id=1, source_target_pairs={{0,2},{2,4},{4,6},{6,8},{8,10},{10,12},{12,14},{1,3},{3,5},{5,7},{... | collective-permute-start | bytes 786440 | tf_op jit(solution)/shard_map/ppermute | solution.py:34
  16.3 0.0 collective-permute-done.1
  16.3 1.9 %collective-permute-start.9 = (bf16[4,256,128]{2,1,0:T(8,128)(2,1)}, bf16[4,256,128]{2,1,0:T(8,128)(2,1)S(1)}, u32[]{:S(2)}, u32[]{:S(2)}) collective-permute-start(bf16[4,256,128]{2,1,0:T(8,128)(2,1)} %param.6), channel_id=1, source_target_pairs={{0,4},{2,6},{4,8},{6,10},{8,12},{10,14},{1,5},{3,7},{5,9},{7,11},{... | collective-permute-start | bytes 786440 | tf_op jit(solution)/shard_map/ppermute | solution.py:34
  18.2 0.0 collective-permute-done
  18.2 0.0 copy-start.6
  18.2 3.9 %collective-permute-start.12 = (bf16[4,256,128]{2,1,0:T(8,128)(2,1)}, bf16[4,256,128]{2,1,0:T(8,128)(2,1)S(1)}, u32[]{:S(2)}, u32[]{:S(2)}) collective-permute-start(bf16[4,256,128]{2,1,0:T(8,128)(2,1)} %param.6), channel_id=1, source_target_pairs={{4,0},{6,2},{8,4},{10,6},{12,8},{14,10},{5,1},{7,3},{9,5},{11,7},{... | collective-permute-start | bytes 786440 | tf_op jit(solution)/shard_map/ppermute | solution.py:34
  22.2 0.1 fusion
  22.2 0.0 collective-permute-done.3
  22.3 1.9 %collective-permute-start.11 = (bf16[4,256,128]{2,1,0:T(8,128)(2,1)}, bf16[4,256,128]{2,1,0:T(8,128)(2,1)S(1)}, u32[]{:S(2)}, u32[]{:S(2)}) collective-permute-start(bf16[4,256,128]{2,1,0:T(8,128)(2,1)} %param.6), channel_id=1, source_target_pairs={{2,0},{4,2},{6,4},{8,6},{10,8},{12,10},{14,12},{3,1},{5,3},{7,5},{... | collective-permute-start | bytes 786440 | tf_op jit(solution)/shard_map/ppermute | solution.py:34
  24.2 0.0 collective-permute-done.2
  24.2 0.1 collective-permute-start.5
  24.3 3.2 %collective-permute-done.10 = bf16[4,256,128]{2,1,0:T(8,128)(2,1)S(1)} collective-permute-done((bf16[4,256,128]{2,1,0:T(8,128)(2,1)}, bf16[4,256,128]{2,1,0:T(8,128)(2,1)S(1)}, u32[]{:S(2)}, u32[]{:S(2)}) %collective-permute-start.10) | collective-permute-done | bytes 262176 | tf_op jit(solution)/shard_map/ppermute | solution.py:34
  27.5 0.0 collective-permute-start.4
  27.5 0.5 collective-permute-done.9
  28.0 0.0 collective-permute-start.8
  28.0 0.0 collective-permute-done.12
  28.0 0.5 collective-permute-start.7
  28.5 0.7 reshape.62.act_ref
  29.2 0.1 add_clamp_fusion
  29.3 0.7 reshape.50.slot_ref
  29.9 4.1 %collective-permute-done.11 = bf16[4,256,128]{2,1,0:T(8,128)(2,1)S(1)} collective-permute-done((bf16[4,256,128]{2,1,0:T(8,128)(2,1)}, bf16[4,256,128]{2,1,0:T(8,128)(2,1)S(1)}, u32[]{:S(2)}, u32[]{:S(2)}) %collective-permute-start.11) | collective-permute-done | bytes 262176 | tf_op jit(solution)/shard_map/ppermute | solution.py:34
  34.0 0.0 collective-permute-done.5.refs_6_
  34.0 0.0 collective-permute-done.4.refs_5_
  34.1 0.0 collective-permute-done.8.refs_9_
  34.1 0.0 collective-permute-done.7.refs_8_
  34.1 0.0 copy-start.16
  34.2 0.6 copy-done.12
  34.7 0.1 copy-done.13
  34.8 0.1 copy-done.14
  34.9 0.1 copy-done.15
  35.0 0.1 copy-done.16
  35.1 14.7 %shard_map.55 = (f32[8,128,128]{2,1,0:T(8,128)}, f32[8,1,128]{2,1,0:T(1,128)}, bf16[1040,128]{1,0:T(8,128)(2,1)}, bf16[1040,128]{1,0:T(8,128)(2,1)}, bf16[1040,1...) custom-call(s32[128]{0:T(128)} %reshape.50.slot_ref, s32[8]{0:T(128)} %reshape.62.act_ref, bf16[8,128,128]{2,1,0:T(8,128)(2,1)} %bitcast.18, ...), custom_call_target="tpu_custom_call" | custom-call | tf_op jit(solution)/shard_map/pallas_call | solution.py:182
  49.8 2.3 %collective-permute-start.13 = (bf16[1040,128]{1,0:T(8,128)(2,1)}, bf16[1040,128]{1,0:T(8,128)(2,1)S(1)}, u32[]{:S(2)}, u32[]{:S(2)}) collective-permute-start(bf16[1040,128]{1,0:T(8,128)(2,1)} %get-tuple-element.13), channel_id=1, source_target_pairs={{4,0},{6,2},{8,4},{10,6},{12,8},{14,10},{5,1},{7,3},{9,5},{11,7},{... | collective-permute-start | bytes 798728 | tf_op jit(solution)/shard_map/ppermute | solution.py:34
  52.2 1.9 %collective-permute-start.14 = (bf16[1040,128]{1,0:T(8,128)(2,1)}, bf16[1040,128]{1,0:T(8,128)(2,1)S(1)}, u32[]{:S(2)}, u32[]{:S(2)}) collective-permute-start(bf16[1040,128]{1,0:T(8,128)(2,1)} %get-tuple-element.14), channel_id=1, source_target_pairs={{2,0},{4,2},{6,4},{8,6},{10,8},{12,10},{14,12},{3,1},{5,3},{7,5},{... | collective-permute-start | bytes 798728 | tf_op jit(solution)/shard_map/ppermute | solution.py:34
  54.1 4.8 %collective-permute-start.15 = (bf16[1040,128]{1,0:T(8,128)(2,1)}, bf16[1040,128]{1,0:T(8,128)(2,1)S(1)}, u32[]{:S(2)}, u32[]{:S(2)}) collective-permute-start(bf16[1040,128]{1,0:T(8,128)(2,1)} %get-tuple-element.15), channel_id=1, source_target_pairs={{0,2},{2,4},{4,6},{6,8},{8,10},{10,12},{12,14},{1,3},{3,5},{5,7},{... | collective-permute-start | bytes 798728 | tf_op jit(solution)/shard_map/ppermute | solution.py:34
  58.9 1.9 %collective-permute-start.16 = (bf16[1040,128]{1,0:T(8,128)(2,1)}, bf16[1040,128]{1,0:T(8,128)(2,1)S(1)}, u32[]{:S(2)}, u32[]{:S(2)}) collective-permute-start(bf16[1040,128]{1,0:T(8,128)(2,1)} %get-tuple-element.16), channel_id=1, source_target_pairs={{0,4},{2,6},{4,8},{6,10},{8,12},{10,14},{1,5},{3,7},{5,9},{7,11},{... | collective-permute-start | bytes 798728 | tf_op jit(solution)/shard_map/ppermute | solution.py:34
  60.9 0.0 collective-permute-done.13.refs_0_
  60.9 3.3 %collective-permute-done.14.refs_1_ = bf16[1040,128]{1,0:T(8,128)(2,1)S(1)} collective-permute-done((bf16[1040,128]{1,0:T(8,128)(2,1)}, bf16[1040,128]{1,0:T(8,128)(2,1)S(1)}, u32[]{:S(2)}, u32[]{:S(2)}) %collective-permute-start.14) | collective-permute-done | bytes 266272 | tf_op jit(solution)/shard_map/ppermute | solution.py:34
  64.1 4.2 %collective-permute-done.15.refs_2_ = bf16[1040,128]{1,0:T(8,128)(2,1)S(1)} collective-permute-done((bf16[1040,128]{1,0:T(8,128)(2,1)}, bf16[1040,128]{1,0:T(8,128)(2,1)S(1)}, u32[]{:S(2)}, u32[]{:S(2)}) %collective-permute-start.15) | collective-permute-done | bytes 266272 | tf_op jit(solution)/shard_map/ppermute | solution.py:34
  68.3 1.4 %collective-permute-done.16.refs_3_ = bf16[1040,128]{1,0:T(8,128)(2,1)S(1)} collective-permute-done((bf16[1040,128]{1,0:T(8,128)(2,1)}, bf16[1040,128]{1,0:T(8,128)(2,1)S(1)}, u32[]{:S(2)}, u32[]{:S(2)}) %collective-permute-start.16) | collective-permute-done | bytes 266272 | tf_op jit(solution)/shard_map/ppermute | solution.py:34
  69.7 0.7 copy-done.3
  70.4 2.5 %shard_map.56 = bf16[8,128,128]{2,1,0:T(8,128)(2,1)} custom-call(f32[8,128,128]{2,1,0:T(8,128)} %get-tuple-element.11.num_ref, f32[8,1,128]{2,1,0:T(1,128)} %get-tuple-element.12.mass_ref, bf16[8,128,128]{2,1,0:T(8,128)(2,1)} %bitcast.12, bf16[1040,128]{1,0:T(8,128)(2,1)} %copy-done, bf16[1040,128]{1,0:T(8,128)(2,1)} %copy-done.1, ...), custom_call_target="tpu_custom_call" | custom-call | tf_op jit(solution)/shard_map/pallas_call | solution.py:202
  (33 shorter events, 0.1 us)
Async XLA Ops:
  0.0 22.2 %copy-start.19 = (s32[4]{0:T(128)S(1)}, s32[4]{0:T(128)}, u32[]{:S(2)}) copy-start(s32[4]{0:T(128)} %param.9) | copy-start | bytes 52
  0.0 11.9 %collective-permute-start.6 = (bf16[8,128,128]{2,1,0:T(8,128)(2,1)}, bf16[8,128,128]{2,1,0:T(8,128)(2,1)S(1)}, u32[]{:S(2)}, u32[]{:S(2)}) collective-permute-start(bf16[8,128,128]{2,1,0:T(8,128)(2,1)} %bitcast.13), channel_id=1, source_target_pairs={{0,1},{1,0},{2,3},{3,2},{4,5},{5,4},{6,7},{7,6},{8,9},{9,8},{10,11... | collective-permute-start | bytes 786440 | tf_op jit(solution)/shard_map/ppermute | solution.py:147
  0.0 16.3 %collective-permute-start.1 = (bf16[4,256,128]{2,1,0:T(8,128)(2,1)}, bf16[4,256,128]{2,1,0:T(8,128)(2,1)S(1)}, u32[]{:S(2)}, u32[]{:S(2)}) collective-permute-start(bf16[4,256,128]{2,1,0:T(8,128)(2,1)} %param.5), channel_id=1, source_target_pairs={{0,2},{2,4},{4,6},{6,8},{8,10},{10,12},{12,14},{1,3},{3,5},{5,7},{... | collective-permute-start | bytes 786440 | tf_op jit(solution)/shard_map/ppermute | solution.py:34
  3.6 14.6 %collective-permute-start = (bf16[4,256,128]{2,1,0:T(8,128)(2,1)}, bf16[4,256,128]{2,1,0:T(8,128)(2,1)S(1)}, u32[]{:S(2)}, u32[]{:S(2)}) collective-permute-start(bf16[4,256,128]{2,1,0:T(8,128)(2,1)} %param.5), channel_id=1, source_target_pairs={{0,4},{2,6},{4,8},{6,10},{8,12},{10,14},{1,5},{3,7},{5,9},{7,11},{... | collective-permute-start | bytes 786440 | tf_op jit(solution)/shard_map/ppermute | solution.py:34
  5.5 16.7 %collective-permute-start.3 = (bf16[4,256,128]{2,1,0:T(8,128)(2,1)}, bf16[4,256,128]{2,1,0:T(8,128)(2,1)S(1)}, u32[]{:S(2)}, u32[]{:S(2)}) collective-permute-start(bf16[4,256,128]{2,1,0:T(8,128)(2,1)} %param.5), channel_id=1, source_target_pairs={{4,0},{6,2},{8,4},{10,6},{12,8},{14,10},{5,1},{7,3},{9,5},{11,7},{... | collective-permute-start | bytes 786440 | tf_op jit(solution)/shard_map/ppermute | solution.py:34
  9.5 14.7 %collective-permute-start.2 = (bf16[4,256,128]{2,1,0:T(8,128)(2,1)}, bf16[4,256,128]{2,1,0:T(8,128)(2,1)S(1)}, u32[]{:S(2)}, u32[]{:S(2)}) collective-permute-start(bf16[4,256,128]{2,1,0:T(8,128)(2,1)} %param.5), channel_id=1, source_target_pairs={{2,0},{4,2},{6,4},{8,6},{10,8},{12,10},{14,12},{3,1},{5,3},{7,5},{... | collective-permute-start | bytes 786440 | tf_op jit(solution)/shard_map/ppermute | solution.py:34
  11.9 22.2 %copy-start.4 = (bf16[8,128,128]{2,1,0:T(8,128)(2,1)}, bf16[8,128,128]{2,1,0:T(8,128)(2,1)S(1)}, u32[]{:S(2)}) copy-start(bf16[8,128,128]{2,1,0:T(8,128)(2,1)S(1)} %collective-permute-done.6.refs_7_) | copy-start | bytes 786436
  11.9 15.6 %collective-permute-start.10 = (bf16[4,256,128]{2,1,0:T(8,128)(2,1)}, bf16[4,256,128]{2,1,0:T(8,128)(2,1)S(1)}, u32[]{:S(2)}, u32[]{:S(2)}) collective-permute-start(bf16[4,256,128]{2,1,0:T(8,128)(2,1)} %param.6), channel_id=1, source_target_pairs={{0,2},{2,4},{4,6},{6,8},{8,10},{10,12},{12,14},{1,3},{3,5},{5,7},{... | collective-permute-start | bytes 786440 | tf_op jit(solution)/shard_map/ppermute | solution.py:34
  16.3 17.8 %copy-start.5 = (bf16[4,256,128]{2,1,0:T(8,128)(2,1)}, bf16[4,256,128]{2,1,0:T(8,128)(2,1)S(1)}, u32[]{:S(2)}) copy-start(bf16[4,256,128]{2,1,0:T(8,128)(2,1)S(1)} %collective-permute-done.1) | copy-start | bytes 786436
  16.3 11.7 %collective-permute-start.9 = (bf16[4,256,128]{2,1,0:T(8,128)(2,1)}, bf16[4,256,128]{2,1,0:T(8,128)(2,1)S(1)}, u32[]{:S(2)}, u32[]{:S(2)}) collective-permute-start(bf16[4,256,128]{2,1,0:T(8,128)(2,1)} %param.6), channel_id=1, source_target_pairs={{0,4},{2,6},{4,8},{6,10},{8,12},{10,14},{1,5},{3,7},{5,9},{7,11},{... | collective-permute-start | bytes 786440 | tf_op jit(solution)/shard_map/ppermute | solution.py:34
  18.2 15.9 %copy-start.6 = (bf16[4,256,128]{2,1,0:T(8,128)(2,1)}, bf16[4,256,128]{2,1,0:T(8,128)(2,1)S(1)}, u32[]{:S(2)}) copy-start(bf16[4,256,128]{2,1,0:T(8,128)(2,1)S(1)} %collective-permute-done) | copy-start | bytes 786436
  18.2 9.8 %collective-permute-start.12 = (bf16[4,256,128]{2,1,0:T(8,128)(2,1)}, bf16[4,256,128]{2,1,0:T(8,128)(2,1)S(1)}, u32[]{:S(2)}, u32[]{:S(2)}) collective-permute-start(bf16[4,256,128]{2,1,0:T(8,128)(2,1)} %param.6), channel_id=1, source_target_pairs={{4,0},{6,2},{8,4},{10,6},{12,8},{14,10},{5,1},{7,3},{9,5},{11,7},{... | collective-permute-start | bytes 786440 | tf_op jit(solution)/shard_map/ppermute | solution.py:34
  22.2 11.9 %copy-start.7 = (bf16[4,256,128]{2,1,0:T(8,128)(2,1)}, bf16[4,256,128]{2,1,0:T(8,128)(2,1)S(1)}, u32[]{:S(2)}) copy-start(bf16[4,256,128]{2,1,0:T(8,128)(2,1)S(1)} %collective-permute-done.3) | copy-start | bytes 786436
  22.3 11.8 %collective-permute-start.11 = (bf16[4,256,128]{2,1,0:T(8,128)(2,1)}, bf16[4,256,128]{2,1,0:T(8,128)(2,1)S(1)}, u32[]{:S(2)}, u32[]{:S(2)}) collective-permute-start(bf16[4,256,128]{2,1,0:T(8,128)(2,1)} %param.6), channel_id=1, source_target_pairs={{2,0},{4,2},{6,4},{8,6},{10,8},{12,10},{14,12},{3,1},{5,3},{7,5},{... | collective-permute-start | bytes 786440 | tf_op jit(solution)/shard_map/ppermute | solution.py:34
  24.2 10.0 %copy-start.8 = (bf16[4,256,128]{2,1,0:T(8,128)(2,1)}, bf16[4,256,128]{2,1,0:T(8,128)(2,1)S(1)}, u32[]{:S(2)}) copy-start(bf16[4,256,128]{2,1,0:T(8,128)(2,1)S(1)} %collective-permute-done.2) | copy-start | bytes 786436
  24.2 9.8 %collective-permute-start.5 = (bf16[8,128,128]{2,1,0:T(8,128)(2,1)S(1)}, bf16[8,128,128]{2,1,0:T(8,128)(2,1)S(1)}, u32[]{:S(2)}, u32[]{:S(2)}) collective-permute-start(bf16[8,128,128]{2,1,0:T(8,128)(2,1)S(1)} %bitcast.15), channel_id=1, source_target_pairs={{0,1},{1,0},{2,3},{3,2},{4,5},{5,4},{6,7},{7,6},{8,9},{9,8},{10,11... | collective-permute-start | bytes 786440 | tf_op jit(solution)/shard_map/ppermute | solution.py:147
  27.5 6.7 %copy-start.9 = (bf16[4,256,128]{2,1,0:T(8,128)(2,1)}, bf16[4,256,128]{2,1,0:T(8,128)(2,1)S(1)}, u32[]{:S(2)}) copy-start(bf16[4,256,128]{2,1,0:T(8,128)(2,1)S(1)} %collective-permute-done.10) | copy-start | bytes 786436
  27.5 1.7 %copy-start.17 = (s32[4,2,16]{2,1,0:T(2,128)S(1)}, s32[4,2,16]{2,1,0:T(2,128)}, u32[]{:S(2)}) copy-start(s32[4,2,16]{2,1,0:T(2,128)} %param.8) | copy-start | bytes 1540
  27.5 1.7 %copy-start.18 = (s32[4,2,16]{2,1,0:T(2,128)S(1)}, s32[4,2,16]{2,1,0:T(2,128)}, u32[]{:S(2)}) copy-start(s32[4,2,16]{2,1,0:T(2,128)} %param.7) | copy-start | bytes 1540
  27.5 6.6 %collective-permute-start.4 = (bf16[8,128,128]{2,1,0:T(8,128)(2,1)S(1)}, bf16[8,128,128]{2,1,0:T(8,128)(2,1)S(1)}, u32[]{:S(2)}, u32[]{:S(2)}) collective-permute-start(bf16[8,128,128]{2,1,0:T(8,128)(2,1)S(1)} %bitcast.17), channel_id=1, source_target_pairs={{0,1},{1,0},{2,3},{3,2},{4,5},{5,4},{6,7},{7,6},{8,9},{9,8},{10,11... | collective-permute-start | bytes 786440 | tf_op jit(solution)/shard_map/ppermute | solution.py:147
  28.0 6.2 %copy-start.10 = (bf16[4,256,128]{2,1,0:T(8,128)(2,1)}, bf16[4,256,128]{2,1,0:T(8,128)(2,1)S(1)}, u32[]{:S(2)}) copy-start(bf16[4,256,128]{2,1,0:T(8,128)(2,1)S(1)} %collective-permute-done.9) | copy-start | bytes 786436
  28.0 6.1 %collective-permute-start.8 = (bf16[8,128,128]{2,1,0:T(8,128)(2,1)S(1)}, bf16[8,128,128]{2,1,0:T(8,128)(2,1)S(1)}, u32[]{:S(2)}, u32[]{:S(2)}) collective-permute-start(bf16[8,128,128]{2,1,0:T(8,128)(2,1)S(1)} %bitcast.19), channel_id=1, source_target_pairs={{0,1},{1,0},{2,3},{3,2},{4,5},{5,4},{6,7},{7,6},{8,9},{9,8},{10,11... | collective-permute-start | bytes 786440 | tf_op jit(solution)/shard_map/ppermute | solution.py:147
  28.0 6.2 %copy-start.11 = (bf16[4,256,128]{2,1,0:T(8,128)(2,1)}, bf16[4,256,128]{2,1,0:T(8,128)(2,1)S(1)}, u32[]{:S(2)}) copy-start(bf16[4,256,128]{2,1,0:T(8,128)(2,1)S(1)} %collective-permute-done.12) | copy-start | bytes 786436
  28.0 6.1 %collective-permute-start.7 = (bf16[8,128,128]{2,1,0:T(8,128)(2,1)S(1)}, bf16[8,128,128]{2,1,0:T(8,128)(2,1)S(1)}, u32[]{:S(2)}, u32[]{:S(2)}) collective-permute-start(bf16[8,128,128]{2,1,0:T(8,128)(2,1)S(1)} %bitcast.21), channel_id=1, source_target_pairs={{0,1},{1,0},{2,3},{3,2},{4,5},{5,4},{6,7},{7,6},{8,9},{9,8},{10,11... | collective-permute-start | bytes 786440 | tf_op jit(solution)/shard_map/ppermute | solution.py:147
  34.0 0.7 copy-start.12
  34.0 0.8 %copy-start.13 = (bf16[8,128,128]{2,1,0:T(8,128)(2,1)}, bf16[8,128,128]{2,1,0:T(8,128)(2,1)S(1)}, u32[]{:S(2)}) copy-start(bf16[8,128,128]{2,1,0:T(8,128)(2,1)S(1)} %collective-permute-done.5.refs_6_) | copy-start | bytes 786436
  34.0 0.9 %copy-start.14 = (bf16[8,128,128]{2,1,0:T(8,128)(2,1)}, bf16[8,128,128]{2,1,0:T(8,128)(2,1)S(1)}, u32[]{:S(2)}) copy-start(bf16[8,128,128]{2,1,0:T(8,128)(2,1)S(1)} %collective-permute-done.4.refs_5_) | copy-start | bytes 786436
  34.1 0.9 %copy-start.15 = (bf16[8,128,128]{2,1,0:T(8,128)(2,1)}, bf16[8,128,128]{2,1,0:T(8,128)(2,1)S(1)}, u32[]{:S(2)}) copy-start(bf16[8,128,128]{2,1,0:T(8,128)(2,1)S(1)} %collective-permute-done.8.refs_9_) | copy-start | bytes 786436
  34.1 1.0 %copy-start.16 = (bf16[8,128,128]{2,1,0:T(8,128)(2,1)}, bf16[8,128,128]{2,1,0:T(8,128)(2,1)S(1)}, u32[]{:S(2)}) copy-start(bf16[8,128,128]{2,1,0:T(8,128)(2,1)S(1)} %collective-permute-done.7.refs_8_) | copy-start | bytes 786436
  49.8 11.0 %collective-permute-start.13 = (bf16[1040,128]{1,0:T(8,128)(2,1)}, bf16[1040,128]{1,0:T(8,128)(2,1)S(1)}, u32[]{:S(2)}, u32[]{:S(2)}) collective-permute-start(bf16[1040,128]{1,0:T(8,128)(2,1)} %get-tuple-element.13), channel_id=1, source_target_pairs={{4,0},{6,2},{8,4},{10,6},{12,8},{14,10},{5,1},{7,3},{9,5},{11,7},{... | collective-permute-start | bytes 798728 | tf_op jit(solution)/shard_map/ppermute | solution.py:34
  52.2 12.0 %collective-permute-start.14 = (bf16[1040,128]{1,0:T(8,128)(2,1)}, bf16[1040,128]{1,0:T(8,128)(2,1)S(1)}, u32[]{:S(2)}, u32[]{:S(2)}) collective-permute-start(bf16[1040,128]{1,0:T(8,128)(2,1)} %get-tuple-element.14), channel_id=1, source_target_pairs={{2,0},{4,2},{6,4},{8,6},{10,8},{12,10},{14,12},{3,1},{5,3},{7,5},{... | collective-permute-start | bytes 798728 | tf_op jit(solution)/shard_map/ppermute | solution.py:34
  54.1 14.2 %collective-permute-start.15 = (bf16[1040,128]{1,0:T(8,128)(2,1)}, bf16[1040,128]{1,0:T(8,128)(2,1)S(1)}, u32[]{:S(2)}, u32[]{:S(2)}) collective-permute-start(bf16[1040,128]{1,0:T(8,128)(2,1)} %get-tuple-element.15), channel_id=1, source_target_pairs={{0,2},{2,4},{4,6},{6,8},{8,10},{10,12},{12,14},{1,3},{3,5},{5,7},{... | collective-permute-start | bytes 798728 | tf_op jit(solution)/shard_map/ppermute | solution.py:34
  58.9 10.8 %collective-permute-start.16 = (bf16[1040,128]{1,0:T(8,128)(2,1)}, bf16[1040,128]{1,0:T(8,128)(2,1)S(1)}, u32[]{:S(2)}, u32[]{:S(2)}) collective-permute-start(bf16[1040,128]{1,0:T(8,128)(2,1)} %get-tuple-element.16), channel_id=1, source_target_pairs={{0,4},{2,6},{4,8},{6,10},{8,12},{10,14},{1,5},{3,7},{5,9},{7,11},{... | collective-permute-start | bytes 798728 | tf_op jit(solution)/shard_map/ppermute | solution.py:34
  60.9 8.8 %copy-start = (bf16[1040,128]{1,0:T(8,128)(2,1)}, bf16[1040,128]{1,0:T(8,128)(2,1)S(1)}, u32[]{:S(2)}) copy-start(bf16[1040,128]{1,0:T(8,128)(2,1)S(1)} %collective-permute-done.13.refs_0_) | copy-start | bytes 798724
  64.1 5.6 %copy-start.1 = (bf16[1040,128]{1,0:T(8,128)(2,1)}, bf16[1040,128]{1,0:T(8,128)(2,1)S(1)}, u32[]{:S(2)}) copy-start(bf16[1040,128]{1,0:T(8,128)(2,1)S(1)} %collective-permute-done.14.refs_1_) | copy-start | bytes 798724
  68.3 1.4 %copy-start.2 = (bf16[1040,128]{1,0:T(8,128)(2,1)}, bf16[1040,128]{1,0:T(8,128)(2,1)S(1)}, u32[]{:S(2)}) copy-start(bf16[1040,128]{1,0:T(8,128)(2,1)S(1)} %collective-permute-done.15.refs_2_) | copy-start | bytes 798724
  69.7 0.7 copy-start.3

commit v12 on v11

--- a/solution.py
+++ b/solution.py
@@ -62,21 +62,21 @@
     score_scale = 1.0 / math.sqrt(W)
     dims_t = (((1,), (1,)), ((), ()))
 
-    def one_query(i, carry):
+    def one_query(i, buf):
         q_slot = center + (i // blocks) * rimmed + halo + i % blocks
         query = key_e[q_slot] * jnp.asarray(score_scale, jnp.bfloat16)
         slots = [slot_ref[i * K + k] for k in range(K)]
         for k in range(K):
             s = slots[k]
             part = lax.dot_general(query, key_e[s], dims_t, preferred_element_type=jnp.float32)
-            score_ref[:, k * BLOCK : (k + 1) * BLOCK] = part
-            value_ref[k * BLOCK : (k + 1) * BLOCK, :] = key_v[s]
-        score = score_ref[...]
+            score_ref[buf, :, k * BLOCK : (k + 1) * BLOCK] = part
+            value_ref[buf, k * BLOCK : (k + 1) * BLOCK, :] = key_v[s]
+        score = score_ref[buf]
         peak = jnp.max(score, axis=-1, keepdims=True)
         exponent = jnp.exp(score - peak)
         prob = exponent / jnp.sum(exponent, axis=-1, keepdims=True)
         attention = prob.astype(jnp.bfloat16)
-        estimate = jnp.dot(attention, value_ref[...], preferred_element_type=jnp.float32)
+        estimate = jnp.dot(attention, value_ref[buf], preferred_element_type=jnp.float32)
         active = act_ref[i].astype(jnp.float32)
         estimate = estimate.astype(jnp.bfloat16).astype(jnp.float32) * active
         estimate_t = estimate.T.astype(jnp.bfloat16)
@@ -86,9 +86,15 @@
             s = slots[k]
             acc[s] = acc[s] + contrib_t[:, k * BLOCK : (k + 1) * BLOCK]
             macc[s] = macc[s] + weights[:, k * BLOCK : (k + 1) * BLOCK]
+
+    def query_pair(p, carry):
+        one_query(2 * p, 0)
+        one_query(2 * p + 1, 1)
         return carry
 
-    lax.fori_loop(0, queries, one_query, 0)
+    lax.fori_loop(0, queries // 2, query_pair, 0)
+    if queries % 2:
+        one_query(queries - 1, 0)
 
     own = pl.ds(center, per_slab)
     own_num_ref[...] = acc[own]
@@ -189,8 +195,8 @@
             pltpu.VMEM((total, BLOCK, half), jnp.bfloat16),
             pltpu.VMEM((total, half, BLOCK), jnp.float32),
             pltpu.VMEM((total, 1, BLOCK), jnp.float32),
-            pltpu.VMEM((BLOCK, K * BLOCK), jnp.float32),
-            pltpu.VMEM((K * BLOCK, half), jnp.bfloat16),
+            pltpu.VMEM((2, BLOCK, K * BLOCK), jnp.float32),
+            pltpu.VMEM((2, K * BLOCK, half), jnp.bfloat16),
             pltpu.SemaphoreType.DMA((3, slabs)),
         ],
     )(slot, active.reshape(-1), *window_e, *others, *window_v)

time: 73.3 us -> 72.7 us (level)
  no operation moved by 1% of the time
where the time goes in v12:
time: 72.7 us; the launch traced here: 72.3 us
  starting transfers between devices  35.5 us (49%)
  waiting for transfers between devices  16.7 us (23%)
  Pallas kernels  16.6 us (23%)
  local copies, waits for them, and re-layouts  3.01 us (4%)
    ppermute x12, starting transfers between devices, passed_along(): return lax.ppermute(block, axis, route)  35 us
    ppermute x12, waiting for transfers between devices, passed_along(): return lax.ppermute(block, axis, route)  16.6 us
    pallas_call x1, Pallas kernels, shards(): pl.pallas_call(kernel, out_shape=out_shape, in_specs=[smem, smem] + [vmem...  14.1 us
    pallas_call x1, Pallas kernels, shards(): pl.pallas_call(functools.partial(combine_kernel, per_slab=per_slab, half=...  2.45 us
    unnamed x40, local copies, waits for them, and re-layouts  1.69 us
  transfers between devices with their start and end apart: 17, of which 6 were waited for; matrix products, arithmetic and copies ran while one was open for 2% of the time, Pallas kernels for 0%

profile of v12, /device:TPU:22, one launch (start us, length us, event | category | flops | bytes accessed | tf_op | source)
XLA Modules:
  0.0 72.3 jit_solution(9164636547037265772)
XLA Ops:
  0.0 0.0 collective-permute-start.6
  0.0 3.6 %collective-permute-start.1 = (bf16[4,256,128]{2,1,0:T(8,128)(2,1)}, bf16[4,256,128]{2,1,0:T(8,128)(2,1)S(1)}, u32[]{:S(2)}, u32[]{:S(2)}) collective-permute-start(bf16[4,256,128]{2,1,0:T(8,128)(2,1)} %param.5), channel_id=1, source_target_pairs={{0,2},{2,4},{4,6},{6,8},{8,10},{10,12},{12,14},{1,3},{3,5},{5,7},{... | collective-permute-start | bytes 786440 | tf_op jit(solution)/shard_map/ppermute | solution.py:34
  3.6 1.9 %collective-permute-start = (bf16[4,256,128]{2,1,0:T(8,128)(2,1)}, bf16[4,256,128]{2,1,0:T(8,128)(2,1)S(1)}, u32[]{:S(2)}, u32[]{:S(2)}) collective-permute-start(bf16[4,256,128]{2,1,0:T(8,128)(2,1)} %param.5), channel_id=1, source_target_pairs={{0,4},{2,6},{4,8},{6,10},{8,12},{10,14},{1,5},{3,7},{5,9},{7,11},{... | collective-permute-start | bytes 786440 | tf_op jit(solution)/shard_map/ppermute | solution.py:34
  5.5 3.9 %collective-permute-start.3 = (bf16[4,256,128]{2,1,0:T(8,128)(2,1)}, bf16[4,256,128]{2,1,0:T(8,128)(2,1)S(1)}, u32[]{:S(2)}, u32[]{:S(2)}) collective-permute-start(bf16[4,256,128]{2,1,0:T(8,128)(2,1)} %param.5), channel_id=1, source_target_pairs={{4,0},{6,2},{8,4},{10,6},{12,8},{14,10},{5,1},{7,3},{9,5},{11,7},{... | collective-permute-start | bytes 786440 | tf_op jit(solution)/shard_map/ppermute | solution.py:34
  9.5 2.4 %collective-permute-start.2 = (bf16[4,256,128]{2,1,0:T(8,128)(2,1)}, bf16[4,256,128]{2,1,0:T(8,128)(2,1)S(1)}, u32[]{:S(2)}, u32[]{:S(2)}) collective-permute-start(bf16[4,256,128]{2,1,0:T(8,128)(2,1)} %param.5), channel_id=1, source_target_pairs={{2,0},{4,2},{6,4},{8,6},{10,8},{12,10},{14,12},{3,1},{5,3},{7,5},{... | collective-permute-start | bytes 786440 | tf_op jit(solution)/shard_map/ppermute | solution.py:34
  11.9 0.0 collective-permute-done.6.refs_7_
  11.9 4.4 %collective-permute-start.10 = (bf16[4,256,128]{2,1,0:T(8,128)(2,1)}, bf16[4,256,128]{2,1,0:T(8,128)(2,1)S(1)}, u32[]{:S(2)}, u32[]{:S(2)}) collective-permute-start(bf16[4,256,128]{2,1,0:T(8,128)(2,1)} %param.6), channel_id=1, source_target_pairs={{0,2},{2,4},{4,6},{6,8},{8,10},{10,12},{12,14},{1,3},{3,5},{5,7},{... | collective-permute-start | bytes 786440 | tf_op jit(solution)/shard_map/ppermute | solution.py:34
  16.3 0.0 collective-permute-done.1
  16.3 0.0 copy-start.5
  16.3 1.9 %collective-permute-start.9 = (bf16[4,256,128]{2,1,0:T(8,128)(2,1)}, bf16[4,256,128]{2,1,0:T(8,128)(2,1)S(1)}, u32[]{:S(2)}, u32[]{:S(2)}) collective-permute-start(bf16[4,256,128]{2,1,0:T(8,128)(2,1)} %param.6), channel_id=1, source_target_pairs={{0,4},{2,6},{4,8},{6,10},{8,12},{10,14},{1,5},{3,7},{5,9},{7,11},{... | collective-permute-start | bytes 786440 | tf_op jit(solution)/shard_map/ppermute | solution.py:34
  18.2 0.0 collective-permute-done
  18.2 0.0 copy-start.6
  18.2 3.9 %collective-permute-start.12 = (bf16[4,256,128]{2,1,0:T(8,128)(2,1)}, bf16[4,256,128]{2,1,0:T(8,128)(2,1)S(1)}, u32[]{:S(2)}, u32[]{:S(2)}) collective-permute-start(bf16[4,256,128]{2,1,0:T(8,128)(2,1)} %param.6), channel_id=1, source_target_pairs={{4,0},{6,2},{8,4},{10,6},{12,8},{14,10},{5,1},{7,3},{9,5},{11,7},{... | collective-permute-start | bytes 786440 | tf_op jit(solution)/shard_map/ppermute | solution.py:34
  22.2 0.1 fusion
  22.2 0.0 collective-permute-done.3
  22.3 1.9 %collective-permute-start.11 = (bf16[4,256,128]{2,1,0:T(8,128)(2,1)}, bf16[4,256,128]{2,1,0:T(8,128)(2,1)S(1)}, u32[]{:S(2)}, u32[]{:S(2)}) collective-permute-start(bf16[4,256,128]{2,1,0:T(8,128)(2,1)} %param.6), channel_id=1, source_target_pairs={{2,0},{4,2},{6,4},{8,6},{10,8},{12,10},{14,12},{3,1},{5,3},{7,5},{... | collective-permute-start | bytes 786440 | tf_op jit(solution)/shard_map/ppermute | solution.py:34
  24.2 0.0 collective-permute-done.2
  24.2 0.1 collective-permute-start.5
  24.3 3.2 %collective-permute-done.10 = bf16[4,256,128]{2,1,0:T(8,128)(2,1)S(1)} collective-permute-done((bf16[4,256,128]{2,1,0:T(8,128)(2,1)}, bf16[4,256,128]{2,1,0:T(8,128)(2,1)S(1)}, u32[]{:S(2)}, u32[]{:S(2)}) %collective-permute-start.10) | collective-permute-done | bytes 262176 | tf_op jit(solution)/shard_map/ppermute | solution.py:34
  27.5 0.0 collective-permute-start.4
  27.5 0.5 collective-permute-done.9
  28.0 0.0 collective-permute-start.8
  28.0 0.0 collective-permute-done.12
  28.0 0.5 collective-permute-start.7
  28.5 0.7 reshape.62.act_ref
  29.2 0.1 add_clamp_fusion
  29.3 0.7 reshape.50.slot_ref
  29.9 4.1 %collective-permute-done.11 = bf16[4,256,128]{2,1,0:T(8,128)(2,1)S(1)} collective-permute-done((bf16[4,256,128]{2,1,0:T(8,128)(2,1)}, bf16[4,256,128]{2,1,0:T(8,128)(2,1)S(1)}, u32[]{:S(2)}, u32[]{:S(2)}) %collective-permute-start.11) | collective-permute-done | bytes 262176 | tf_op jit(solution)/shard_map/ppermute | solution.py:34
  34.0 0.0 collective-permute-done.5.refs_6_
  34.0 0.0 collective-permute-done.4.refs_5_
  34.1 0.0 collective-permute-done.8.refs_9_
  34.1 0.0 collective-permute-done.7.refs_8_
  34.2 0.6 copy-done.12
  34.7 0.1 copy-done.13
  34.8 0.1 copy-done.14
  34.9 0.1 copy-done.15
  35.0 0.1 copy-done.16
  35.1 14.1 %shard_map.55 = (f32[8,128,128]{2,1,0:T(8,128)}, f32[8,1,128]{2,1,0:T(1,128)}, bf16[1040,128]{1,0:T(8,128)(2,1)}, bf16[1040,128]{1,0:T(8,128)(2,1)}, bf16[1040,1...) custom-call(s32[128]{0:T(128)} %reshape.50.slot_ref, s32[8]{0:T(128)} %reshape.62.act_ref, bf16[8,128,128]{2,1,0:T(8,128)(2,1)} %bitcast.18, ...), custom_call_target="tpu_custom_call" | custom-call | tf_op jit(solution)/shard_map/pallas_call | solution.py:188
  49.2 2.4 %collective-permute-start.13 = (bf16[1040,128]{1,0:T(8,128)(2,1)}, bf16[1040,128]{1,0:T(8,128)(2,1)S(1)}, u32[]{:S(2)}, u32[]{:S(2)}) collective-permute-start(bf16[1040,128]{1,0:T(8,128)(2,1)} %get-tuple-element.13), channel_id=1, source_target_pairs={{4,0},{6,2},{8,4},{10,6},{12,8},{14,10},{5,1},{7,3},{9,5},{11,7},{... | collective-permute-start | bytes 798728 | tf_op jit(solution)/shard_map/ppermute | solution.py:34
  51.6 1.9 %collective-permute-start.14 = (bf16[1040,128]{1,0:T(8,128)(2,1)}, bf16[1040,128]{1,0:T(8,128)(2,1)S(1)}, u32[]{:S(2)}, u32[]{:S(2)}) collective-permute-start(bf16[1040,128]{1,0:T(8,128)(2,1)} %get-tuple-element.14), channel_id=1, source_target_pairs={{2,0},{4,2},{6,4},{8,6},{10,8},{12,10},{14,12},{3,1},{5,3},{7,5},{... | collective-permute-start | bytes 798728 | tf_op jit(solution)/shard_map/ppermute | solution.py:34
  53.5 4.8 %collective-permute-start.15 = (bf16[1040,128]{1,0:T(8,128)(2,1)}, bf16[1040,128]{1,0:T(8,128)(2,1)S(1)}, u32[]{:S(2)}, u32[]{:S(2)}) collective-permute-start(bf16[1040,128]{1,0:T(8,128)(2,1)} %get-tuple-element.15), channel_id=1, source_target_pairs={{0,2},{2,4},{4,6},{6,8},{8,10},{10,12},{12,14},{1,3},{3,5},{5,7},{... | collective-permute-start | bytes 798728 | tf_op jit(solution)/shard_map/ppermute | solution.py:34
  58.3 1.9 %collective-permute-start.16 = (bf16[1040,128]{1,0:T(8,128)(2,1)}, bf16[1040,128]{1,0:T(8,128)(2,1)S(1)}, u32[]{:S(2)}, u32[]{:S(2)}) collective-permute-start(bf16[1040,128]{1,0:T(8,128)(2,1)} %get-tuple-element.16), channel_id=1, source_target_pairs={{0,4},{2,6},{4,8},{6,10},{8,12},{10,14},{1,5},{3,7},{5,9},{7,11},{... | collective-permute-start | bytes 798728 | tf_op jit(solution)/shard_map/ppermute | solution.py:34
  60.3 0.0 collective-permute-done.13.refs_0_
  60.3 3.2 %collective-permute-done.14.refs_1_ = bf16[1040,128]{1,0:T(8,128)(2,1)S(1)} collective-permute-done((bf16[1040,128]{1,0:T(8,128)(2,1)}, bf16[1040,128]{1,0:T(8,128)(2,1)S(1)}, u32[]{:S(2)}, u32[]{:S(2)}) %collective-permute-start.14) | collective-permute-done | bytes 266272 | tf_op jit(solution)/shard_map/ppermute | solution.py:34
  63.5 4.2 %collective-permute-done.15.refs_2_ = bf16[1040,128]{1,0:T(8,128)(2,1)S(1)} collective-permute-done((bf16[1040,128]{1,0:T(8,128)(2,1)}, bf16[1040,128]{1,0:T(8,128)(2,1)S(1)}, u32[]{:S(2)}, u32[]{:S(2)}) %collective-permute-start.15) | collective-permute-done | bytes 266272 | tf_op jit(solution)/shard_map/ppermute | solution.py:34
  67.7 1.4 %collective-permute-done.16.refs_3_ = bf16[1040,128]{1,0:T(8,128)(2,1)S(1)} collective-permute-done((bf16[1040,128]{1,0:T(8,128)(2,1)}, bf16[1040,128]{1,0:T(8,128)(2,1)S(1)}, u32[]{:S(2)}, u32[]{:S(2)}) %collective-permute-start.16) | collective-permute-done | bytes 266272 | tf_op jit(solution)/shard_map/ppermute | solution.py:34
  69.1 0.7 copy-done.3
  69.8 2.5 %shard_map.56 = bf16[8,128,128]{2,1,0:T(8,128)(2,1)} custom-call(f32[8,128,128]{2,1,0:T(8,128)} %get-tuple-element.11.num_ref, f32[8,1,128]{2,1,0:T(1,128)} %get-tuple-element.12.mass_ref, bf16[8,128,128]{2,1,0:T(8,128)(2,1)} %bitcast.12, bf16[1040,128]{1,0:T(8,128)(2,1)} %copy-done, bf16[1040,128]{1,0:T(8,128)(2,1)} %copy-done.1, ...), custom_call_target="tpu_custom_call" | custom-call | tf_op jit(solution)/shard_map/pallas_call | solution.py:208
  (33 shorter events, 0.1 us)
Async XLA Ops:
  0.0 22.2 %copy-start.19 = (s32[4]{0:T(128)S(1)}, s32[4]{0:T(128)}, u32[]{:S(2)}) copy-start(s32[4]{0:T(128)} %param.9) | copy-start | bytes 52
  0.0 11.9 %collective-permute-start.6 = (bf16[8,128,128]{2,1,0:T(8,128)(2,1)}, bf16[8,128,128]{2,1,0:T(8,128)(2,1)S(1)}, u32[]{:S(2)}, u32[]{:S(2)}) collective-permute-start(bf16[8,128,128]{2,1,0:T(8,128)(2,1)} %bitcast.13), channel_id=1, source_target_pairs={{0,1},{1,0},{2,3},{3,2},{4,5},{5,4},{6,7},{7,6},{8,9},{9,8},{10,11... | collective-permute-start | bytes 786440 | tf_op jit(solution)/shard_map/ppermute | solution.py:153
  0.0 16.3 %collective-permute-start.1 = (bf16[4,256,128]{2,1,0:T(8,128)(2,1)}, bf16[4,256,128]{2,1,0:T(8,128)(2,1)S(1)}, u32[]{:S(2)}, u32[]{:S(2)}) collective-permute-start(bf16[4,256,128]{2,1,0:T(8,128)(2,1)} %param.5), channel_id=1, source_target_pairs={{0,2},{2,4},{4,6},{6,8},{8,10},{10,12},{12,14},{1,3},{3,5},{5,7},{... | collective-permute-start | bytes 786440 | tf_op jit(solution)/shard_map/ppermute | solution.py:34
  3.6 14.6 %collective-permute-start = (bf16[4,256,128]{2,1,0:T(8,128)(2,1)}, bf16[4,256,128]{2,1,0:T(8,128)(2,1)S(1)}, u32[]{:S(2)}, u32[]{:S(2)}) collective-permute-start(bf16[4,256,128]{2,1,0:T(8,128)(2,1)} %param.5), channel_id=1, source_target_pairs={{0,4},{2,6},{4,8},{6,10},{8,12},{10,14},{1,5},{3,7},{5,9},{7,11},{... | collective-permute-start | bytes 786440 | tf_op jit(solution)/shard_map/ppermute | solution.py:34
  5.5 16.7 %collective-permute-start.3 = (bf16[4,256,128]{2,1,0:T(8,128)(2,1)}, bf16[4,256,128]{2,1,0:T(8,128)(2,1)S(1)}, u32[]{:S(2)}, u32[]{:S(2)}) collective-permute-start(bf16[4,256,128]{2,1,0:T(8,128)(2,1)} %param.5), channel_id=1, source_target_pairs={{4,0},{6,2},{8,4},{10,6},{12,8},{14,10},{5,1},{7,3},{9,5},{11,7},{... | collective-permute-start | bytes 786440 | tf_op jit(solution)/shard_map/ppermute | solution.py:34
  9.5 14.7 %collective-permute-start.2 = (bf16[4,256,128]{2,1,0:T(8,128)(2,1)}, bf16[4,256,128]{2,1,0:T(8,128)(2,1)S(1)}, u32[]{:S(2)}, u32[]{:S(2)}) collective-permute-start(bf16[4,256,128]{2,1,0:T(8,128)(2,1)} %param.5), channel_id=1, source_target_pairs={{2,0},{4,2},{6,4},{8,6},{10,8},{12,10},{14,12},{3,1},{5,3},{7,5},{... | collective-permute-start | bytes 786440 | tf_op jit(solution)/shard_map/ppermute | solution.py:34
  11.9 22.2 %copy-start.4 = (bf16[8,128,128]{2,1,0:T(8,128)(2,1)}, bf16[8,128,128]{2,1,0:T(8,128)(2,1)S(1)}, u32[]{:S(2)}) copy-start(bf16[8,128,128]{2,1,0:T(8,128)(2,1)S(1)} %collective-permute-done.6.refs_7_) | copy-start | bytes 786436
  11.9 15.6 %collective-permute-start.10 = (bf16[4,256,128]{2,1,0:T(8,128)(2,1)}, bf16[4,256,128]{2,1,0:T(8,128)(2,1)S(1)}, u32[]{:S(2)}, u32[]{:S(2)}) collective-permute-start(bf16[4,256,128]{2,1,0:T(8,128)(2,1)} %param.6), channel_id=1, source_target_pairs={{0,2},{2,4},{4,6},{6,8},{8,10},{10,12},{12,14},{1,3},{3,5},{5,7},{... | collective-permute-start | bytes 786440 | tf_op jit(solution)/shard_map/ppermute | solution.py:34
  16.3 17.8 %copy-start.5 = (bf16[4,256,128]{2,1,0:T(8,128)(2,1)}, bf16[4,256,128]{2,1,0:T(8,128)(2,1)S(1)}, u32[]{:S(2)}) copy-start(bf16[4,256,128]{2,1,0:T(8,128)(2,1)S(1)} %collective-permute-done.1) | copy-start | bytes 786436
  16.3 11.7 %collective-permute-start.9 = (bf16[4,256,128]{2,1,0:T(8,128)(2,1)}, bf16[4,256,128]{2,1,0:T(8,128)(2,1)S(1)}, u32[]{:S(2)}, u32[]{:S(2)}) collective-permute-start(bf16[4,256,128]{2,1,0:T(8,128)(2,1)} %param.6), channel_id=1, source_target_pairs={{0,4},{2,6},{4,8},{6,10},{8,12},{10,14},{1,5},{3,7},{5,9},{7,11},{... | collective-permute-start | bytes 786440 | tf_op jit(solution)/shard_map/ppermute | solution.py:34
  18.2 15.9 %copy-start.6 = (bf16[4,256,128]{2,1,0:T(8,128)(2,1)}, bf16[4,256,128]{2,1,0:T(8,128)(2,1)S(1)}, u32[]{:S(2)}) copy-start(bf16[4,256,128]{2,1,0:T(8,128)(2,1)S(1)} %collective-permute-done) | copy-start | bytes 786436
  18.2 9.8 %collective-permute-start.12 = (bf16[4,256,128]{2,1,0:T(8,128)(2,1)}, bf16[4,256,128]{2,1,0:T(8,128)(2,1)S(1)}, u32[]{:S(2)}, u32[]{:S(2)}) collective-permute-start(bf16[4,256,128]{2,1,0:T(8,128)(2,1)} %param.6), channel_id=1, source_target_pairs={{4,0},{6,2},{8,4},{10,6},{12,8},{14,10},{5,1},{7,3},{9,5},{11,7},{... | collective-permute-start | bytes 786440 | tf_op jit(solution)/shard_map/ppermute | solution.py:34
  22.2 11.9 %copy-start.7 = (bf16[4,256,128]{2,1,0:T(8,128)(2,1)}, bf16[4,256,128]{2,1,0:T(8,128)(2,1)S(1)}, u32[]{:S(2)}) copy-start(bf16[4,256,128]{2,1,0:T(8,128)(2,1)S(1)} %collective-permute-done.3) | copy-start | bytes 786436
  22.3 11.8 %collective-permute-start.11 = (bf16[4,256,128]{2,1,0:T(8,128)(2,1)}, bf16[4,256,128]{2,1,0:T(8,128)(2,1)S(1)}, u32[]{:S(2)}, u32[]{:S(2)}) collective-permute-start(bf16[4,256,128]{2,1,0:T(8,128)(2,1)} %param.6), channel_id=1, source_target_pairs={{2,0},{4,2},{6,4},{8,6},{10,8},{12,10},{14,12},{3,1},{5,3},{7,5},{... | collective-permute-start | bytes 786440 | tf_op jit(solution)/shard_map/ppermute | solution.py:34
  24.2 10.0 %copy-start.8 = (bf16[4,256,128]{2,1,0:T(8,128)(2,1)}, bf16[4,256,128]{2,1,0:T(8,128)(2,1)S(1)}, u32[]{:S(2)}) copy-start(bf16[4,256,128]{2,1,0:T(8,128)(2,1)S(1)} %collective-permute-done.2) | copy-start | bytes 786436
  24.2 9.8 %collective-permute-start.5 = (bf16[8,128,128]{2,1,0:T(8,128)(2,1)S(1)}, bf16[8,128,128]{2,1,0:T(8,128)(2,1)S(1)}, u32[]{:S(2)}, u32[]{:S(2)}) collective-permute-start(bf16[8,128,128]{2,1,0:T(8,128)(2,1)S(1)} %bitcast.15), channel_id=1, source_target_pairs={{0,1},{1,0},{2,3},{3,2},{4,5},{5,4},{6,7},{7,6},{8,9},{9,8},{10,11... | collective-permute-start | bytes 786440 | tf_op jit(solution)/shard_map/ppermute | solution.py:153
  27.5 6.7 %copy-start.9 = (bf16[4,256,128]{2,1,0:T(8,128)(2,1)}, bf16[4,256,128]{2,1,0:T(8,128)(2,1)S(1)}, u32[]{:S(2)}) copy-start(bf16[4,256,128]{2,1,0:T(8,128)(2,1)S(1)} %collective-permute-done.10) | copy-start | bytes 786436
  27.5 1.7 %copy-start.17 = (s32[4,2,16]{2,1,0:T(2,128)S(1)}, s32[4,2,16]{2,1,0:T(2,128)}, u32[]{:S(2)}) copy-start(s32[4,2,16]{2,1,0:T(2,128)} %param.8) | copy-start | bytes 1540
  27.5 1.7 %copy-start.18 = (s32[4,2,16]{2,1,0:T(2,128)S(1)}, s32[4,2,16]{2,1,0:T(2,128)}, u32[]{:S(2)}) copy-start(s32[4,2,16]{2,1,0:T(2,128)} %param.7) | copy-start | bytes 1540
  27.5 6.6 %collective-permute-start.4 = (bf16[8,128,128]{2,1,0:T(8,128)(2,1)S(1)}, bf16[8,128,128]{2,1,0:T(8,128)(2,1)S(1)}, u32[]{:S(2)}, u32[]{:S(2)}) collective-permute-start(bf16[8,128,128]{2,1,0:T(8,128)(2,1)S(1)} %bitcast.17), channel_id=1, source_target_pairs={{0,1},{1,0},{2,3},{3,2},{4,5},{5,4},{6,7},{7,6},{8,9},{9,8},{10,11... | collective-permute-start | bytes 786440 | tf_op jit(solution)/shard_map/ppermute | solution.py:153
  28.0 6.2 %copy-start.10 = (bf16[4,256,128]{2,1,0:T(8,128)(2,1)}, bf16[4,256,128]{2,1,0:T(8,128)(2,1)S(1)}, u32[]{:S(2)}) copy-start(bf16[4,256,128]{2,1,0:T(8,128)(2,1)S(1)} %collective-permute-done.9) | copy-start | bytes 786436
  28.0 6.1 %collective-permute-start.8 = (bf16[8,128,128]{2,1,0:T(8,128)(2,1)S(1)}, bf16[8,128,128]{2,1,0:T(8,128)(2,1)S(1)}, u32[]{:S(2)}, u32[]{:S(2)}) collective-permute-start(bf16[8,128,128]{2,1,0:T(8,128)(2,1)S(1)} %bitcast.19), channel_id=1, source_target_pairs={{0,1},{1,0},{2,3},{3,2},{4,5},{5,4},{6,7},{7,6},{8,9},{9,8},{10,11... | collective-permute-start | bytes 786440 | tf_op jit(solution)/shard_map/ppermute | solution.py:153
  28.0 6.2 %copy-start.11 = (bf16[4,256,128]{2,1,0:T(8,128)(2,1)}, bf16[4,256,128]{2,1,0:T(8,128)(2,1)S(1)}, u32[]{:S(2)}) copy-start(bf16[4,256,128]{2,1,0:T(8,128)(2,1)S(1)} %collective-permute-done.12) | copy-start | bytes 786436
  28.0 6.1 %collective-permute-start.7 = (bf16[8,128,128]{2,1,0:T(8,128)(2,1)S(1)}, bf16[8,128,128]{2,1,0:T(8,128)(2,1)S(1)}, u32[]{:S(2)}, u32[]{:S(2)}) collective-permute-start(bf16[8,128,128]{2,1,0:T(8,128)(2,1)S(1)} %bitcast.21), channel_id=1, source_target_pairs={{0,1},{1,0},{2,3},{3,2},{4,5},{5,4},{6,7},{7,6},{8,9},{9,8},{10,11... | collective-permute-start | bytes 786440 | tf_op jit(solution)/shard_map/ppermute | solution.py:153
  34.0 0.7 copy-start.12
  34.0 0.8 %copy-start.13 = (bf16[8,128,128]{2,1,0:T(8,128)(2,1)}, bf16[8,128,128]{2,1,0:T(8,128)(2,1)S(1)}, u32[]{:S(2)}) copy-start(bf16[8,128,128]{2,1,0:T(8,128)(2,1)S(1)} %collective-permute-done.5.refs_6_) | copy-start | bytes 786436
  34.0 0.9 %copy-start.14 = (bf16[8,128,128]{2,1,0:T(8,128)(2,1)}, bf16[8,128,128]{2,1,0:T(8,128)(2,1)S(1)}, u32[]{:S(2)}) copy-start(bf16[8,128,128]{2,1,0:T(8,128)(2,1)S(1)} %collective-permute-done.4.refs_5_) | copy-start | bytes 786436
  34.1 0.9 %copy-start.15 = (bf16[8,128,128]{2,1,0:T(8,128)(2,1)}, bf16[8,128,128]{2,1,0:T(8,128)(2,1)S(1)}, u32[]{:S(2)}) copy-start(bf16[8,128,128]{2,1,0:T(8,128)(2,1)S(1)} %collective-permute-done.8.refs_9_) | copy-start | bytes 786436
  34.1 1.0 %copy-start.16 = (bf16[8,128,128]{2,1,0:T(8,128)(2,1)}, bf16[8,128,128]{2,1,0:T(8,128)(2,1)S(1)}, u32[]{:S(2)}) copy-start(bf16[8,128,128]{2,1,0:T(8,128)(2,1)S(1)} %collective-permute-done.7.refs_8_) | copy-start | bytes 786436
  49.2 11.1 %collective-permute-start.13 = (bf16[1040,128]{1,0:T(8,128)(2,1)}, bf16[1040,128]{1,0:T(8,128)(2,1)S(1)}, u32[]{:S(2)}, u32[]{:S(2)}) collective-permute-start(bf16[1040,128]{1,0:T(8,128)(2,1)} %get-tuple-element.13), channel_id=1, source_target_pairs={{4,0},{6,2},{8,4},{10,6},{12,8},{14,10},{5,1},{7,3},{9,5},{11,7},{... | collective-permute-start | bytes 798728 | tf_op jit(solution)/shard_map/ppermute | solution.py:34
  51.6 11.9 %collective-permute-start.14 = (bf16[1040,128]{1,0:T(8,128)(2,1)}, bf16[1040,128]{1,0:T(8,128)(2,1)S(1)}, u32[]{:S(2)}, u32[]{:S(2)}) collective-permute-start(bf16[1040,128]{1,0:T(8,128)(2,1)} %get-tuple-element.14), channel_id=1, source_target_pairs={{2,0},{4,2},{6,4},{8,6},{10,8},{12,10},{14,12},{3,1},{5,3},{7,5},{... | collective-permute-start | bytes 798728 | tf_op jit(solution)/shard_map/ppermute | solution.py:34
  53.5 14.2 %collective-permute-start.15 = (bf16[1040,128]{1,0:T(8,128)(2,1)}, bf16[1040,128]{1,0:T(8,128)(2,1)S(1)}, u32[]{:S(2)}, u32[]{:S(2)}) collective-permute-start(bf16[1040,128]{1,0:T(8,128)(2,1)} %get-tuple-element.15), channel_id=1, source_target_pairs={{0,2},{2,4},{4,6},{6,8},{8,10},{10,12},{12,14},{1,3},{3,5},{5,7},{... | collective-permute-start | bytes 798728 | tf_op jit(solution)/shard_map/ppermute | solution.py:34
  58.3 10.8 %collective-permute-start.16 = (bf16[1040,128]{1,0:T(8,128)(2,1)}, bf16[1040,128]{1,0:T(8,128)(2,1)S(1)}, u32[]{:S(2)}, u32[]{:S(2)}) collective-permute-start(bf16[1040,128]{1,0:T(8,128)(2,1)} %get-tuple-element.16), channel_id=1, source_target_pairs={{0,4},{2,6},{4,8},{6,10},{8,12},{10,14},{1,5},{3,7},{5,9},{7,11},{... | collective-permute-start | bytes 798728 | tf_op jit(solution)/shard_map/ppermute | solution.py:34
  60.3 8.8 %copy-start = (bf16[1040,128]{1,0:T(8,128)(2,1)}, bf16[1040,128]{1,0:T(8,128)(2,1)S(1)}, u32[]{:S(2)}) copy-start(bf16[1040,128]{1,0:T(8,128)(2,1)S(1)} %collective-permute-done.13.refs_0_) | copy-start | bytes 798724
  63.5 5.6 %copy-start.1 = (bf16[1040,128]{1,0:T(8,128)(2,1)}, bf16[1040,128]{1,0:T(8,128)(2,1)S(1)}, u32[]{:S(2)}) copy-start(bf16[1040,128]{1,0:T(8,128)(2,1)S(1)} %collective-permute-done.14.refs_1_) | copy-start | bytes 798724
  67.7 1.4 %copy-start.2 = (bf16[1040,128]{1,0:T(8,128)(2,1)}, bf16[1040,128]{1,0:T(8,128)(2,1)S(1)}, u32[]{:S(2)}) copy-start(bf16[1040,128]{1,0:T(8,128)(2,1)S(1)} %collective-permute-done.15.refs_2_) | copy-start | bytes 798724
  69.1 0.7 copy-start.3

commit v13 on v12

--- a/solution.py
+++ b/solution.py
@@ -13,6 +13,7 @@
 K = 16
 REACH = 8
 MASS_ROWS = 16
+GROUP = 4
 
 
 def with_halo(x, sides, width):
@@ -87,14 +88,14 @@
             acc[s] = acc[s] + contrib_t[:, k * BLOCK : (k + 1) * BLOCK]
             macc[s] = macc[s] + weights[:, k * BLOCK : (k + 1) * BLOCK]
 
-    def query_pair(p, carry):
-        one_query(2 * p, 0)
-        one_query(2 * p + 1, 1)
+    def query_group(p, carry):
+        for b in range(GROUP):
+            one_query(GROUP * p + b, b)
         return carry
 
-    lax.fori_loop(0, queries // 2, query_pair, 0)
-    if queries % 2:
-        one_query(queries - 1, 0)
+    lax.fori_loop(0, queries // GROUP, query_group, 0)
+    for b in range(queries % GROUP):
+        one_query(queries - queries % GROUP + b, b)
 
     own = pl.ds(center, per_slab)
     own_num_ref[...] = acc[own]
@@ -195,8 +196,8 @@
             pltpu.VMEM((total, BLOCK, half), jnp.bfloat16),
             pltpu.VMEM((total, half, BLOCK), jnp.float32),
             pltpu.VMEM((total, 1, BLOCK), jnp.float32),
-            pltpu.VMEM((2, BLOCK, K * BLOCK), jnp.float32),
-            pltpu.VMEM((2, K * BLOCK, half), jnp.bfloat16),
+            pltpu.VMEM((GROUP, BLOCK, K * BLOCK), jnp.float32),
+            pltpu.VMEM((GROUP, K * BLOCK, half), jnp.bfloat16),
             pltpu.SemaphoreType.DMA((3, slabs)),
         ],
     )(slot, active.reshape(-1), *window_e, *others, *window_v)

time: 72.7 us -> 72.3 us (level)
  no operation moved by 1% of the time
where the time goes in v13:
time: 72.3 us; the launch traced here: 71.8 us
  starting transfers between devices  35.5 us (49%)
  waiting for transfers between devices  16.7 us (23%)
  Pallas kernels  16.1 us (22%)
  local copies, waits for them, and re-layouts  3.01 us (4%)
    ppermute x12, starting transfers between devices, passed_along(): return lax.ppermute(block, axis, route)  35 us
    ppermute x12, waiting for transfers between devices, passed_along(): return lax.ppermute(block, axis, route)  16.6 us
    pallas_call x1, Pallas kernels, shards(): pl.pallas_call(kernel, out_shape=out_shape, in_specs=[smem, smem] + [vmem...  13.7 us
    pallas_call x1, Pallas kernels, shards(): pl.pallas_call(functools.partial(combine_kernel, per_slab=per_slab, half=...  2.45 us
    unnamed x40, local copies, waits for them, and re-layouts  1.69 us
  transfers between devices with their start and end apart: 17, of which 6 were waited for; matrix products, arithmetic and copies ran while one was open for 2% of the time, Pallas kernels for 0%

profile of v13, /device:TPU:22, one launch (start us, length us, event | category | flops | bytes accessed | tf_op | source)
XLA Modules:
  0.0 71.8 jit_solution(108550039138397544)
XLA Ops:
  0.0 0.0 collective-permute-start.6
  0.0 3.6 %collective-permute-start.1 = (bf16[4,256,128]{2,1,0:T(8,128)(2,1)}, bf16[4,256,128]{2,1,0:T(8,128)(2,1)S(1)}, u32[]{:S(2)}, u32[]{:S(2)}) collective-permute-start(bf16[4,256,128]{2,1,0:T(8,128)(2,1)} %param.5), channel_id=1, source_target_pairs={{0,2},{2,4},{4,6},{6,8},{8,10},{10,12},{12,14},{1,3},{3,5},{5,7},{... | collective-permute-start | bytes 786440 | tf_op jit(solution)/shard_map/ppermute | solution.py:35
  3.6 1.9 %collective-permute-start = (bf16[4,256,128]{2,1,0:T(8,128)(2,1)}, bf16[4,256,128]{2,1,0:T(8,128)(2,1)S(1)}, u32[]{:S(2)}, u32[]{:S(2)}) collective-permute-start(bf16[4,256,128]{2,1,0:T(8,128)(2,1)} %param.5), channel_id=1, source_target_pairs={{0,4},{2,6},{4,8},{6,10},{8,12},{10,14},{1,5},{3,7},{5,9},{7,11},{... | collective-permute-start | bytes 786440 | tf_op jit(solution)/shard_map/ppermute | solution.py:35
  5.5 3.9 %collective-permute-start.3 = (bf16[4,256,128]{2,1,0:T(8,128)(2,1)}, bf16[4,256,128]{2,1,0:T(8,128)(2,1)S(1)}, u32[]{:S(2)}, u32[]{:S(2)}) collective-permute-start(bf16[4,256,128]{2,1,0:T(8,128)(2,1)} %param.5), channel_id=1, source_target_pairs={{4,0},{6,2},{8,4},{10,6},{12,8},{14,10},{5,1},{7,3},{9,5},{11,7},{... | collective-permute-start | bytes 786440 | tf_op jit(solution)/shard_map/ppermute | solution.py:35
  9.5 2.4 %collective-permute-start.2 = (bf16[4,256,128]{2,1,0:T(8,128)(2,1)}, bf16[4,256,128]{2,1,0:T(8,128)(2,1)S(1)}, u32[]{:S(2)}, u32[]{:S(2)}) collective-permute-start(bf16[4,256,128]{2,1,0:T(8,128)(2,1)} %param.5), channel_id=1, source_target_pairs={{2,0},{4,2},{6,4},{8,6},{10,8},{12,10},{14,12},{3,1},{5,3},{7,5},{... | collective-permute-start | bytes 786440 | tf_op jit(solution)/shard_map/ppermute | solution.py:35
  11.9 0.0 collective-permute-done.6.refs_7_
  11.9 4.4 %collective-permute-start.10 = (bf16[4,256,128]{2,1,0:T(8,128)(2,1)}, bf16[4,256,128]{2,1,0:T(8,128)(2,1)S(1)}, u32[]{:S(2)}, u32[]{:S(2)}) collective-permute-start(bf16[4,256,128]{2,1,0:T(8,128)(2,1)} %param.6), channel_id=1, source_target_pairs={{0,2},{2,4},{4,6},{6,8},{8,10},{10,12},{12,14},{1,3},{3,5},{5,7},{... | collective-permute-start | bytes 786440 | tf_op jit(solution)/shard_map/ppermute | solution.py:35
  16.3 0.0 collective-permute-done.1
  16.3 1.9 %collective-permute-start.9 = (bf16[4,256,128]{2,1,0:T(8,128)(2,1)}, bf16[4,256,128]{2,1,0:T(8,128)(2,1)S(1)}, u32[]{:S(2)}, u32[]{:S(2)}) collective-permute-start(bf16[4,256,128]{2,1,0:T(8,128)(2,1)} %param.6), channel_id=1, source_target_pairs={{0,4},{2,6},{4,8},{6,10},{8,12},{10,14},{1,5},{3,7},{5,9},{7,11},{... | collective-permute-start | bytes 786440 | tf_op jit(solution)/shard_map/ppermute | solution.py:35
  18.2 0.0 collective-permute-done
  18.2 0.0 copy-start.6
  18.2 3.9 %collective-permute-start.12 = (bf16[4,256,128]{2,1,0:T(8,128)(2,1)}, bf16[4,256,128]{2,1,0:T(8,128)(2,1)S(1)}, u32[]{:S(2)}, u32[]{:S(2)}) collective-permute-start(bf16[4,256,128]{2,1,0:T(8,128)(2,1)} %param.6), channel_id=1, source_target_pairs={{4,0},{6,2},{8,4},{10,6},{12,8},{14,10},{5,1},{7,3},{9,5},{11,7},{... | collective-permute-start | bytes 786440 | tf_op jit(solution)/shard_map/ppermute | solution.py:35
  22.2 0.1 fusion
  22.2 0.0 collective-permute-done.3
  22.3 1.9 %collective-permute-start.11 = (bf16[4,256,128]{2,1,0:T(8,128)(2,1)}, bf16[4,256,128]{2,1,0:T(8,128)(2,1)S(1)}, u32[]{:S(2)}, u32[]{:S(2)}) collective-permute-start(bf16[4,256,128]{2,1,0:T(8,128)(2,1)} %param.6), channel_id=1, source_target_pairs={{2,0},{4,2},{6,4},{8,6},{10,8},{12,10},{14,12},{3,1},{5,3},{7,5},{... | collective-permute-start | bytes 786440 | tf_op jit(solution)/shard_map/ppermute | solution.py:35
  24.2 0.0 collective-permute-done.2
  24.2 0.0 copy-start.8
  24.2 0.1 collective-permute-start.5
  24.3 3.2 %collective-permute-done.10 = bf16[4,256,128]{2,1,0:T(8,128)(2,1)S(1)} collective-permute-done((bf16[4,256,128]{2,1,0:T(8,128)(2,1)}, bf16[4,256,128]{2,1,0:T(8,128)(2,1)S(1)}, u32[]{:S(2)}, u32[]{:S(2)}) %collective-permute-start.10) | collective-permute-done | bytes 262176 | tf_op jit(solution)/shard_map/ppermute | solution.py:35
  27.5 0.0 collective-permute-start.4
  27.5 0.5 collective-permute-done.9
  28.0 0.0 collective-permute-start.8
  28.0 0.0 collective-permute-done.12
  28.0 0.5 collective-permute-start.7
  28.5 0.7 reshape.62.act_ref
  29.2 0.1 add_clamp_fusion
  29.3 0.7 reshape.50.slot_ref
  29.9 4.1 %collective-permute-done.11 = bf16[4,256,128]{2,1,0:T(8,128)(2,1)S(1)} collective-permute-done((bf16[4,256,128]{2,1,0:T(8,128)(2,1)}, bf16[4,256,128]{2,1,0:T(8,128)(2,1)S(1)}, u32[]{:S(2)}, u32[]{:S(2)}) %collective-permute-start.11) | collective-permute-done | bytes 262176 | tf_op jit(solution)/shard_map/ppermute | solution.py:35
  34.0 0.0 collective-permute-done.5.refs_6_
  34.0 0.0 collective-permute-done.4.refs_5_
  34.1 0.0 collective-permute-done.8.refs_9_
  34.1 0.0 collective-permute-done.7.refs_8_
  34.2 0.6 copy-done.12
  34.7 0.1 copy-done.13
  34.8 0.1 copy-done.14
  34.9 0.1 copy-done.15
  35.0 0.1 copy-done.16
  35.1 13.7 %shard_map.55 = (f32[8,128,128]{2,1,0:T(8,128)}, f32[8,1,128]{2,1,0:T(1,128)}, bf16[1040,128]{1,0:T(8,128)(2,1)}, bf16[1040,128]{1,0:T(8,128)(2,1)}, bf16[1040,1...) custom-call(s32[128]{0:T(128)} %reshape.50.slot_ref, s32[8]{0:T(128)} %reshape.62.act_ref, bf16[8,128,128]{2,1,0:T(8,128)(2,1)} %bitcast.18, ...), custom_call_target="tpu_custom_call" | custom-call | tf_op jit(solution)/shard_map/pallas_call | solution.py:189
  48.8 2.3 %collective-permute-start.13 = (bf16[1040,128]{1,0:T(8,128)(2,1)}, bf16[1040,128]{1,0:T(8,128)(2,1)S(1)}, u32[]{:S(2)}, u32[]{:S(2)}) collective-permute-start(bf16[1040,128]{1,0:T(8,128)(2,1)} %get-tuple-element.13), channel_id=1, source_target_pairs={{4,0},{6,2},{8,4},{10,6},{12,8},{14,10},{5,1},{7,3},{9,5},{11,7},{... | collective-permute-start | bytes 798728 | tf_op jit(solution)/shard_map/ppermute | solution.py:35
  51.2 1.9 %collective-permute-start.14 = (bf16[1040,128]{1,0:T(8,128)(2,1)}, bf16[1040,128]{1,0:T(8,128)(2,1)S(1)}, u32[]{:S(2)}, u32[]{:S(2)}) collective-permute-start(bf16[1040,128]{1,0:T(8,128)(2,1)} %get-tuple-element.14), channel_id=1, source_target_pairs={{2,0},{4,2},{6,4},{8,6},{10,8},{12,10},{14,12},{3,1},{5,3},{7,5},{... | collective-permute-start | bytes 798728 | tf_op jit(solution)/shard_map/ppermute | solution.py:35
  53.1 4.8 %collective-permute-start.15 = (bf16[1040,128]{1,0:T(8,128)(2,1)}, bf16[1040,128]{1,0:T(8,128)(2,1)S(1)}, u32[]{:S(2)}, u32[]{:S(2)}) collective-permute-start(bf16[1040,128]{1,0:T(8,128)(2,1)} %get-tuple-element.15), channel_id=1, source_target_pairs={{0,2},{2,4},{4,6},{6,8},{8,10},{10,12},{12,14},{1,3},{3,5},{5,7},{... | collective-permute-start | bytes 798728 | tf_op jit(solution)/shard_map/ppermute | solution.py:35
  57.9 1.9 %collective-permute-start.16 = (bf16[1040,128]{1,0:T(8,128)(2,1)}, bf16[1040,128]{1,0:T(8,128)(2,1)S(1)}, u32[]{:S(2)}, u32[]{:S(2)}) collective-permute-start(bf16[1040,128]{1,0:T(8,128)(2,1)} %get-tuple-element.16), channel_id=1, source_target_pairs={{0,4},{2,6},{4,8},{6,10},{8,12},{10,14},{1,5},{3,7},{5,9},{7,11},{... | collective-permute-start | bytes 798728 | tf_op jit(solution)/shard_map/ppermute | solution.py:35
  59.9 0.0 collective-permute-done.13.refs_0_
  59.9 3.2 %collective-permute-done.14.refs_1_ = bf16[1040,128]{1,0:T(8,128)(2,1)S(1)} collective-permute-done((bf16[1040,128]{1,0:T(8,128)(2,1)}, bf16[1040,128]{1,0:T(8,128)(2,1)S(1)}, u32[]{:S(2)}, u32[]{:S(2)}) %collective-permute-start.14) | collective-permute-done | bytes 266272 | tf_op jit(solution)/shard_map/ppermute | solution.py:35
  63.1 4.2 %collective-permute-done.15.refs_2_ = bf16[1040,128]{1,0:T(8,128)(2,1)S(1)} collective-permute-done((bf16[1040,128]{1,0:T(8,128)(2,1)}, bf16[1040,128]{1,0:T(8,128)(2,1)S(1)}, u32[]{:S(2)}, u32[]{:S(2)}) %collective-permute-start.15) | collective-permute-done | bytes 266272 | tf_op jit(solution)/shard_map/ppermute | solution.py:35
  67.3 1.4 %collective-permute-done.16.refs_3_ = bf16[1040,128]{1,0:T(8,128)(2,1)S(1)} collective-permute-done((bf16[1040,128]{1,0:T(8,128)(2,1)}, bf16[1040,128]{1,0:T(8,128)(2,1)S(1)}, u32[]{:S(2)}, u32[]{:S(2)}) %collective-permute-start.16) | collective-permute-done | bytes 266272 | tf_op jit(solution)/shard_map/ppermute | solution.py:35
  68.7 0.7 copy-done.3
  69.4 2.5 %shard_map.56 = bf16[8,128,128]{2,1,0:T(8,128)(2,1)} custom-call(f32[8,128,128]{2,1,0:T(8,128)} %get-tuple-element.11.num_ref, f32[8,1,128]{2,1,0:T(1,128)} %get-tuple-element.12.mass_ref, bf16[8,128,128]{2,1,0:T(8,128)(2,1)} %bitcast.12, bf16[1040,128]{1,0:T(8,128)(2,1)} %copy-done, bf16[1040,128]{1,0:T(8,128)(2,1)} %copy-done.1, ...), custom_call_target="tpu_custom_call" | custom-call | tf_op jit(solution)/shard_map/pallas_call | solution.py:209
  (33 shorter events, 0.1 us)
Async XLA Ops:
  0.0 22.2 %copy-start.19 = (s32[4]{0:T(128)S(1)}, s32[4]{0:T(128)}, u32[]{:S(2)}) copy-start(s32[4]{0:T(128)} %param.9) | copy-start | bytes 52
  0.0 11.9 %collective-permute-start.6 = (bf16[8,128,128]{2,1,0:T(8,128)(2,1)}, bf16[8,128,128]{2,1,0:T(8,128)(2,1)S(1)}, u32[]{:S(2)}, u32[]{:S(2)}) collective-permute-start(bf16[8,128,128]{2,1,0:T(8,128)(2,1)} %bitcast.13), channel_id=1, source_target_pairs={{0,1},{1,0},{2,3},{3,2},{4,5},{5,4},{6,7},{7,6},{8,9},{9,8},{10,11... | collective-permute-start | bytes 786440 | tf_op jit(solution)/shard_map/ppermute | solution.py:154
  0.0 16.3 %collective-permute-start.1 = (bf16[4,256,128]{2,1,0:T(8,128)(2,1)}, bf16[4,256,128]{2,1,0:T(8,128)(2,1)S(1)}, u32[]{:S(2)}, u32[]{:S(2)}) collective-permute-start(bf16[4,256,128]{2,1,0:T(8,128)(2,1)} %param.5), channel_id=1, source_target_pairs={{0,2},{2,4},{4,6},{6,8},{8,10},{10,12},{12,14},{1,3},{3,5},{5,7},{... | collective-permute-start | bytes 786440 | tf_op jit(solution)/shard_map/ppermute | solution.py:35
  3.6 14.6 %collective-permute-start = (bf16[4,256,128]{2,1,0:T(8,128)(2,1)}, bf16[4,256,128]{2,1,0:T(8,128)(2,1)S(1)}, u32[]{:S(2)}, u32[]{:S(2)}) collective-permute-start(bf16[4,256,128]{2,1,0:T(8,128)(2,1)} %param.5), channel_id=1, source_target_pairs={{0,4},{2,6},{4,8},{6,10},{8,12},{10,14},{1,5},{3,7},{5,9},{7,11},{... | collective-permute-start | bytes 786440 | tf_op jit(solution)/shard_map/ppermute | solution.py:35
  5.5 16.7 %collective-permute-start.3 = (bf16[4,256,128]{2,1,0:T(8,128)(2,1)}, bf16[4,256,128]{2,1,0:T(8,128)(2,1)S(1)}, u32[]{:S(2)}, u32[]{:S(2)}) collective-permute-start(bf16[4,256,128]{2,1,0:T(8,128)(2,1)} %param.5), channel_id=1, source_target_pairs={{4,0},{6,2},{8,4},{10,6},{12,8},{14,10},{5,1},{7,3},{9,5},{11,7},{... | collective-permute-start | bytes 786440 | tf_op jit(solution)/shard_map/ppermute | solution.py:35
  9.5 14.7 %collective-permute-start.2 = (bf16[4,256,128]{2,1,0:T(8,128)(2,1)}, bf16[4,256,128]{2,1,0:T(8,128)(2,1)S(1)}, u32[]{:S(2)}, u32[]{:S(2)}) collective-permute-start(bf16[4,256,128]{2,1,0:T(8,128)(2,1)} %param.5), channel_id=1, source_target_pairs={{2,0},{4,2},{6,4},{8,6},{10,8},{12,10},{14,12},{3,1},{5,3},{7,5},{... | collective-permute-start | bytes 786440 | tf_op jit(solution)/shard_map/ppermute | solution.py:35
  11.9 22.2 %copy-start.4 = (bf16[8,128,128]{2,1,0:T(8,128)(2,1)}, bf16[8,128,128]{2,1,0:T(8,128)(2,1)S(1)}, u32[]{:S(2)}) copy-start(bf16[8,128,128]{2,1,0:T(8,128)(2,1)S(1)} %collective-permute-done.6.refs_7_) | copy-start | bytes 786436
  11.9 15.6 %collective-permute-start.10 = (bf16[4,256,128]{2,1,0:T(8,128)(2,1)}, bf16[4,256,128]{2,1,0:T(8,128)(2,1)S(1)}, u32[]{:S(2)}, u32[]{:S(2)}) collective-permute-start(bf16[4,256,128]{2,1,0:T(8,128)(2,1)} %param.6), channel_id=1, source_target_pairs={{0,2},{2,4},{4,6},{6,8},{8,10},{10,12},{12,14},{1,3},{3,5},{5,7},{... | collective-permute-start | bytes 786440 | tf_op jit(solution)/shard_map/ppermute | solution.py:35
  16.3 17.8 %copy-start.5 = (bf16[4,256,128]{2,1,0:T(8,128)(2,1)}, bf16[4,256,128]{2,1,0:T(8,128)(2,1)S(1)}, u32[]{:S(2)}) copy-start(bf16[4,256,128]{2,1,0:T(8,128)(2,1)S(1)} %collective-permute-done.1) | copy-start | bytes 786436
  16.3 11.7 %collective-permute-start.9 = (bf16[4,256,128]{2,1,0:T(8,128)(2,1)}, bf16[4,256,128]{2,1,0:T(8,128)(2,1)S(1)}, u32[]{:S(2)}, u32[]{:S(2)}) collective-permute-start(bf16[4,256,128]{2,1,0:T(8,128)(2,1)} %param.6), channel_id=1, source_target_pairs={{0,4},{2,6},{4,8},{6,10},{8,12},{10,14},{1,5},{3,7},{5,9},{7,11},{... | collective-permute-start | bytes 786440 | tf_op jit(solution)/shard_map/ppermute | solution.py:35
  18.2 15.9 %copy-start.6 = (bf16[4,256,128]{2,1,0:T(8,128)(2,1)}, bf16[4,256,128]{2,1,0:T(8,128)(2,1)S(1)}, u32[]{:S(2)}) copy-start(bf16[4,256,128]{2,1,0:T(8,128)(2,1)S(1)} %collective-permute-done) | copy-start | bytes 786436
  18.2 9.8 %collective-permute-start.12 = (bf16[4,256,128]{2,1,0:T(8,128)(2,1)}, bf16[4,256,128]{2,1,0:T(8,128)(2,1)S(1)}, u32[]{:S(2)}, u32[]{:S(2)}) collective-permute-start(bf16[4,256,128]{2,1,0:T(8,128)(2,1)} %param.6), channel_id=1, source_target_pairs={{4,0},{6,2},{8,4},{10,6},{12,8},{14,10},{5,1},{7,3},{9,5},{11,7},{... | collective-permute-start | bytes 786440 | tf_op jit(solution)/shard_map/ppermute | solution.py:35
  22.2 11.9 %copy-start.7 = (bf16[4,256,128]{2,1,0:T(8,128)(2,1)}, bf16[4,256,128]{2,1,0:T(8,128)(2,1)S(1)}, u32[]{:S(2)}) copy-start(bf16[4,256,128]{2,1,0:T(8,128)(2,1)S(1)} %collective-permute-done.3) | copy-start | bytes 786436
  22.3 11.8 %collective-permute-start.11 = (bf16[4,256,128]{2,1,0:T(8,128)(2,1)}, bf16[4,256,128]{2,1,0:T(8,128)(2,1)S(1)}, u32[]{:S(2)}, u32[]{:S(2)}) collective-permute-start(bf16[4,256,128]{2,1,0:T(8,128)(2,1)} %param.6), channel_id=1, source_target_pairs={{2,0},{4,2},{6,4},{8,6},{10,8},{12,10},{14,12},{3,1},{5,3},{7,5},{... | collective-permute-start | bytes 786440 | tf_op jit(solution)/shard_map/ppermute | solution.py:35
  24.2 10.0 %copy-start.8 = (bf16[4,256,128]{2,1,0:T(8,128)(2,1)}, bf16[4,256,128]{2,1,0:T(8,128)(2,1)S(1)}, u32[]{:S(2)}) copy-start(bf16[4,256,128]{2,1,0:T(8,128)(2,1)S(1)} %collective-permute-done.2) | copy-start | bytes 786436
  24.2 9.8 %collective-permute-start.5 = (bf16[8,128,128]{2,1,0:T(8,128)(2,1)S(1)}, bf16[8,128,128]{2,1,0:T(8,128)(2,1)S(1)}, u32[]{:S(2)}, u32[]{:S(2)}) collective-permute-start(bf16[8,128,128]{2,1,0:T(8,128)(2,1)S(1)} %bitcast.15), channel_id=1, source_target_pairs={{0,1},{1,0},{2,3},{3,2},{4,5},{5,4},{6,7},{7,6},{8,9},{9,8},{10,11... | collective-permute-start | bytes 786440 | tf_op jit(solution)/shard_map/ppermute | solution.py:154
  27.5 6.7 %copy-start.9 = (bf16[4,256,128]{2,1,0:T(8,128)(2,1)}, bf16[4,256,128]{2,1,0:T(8,128)(2,1)S(1)}, u32[]{:S(2)}) copy-start(bf16[4,256,128]{2,1,0:T(8,128)(2,1)S(1)} %collective-permute-done.10) | copy-start | bytes 786436
  27.5 1.7 %copy-start.17 = (s32[4,2,16]{2,1,0:T(2,128)S(1)}, s32[4,2,16]{2,1,0:T(2,128)}, u32[]{:S(2)}) copy-start(s32[4,2,16]{2,1,0:T(2,128)} %param.8) | copy-start | bytes 1540
  27.5 1.7 %copy-start.18 = (s32[4,2,16]{2,1,0:T(2,128)S(1)}, s32[4,2,16]{2,1,0:T(2,128)}, u32[]{:S(2)}) copy-start(s32[4,2,16]{2,1,0:T(2,128)} %param.7) | copy-start | bytes 1540
  27.5 6.6 %collective-permute-start.4 = (bf16[8,128,128]{2,1,0:T(8,128)(2,1)S(1)}, bf16[8,128,128]{2,1,0:T(8,128)(2,1)S(1)}, u32[]{:S(2)}, u32[]{:S(2)}) collective-permute-start(bf16[8,128,128]{2,1,0:T(8,128)(2,1)S(1)} %bitcast.17), channel_id=1, source_target_pairs={{0,1},{1,0},{2,3},{3,2},{4,5},{5,4},{6,7},{7,6},{8,9},{9,8},{10,11... | collective-permute-start | bytes 786440 | tf_op jit(solution)/shard_map/ppermute | solution.py:154
  28.0 6.2 %copy-start.10 = (bf16[4,256,128]{2,1,0:T(8,128)(2,1)}, bf16[4,256,128]{2,1,0:T(8,128)(2,1)S(1)}, u32[]{:S(2)}) copy-start(bf16[4,256,128]{2,1,0:T(8,128)(2,1)S(1)} %collective-permute-done.9) | copy-start | bytes 786436
  28.0 6.1 %collective-permute-start.8 = (bf16[8,128,128]{2,1,0:T(8,128)(2,1)S(1)}, bf16[8,128,128]{2,1,0:T(8,128)(2,1)S(1)}, u32[]{:S(2)}, u32[]{:S(2)}) collective-permute-start(bf16[8,128,128]{2,1,0:T(8,128)(2,1)S(1)} %bitcast.19), channel_id=1, source_target_pairs={{0,1},{1,0},{2,3},{3,2},{4,5},{5,4},{6,7},{7,6},{8,9},{9,8},{10,11... | collective-permute-start | bytes 786440 | tf_op jit(solution)/shard_map/ppermute | solution.py:154
  28.0 6.2 %copy-start.11 = (bf16[4,256,128]{2,1,0:T(8,128)(2,1)}, bf16[4,256,128]{2,1,0:T(8,128)(2,1)S(1)}, u32[]{:S(2)}) copy-start(bf16[4,256,128]{2,1,0:T(8,128)(2,1)S(1)} %collective-permute-done.12) | copy-start | bytes 786436
  28.0 6.1 %collective-permute-start.7 = (bf16[8,128,128]{2,1,0:T(8,128)(2,1)S(1)}, bf16[8,128,128]{2,1,0:T(8,128)(2,1)S(1)}, u32[]{:S(2)}, u32[]{:S(2)}) collective-permute-start(bf16[8,128,128]{2,1,0:T(8,128)(2,1)S(1)} %bitcast.21), channel_id=1, source_target_pairs={{0,1},{1,0},{2,3},{3,2},{4,5},{5,4},{6,7},{7,6},{8,9},{9,8},{10,11... | collective-permute-start | bytes 786440 | tf_op jit(solution)/shard_map/ppermute | solution.py:154
  34.0 0.7 copy-start.12
  34.0 0.8 %copy-start.13 = (bf16[8,128,128]{2,1,0:T(8,128)(2,1)}, bf16[8,128,128]{2,1,0:T(8,128)(2,1)S(1)}, u32[]{:S(2)}) copy-start(bf16[8,128,128]{2,1,0:T(8,128)(2,1)S(1)} %collective-permute-done.5.refs_6_) | copy-start | bytes 786436
  34.0 0.9 %copy-start.14 = (bf16[8,128,128]{2,1,0:T(8,128)(2,1)}, bf16[8,128,128]{2,1,0:T(8,128)(2,1)S(1)}, u32[]{:S(2)}) copy-start(bf16[8,128,128]{2,1,0:T(8,128)(2,1)S(1)} %collective-permute-done.4.refs_5_) | copy-start | bytes 786436
  34.1 0.9 %copy-start.15 = (bf16[8,128,128]{2,1,0:T(8,128)(2,1)}, bf16[8,128,128]{2,1,0:T(8,128)(2,1)S(1)}, u32[]{:S(2)}) copy-start(bf16[8,128,128]{2,1,0:T(8,128)(2,1)S(1)} %collective-permute-done.8.refs_9_) | copy-start | bytes 786436
  34.1 1.0 %copy-start.16 = (bf16[8,128,128]{2,1,0:T(8,128)(2,1)}, bf16[8,128,128]{2,1,0:T(8,128)(2,1)S(1)}, u32[]{:S(2)}) copy-start(bf16[8,128,128]{2,1,0:T(8,128)(2,1)S(1)} %collective-permute-done.7.refs_8_) | copy-start | bytes 786436
  48.8 11.0 %collective-permute-start.13 = (bf16[1040,128]{1,0:T(8,128)(2,1)}, bf16[1040,128]{1,0:T(8,128)(2,1)S(1)}, u32[]{:S(2)}, u32[]{:S(2)}) collective-permute-start(bf16[1040,128]{1,0:T(8,128)(2,1)} %get-tuple-element.13), channel_id=1, source_target_pairs={{4,0},{6,2},{8,4},{10,6},{12,8},{14,10},{5,1},{7,3},{9,5},{11,7},{... | collective-permute-start | bytes 798728 | tf_op jit(solution)/shard_map/ppermute | solution.py:35
  51.2 11.9 %collective-permute-start.14 = (bf16[1040,128]{1,0:T(8,128)(2,1)}, bf16[1040,128]{1,0:T(8,128)(2,1)S(1)}, u32[]{:S(2)}, u32[]{:S(2)}) collective-permute-start(bf16[1040,128]{1,0:T(8,128)(2,1)} %get-tuple-element.14), channel_id=1, source_target_pairs={{2,0},{4,2},{6,4},{8,6},{10,8},{12,10},{14,12},{3,1},{5,3},{7,5},{... | collective-permute-start | bytes 798728 | tf_op jit(solution)/shard_map/ppermute | solution.py:35
  53.1 14.2 %collective-permute-start.15 = (bf16[1040,128]{1,0:T(8,128)(2,1)}, bf16[1040,128]{1,0:T(8,128)(2,1)S(1)}, u32[]{:S(2)}, u32[]{:S(2)}) collective-permute-start(bf16[1040,128]{1,0:T(8,128)(2,1)} %get-tuple-element.15), channel_id=1, source_target_pairs={{0,2},{2,4},{4,6},{6,8},{8,10},{10,12},{12,14},{1,3},{3,5},{5,7},{... | collective-permute-start | bytes 798728 | tf_op jit(solution)/shard_map/ppermute | solution.py:35
  57.9 10.8 %collective-permute-start.16 = (bf16[1040,128]{1,0:T(8,128)(2,1)}, bf16[1040,128]{1,0:T(8,128)(2,1)S(1)}, u32[]{:S(2)}, u32[]{:S(2)}) collective-permute-start(bf16[1040,128]{1,0:T(8,128)(2,1)} %get-tuple-element.16), channel_id=1, source_target_pairs={{0,4},{2,6},{4,8},{6,10},{8,12},{10,14},{1,5},{3,7},{5,9},{7,11},{... | collective-permute-start | bytes 798728 | tf_op jit(solution)/shard_map/ppermute | solution.py:35
  59.9 8.8 %copy-start = (bf16[1040,128]{1,0:T(8,128)(2,1)}, bf16[1040,128]{1,0:T(8,128)(2,1)S(1)}, u32[]{:S(2)}) copy-start(bf16[1040,128]{1,0:T(8,128)(2,1)S(1)} %collective-permute-done.13.refs_0_) | copy-start | bytes 798724
  63.1 5.6 %copy-start.1 = (bf16[1040,128]{1,0:T(8,128)(2,1)}, bf16[1040,128]{1,0:T(8,128)(2,1)S(1)}, u32[]{:S(2)}) copy-start(bf16[1040,128]{1,0:T(8,128)(2,1)S(1)} %collective-permute-done.14.refs_1_) | copy-start | bytes 798724
  67.3 1.4 %copy-start.2 = (bf16[1040,128]{1,0:T(8,128)(2,1)}, bf16[1040,128]{1,0:T(8,128)(2,1)S(1)}, u32[]{:S(2)}) copy-start(bf16[1040,128]{1,0:T(8,128)(2,1)S(1)} %collective-permute-done.15.refs_2_) | copy-start | bytes 798724
  68.7 0.7 copy-start.3

commit v14 on v13

--- a/solution.py
+++ b/solution.py
@@ -57,6 +57,10 @@
         c.start()
     acc[...] = jnp.zeros(acc.shape, acc.dtype)
     macc[...] = jnp.zeros(macc.shape, macc.dtype)
+    if not halo:
+        own_values = sources[1][center // per_slab]
+        for j in range(per_slab):
+            acc[center + j] = own_values[j].astype(jnp.float32).T
     for c in copies:
         c.wait()
 
@@ -111,7 +115,7 @@
         ref[per_slab * half :, :] = jnp.concatenate(spread, axis=0).astype(jnp.bfloat16)
 
 
-def combine_kernel(num_ref, mass_ref, values_ref, *refs, per_slab, half):
+def combine_kernel(num_ref, mass_ref, *refs, per_slab, half):
     arrived_refs = refs[:-1]
     out_ref = refs[-1]
     tail = per_slab * half
@@ -122,8 +126,7 @@
         for ref, rows in zip(arrived_refs, masses):
             numer = numer + ref[j * half : (j + 1) * half, :].astype(jnp.float32)
             mass = mass + rows[j : j + 1]
-        own = values_ref[j].astype(jnp.float32).T
-        result = (numer + own) / (mass + 1.0)
+        result = numer / (mass + 1.0)
         out_ref[j] = result.T.astype(jnp.bfloat16)
 
 
@@ -209,9 +212,9 @@
         result = pl.pallas_call(
             functools.partial(combine_kernel, per_slab=per_slab, half=half),
             out_shape=jax.ShapeDtypeStruct((per_slab, BLOCK, half), jnp.bfloat16),
-            in_specs=[vmem] * (3 + len(arrivals)),
+            in_specs=[vmem] * (2 + len(arrivals)),
             out_specs=vmem,
-        )(own_num, own_mass, values.reshape(per_slab, BLOCK, half), *arrivals)
+        )(own_num, own_mass, *arrivals)
         return result.reshape(frames, band_rows, half)
     for offset, outgoing in zip(offsets, remote):
         arrived = passed_along(outgoing, "frame", offset).astype(jnp.float32)

time: 72.3 us -> 72.2 us (level)
  no operation moved by 1% of the time
where the time goes in v14:
time: 72.2 us; the launch traced here: 71.8 us
  starting transfers between devices  35.5 us (49%)
  waiting for transfers between devices  16.6 us (23%)
  Pallas kernels  16.1 us (22%)
  local copies, waits for them, and re-layouts  3.01 us (4%)
    ppermute x12, starting transfers between devices, passed_along(): return lax.ppermute(block, axis, route)  35 us
    ppermute x12, waiting for transfers between devices, passed_along(): return lax.ppermute(block, axis, route)  16.6 us
    pallas_call x1, Pallas kernels, shards(): pl.pallas_call(kernel, out_shape=out_shape, in_specs=[smem, smem] + [vmem...  13.8 us
    pallas_call x1, Pallas kernels, shards(): pl.pallas_call(functools.partial(combine_kernel, per_slab=per_slab, half=...  2.31 us
    unnamed x40, local copies, waits for them, and re-layouts  1.69 us
  transfers between devices with their start and end apart: 17, of which 6 were waited for; matrix products, arithmetic and copies ran while one was open for 2% of the time, Pallas kernels for 0%

profile of v14, /device:TPU:22, one launch (start us, length us, event | category | flops | bytes accessed | tf_op | source)
XLA Modules:
  0.0 71.8 jit_solution(5807139132881242120)
XLA Ops:
  0.0 0.0 collective-permute-start.6
  0.0 3.6 %collective-permute-start.1 = (bf16[4,256,128]{2,1,0:T(8,128)(2,1)}, bf16[4,256,128]{2,1,0:T(8,128)(2,1)S(1)}, u32[]{:S(2)}, u32[]{:S(2)}) collective-permute-start(bf16[4,256,128]{2,1,0:T(8,128)(2,1)} %param.5), channel_id=1, source_target_pairs={{0,2},{2,4},{4,6},{6,8},{8,10},{10,12},{12,14},{1,3},{3,5},{5,7},{... | collective-permute-start | bytes 786440 | tf_op jit(solution)/shard_map/ppermute | solution.py:35
  3.6 1.9 %collective-permute-start = (bf16[4,256,128]{2,1,0:T(8,128)(2,1)}, bf16[4,256,128]{2,1,0:T(8,128)(2,1)S(1)}, u32[]{:S(2)}, u32[]{:S(2)}) collective-permute-start(bf16[4,256,128]{2,1,0:T(8,128)(2,1)} %param.5), channel_id=1, source_target_pairs={{0,4},{2,6},{4,8},{6,10},{8,12},{10,14},{1,5},{3,7},{5,9},{7,11},{... | collective-permute-start | bytes 786440 | tf_op jit(solution)/shard_map/ppermute | solution.py:35
  5.5 3.9 %collective-permute-start.3 = (bf16[4,256,128]{2,1,0:T(8,128)(2,1)}, bf16[4,256,128]{2,1,0:T(8,128)(2,1)S(1)}, u32[]{:S(2)}, u32[]{:S(2)}) collective-permute-start(bf16[4,256,128]{2,1,0:T(8,128)(2,1)} %param.5), channel_id=1, source_target_pairs={{4,0},{6,2},{8,4},{10,6},{12,8},{14,10},{5,1},{7,3},{9,5},{11,7},{... | collective-permute-start | bytes 786440 | tf_op jit(solution)/shard_map/ppermute | solution.py:35
  9.5 2.4 %collective-permute-start.2 = (bf16[4,256,128]{2,1,0:T(8,128)(2,1)}, bf16[4,256,128]{2,1,0:T(8,128)(2,1)S(1)}, u32[]{:S(2)}, u32[]{:S(2)}) collective-permute-start(bf16[4,256,128]{2,1,0:T(8,128)(2,1)} %param.5), channel_id=1, source_target_pairs={{2,0},{4,2},{6,4},{8,6},{10,8},{12,10},{14,12},{3,1},{5,3},{7,5},{... | collective-permute-start | bytes 786440 | tf_op jit(solution)/shard_map/ppermute | solution.py:35
  11.9 0.0 collective-permute-done.6.refs_7_
  11.9 4.4 %collective-permute-start.10 = (bf16[4,256,128]{2,1,0:T(8,128)(2,1)}, bf16[4,256,128]{2,1,0:T(8,128)(2,1)S(1)}, u32[]{:S(2)}, u32[]{:S(2)}) collective-permute-start(bf16[4,256,128]{2,1,0:T(8,128)(2,1)} %param.6), channel_id=1, source_target_pairs={{0,2},{2,4},{4,6},{6,8},{8,10},{10,12},{12,14},{1,3},{3,5},{5,7},{... | collective-permute-start | bytes 786440 | tf_op jit(solution)/shard_map/ppermute | solution.py:35
  16.3 0.0 collective-permute-done.1
  16.3 0.0 copy-start.5
  16.3 1.9 %collective-permute-start.9 = (bf16[4,256,128]{2,1,0:T(8,128)(2,1)}, bf16[4,256,128]{2,1,0:T(8,128)(2,1)S(1)}, u32[]{:S(2)}, u32[]{:S(2)}) collective-permute-start(bf16[4,256,128]{2,1,0:T(8,128)(2,1)} %param.6), channel_id=1, source_target_pairs={{0,4},{2,6},{4,8},{6,10},{8,12},{10,14},{1,5},{3,7},{5,9},{7,11},{... | collective-permute-start | bytes 786440 | tf_op jit(solution)/shard_map/ppermute | solution.py:35
  18.2 0.0 collective-permute-done
  18.2 0.0 copy-start.6
  18.2 3.9 %collective-permute-start.12 = (bf16[4,256,128]{2,1,0:T(8,128)(2,1)}, bf16[4,256,128]{2,1,0:T(8,128)(2,1)S(1)}, u32[]{:S(2)}, u32[]{:S(2)}) collective-permute-start(bf16[4,256,128]{2,1,0:T(8,128)(2,1)} %param.6), channel_id=1, source_target_pairs={{4,0},{6,2},{8,4},{10,6},{12,8},{14,10},{5,1},{7,3},{9,5},{11,7},{... | collective-permute-start | bytes 786440 | tf_op jit(solution)/shard_map/ppermute | solution.py:35
  22.2 0.1 fusion
  22.2 0.0 collective-permute-done.3
  22.3 1.9 %collective-permute-start.11 = (bf16[4,256,128]{2,1,0:T(8,128)(2,1)}, bf16[4,256,128]{2,1,0:T(8,128)(2,1)S(1)}, u32[]{:S(2)}, u32[]{:S(2)}) collective-permute-start(bf16[4,256,128]{2,1,0:T(8,128)(2,1)} %param.6), channel_id=1, source_target_pairs={{2,0},{4,2},{6,4},{8,6},{10,8},{12,10},{14,12},{3,1},{5,3},{7,5},{... | collective-permute-start | bytes 786440 | tf_op jit(solution)/shard_map/ppermute | solution.py:35
  24.2 0.0 collective-permute-done.2
  24.2 0.1 collective-permute-start.5
  24.3 3.2 %collective-permute-done.10 = bf16[4,256,128]{2,1,0:T(8,128)(2,1)S(1)} collective-permute-done((bf16[4,256,128]{2,1,0:T(8,128)(2,1)}, bf16[4,256,128]{2,1,0:T(8,128)(2,1)S(1)}, u32[]{:S(2)}, u32[]{:S(2)}) %collective-permute-start.10) | collective-permute-done | bytes 262176 | tf_op jit(solution)/shard_map/ppermute | solution.py:35
  27.5 0.0 collective-permute-start.4
  27.5 0.5 collective-permute-done.9
  28.0 0.0 collective-permute-start.8
  28.0 0.0 collective-permute-done.12
  28.0 0.5 collective-permute-start.7
  28.5 0.7 reshape.61.act_ref
  29.2 0.1 add_clamp_fusion
  29.3 0.7 reshape.49.slot_ref
  29.9 4.1 %collective-permute-done.11 = bf16[4,256,128]{2,1,0:T(8,128)(2,1)S(1)} collective-permute-done((bf16[4,256,128]{2,1,0:T(8,128)(2,1)}, bf16[4,256,128]{2,1,0:T(8,128)(2,1)S(1)}, u32[]{:S(2)}, u32[]{:S(2)}) %collective-permute-start.11) | collective-permute-done | bytes 262176 | tf_op jit(solution)/shard_map/ppermute | solution.py:35
  34.0 0.0 collective-permute-done.5.refs_6_
  34.0 0.0 collective-permute-done.4.refs_5_
  34.1 0.0 collective-permute-done.8.refs_9_
  34.1 0.0 collective-permute-done.7.refs_8_
  34.2 0.6 copy-done.12
  34.7 0.1 copy-done.13
  34.8 0.1 copy-done.14
  34.9 0.1 copy-done.15
  35.0 0.1 copy-done.16
  35.1 13.8 %shard_map.55 = (f32[8,128,128]{2,1,0:T(8,128)}, f32[8,1,128]{2,1,0:T(1,128)}, bf16[1040,128]{1,0:T(8,128)(2,1)}, bf16[1040,128]{1,0:T(8,128)(2,1)}, bf16[1040,1...) custom-call(s32[128]{0:T(128)} %reshape.49.slot_ref, s32[8]{0:T(128)} %reshape.61.act_ref, bf16[8,128,128]{2,1,0:T(8,128)(2,1)} %bitcast.17, ...), custom_call_target="tpu_custom_call" | custom-call | tf_op jit(solution)/shard_map/pallas_call | solution.py:192
  48.9 2.3 %collective-permute-start.13 = (bf16[1040,128]{1,0:T(8,128)(2,1)}, bf16[1040,128]{1,0:T(8,128)(2,1)S(1)}, u32[]{:S(2)}, u32[]{:S(2)}) collective-permute-start(bf16[1040,128]{1,0:T(8,128)(2,1)} %get-tuple-element.13), channel_id=1, source_target_pairs={{4,0},{6,2},{8,4},{10,6},{12,8},{14,10},{5,1},{7,3},{9,5},{11,7},{... | collective-permute-start | bytes 798728 | tf_op jit(solution)/shard_map/ppermute | solution.py:35
  51.3 1.9 %collective-permute-start.14 = (bf16[1040,128]{1,0:T(8,128)(2,1)}, bf16[1040,128]{1,0:T(8,128)(2,1)S(1)}, u32[]{:S(2)}, u32[]{:S(2)}) collective-permute-start(bf16[1040,128]{1,0:T(8,128)(2,1)} %get-tuple-element.14), channel_id=1, source_target_pairs={{2,0},{4,2},{6,4},{8,6},{10,8},{12,10},{14,12},{3,1},{5,3},{7,5},{... | collective-permute-start | bytes 798728 | tf_op jit(solution)/shard_map/ppermute | solution.py:35
  53.2 4.8 %collective-permute-start.15 = (bf16[1040,128]{1,0:T(8,128)(2,1)}, bf16[1040,128]{1,0:T(8,128)(2,1)S(1)}, u32[]{:S(2)}, u32[]{:S(2)}) collective-permute-start(bf16[1040,128]{1,0:T(8,128)(2,1)} %get-tuple-element.15), channel_id=1, source_target_pairs={{0,2},{2,4},{4,6},{6,8},{8,10},{10,12},{12,14},{1,3},{3,5},{5,7},{... | collective-permute-start | bytes 798728 | tf_op jit(solution)/shard_map/ppermute | solution.py:35
  58.0 1.9 %collective-permute-start.16 = (bf16[1040,128]{1,0:T(8,128)(2,1)}, bf16[1040,128]{1,0:T(8,128)(2,1)S(1)}, u32[]{:S(2)}, u32[]{:S(2)}) collective-permute-start(bf16[1040,128]{1,0:T(8,128)(2,1)} %get-tuple-element.16), channel_id=1, source_target_pairs={{0,4},{2,6},{4,8},{6,10},{8,12},{10,14},{1,5},{3,7},{5,9},{7,11},{... | collective-permute-start | bytes 798728 | tf_op jit(solution)/shard_map/ppermute | solution.py:35
  59.9 0.0 collective-permute-done.13.refs_0_
  60.0 3.2 %collective-permute-done.14.refs_1_ = bf16[1040,128]{1,0:T(8,128)(2,1)S(1)} collective-permute-done((bf16[1040,128]{1,0:T(8,128)(2,1)}, bf16[1040,128]{1,0:T(8,128)(2,1)S(1)}, u32[]{:S(2)}, u32[]{:S(2)}) %collective-permute-start.14) | collective-permute-done | bytes 266272 | tf_op jit(solution)/shard_map/ppermute | solution.py:35
  63.2 4.2 %collective-permute-done.15.refs_2_ = bf16[1040,128]{1,0:T(8,128)(2,1)S(1)} collective-permute-done((bf16[1040,128]{1,0:T(8,128)(2,1)}, bf16[1040,128]{1,0:T(8,128)(2,1)S(1)}, u32[]{:S(2)}, u32[]{:S(2)}) %collective-permute-start.15) | collective-permute-done | bytes 266272 | tf_op jit(solution)/shard_map/ppermute | solution.py:35
  67.4 1.4 %collective-permute-done.16.refs_3_ = bf16[1040,128]{1,0:T(8,128)(2,1)S(1)} collective-permute-done((bf16[1040,128]{1,0:T(8,128)(2,1)}, bf16[1040,128]{1,0:T(8,128)(2,1)S(1)}, u32[]{:S(2)}, u32[]{:S(2)}) %collective-permute-start.16) | collective-permute-done | bytes 266272 | tf_op jit(solution)/shard_map/ppermute | solution.py:35
  68.8 0.7 copy-done.3
  69.5 2.3 %shard_map.56 = bf16[8,128,128]{2,1,0:T(8,128)(2,1)} custom-call(f32[8,128,128]{2,1,0:T(8,128)} %get-tuple-element.11.num_ref, f32[8,1,128]{2,1,0:T(1,128)} %get-tuple-element.12.mass_ref, bf16[1040,128]{1,0:T(8,128)(2,1)} %copy-done, bf16[1040,128]{1,0:T(8,128)(2,1)} %copy-done.1, bf16[1040,128]{1,0:T(8,128)(2,1)} %copy-done.2, bf16[1040,128]{1,0:T(8,128)(2,1)} %copy-done.3), custom_call_target="tpu_custom_call" | custom-call | tf_op jit(solution)/shard_map/pallas_call | solution.py:212
  (33 shorter events, 0.1 us)
Async XLA Ops:
  0.0 22.2 %copy-start.19 = (s32[4]{0:T(128)S(1)}, s32[4]{0:T(128)}, u32[]{:S(2)}) copy-start(s32[4]{0:T(128)} %param.9) | copy-start | bytes 52
  0.0 11.9 %collective-permute-start.6 = (bf16[8,128,128]{2,1,0:T(8,128)(2,1)}, bf16[8,128,128]{2,1,0:T(8,128)(2,1)S(1)}, u32[]{:S(2)}, u32[]{:S(2)}) collective-permute-start(bf16[8,128,128]{2,1,0:T(8,128)(2,1)} %bitcast.11), channel_id=1, source_target_pairs={{0,1},{1,0},{2,3},{3,2},{4,5},{5,4},{6,7},{7,6},{8,9},{9,8},{10,11... | collective-permute-start | bytes 786440 | tf_op jit(solution)/shard_map/ppermute | solution.py:157
  0.0 16.3 %collective-permute-start.1 = (bf16[4,256,128]{2,1,0:T(8,128)(2,1)}, bf16[4,256,128]{2,1,0:T(8,128)(2,1)S(1)}, u32[]{:S(2)}, u32[]{:S(2)}) collective-permute-start(bf16[4,256,128]{2,1,0:T(8,128)(2,1)} %param.5), channel_id=1, source_target_pairs={{0,2},{2,4},{4,6},{6,8},{8,10},{10,12},{12,14},{1,3},{3,5},{5,7},{... | collective-permute-start | bytes 786440 | tf_op jit(solution)/shard_map/ppermute | solution.py:35
  3.6 14.6 %collective-permute-start = (bf16[4,256,128]{2,1,0:T(8,128)(2,1)}, bf16[4,256,128]{2,1,0:T(8,128)(2,1)S(1)}, u32[]{:S(2)}, u32[]{:S(2)}) collective-permute-start(bf16[4,256,128]{2,1,0:T(8,128)(2,1)} %param.5), channel_id=1, source_target_pairs={{0,4},{2,6},{4,8},{6,10},{8,12},{10,14},{1,5},{3,7},{5,9},{7,11},{... | collective-permute-start | bytes 786440 | tf_op jit(solution)/shard_map/ppermute | solution.py:35
  5.5 16.7 %collective-permute-start.3 = (bf16[4,256,128]{2,1,0:T(8,128)(2,1)}, bf16[4,256,128]{2,1,0:T(8,128)(2,1)S(1)}, u32[]{:S(2)}, u32[]{:S(2)}) collective-permute-start(bf16[4,256,128]{2,1,0:T(8,128)(2,1)} %param.5), channel_id=1, source_target_pairs={{4,0},{6,2},{8,4},{10,6},{12,8},{14,10},{5,1},{7,3},{9,5},{11,7},{... | collective-permute-start | bytes 786440 | tf_op jit(solution)/shard_map/ppermute | solution.py:35
  9.5 14.7 %collective-permute-start.2 = (bf16[4,256,128]{2,1,0:T(8,128)(2,1)}, bf16[4,256,128]{2,1,0:T(8,128)(2,1)S(1)}, u32[]{:S(2)}, u32[]{:S(2)}) collective-permute-start(bf16[4,256,128]{2,1,0:T(8,128)(2,1)} %param.5), channel_id=1, source_target_pairs={{2,0},{4,2},{6,4},{8,6},{10,8},{12,10},{14,12},{3,1},{5,3},{7,5},{... | collective-permute-start | bytes 786440 | tf_op jit(solution)/shard_map/ppermute | solution.py:35
  11.9 22.2 %copy-start.4 = (bf16[8,128,128]{2,1,0:T(8,128)(2,1)}, bf16[8,128,128]{2,1,0:T(8,128)(2,1)S(1)}, u32[]{:S(2)}) copy-start(bf16[8,128,128]{2,1,0:T(8,128)(2,1)S(1)} %collective-permute-done.6.refs_7_) | copy-start | bytes 786436
  11.9 15.6 %collective-permute-start.10 = (bf16[4,256,128]{2,1,0:T(8,128)(2,1)}, bf16[4,256,128]{2,1,0:T(8,128)(2,1)S(1)}, u32[]{:S(2)}, u32[]{:S(2)}) collective-permute-start(bf16[4,256,128]{2,1,0:T(8,128)(2,1)} %param.6), channel_id=1, source_target_pairs={{0,2},{2,4},{4,6},{6,8},{8,10},{10,12},{12,14},{1,3},{3,5},{5,7},{... | collective-permute-start | bytes 786440 | tf_op jit(solution)/shard_map/ppermute | solution.py:35
  16.3 17.8 %copy-start.5 = (bf16[4,256,128]{2,1,0:T(8,128)(2,1)}, bf16[4,256,128]{2,1,0:T(8,128)(2,1)S(1)}, u32[]{:S(2)}) copy-start(bf16[4,256,128]{2,1,0:T(8,128)(2,1)S(1)} %collective-permute-done.1) | copy-start | bytes 786436
  16.3 11.7 %collective-permute-start.9 = (bf16[4,256,128]{2,1,0:T(8,128)(2,1)}, bf16[4,256,128]{2,1,0:T(8,128)(2,1)S(1)}, u32[]{:S(2)}, u32[]{:S(2)}) collective-permute-start(bf16[4,256,128]{2,1,0:T(8,128)(2,1)} %param.6), channel_id=1, source_target_pairs={{0,4},{2,6},{4,8},{6,10},{8,12},{10,14},{1,5},{3,7},{5,9},{7,11},{... | collective-permute-start | bytes 786440 | tf_op jit(solution)/shard_map/ppermute | solution.py:35
  18.2 15.9 %copy-start.6 = (bf16[4,256,128]{2,1,0:T(8,128)(2,1)}, bf16[4,256,128]{2,1,0:T(8,128)(2,1)S(1)}, u32[]{:S(2)}) copy-start(bf16[4,256,128]{2,1,0:T(8,128)(2,1)S(1)} %collective-permute-done) | copy-start | bytes 786436
  18.2 9.8 %collective-permute-start.12 = (bf16[4,256,128]{2,1,0:T(8,128)(2,1)}, bf16[4,256,128]{2,1,0:T(8,128)(2,1)S(1)}, u32[]{:S(2)}, u32[]{:S(2)}) collective-permute-start(bf16[4,256,128]{2,1,0:T(8,128)(2,1)} %param.6), channel_id=1, source_target_pairs={{4,0},{6,2},{8,4},{10,6},{12,8},{14,10},{5,1},{7,3},{9,5},{11,7},{... | collective-permute-start | bytes 786440 | tf_op jit(solution)/shard_map/ppermute | solution.py:35
  22.2 11.9 %copy-start.7 = (bf16[4,256,128]{2,1,0:T(8,128)(2,1)}, bf16[4,256,128]{2,1,0:T(8,128)(2,1)S(1)}, u32[]{:S(2)}) copy-start(bf16[4,256,128]{2,1,0:T(8,128)(2,1)S(1)} %collective-permute-done.3) | copy-start | bytes 786436
  22.3 11.8 %collective-permute-start.11 = (bf16[4,256,128]{2,1,0:T(8,128)(2,1)}, bf16[4,256,128]{2,1,0:T(8,128)(2,1)S(1)}, u32[]{:S(2)}, u32[]{:S(2)}) collective-permute-start(bf16[4,256,128]{2,1,0:T(8,128)(2,1)} %param.6), channel_id=1, source_target_pairs={{2,0},{4,2},{6,4},{8,6},{10,8},{12,10},{14,12},{3,1},{5,3},{7,5},{... | collective-permute-start | bytes 786440 | tf_op jit(solution)/shard_map/ppermute | solution.py:35
  24.2 10.0 %copy-start.8 = (bf16[4,256,128]{2,1,0:T(8,128)(2,1)}, bf16[4,256,128]{2,1,0:T(8,128)(2,1)S(1)}, u32[]{:S(2)}) copy-start(bf16[4,256,128]{2,1,0:T(8,128)(2,1)S(1)} %collective-permute-done.2) | copy-start | bytes 786436
  24.2 9.8 %collective-permute-start.5 = (bf16[8,128,128]{2,1,0:T(8,128)(2,1)S(1)}, bf16[8,128,128]{2,1,0:T(8,128)(2,1)S(1)}, u32[]{:S(2)}, u32[]{:S(2)}) collective-permute-start(bf16[8,128,128]{2,1,0:T(8,128)(2,1)S(1)} %bitcast.14), channel_id=1, source_target_pairs={{0,1},{1,0},{2,3},{3,2},{4,5},{5,4},{6,7},{7,6},{8,9},{9,8},{10,11... | collective-permute-start | bytes 786440 | tf_op jit(solution)/shard_map/ppermute | solution.py:157
  27.5 6.7 %copy-start.9 = (bf16[4,256,128]{2,1,0:T(8,128)(2,1)}, bf16[4,256,128]{2,1,0:T(8,128)(2,1)S(1)}, u32[]{:S(2)}) copy-start(bf16[4,256,128]{2,1,0:T(8,128)(2,1)S(1)} %collective-permute-done.10) | copy-start | bytes 786436
  27.5 1.7 %copy-start.17 = (s32[4,2,16]{2,1,0:T(2,128)S(1)}, s32[4,2,16]{2,1,0:T(2,128)}, u32[]{:S(2)}) copy-start(s32[4,2,16]{2,1,0:T(2,128)} %param.8) | copy-start | bytes 1540
  27.5 1.7 %copy-start.18 = (s32[4,2,16]{2,1,0:T(2,128)S(1)}, s32[4,2,16]{2,1,0:T(2,128)}, u32[]{:S(2)}) copy-start(s32[4,2,16]{2,1,0:T(2,128)} %param.7) | copy-start | bytes 1540
  27.5 6.6 %collective-permute-start.4 = (bf16[8,128,128]{2,1,0:T(8,128)(2,1)S(1)}, bf16[8,128,128]{2,1,0:T(8,128)(2,1)S(1)}, u32[]{:S(2)}, u32[]{:S(2)}) collective-permute-start(bf16[8,128,128]{2,1,0:T(8,128)(2,1)S(1)} %bitcast.16), channel_id=1, source_target_pairs={{0,1},{1,0},{2,3},{3,2},{4,5},{5,4},{6,7},{7,6},{8,9},{9,8},{10,11... | collective-permute-start | bytes 786440 | tf_op jit(solution)/shard_map/ppermute | solution.py:157
  28.0 6.2 %copy-start.10 = (bf16[4,256,128]{2,1,0:T(8,128)(2,1)}, bf16[4,256,128]{2,1,0:T(8,128)(2,1)S(1)}, u32[]{:S(2)}) copy-start(bf16[4,256,128]{2,1,0:T(8,128)(2,1)S(1)} %collective-permute-done.9) | copy-start | bytes 786436
  28.0 6.1 %collective-permute-start.8 = (bf16[8,128,128]{2,1,0:T(8,128)(2,1)S(1)}, bf16[8,128,128]{2,1,0:T(8,128)(2,1)S(1)}, u32[]{:S(2)}, u32[]{:S(2)}) collective-permute-start(bf16[8,128,128]{2,1,0:T(8,128)(2,1)S(1)} %bitcast.18), channel_id=1, source_target_pairs={{0,1},{1,0},{2,3},{3,2},{4,5},{5,4},{6,7},{7,6},{8,9},{9,8},{10,11... | collective-permute-start | bytes 786440 | tf_op jit(solution)/shard_map/ppermute | solution.py:157
  28.0 6.2 %copy-start.11 = (bf16[4,256,128]{2,1,0:T(8,128)(2,1)}, bf16[4,256,128]{2,1,0:T(8,128)(2,1)S(1)}, u32[]{:S(2)}) copy-start(bf16[4,256,128]{2,1,0:T(8,128)(2,1)S(1)} %collective-permute-done.12) | copy-start | bytes 786436
  28.0 6.1 %collective-permute-start.7 = (bf16[8,128,128]{2,1,0:T(8,128)(2,1)S(1)}, bf16[8,128,128]{2,1,0:T(8,128)(2,1)S(1)}, u32[]{:S(2)}, u32[]{:S(2)}) collective-permute-start(bf16[8,128,128]{2,1,0:T(8,128)(2,1)S(1)} %bitcast.20), channel_id=1, source_target_pairs={{0,1},{1,0},{2,3},{3,2},{4,5},{5,4},{6,7},{7,6},{8,9},{9,8},{10,11... | collective-permute-start | bytes 786440 | tf_op jit(solution)/shard_map/ppermute | solution.py:157
  34.0 0.7 copy-start.12
  34.0 0.8 %copy-start.13 = (bf16[8,128,128]{2,1,0:T(8,128)(2,1)}, bf16[8,128,128]{2,1,0:T(8,128)(2,1)S(1)}, u32[]{:S(2)}) copy-start(bf16[8,128,128]{2,1,0:T(8,128)(2,1)S(1)} %collective-permute-done.5.refs_6_) | copy-start | bytes 786436
  34.0 0.9 %copy-start.14 = (bf16[8,128,128]{2,1,0:T(8,128)(2,1)}, bf16[8,128,128]{2,1,0:T(8,128)(2,1)S(1)}, u32[]{:S(2)}) copy-start(bf16[8,128,128]{2,1,0:T(8,128)(2,1)S(1)} %collective-permute-done.4.refs_5_) | copy-start | bytes 786436
  34.1 0.9 %copy-start.15 = (bf16[8,128,128]{2,1,0:T(8,128)(2,1)}, bf16[8,128,128]{2,1,0:T(8,128)(2,1)S(1)}, u32[]{:S(2)}) copy-start(bf16[8,128,128]{2,1,0:T(8,128)(2,1)S(1)} %collective-permute-done.8.refs_9_) | copy-start | bytes 786436
  34.1 1.0 %copy-start.16 = (bf16[8,128,128]{2,1,0:T(8,128)(2,1)}, bf16[8,128,128]{2,1,0:T(8,128)(2,1)S(1)}, u32[]{:S(2)}) copy-start(bf16[8,128,128]{2,1,0:T(8,128)(2,1)S(1)} %collective-permute-done.7.refs_8_) | copy-start | bytes 786436
  48.9 11.0 %collective-permute-start.13 = (bf16[1040,128]{1,0:T(8,128)(2,1)}, bf16[1040,128]{1,0:T(8,128)(2,1)S(1)}, u32[]{:S(2)}, u32[]{:S(2)}) collective-permute-start(bf16[1040,128]{1,0:T(8,128)(2,1)} %get-tuple-element.13), channel_id=1, source_target_pairs={{4,0},{6,2},{8,4},{10,6},{12,8},{14,10},{5,1},{7,3},{9,5},{11,7},{... | collective-permute-start | bytes 798728 | tf_op jit(solution)/shard_map/ppermute | solution.py:35
  51.3 11.9 %collective-permute-start.14 = (bf16[1040,128]{1,0:T(8,128)(2,1)}, bf16[1040,128]{1,0:T(8,128)(2,1)S(1)}, u32[]{:S(2)}, u32[]{:S(2)}) collective-permute-start(bf16[1040,128]{1,0:T(8,128)(2,1)} %get-tuple-element.14), channel_id=1, source_target_pairs={{2,0},{4,2},{6,4},{8,6},{10,8},{12,10},{14,12},{3,1},{5,3},{7,5},{... | collective-permute-start | bytes 798728 | tf_op jit(solution)/shard_map/ppermute | solution.py:35
  53.2 14.2 %collective-permute-start.15 = (bf16[1040,128]{1,0:T(8,128)(2,1)}, bf16[1040,128]{1,0:T(8,128)(2,1)S(1)}, u32[]{:S(2)}, u32[]{:S(2)}) collective-permute-start(bf16[1040,128]{1,0:T(8,128)(2,1)} %get-tuple-element.15), channel_id=1, source_target_pairs={{0,2},{2,4},{4,6},{6,8},{8,10},{10,12},{12,14},{1,3},{3,5},{5,7},{... | collective-permute-start | bytes 798728 | tf_op jit(solution)/shard_map/ppermute | solution.py:35
  58.0 10.7 %collective-permute-start.16 = (bf16[1040,128]{1,0:T(8,128)(2,1)}, bf16[1040,128]{1,0:T(8,128)(2,1)S(1)}, u32[]{:S(2)}, u32[]{:S(2)}) collective-permute-start(bf16[1040,128]{1,0:T(8,128)(2,1)} %get-tuple-element.16), channel_id=1, source_target_pairs={{0,4},{2,6},{4,8},{6,10},{8,12},{10,14},{1,5},{3,7},{5,9},{7,11},{... | collective-permute-start | bytes 798728 | tf_op jit(solution)/shard_map/ppermute | solution.py:35
  60.0 8.8 %copy-start = (bf16[1040,128]{1,0:T(8,128)(2,1)}, bf16[1040,128]{1,0:T(8,128)(2,1)S(1)}, u32[]{:S(2)}) copy-start(bf16[1040,128]{1,0:T(8,128)(2,1)S(1)} %collective-permute-done.13.refs_0_) | copy-start | bytes 798724
  63.2 5.6 %copy-start.1 = (bf16[1040,128]{1,0:T(8,128)(2,1)}, bf16[1040,128]{1,0:T(8,128)(2,1)S(1)}, u32[]{:S(2)}) copy-start(bf16[1040,128]{1,0:T(8,128)(2,1)S(1)} %collective-permute-done.14.refs_1_) | copy-start | bytes 798724
  67.4 1.4 %copy-start.2 = (bf16[1040,128]{1,0:T(8,128)(2,1)}, bf16[1040,128]{1,0:T(8,128)(2,1)S(1)}, u32[]{:S(2)}) copy-start(bf16[1040,128]{1,0:T(8,128)(2,1)S(1)} %collective-permute-done.15.refs_2_) | copy-start | bytes 798724
  68.8 0.7 copy-start.3
